TPU v7x, 32 devices: a whole 2x2x4 slice. The times are simulated.
32 devices in a mesh: groups: 2 (over y), pipe: 4 (over z), dp: 2 (over x), mp: 2 (over core).
Axes of the slice: x: 2, y: 2, z: 4, core: 2. Of those that a mesh axis runs over, the one named last changes fastest.
Arguments:
- latent: bfloat16 [4, 2, 2, 4, 16, 320], P(('groups', 'dp')), parts along dimension 0, may hold values from -6 to 6
- section_weight: bfloat16 [4, 2, 921600], P('pipe', None, 'mp'), may hold values from -0.01613743 to 0.01613743, as said below
- out_grad: bfloat16 [4, 2, 2, 4, 16, 320], P(('groups', 'dp')), parts along dimension 0, may hold values from -0.29882812 to 0.29882812
Outputs:
- section_grad: float32 [8, 921600], P(('groups', 'pipe'), 'mp'), parts along dimension 0
There are 2 independent parts, one for each index of `groups`. A program takes and returns all parts, laid end to end along the dimension named above; an argument that names none is the same for every part. Nothing has to cross between parts.
Inputs may be any that keep to these rules, and one draw needn't show every extreme that they name: section_weight[j, 0] equals section_weight[3 - j, 0] and section_weight[j, 1] equals section_weight[3 - j, 1] for every j: both devices of a mirrored pair hold the same two blocks.
All inputs are finite; a program needn't handle non-finite values.
Results may differ from a plain program's by a relative error of at most 0.0065.
Values may be sent and summed in bfloat16 or wider, within the bound.
No kernel may reach another device: no remote copies, remote signals or barrier semaphores. Data moves between devices by JAX's collectives and lax.ppermute only.
A program may use at most 64 MiB of HBM per device.

v0:
```python
import jax
import jax.numpy as jnp
from jax import lax
from jax.sharding import PartitionSpec as P


def shifted_2(block, axis, distance):
    devices = range(lax.axis_size(axis))
    route = [(i - distance, i) for i in devices if i - distance in devices]
    return lax.ppermute(block, axis, route)


def patches(image_in):
    img_rows, img_cols, channels = (image_in.shape[-3], image_in.shape[-2], image_in.shape[-1])
    padded = jnp.pad(image_in, [(0, 0)] * (image_in.ndim - 3) + [(1, 1), (1, 1), (0, 0)])
    shifted = [
        padded[..., row_off : row_off + img_rows, col_off : col_off + img_cols, :]
        for row_off in range(3)
        for col_off in range(3)
    ]
    return jnp.stack(shifted, axis=-2).reshape(-1, 9 * channels)


def silu_slope(pre_act):
    sigmoid = jax.nn.sigmoid(pre_act)
    return sigmoid * (1.0 + pre_act * (1.0 - sigmoid))


def mirror(payload):
    blocks = payload.reshape(lax.axis_size("pipe"), -1)
    spread = lax.all_to_all(blocks, "pipe", split_axis=0, concat_axis=0, tiled=True)
    returned = lax.all_to_all(jnp.flip(spread, 0), "pipe", split_axis=0, concat_axis=0, tiled=True)
    return returned.reshape(payload.shape)


def mirror_sums(payload):
    blocks = payload.reshape(lax.axis_size("pipe"), -1)
    spread = lax.all_to_all(blocks, "pipe", split_axis=0, concat_axis=0, tiled=True)
    returned = lax.all_to_all(jnp.flip(spread, 0), "pipe", split_axis=0, concat_axis=0, tiled=True)
    return returned.reshape(payload.shape)


def pass_on(payload, from_below):
    from_lower = shifted_2(payload, "pipe", 1)
    from_upper = shifted_2(payload, "pipe", -1)
    return (
        jnp.where(from_below, from_lower, from_upper),
        jnp.where(from_below, from_upper, from_lower),
    )


def take_slot(buffer, slot_index):
    return lax.dynamic_index_in_dim(buffer, slot_index, 0, keepdims=False)


def put_slot(buffer, payload, slot_index, active):
    return jnp.where(
        active, lax.dynamic_update_index_in_dim(buffer, payload, slot_index, 0), buffer
    )


def run_forward(source, skip_in, weight_half, position, from_below, tick_count):
    micro_count = source.shape[0]
    img_rows, img_cols, channels = (source.shape[1], source.shape[2], source.shape[3])
    chan_half = weight_half.shape[0] // (9 * channels)
    offset = lax.axis_index("mp") * chan_half
    row_weight = weight_half.reshape(chan_half, 9 * channels)

    def one_tick(tick_idx, state_carry):
        incoming, inputs, actives, outputs, crossed = state_carry
        micro_idx = tick_idx - position
        active = (micro_idx >= 0) & (micro_idx < micro_count)
        clipped = jnp.clip(micro_idx, 0, micro_count - 1)
        current = jnp.where(position == 0, take_slot(source, clipped), incoming)
        pre_act = current.astype(jnp.float32) + take_slot(skip_in, clipped).astype(jnp.float32)
        activation = jax.nn.silu(pre_act).astype(jnp.bfloat16)
        conv_out = lax.dot_general(
            patches(activation),
            row_weight,
            (((1,), (1,)), ((), ())),
            preferred_element_type=jnp.float32,
        )
        own_part = lax.dynamic_slice_in_dim(current, offset, chan_half, 2)
        output_half = (
            own_part.astype(jnp.float32) + conv_out.reshape(img_rows, img_cols, chan_half)
        ).astype(jnp.bfloat16)
        output = lax.all_gather(output_half, "mp", axis=2, tiled=True)
        chosen, other_side = pass_on(output, from_below)
        return (
            chosen,
            put_slot(inputs, current, clipped, active),
            put_slot(actives, activation, clipped, active),
            put_slot(outputs, output, clipped, active),
            put_slot(crossed, other_side, clipped, active),
        )

    initial = (
        jnp.zeros_like(source[0]),
        jnp.zeros_like(source),
        jnp.zeros_like(source),
        jnp.zeros_like(source),
        jnp.zeros_like(source),
    )
    final_state = lax.fori_loop(0, tick_count, one_tick, initial)
    return (final_state[1], final_state[2], final_state[3], final_state[4])


def run_backward(
    extra_cot, inputs, actives, skip_in, weight_half, position, from_below, tick_count, end_flag
):
    micro_count = inputs.shape[0]
    img_rows, img_cols, channels = (inputs.shape[1], inputs.shape[2], inputs.shape[3])
    chan_half = weight_half.shape[0] // (9 * channels)
    offset = lax.axis_index("mp") * chan_half
    back_weight = (
        jnp.flip(weight_half.reshape(chan_half, 3, 3, channels), (1, 2))
        .transpose(1, 2, 0, 3)
        .reshape(9 * chan_half, channels)
    )

    def one_tick(tick_idx, state_carry):
        incoming, cot_parts, skip_terms = state_carry
        micro_idx = tick_idx - position
        active = (micro_idx >= 0) & (micro_idx < micro_count)
        clipped = jnp.clip(micro_idx, 0, micro_count - 1)
        received = jnp.where(position == 0, 0.0, incoming.astype(jnp.float32))
        cotangent = (received + take_slot(extra_cot, clipped)).astype(jnp.bfloat16)
        cot_half = lax.dynamic_slice_in_dim(cotangent, offset, chan_half, 2)
        partial_value = jnp.dot(
            patches(cot_half), back_weight, preferred_element_type=jnp.float32
        ).reshape(img_rows, img_cols, channels)
        summed = lax.psum(partial_value, "mp")
        pre_act = take_slot(inputs, clipped).astype(jnp.float32) + take_slot(
            skip_in, clipped
        ).astype(jnp.float32)
        slope_term = summed * silu_slope(pre_act)
        passed = (cotangent.astype(jnp.float32) + slope_term).astype(jnp.bfloat16)
        skip_term = (slope_term + jnp.where(end_flag, passed.astype(jnp.float32), 0.0)).astype(
            jnp.bfloat16
        )
        chosen, other_side = pass_on(passed, from_below)
        return (
            chosen,
            put_slot(cot_parts, cot_half, clipped, active),
            put_slot(skip_terms, skip_term, clipped, active),
        )

    initial = (
        jnp.zeros_like(inputs[0]),
        jnp.zeros((micro_count, img_rows, img_cols, chan_half), jnp.bfloat16),
        jnp.zeros_like(inputs),
    )
    final_state = lax.fori_loop(0, tick_count, one_tick, initial)
    weight_grad = lax.dot_general(
        final_state[1].reshape(-1, chan_half),
        patches(actives),
        (((0,), (0,)), ((), ())),
        preferred_element_type=jnp.float32,
    )
    return (weight_grad.reshape(weight_half.shape), final_state[2])


def local(latent, section_weight, out_grad):
    pipe_size = lax.axis_size("pipe")
    half_size = pipe_size // 2
    device = lax.axis_index("pipe")
    lower_half = device < half_size
    upper_half = jnp.logical_not(lower_half)
    pair_index = jnp.minimum(device, pipe_size - 1 - device)
    tick_count = half_size + latent.shape[2] - 1
    encoder_weight = section_weight[0, 0]
    decoder_weight = section_weight[0, 1]
    first_dir = jnp.where(lower_half, 0, 1)
    samples = take_slot(latent[0], first_dir)
    zero_skip = jnp.zeros_like(samples)
    enc_inputs, enc_acts, enc_out, middle_in = run_forward(
        samples, zero_skip, encoder_weight, pair_index, lower_half, tick_count
    )
    skip_in = mirror(enc_out)
    dec_source = jnp.where(pair_index == half_size - 1, middle_in, skip_in)
    dec_inputs, dec_acts, dec_out, unused_in = run_forward(
        dec_source, skip_in, decoder_weight, half_size - 1 - pair_index, upper_half, tick_count
    )
    seed_cot = take_slot(out_grad[0], 1 - first_dir).astype(jnp.float32)
    seed_cot = jnp.where(pair_index == 0, seed_cot, 0.0)
    decoder_grad, dec_terms = run_backward(
        seed_cot,
        dec_inputs,
        dec_acts,
        skip_in,
        decoder_weight,
        pair_index,
        lower_half,
        tick_count,
        pair_index == half_size - 1,
    )
    terms_in = mirror(dec_terms).astype(jnp.float32)
    encoder_grad, enc_terms = run_backward(
        terms_in,
        enc_inputs,
        enc_acts,
        zero_skip,
        encoder_weight,
        half_size - 1 - pair_index,
        upper_half,
        tick_count,
        False,
    )
    kept_grad = jnp.where(lower_half, encoder_grad, decoder_grad)
    sent_grad = jnp.where(lower_half, decoder_grad, encoder_grad)
    combined = kept_grad + mirror_sums(sent_grad)
    combined = lax.psum(combined, "dp")
    return combined.reshape(1, -1)


def solution(mesh):
    return jax.shard_map(
        local,
        mesh=mesh,
        in_specs=(
            P(("groups", "dp"), None, None, None, None, None),
            P("pipe", None, "mp"),
            P(("groups", "dp"), None, None, None, None, None),
        ),
        out_specs=P(("groups", "pipe"), "mp"),
        check_vma=False,
    )
```

profile of v0, /device:TPU:0, one launch (start us, length us, event | category | flops | bytes accessed | tf_op | source)
XLA Modules:
  0.0 979.8 jit_solution(13960116564052826964)
XLA Ops:
  7.4 21.7 %slice_reduce_fusion = (bf16[460800]{0:T(1024)(128)(2,1)S(1)}, bf16[460800]{0:T(1024)(128)(2,1)}) fusion(bf16[1,2,460800]{2,1,0:T(2,128)(2,1)} %param.12), kind=kLoop, calls=%fused_computation.170 | loop fusion | bytes 3686400 | tf_op jit(solution)/shard_map/slice | solution.py:171
  31.8 46.2 %while.82 = (s32[]{:T(128)}, bf16[4,16,320]{2,1,0:T(8,128)(2,1)S(1)}, bf16[2,4,16,320]{3,2,1,0:T(8,128)(2,1)S(1)}, bf16[2,4,16,320]{3,2,1,0:T(8,128)(2,1)S(1)}, ...) while((s32[]{:T(128)}, ...), condition=%wide.region_1.2_spmd.clone, body=%wide.region_0.1_spmd.clone.sunk | while | flops 59545608 | bytes 6439339 | solution.py:104
  36.7 4.8 collective-permute-start
  43.2 4.3 collective-permute-done.1
  58.2 4.3 collective-permute-done.1
  73.1 4.3 collective-permute-done.1
  85.1 5.5 all-to-all-done
  108.3 8.3 rev.18
  118.0 11.2 %rev.21 = bf16[160,3,3,320]{3,2,1,0:T(4,128)(2,1)} reverse(bf16[160,3,3,320]{3,2,1,0:T(4,128)(2,1)} %reshape_squeeze.15), dimensions={1,2} | reverse | bytes 1843200 | tf_op jit(solution)/shard_map/jit(_flip)/rev | solution.py:116
  135.4 69.2 %while.83 = (s32[]{:T(128)}, bf16[4,16,320]{1,0,2:T(4,128)(2,1)}, bf16[2,4,16,320]{3,2,1,0:T(8,128)(2,1)}, bf16[2,4,16,320]{3,2,1,0:T(8,128)(2,1)S(1)}, pred[]{:...) while((s32[]{:T(128)}, bf16[4,16,320]{1,0,2:T(4,128)(2,1)}, ...), condition=%wide.region_3.4_spmd.clone, body=%wide.region_2.3_spmd.clone.sunk | while | flops 59279368 | bytes 5611900 | solution.py:104
  142.9 3.7 collective-permute-start.2
  148.0 5.9 collective-permute-done.2
  153.9 4.1 collective-permute-done.3
  170.9 5.9 collective-permute-done.2
  176.8 4.1 collective-permute-done.3
  193.8 5.9 collective-permute-done.2
  199.7 4.1 collective-permute-done.3
  205.7 95.1 %while.84 = (s32[]{:T(128)}, bf16[4,16,320]{2,1,0:T(8,128)(2,1)}, bf16[2,4,16,160]{3,2,1,0:T(8,128)(2,1)S(1)}, bf16[2,4,16,320]{3,2,1,0:T(8,128)(2,1)S(1)}, pred...) while((s32[]{:T(128)}, bf16[4,16,320]{2,1,0:T(8,128)(2,1)}, ...), condition=%wide.region_6.7_spmd.clone, body=%wide.region_4.6_spmd.clone.sunk | while | flops 59811848 | bytes 4673925 | solution.py:153
  208.8 16.3 %all-reduce.12.cloned.1.call-done = f32[4,16,320]{2,1,0:T(8,128)} async-done(((f32[4,16,320]{2,1,0:T(8,128)}), f32[4,16,320]{2,1,0:T(8,128)}) %all-reduce.12.cloned.1.call-update) | async-done | bytes 81936 | tf_op jit(solution)/shard_map/while/body/eval_jaxpr/psum | solution.py:132
  226.0 3.7 collective-permute-start.4
  231.9 3.7 collective-permute-done.5
  239.2 18.1 %all-reduce.12.cloned.1.call-done = f32[4,16,320]{2,1,0:T(8,128)} async-done(((f32[4,16,320]{2,1,0:T(8,128)}), f32[4,16,320]{2,1,0:T(8,128)}) %all-reduce.12.cloned.1.call-update) | async-done | bytes 81936 | tf_op jit(solution)/shard_map/while/body/eval_jaxpr/psum | solution.py:132
  258.3 3.7 collective-permute-start.4
  264.2 3.7 collective-permute-done.5
  271.5 18.1 %all-reduce.12.cloned.1.call-done = f32[4,16,320]{2,1,0:T(8,128)} async-done(((f32[4,16,320]{2,1,0:T(8,128)}), f32[4,16,320]{2,1,0:T(8,128)}) %all-reduce.12.cloned.1.call-update) | async-done | bytes 81936 | tf_op jit(solution)/shard_map/while/body/eval_jaxpr/psum | solution.py:132
  290.5 3.7 collective-permute-start.4
  296.5 3.7 collective-permute-done.5
  302.8 3.7 all-to-all-start.2
  307.8 4.5 all-to-all-done.2
  315.8 3.5 all-to-all-start.3
  325.6 94.5 %while.85 = (s32[]{:T(128)}, bf16[4,16,320]{2,1,0:T(8,128)(2,1)S(1)}, bf16[2,4,16,160]{3,2,1,0:T(8,128)(2,1)S(1)}, pred[]{:T(512)}, pred[]{:T(512)}, /*index=5*/...) while((s32[]{:T(128)}, ...), condition=%wide.region_9.10_spmd.clone, body=%wide.region_7.9_spmd.clone.sunk | while | flops 59381768 | bytes 3977547 | solution.py:153
  327.7 19.0 %all-reduce.14.cloned.1.call-done = f32[4,16,320]{2,1,0:T(8,128)} async-done(((f32[4,16,320]{2,1,0:T(8,128)}), f32[4,16,320]{2,1,0:T(8,128)}) %all-reduce.14.cloned.1.call-update) | async-done | bytes 81936 | tf_op jit(solution)/shard_map/while/body/eval_jaxpr/psum | solution.py:132
  347.7 3.7 collective-permute-start.6
  353.1 4.3 collective-permute-done.7
  359.5 18.7 %all-reduce.14.cloned.1.call-done = f32[4,16,320]{2,1,0:T(8,128)} async-done(((f32[4,16,320]{2,1,0:T(8,128)}), f32[4,16,320]{2,1,0:T(8,128)}) %all-reduce.14.cloned.1.call-update) | async-done | bytes 81936 | tf_op jit(solution)/shard_map/while/body/eval_jaxpr/psum | solution.py:132
  379.1 3.7 collective-permute-start.6
  384.5 4.3 collective-permute-done.7
  390.8 18.7 %all-reduce.14.cloned.1.call-done = f32[4,16,320]{2,1,0:T(8,128)} async-done(((f32[4,16,320]{2,1,0:T(8,128)}), f32[4,16,320]{2,1,0:T(8,128)}) %all-reduce.14.cloned.1.call-update) | async-done | bytes 81936 | tf_op jit(solution)/shard_map/while/body/eval_jaxpr/psum | solution.py:132
  410.4 3.7 collective-permute-start.6
  415.8 4.3 collective-permute-done.7
  422.9 4.7 select_n.488
  427.7 45.6 %all_to_all.62 = f32[4,1,115200]{2,1,0:T(1,128)S(1)} all-to-all(f32[4,1,115200]{2,1,0:T(1,128)} %select_n.488), channel_id=1, replica_groups=mesh['groups'=2,'pipe'=4,'dp'=2,'mp'=2] {'pipe'}, dimensions={0} | all-to-all | bytes 3686400 | tf_op jit(solution)/shard_map/all_to_all | solution.py:38
  475.0 383.0 %rev.22 = f32[4,115200]{1,0:T(4,128)} reverse(f32[4,115200]{1,0:T(4,128)} %bitcast.459), dimensions={0} | reverse | bytes 3686400 | tf_op jit(solution)/shard_map/jit(_flip)/rev | solution.py:39
  858.0 4.7 copy.61
  862.7 4.4 all-to-all-start.5
  869.4 39.5 %all-to-all-done.5 = f32[4,1,115200]{2,1,0:T(1,128)} async-done(((f32[4,1,115200]{2,1,0:T(1,128)}), f32[4,1,115200]{2,1,0:T(1,128)}, u32[]{:S(2)}, u32[]{:S(2)}) %all-to-all-start.5) | async-done | bytes 1843232 | tf_op jit(solution)/shard_map/all_to_all | solution.py:39
  912.3 56.3 %all-reduce.10.cloned.1.call-done = f32[1,460800]{1,0:T(1,128)} async-done(((f32[1,460800]{1,0:T(1,128)}), f32[1,460800]{1,0:T(1,128)}) %all-reduce.10.cloned.1.call-update) | async-done | bytes 1843216 | tf_op jit(solution)/shard_map/psum | solution.py:212
  968.7 3.7 copy.200
  (403 shorter events, 156.8 us)
Async XLA Ops:
  7.4 22.5 %copy-start = (bf16[1,2,2,4,16,320]{5,4,3,2,1,0:T(8,128)(2,1)S(1)}, bf16[1,2,2,4,16,320]{5,4,3,2,1,0:T(8,128)(2,1)}, u32[]{:S(2)}) copy-start(bf16[1,2,2,4,16,320]{5,4,3,2,1,0:T(8,128)(2,1)} %param.11) | copy-start | bytes 491524
  33.7 13.8 %copy-start.13 = (bf16[2,4,16,320]{3,2,1,0:T(8,128)(2,1)S(1)}, bf16[2,4,16,320]{3,2,1,0:T(8,128)(2,1)}, u32[]{:S(2)}) copy-start(bf16[2,4,16,320]{3,2,1,0:T(8,128)(2,1)} %get-tuple-element.1713) | copy-start | bytes 245764 | tf_op jit(solution)/shard_map/while
  36.7 6.6 collective-permute-start
  41.5 6.0 collective-permute-start.1
  50.1 12.4 %copy-start.13 = (bf16[2,4,16,320]{3,2,1,0:T(8,128)(2,1)S(1)}, bf16[2,4,16,320]{3,2,1,0:T(8,128)(2,1)}, u32[]{:S(2)}) copy-start(bf16[2,4,16,320]{3,2,1,0:T(8,128)(2,1)} %get-tuple-element.1713) | copy-start | bytes 245764 | tf_op jit(solution)/shard_map/while
  52.9 5.2 collective-permute-start
  56.4 6.0 collective-permute-start.1
  65.0 12.4 %copy-start.13 = (bf16[2,4,16,320]{3,2,1,0:T(8,128)(2,1)S(1)}, bf16[2,4,16,320]{3,2,1,0:T(8,128)(2,1)}, u32[]{:S(2)}) copy-start(bf16[2,4,16,320]{3,2,1,0:T(8,128)(2,1)} %get-tuple-element.1713) | copy-start | bytes 245764 | tf_op jit(solution)/shard_map/while
  67.9 5.2 collective-permute-start
  71.4 6.0 collective-permute-start.1
  78.1 19.7 %copy-start.7 = (bf16[2,4,16,320]{3,2,1,0:T(8,128)(2,1)}, bf16[2,4,16,320]{3,2,1,0:T(8,128)(2,1)S(1)}, u32[]{:S(2)}) copy-start(bf16[2,4,16,320]{3,2,1,0:T(8,128)(2,1)S(1)} %get-tuple-element.1837) | copy-start | bytes 245764
  78.1 19.7 %copy-start.2 = (bf16[460800]{0:T(1024)(128)(2,1)S(1)}, bf16[460800]{0:T(1024)(128)(2,1)}, u32[]{:S(2)}) copy-start(bf16[460800]{0:T(1024)(128)(2,1)} %get-tuple-element.1291) | copy-start | bytes 2764804
  81.5 9.1 all-to-all-start
  94.2 39.2 %all-to-all-start.1 = ((bf16[4,2,5120]{2,1,0:T(2,128)(2,1)}), bf16[4,2,5120]{2,1,0:T(2,128)(2,1)S(1)}, u32[]{:S(2)}, u32[]{:S(2)}) async-start(bf16[4,2,5120]{2,1,0:T(2,128)(2,1)} %reshape.168), calls=%async_computation.1 | async-start | bytes 163840 | tf_op jit(solution)/shard_map/all_to_all | solution.py:32
  142.9 11.0 %collective-permute-start.2 = (bf16[4,16,320]{1,0,2:T(4,128)(2,1)S(1)}, bf16[4,16,320]{1,0,2:T(4,128)(2,1)S(1)}, u32[]{:S(2)}, u32[]{:S(2)}) collective-permute-start(bf16[4,16,320]{1,0,2:T(4,128)(2,1)S(1)} %all_gather.25), channel_id=1, source_target_pairs={{0,4},{4,8},{8,12},{1,5},{5,9},{9,13},{2,6},{6,10},{10,14},{3,7},{... | collective-permute-start | bytes 122888 | tf_op jit(solution)/shard_map/while/body/eval_jaxpr/ppermute | solution.py:10
  146.6 11.4 %collective-permute-start.3 = (bf16[4,16,320]{1,0,2:T(4,128)(2,1)S(1)}, bf16[4,16,320]{1,0,2:T(4,128)(2,1)S(1)}, u32[]{:S(2)}, u32[]{:S(2)}) collective-permute-start(bf16[4,16,320]{1,0,2:T(4,128)(2,1)S(1)} %all_gather.25), channel_id=1, source_target_pairs={{4,0},{8,4},{12,8},{5,1},{9,5},{13,9},{6,2},{10,6},{14,10},{7,3},{... | collective-permute-start | bytes 122888 | tf_op jit(solution)/shard_map/while/body/eval_jaxpr/ppermute | solution.py:10
  148.0 10.8 %copy-start.4 = (bf16[2,4,16,320]{3,2,1,0:T(8,128)(2,1)}, bf16[2,4,16,320]{3,2,1,0:T(8,128)(2,1)S(1)}, u32[]{:S(2)}) copy-start(bf16[2,4,16,320]{3,2,1,0:T(8,128)(2,1)S(1)} %fusion.229) | copy-start | bytes 245764 | tf_op jit(solution)/shard_map/while
  166.2 10.6 %collective-permute-start.2 = (bf16[4,16,320]{1,0,2:T(4,128)(2,1)S(1)}, bf16[4,16,320]{1,0,2:T(4,128)(2,1)S(1)}, u32[]{:S(2)}, u32[]{:S(2)}) collective-permute-start(bf16[4,16,320]{1,0,2:T(4,128)(2,1)S(1)} %all_gather.25), channel_id=1, source_target_pairs={{0,4},{4,8},{8,12},{1,5},{5,9},{9,13},{2,6},{6,10},{10,14},{3,7},{... | collective-permute-start | bytes 122888 | tf_op jit(solution)/shard_map/while/body/eval_jaxpr/ppermute | solution.py:10
  169.5 11.4 %collective-permute-start.3 = (bf16[4,16,320]{1,0,2:T(4,128)(2,1)S(1)}, bf16[4,16,320]{1,0,2:T(4,128)(2,1)S(1)}, u32[]{:S(2)}, u32[]{:S(2)}) collective-permute-start(bf16[4,16,320]{1,0,2:T(4,128)(2,1)S(1)} %all_gather.25), channel_id=1, source_target_pairs={{4,0},{8,4},{12,8},{5,1},{9,5},{13,9},{6,2},{10,6},{14,10},{7,3},{... | collective-permute-start | bytes 122888 | tf_op jit(solution)/shard_map/while/body/eval_jaxpr/ppermute | solution.py:10
  170.9 10.8 %copy-start.4 = (bf16[2,4,16,320]{3,2,1,0:T(8,128)(2,1)}, bf16[2,4,16,320]{3,2,1,0:T(8,128)(2,1)S(1)}, u32[]{:S(2)}) copy-start(bf16[2,4,16,320]{3,2,1,0:T(8,128)(2,1)S(1)} %fusion.229) | copy-start | bytes 245764 | tf_op jit(solution)/shard_map/while
  189.1 10.6 %collective-permute-start.2 = (bf16[4,16,320]{1,0,2:T(4,128)(2,1)S(1)}, bf16[4,16,320]{1,0,2:T(4,128)(2,1)S(1)}, u32[]{:S(2)}, u32[]{:S(2)}) collective-permute-start(bf16[4,16,320]{1,0,2:T(4,128)(2,1)S(1)} %all_gather.25), channel_id=1, source_target_pairs={{0,4},{4,8},{8,12},{1,5},{5,9},{9,13},{2,6},{6,10},{10,14},{3,7},{... | collective-permute-start | bytes 122888 | tf_op jit(solution)/shard_map/while/body/eval_jaxpr/ppermute | solution.py:10
  192.5 11.4 %collective-permute-start.3 = (bf16[4,16,320]{1,0,2:T(4,128)(2,1)S(1)}, bf16[4,16,320]{1,0,2:T(4,128)(2,1)S(1)}, u32[]{:S(2)}, u32[]{:S(2)}) collective-permute-start(bf16[4,16,320]{1,0,2:T(4,128)(2,1)S(1)} %all_gather.25), channel_id=1, source_target_pairs={{4,0},{8,4},{12,8},{5,1},{9,5},{13,9},{6,2},{10,6},{14,10},{7,3},{... | collective-permute-start | bytes 122888 | tf_op jit(solution)/shard_map/while/body/eval_jaxpr/ppermute | solution.py:10
  205.7 19.3 %all-reduce.12.cloned.1.call-start = ((), (), s32[]{:S(2)}) async-start(), calls=%async_computation.7 | async-start | bytes 196608 | tf_op jit(solution)/shard_map/while/body/eval_jaxpr/psum | solution.py:132
  206.7 18.3 %copy-start.5 = (bf16[2,4,16,320]{3,2,1,0:T(8,128)(2,1)S(1)}, bf16[2,4,16,320]{3,2,1,0:T(8,128)(2,1)}, u32[]{:S(2)}) copy-start(bf16[2,4,16,320]{3,2,1,0:T(8,128)(2,1)} %get-tuple-element.1822) | copy-start | bytes 245764 | tf_op jit(solution)/shard_map/while
  226.0 5.9 collective-permute-start.4
  229.6 6.0 collective-permute-start.5
  236.2 21.1 %all-reduce.12.cloned.1.call-start = ((), (), s32[]{:S(2)}) async-start(), calls=%async_computation.7 | async-start | bytes 196608 | tf_op jit(solution)/shard_map/while/body/eval_jaxpr/psum | solution.py:132
  237.2 20.1 %copy-start.5 = (bf16[2,4,16,320]{3,2,1,0:T(8,128)(2,1)S(1)}, bf16[2,4,16,320]{3,2,1,0:T(8,128)(2,1)}, u32[]{:S(2)}) copy-start(bf16[2,4,16,320]{3,2,1,0:T(8,128)(2,1)} %get-tuple-element.1822) | copy-start | bytes 245764 | tf_op jit(solution)/shard_map/while
  258.3 5.9 collective-permute-start.4
  261.9 6.0 collective-permute-start.5
  268.5 21.1 %all-reduce.12.cloned.1.call-start = ((), (), s32[]{:S(2)}) async-start(), calls=%async_computation.7 | async-start | bytes 196608 | tf_op jit(solution)/shard_map/while/body/eval_jaxpr/psum | solution.py:132
  269.4 20.1 %copy-start.5 = (bf16[2,4,16,320]{3,2,1,0:T(8,128)(2,1)S(1)}, bf16[2,4,16,320]{3,2,1,0:T(8,128)(2,1)}, u32[]{:S(2)}) copy-start(bf16[2,4,16,320]{3,2,1,0:T(8,128)(2,1)} %get-tuple-element.1822) | copy-start | bytes 245764 | tf_op jit(solution)/shard_map/while
  290.5 5.9 collective-permute-start.4
  294.2 6.0 collective-permute-start.5
  302.8 9.5 all-to-all-start.2
  315.8 9.1 all-to-all-start.3
  325.6 94.5 %copy-start.9 = (bf16[128,2880]{1,0:T(8,128)(2,1)S(1)}, bf16[128,2880]{1,0:T(8,128)(2,1)}, u32[]{:S(2)}) copy-start(bf16[128,2880]{1,0:T(8,128)(2,1)} %reshape.146) | copy-start | bytes 2211844
  325.6 21.1 %all-reduce.14.cloned.1.call-start = ((), (), s32[]{:S(2)}) async-start(), calls=%async_computation.8 | async-start | bytes 196608 | tf_op jit(solution)/shard_map/while/body/eval_jaxpr/psum | solution.py:132
  347.7 5.4 collective-permute-start.6
  351.3 6.0 collective-permute-start.7
  357.4 20.8 %all-reduce.14.cloned.1.call-start = ((), (), s32[]{:S(2)}) async-start(), calls=%async_computation.8 | async-start | bytes 196608 | tf_op jit(solution)/shard_map/while/body/eval_jaxpr/psum | solution.py:132
  379.1 5.4 collective-permute-start.6
  382.7 6.0 collective-permute-start.7
  388.7 20.8 %all-reduce.14.cloned.1.call-start = ((), (), s32[]{:S(2)}) async-start(), calls=%async_computation.8 | async-start | bytes 196608 | tf_op jit(solution)/shard_map/while/body/eval_jaxpr/psum | solution.py:132
  410.4 5.4 collective-permute-start.6
  414.1 6.0 collective-permute-start.7
  862.7 46.2 %all-to-all-start.5 = ((f32[4,1,115200]{2,1,0:T(1,128)}), f32[4,1,115200]{2,1,0:T(1,128)}, u32[]{:S(2)}, u32[]{:S(2)}) async-start(f32[4,1,115200]{2,1,0:T(1,128)} %copy.61), calls=%async_computation.5 | async-start | bytes 3686400 | tf_op jit(solution)/shard_map/all_to_all | solution.py:39
  867.1 101.6 %all-reduce.10.cloned.1.call-start = ((), (), s32[]{:S(2)}) async-start(), calls=%async_computation.6 | async-start | bytes 3686400 | tf_op jit(solution)/shard_map/psum | solution.py:212
  (23 other events, 123.2 us)
Sparse Core Ops, SparseCore 0:
  209.0 16.0 all-reduce.11
  239.5 17.7 all-reduce.11
  271.7 17.7 all-reduce.11
  328.5 18.1 all-reduce.13
  360.3 17.7 all-reduce.13
  391.7 17.7 all-reduce.13
Sparse Core Ops, SparseCore 1:
  912.4 56.2 all-reduce.9
where the time goes:
time: 997 us; the launch traced here: 980 us
  local copies, waits for them, and re-layouts  493 us (49%)
  waiting for transfers between devices  284 us (28%)
  starting transfers between devices  78.3 us (8%)
  blocking collectives  58 us (6%)
  other arithmetic  34.1 us (3%)
  between operations  15.3 us (2%)
  matrix products  14.9 us (1%)
    rev x1, local copies, waits for them, and re-layouts, mirror_sums(): jnp.flip(spread, 0)  383 us
    psum x6, waiting for transfers between devices, one_tick(): summed = lax.psum(partial_value, 'mp')  109 us
    ppermute x24, waiting for transfers between devices, shifted_2(): return lax.ppermute(block, axis, route)  69 us
    ppermute x24, starting transfers between devices, shifted_2(): return lax.ppermute(block, axis, route)  59.7 us
    psum x1, waiting for transfers between devices, local(): combined = lax.psum(combined, 'dp')  56.3 us
    all_to_all x1, blocking collectives, mirror_sums(): lax.all_to_all(blocks, 'pipe', split_axis=0, concat_axis=0, tiled=True)  45.6 us
    all_to_all x1, waiting for transfers between devices, mirror_sums(): lax.all_to_all(jnp.flip(spread, 0), 'pipe', split_axis=0, concat_axis=0,...  39.5 us
    slice x1, local copies, waits for them, and re-layouts, local(): encoder_weight = section_weight[0, 0]  21.7 us
  transfers between devices with their start and end apart: 36, of which 32 were waited for; matrix products, arithmetic and copies ran while one was open for 5% of the time, Pallas kernels for 0%

commit v1 on v0

v1 whole, which is shorter than its diff:
```python
import jax
import jax.numpy as jnp
from jax import lax
from jax.sharding import PartitionSpec as P


def silu_slope(pre_act):
    sigmoid = jax.nn.sigmoid(pre_act)
    return sigmoid * (1.0 + pre_act * (1.0 - sigmoid))


def conv(act, weight):
    return lax.conv_general_dilated(
        act, weight, (1, 1), ((1, 1), (1, 1)),
        dimension_numbers=("NHWC", "OHWI", "NHWC"),
        preferred_element_type=jnp.float32,
    )


def conv_t(cot, weight):
    flipped = jnp.flip(cot, (1, 2))
    out = lax.conv_general_dilated(
        flipped, weight, (1, 1), ((1, 1), (1, 1)),
        dimension_numbers=("NHWC", "IHWO", "NHWC"),
        preferred_element_type=jnp.float32,
    )
    return jnp.flip(out, (1, 2))


def weight_grad(act, cot):
    return lax.conv_general_dilated(
        act, cot, (1, 1), ((1, 1), (1, 1)),
        dimension_numbers=("CHWN", "IHWO", "CHWN"),
        preferred_element_type=jnp.float32,
    )


def f32(v):
    return v.astype(jnp.float32)


def bf16(v):
    return v.astype(jnp.bfloat16)


def local(latent, section_weight, out_grad):
    pipe_size = lax.axis_size("pipe")
    half = pipe_size // 2
    device = lax.axis_index("pipe")
    lower = device < half
    stage = jnp.minimum(device, pipe_size - 1 - device)
    mp_size = lax.axis_size("mp")
    lane = lax.axis_index("mp")

    channels = latent.shape[-1]
    img = latent.shape[-3:]
    samples = latent.reshape((-1,) + img)
    grads = out_grad.reshape((-1,) + img)
    per_lane = samples.shape[0] // mp_size
    x0 = lax.dynamic_slice_in_dim(samples, lane * per_lane, per_lane, 0)
    seed = lax.dynamic_slice_in_dim(grads, lane * per_lane, per_lane, 0)

    chan_half = section_weight.shape[-1] // (9 * channels)
    full = lax.all_gather(section_weight[0], "mp", axis=1, tiled=True)
    out_channels = chan_half * mp_size
    w_enc = full[0].reshape(out_channels, 3, 3, channels)
    w_dec = full[1].reshape(out_channels, 3, 3, channels)

    def up(t, v):
        pairs = [(t, t + 1), (pipe_size - 1 - t, pipe_size - 2 - t)]
        return lax.ppermute(v, "pipe", pairs)

    def down(t, v):
        pairs = [(t, t - 1), (pipe_size - 1 - t, pipe_size - t)]
        return lax.ppermute(v, "pipe", pairs)

    u0 = f32(x0)
    a0 = bf16(jax.nn.silu(u0))
    h1 = bf16(u0 + conv(a0, w_enc))
    d_last = conv_t(seed, w_dec)
    h1_r = up(0, h1)
    d_last_r = up(0, d_last)

    enc_in, enc_act, enc_out = {}, {}, {}
    enc_in[0], enc_act[0], enc_out[0] = x0, a0, h1
    received = h1_r
    for t in range(1, half):
        h_in = received
        u = f32(h_in)
        a = bf16(jax.nn.silu(u))
        h_out = bf16(u + conv(a, w_enc))
        enc_in[t], enc_act[t], enc_out[t] = h_in, a, h_out
        if t < half - 1:
            received = up(t, h_out)

    dec_u, dec_act, dec_c = {}, {}, {}
    h_in = enc_out[half - 1]
    u = f32(h_in) + f32(h_in)
    a = bf16(jax.nn.silu(u))
    current = bf16(f32(h_in) + conv(a, w_dec))
    dec_u[half - 1], dec_act[half - 1] = u, a
    for t in range(half - 2, 0, -1):
        h_in = down(t + 1, current)
        u = f32(h_in) + f32(enc_out[t])
        a = bf16(jax.nn.silu(u))
        current = bf16(f32(h_in) + conv(a, w_dec))
        dec_u[t], dec_act[t] = u, a

    u_last = f32(current) + f32(h1_r)
    a_last = bf16(jax.nn.silu(u_last))
    b_last = d_last_r * silu_slope(u_last)
    skip = {1: bf16(b_last)}
    a_last_r = lax.ppermute(a_last, "pipe", [(pipe_size - 2, pipe_size - 1)])
    cot = bf16(f32(seed) + b_last)

    for t in range(1, half):
        if t > 1:
            cot = up(t - 1, cot)
        dec_c[t] = cot
        d = conv_t(cot, w_dec)
        b = d * silu_slope(dec_u[t])
        g = bf16(f32(cot) + b)
        if t < half - 1:
            skip[t + 1] = bf16(b)
            cot = g
        else:
            cot = bf16(f32(g) + b)

    enc_c = {}
    for t in range(half - 1, 0, -1):
        if t < half - 1:
            cot = bf16(f32(down(t + 1, cot)) + f32(skip[t + 1]))
        enc_c[t] = cot
        d = conv_t(cot, w_enc)
        b = d * silu_slope(f32(enc_in[t]))
        cot = bf16(f32(cot) + b)
    c0 = bf16(f32(cot) + f32(skip[1]))
    c0_r = lax.ppermute(c0, "pipe", [(1, 0)])

    acts_lo = jnp.stack([a0] + [enc_act[t] for t in range(1, half)])
    cots_lo = jnp.stack([c0_r] + [enc_c[t] for t in range(1, half)])
    acts_up = jnp.stack([a_last_r] + [dec_act[t] for t in range(1, half)])
    cots_up = jnp.stack([seed] + [dec_c[t] for t in range(1, half)])
    act_sel = jnp.where(lower, acts_lo[stage], acts_up[stage])
    cot_sel = jnp.where(lower, cots_lo[stage], cots_up[stage])

    both = jnp.concatenate([act_sel, cot_sel], axis=-1)
    every = lax.all_gather(both, ("dp", "mp"), axis=0, tiled=True)
    act_all = every[..., :channels]
    cot_all = lax.dynamic_slice_in_dim(every, channels + lane * chan_half, chan_half, 3)
    grad = weight_grad(act_all, cot_all)
    return grad.reshape(1, -1)


def solution(mesh):
    return jax.shard_map(
        local,
        mesh=mesh,
        in_specs=(
            P(("groups", "dp"), None, None, None, None, None),
            P("pipe", None, "mp"),
            P(("groups", "dp"), None, None, None, None, None),
        ),
        out_specs=P(("groups", "pipe"), "mp"),
        check_vma=False,
    )
```

time: 997 us -> 140 us (0.14); the launches traced: 980 us -> 139 us
  local copies, waits for them, and re-layouts: 493 us -> 72.5 us
  waiting for transfers between devices: 284 us -> 20 us
  starting transfers between devices: 78.3 us -> 7.07 us
  blocking collectives: 58 us -> 8.08 us
  other arithmetic: 34.1 us -> 5.75 us
    rev x5 -> x9, local copies, waits for them, and re-layouts: 407 us -> 8.19 us  [the longest x6 4.98 us: conv_t(): flipped = jnp.flip(cot, (1, 2))]
    psum x7 -> x0, waiting for transfers between devices: 165 us -> none  [the longest x6 109 us: one_tick(): summed = lax.psum(partial_value, 'mp')]
    ppermute x24 -> x4, waiting for transfers between devices: 69 us -> 5.9 us  [the longest x1 4.41 us: local(): c0_r = lax.ppermute(c0, 'pipe', [(1, 0)])]
    ppermute x24 -> x4, starting transfers between devices: 59.7 us -> 7.07 us  [the longest x2 5.11 us: up(): return lax.ppermute(v, 'pipe', pairs)]
    all_to_all x5 -> x0, waiting for transfers between devices: 50.3 us -> none  [the longest x1 39.5 us: mirror_sums(): lax.all_to_all(jnp.flip(spread, 0), 'pipe', split_axis=0, concat_axis=0,...]
    all_to_all x1 -> x0, blocking collectives: 45.6 us -> none  [mirror_sums(): lax.all_to_all(blocks, 'pipe', split_axis=0, concat_axis=0, tiled=True)]
    slice x1 -> x2, local copies, waits for them, and re-layouts: 21.7 us -> 41.4 us  [the longest x1 41.4 us: local(): w_enc = full[0].reshape(out_channels, 3, 3, channels)]
    all_to_all x5 -> x0, starting transfers between devices: 18.4 us -> none  [the longest x2 6.99 us: mirror(): lax.all_to_all(jnp.flip(spread, 0), 'pipe', split_axis=0, concat_axis=0,...]
  transfers between devices with their start and end apart: 36 -> 5, of which waited for: 32 -> 3; matrix products, arithmetic and copies ran while one was open for 5% -> 6% of each run, Pallas kernels for 0% -> 0%
where the time goes in v1:
time: 140 us; the launch traced here: 139 us
  local copies, waits for them, and re-layouts  72.5 us (52%)
  waiting for transfers between devices  20 us (14%)
  between operations  13.9 us (10%)
  matrix products  11.9 us (8%)
  blocking collectives  8.08 us (6%)
  starting transfers between devices  7.07 us (5%)
  other arithmetic  5.75 us (4%)
    slice x1, local copies, waits for them, and re-layouts, local(): w_enc = full[0].reshape(out_channels, 3, 3, channels)  41.4 us
    all_gather x1, waiting for transfers between devices, local(): full = lax.all_gather(section_weight[0], 'mp', axis=1, tiled=True)  13.4 us
    all_gather x1, blocking collectives, local(): every = lax.all_gather(both, ('dp', 'mp'), axis=0, tiled=True)  8.08 us
    another operation x1, local copies, waits for them, and re-layouts, local(): w_dec = full[1].reshape(out_channels, 3, 3, channels)  7.28 us
    conv_general_dilated x3, matrix products, conv_t(): lax.conv_general_dilated(flipped, weight, (1, 1), ((1, 1), (1, 1)), dimen...  5.93 us
    ppermute x2, starting transfers between devices, up(): return lax.ppermute(v, 'pipe', pairs)  5.11 us
    conv_general_dilated x3, matrix products, conv(): lax.conv_general_dilated(act, weight, (1, 1), ((1, 1), (1, 1)), dimension...  5.07 us
    rev x6, local copies, waits for them, and re-layouts, conv_t(): flipped = jnp.flip(cot, (1, 2))  4.98 us
  transfers between devices with their start and end apart: 5, of which 3 were waited for; matrix products, arithmetic and copies ran while one was open for 6% of the time, Pallas kernels for 0%

profile of v1, /device:TPU:0, one launch (start us, length us, event | category | flops | bytes accessed | tf_op | source)
XLA Modules:
  0.0 139.2 jit_solution(5886287574734781006)
XLA Ops:
  6.5 0.7 all-gather.3.cloned.1.call-update
  7.3 1.0 copy.64
  8.3 0.3 rev.20
  8.8 0.1 fusion.113
  9.1 0.7 slice.26
  9.7 0.7 fusion.111
  10.4 0.8 fusion.109
  11.1 13.4 %all-gather.3.cloned.1.call-done = bf16[1,2,921600]{2,1,0:T(2,128)(2,1)} async-done(((bf16[1,2,460800]{2,1,0:T(2,128)(2,1)}), bf16[1,2,921600]{2,1,0:T(2,128)(2,1)}) %all-gather.3.cloned.1.call-update) | async-done | bytes 3686416 | tf_op jit(solution)/shard_map/all_gather | solution.py:64
  24.6 41.4 %slice_reduce_fusion.1 = (bf16[921600]{0:T(1024)(128)(2,1)S(1)}, bf16[921600]{0:T(1024)(128)(2,1)}) fusion(bf16[1,2,921600]{2,1,0:T(2,128)(2,1)} %all-gather.3.cloned.1.call-done), kind=kLoop, calls=%fused_computation.1 | loop fusion | bytes 7372800 | tf_op jit(solution)/shard_map/slice | solution.py:66
  65.9 7.3 %reshape_squeeze.7 = bf16[320,3,3,320]{3,2,1,0:T(4,128)(2,1)} reshape(bf16[921600]{0:T(1024)(128)(2,1)} %get-tuple-element.6) | data formatting | bytes 3686400 | tf_op jit(solution)/shard_map/reshape;squeeze | solution.py:67
  73.2 2.6 %convolution_select_fusion.2 = f32[4,16,3,320]{3,1,2,0:T(8,128)S(1)} fusion(bf16[320,3,3,320]{3,2,1,0:T(4,128)(2,1)} %reshape_squeeze.7, bf16[4,2,7,2,320]{4,2,1,3,0:T(8,128)(2,1)S(1)} %slice.34, bf16[4,2,8,3,320]{4,2,1,3,0:T(8,128)(2,1)S(1)} %copy.66, pred[16,3]{0,1:T(4,128)(4,1)S(1)} %copy-done.6), kind=kOutput, calls=%fused_computation.4 | convolution fusion | flops 295587840 | bytes 2283568 | tf_op jit(solution)/shard_map/conv_general_dilated | solution.py:22
  75.8 0.8 copy.68
  76.6 4.6 %reshape_squeeze.6 = bf16[320,3,3,320]{3,2,1,0:T(4,128)(2,1)} reshape(bf16[921600]{0:T(1024)(128)(2,1)S(1)} %get-tuple-element.5) | data formatting | bytes 3686400 | tf_op jit(solution)/shard_map/reshape;squeeze | solution.py:66
  81.2 3.0 %convolution_select_fusion.5 = f32[4,16,3,320]{3,1,2,0:T(8,128)S(1)} fusion(bf16[320,3,3,320]{3,2,1,0:T(4,128)(2,1)} %reshape_squeeze.6, bf16[4,2,7,2,320]{4,2,1,3,0:T(8,128)(2,1)} %slice.26, bf16[4,2,8,3,320]{4,2,1,3,0:T(8,128)(2,1)S(1)} %copy.53, pred[16,3]{0,1:T(4,128)(4,1)S(1)} %copy-done.6), kind=kOutput, calls=%fused_computation.7 | convolution fusion | flops 295587840 | bytes 2283568 | tf_op jit(solution)/shard_map/conv_general_dilated | solution.py:13
  84.3 0.1 copy.55
  84.4 0.7 fusion.65
  85.1 3.6 %collective-permute-start = (bf16[2,4,16,320]{3,1,2,0:T(4,128)(2,1)}, bf16[2,4,16,320]{3,1,2,0:T(4,128)(2,1)S(1)}, u32[]{:S(2)}, u32[]{:S(2)}) collective-permute-start(bf16[2,4,16,320]{3,1,2,0:T(4,128)(2,1)} %fusion.65), channel_id=1, source_target_pairs={{0,4},{12,8},{1,5},{13,9},{2,6},{14,10},{3,7},{15,11},{16,20},{28,... | collective-permute-start | bytes 245768 | tf_op jit(solution)/shard_map/ppermute | solution.py:71
  88.8 1.4 %rev.21 = f32[2,4,16,320]{3,1,2,0:T(4,128)} reverse(f32[2,4,16,320]{3,1,2,0:T(4,128)S(1)} %slice_bitcast_fusion.2), dimensions={1,2} | reverse | bytes 327680 | tf_op jit(solution)/shard_map/jit(_flip)/rev | solution.py:27
  90.2 1.5 %collective-permute-start.2 = (f32[2,4,16,320]{3,1,2,0:T(4,128)}, f32[2,4,16,320]{3,1,2,0:T(4,128)S(1)}, u32[]{:S(2)}, u32[]{:S(2)}) collective-permute-start(f32[2,4,16,320]{3,1,2,0:T(4,128)} %rev.21), channel_id=1, source_target_pairs={{0,4},{12,8},{1,5},{13,9},{2,6},{14,10},{3,7},{15,11},{16,20},{28,... | collective-permute-start | bytes 491528 | tf_op jit(solution)/shard_map/ppermute | solution.py:71
  92.0 1.0 convolution_select_fusion.4
  93.0 0.1 copy.59
  93.1 0.1 fusion.57
  93.4 0.4 copy-done.1
  93.8 1.0 convolution_select_fusion.3
  94.8 0.1 copy.63
  95.0 1.5 %collective-permute-done.2 = f32[2,4,16,320]{3,1,2,0:T(4,128)S(1)} collective-permute-done((f32[2,4,16,320]{3,1,2,0:T(4,128)}, f32[2,4,16,320]{3,1,2,0:T(4,128)S(1)}, u32[]{:S(2)}, u32[]{:S(2)}) %collective-permute-start.2) | collective-permute-done | bytes 163872 | tf_op jit(solution)/shard_map/ppermute | solution.py:71
  96.4 0.9 add_convert_fusion.3
  97.4 1.4 rev.22
  98.8 0.9 pad.8
  99.8 2.6 %convolution_select_fusion.1 = f32[4,16,3,320]{3,1,2,0:T(8,128)S(1)} fusion(bf16[320,3,3,320]{3,2,1,0:T(4,128)(2,1)} %reshape_squeeze.7, bf16[4,2,7,2,320]{4,2,1,3,0:T(8,128)(2,1)S(1)} %slice.36, bf16[4,2,8,3,320]{4,2,1,3,0:T(8,128)(2,1)S(1)} %copy.70, pred[16,3]{0,1:T(4,128)(4,1)S(1)} %copy-done.6), kind=kOutput, calls=%fused_computation.3 | convolution fusion | flops 295587840 | bytes 2283568 | tf_op jit(solution)/shard_map/conv_general_dilated | solution.py:22
  102.5 1.4 %rev.23 = f32[2,4,16,320]{3,1,2,0:T(4,128)} reverse(f32[2,4,16,320]{3,1,2,0:T(4,128)S(1)} %slice_bitcast_fusion.1), dimensions={1,2} | reverse | bytes 327680 | tf_op jit(solution)/shard_map/jit(_flip)/rev | solution.py:27
  103.9 1.1 add_convert_fusion.1
  105.1 1.4 rev.24
  106.5 0.9 pad.10
  107.5 0.8 convolution_select_fusion
  108.4 0.3 rev.25
  108.8 1.1 add_convert_fusion
  109.9 1.3 collective-permute-start.3
  111.3 0.7 collective-permute-start.1
  112.0 4.4 %collective-permute-done.3 = bf16[2,4,16,320]{3,1,2,0:T(4,128)(2,1)S(1)} collective-permute-done((bf16[2,4,16,320]{3,1,2,0:T(4,128)(2,1)S(1)}, bf16[2,4,16,320]{3,1,2,0:T(4,128)(2,1)S(1)}, u32[]{:S(2)}, u32[]{:S(2)}) %collective-permute-start.3) | collective-permute-done | bytes 81952 | tf_op jit(solution)/shard_map/ppermute | solution.py:138
  116.4 0.2 fusion.89
  116.6 0.3 fusion.88
  116.9 0.1 pad_maximum_fusion
  117.1 8.1 %all_gather.7 = bf16[8,4,16,640]{3,2,1,0:T(8,128)(2,1)S(1)} all-gather(bf16[2,4,16,640]{3,2,1,0:T(8,128)(2,1)S(1)} %copy.77), channel_id=1, replica_groups=mesh['groups'=2,'pipe'=4,'dp'=2,'mp'=2] {'dp','mp'}, dimensions={0}, use_global_device_ids=true | all-gather | bytes 819200 | tf_op jit(solution)/shard_map/all_gather | solution.py:148
  125.2 0.2 constant_dynamic-slice_fusion.1
  125.4 0.9 fusion.12
  126.2 1.5 %copy.80 = f32[160,3,3,320]{3,2,1,0:T(4,128)S(1)} copy(f32[160,3,3,320]{3,0,2,1:T(8,128)S(1)} %fusion.12) | data formatting | bytes 3686400 | tf_op jit(solution)/shard_map/conv_general_dilated | solution.py:31
  127.7 4.6 %reshape.15 = f32[1,460800]{1,0:T(1,128)} reshape(f32[160,3,3,320]{3,2,1,0:T(4,128)S(1)} %copy.80) | data formatting | bytes 3686400 | tf_op jit(solution)/shard_map/reshape | solution.py:152
  (42 shorter events, 1.2 us)
Async XLA Ops:
  6.5 2.2 %copy-start.5 = (bf16[1,2,2,4,16,320]{5,4,3,2,1,0:T(8,128)(2,1)S(1)}, bf16[1,2,2,4,16,320]{5,4,3,2,1,0:T(8,128)(2,1)}, u32[]{:S(2)}) copy-start(bf16[1,2,2,4,16,320]{5,4,3,2,1,0:T(8,128)(2,1)} %param.3) | copy-start | bytes 491524
  6.5 18.0 %all-gather.3.cloned.1.call-start = ((), (), s32[]{:S(2)}) async-start(), calls=%async_computation | async-start | bytes 5529600 | tf_op jit(solution)/shard_map/all_gather | solution.py:64
  65.9 7.3 %copy-start.6 = (pred[16,3]{0,1:T(4,128)(4,1)S(1)}, pred[16,3]{0,1:T(4,128)(4,1)}, u32[]{:S(2)}) copy-start(pred[16,3]{0,1:T(4,128)(4,1)} %constant.58) | copy-start | bytes 148
  81.2 7.5 %copy-start.2 = (f32[4,16,3,320]{3,0,2,1:T(4,128)S(1)}, f32[4,16,3,320]{3,0,2,1:T(4,128)}, u32[]{:S(2)}) copy-start(f32[4,16,3,320]{3,0,2,1:T(4,128)} %copy.68) | copy-start | bytes 737284
  81.2 10.7 %copy-start = (bf16[320,3,3,320]{3,2,1,0:T(4,128)(2,1)S(1)}, bf16[320,3,3,320]{3,2,1,0:T(4,128)(2,1)}, u32[]{:S(2)}) copy-start(bf16[320,3,3,320]{3,2,1,0:T(4,128)(2,1)} %reshape_squeeze.6) | copy-start | bytes 5529604
  85.1 6.6 %collective-permute-start = (bf16[2,4,16,320]{3,1,2,0:T(4,128)(2,1)}, bf16[2,4,16,320]{3,1,2,0:T(4,128)(2,1)S(1)}, u32[]{:S(2)}, u32[]{:S(2)}) collective-permute-start(bf16[2,4,16,320]{3,1,2,0:T(4,128)(2,1)} %fusion.65), channel_id=1, source_target_pairs={{0,4},{12,8},{1,5},{13,9},{2,6},{14,10},{3,7},{15,11},{16,20},{28,... | collective-permute-start | bytes 245768 | tf_op jit(solution)/shard_map/ppermute | solution.py:71
  90.2 6.2 %collective-permute-start.2 = (f32[2,4,16,320]{3,1,2,0:T(4,128)}, f32[2,4,16,320]{3,1,2,0:T(4,128)S(1)}, u32[]{:S(2)}, u32[]{:S(2)}) collective-permute-start(f32[2,4,16,320]{3,1,2,0:T(4,128)} %rev.21), channel_id=1, source_target_pairs={{0,4},{12,8},{1,5},{13,9},{2,6},{14,10},{3,7},{15,11},{16,20},{28,... | collective-permute-start | bytes 491528 | tf_op jit(solution)/shard_map/ppermute | solution.py:71
  92.0 1.8 %copy-start.1 = (bf16[320,3,3,320]{3,2,1,0:T(4,128)(2,1)S(1)}, bf16[320,3,3,320]{3,2,1,0:T(4,128)(2,1)}, u32[]{:S(2)}) copy-start(bf16[320,3,3,320]{3,2,1,0:T(4,128)(2,1)} %reshape_squeeze.7) | copy-start | bytes 5529604
  108.2 8.1 %copy-start.4 = (bf16[1,2,4,16,320]{4,2,3,1,0:T(4,128)(2,1)S(1)}, bf16[1,2,4,16,320]{4,2,3,1,0:T(4,128)(2,1)}, u32[]{:S(2)}) copy-start(bf16[1,2,4,16,320]{4,2,3,1,0:T(4,128)(2,1)} %fusion.111) | copy-start | bytes 245764
  108.2 8.4 %copy-start.3 = (bf16[1,2,4,16,320]{4,2,3,1,0:T(4,128)(2,1)S(1)}, bf16[1,2,4,16,320]{4,2,3,1,0:T(4,128)(2,1)}, u32[]{:S(2)}) copy-start(bf16[1,2,4,16,320]{4,2,3,1,0:T(4,128)(2,1)} %fusion.109) | copy-start | bytes 245764
  109.9 6.5 %collective-permute-start.3 = (bf16[2,4,16,320]{3,1,2,0:T(4,128)(2,1)S(1)}, bf16[2,4,16,320]{3,1,2,0:T(4,128)(2,1)S(1)}, u32[]{:S(2)}, u32[]{:S(2)}) collective-permute-start(bf16[2,4,16,320]{3,1,2,0:T(4,128)(2,1)S(1)} %add_convert_fusion), channel_id=1, source_target_pairs={{4,0},{5,1},{6,2},{7,3},{20,16},{21,17},{22,18},{23,19}} | collective-permute-start | bytes 245768 | tf_op jit(solution)/shard_map/ppermute | solution.py:138
  111.3 5.3 %collective-permute-start.1 = (bf16[2,4,16,320]{3,1,2,0:T(4,128)(2,1)}, bf16[2,4,16,320]{3,1,2,0:T(4,128)(2,1)S(1)}, u32[]{:S(2)}, u32[]{:S(2)}) collective-permute-start(bf16[2,4,16,320]{3,1,2,0:T(4,128)(2,1)} %get-tuple-element.11), channel_id=1, source_target_pairs={{8,12},{9,13},{10,14},{11,15},{24,28},{25,29},{26,30},{27,31}} | collective-permute-start | bytes 245768 | tf_op jit(solution)/shard_map/ppermute | solution.py:113
Sparse Core Ops, SparseCore 0:
  8.9 15.6 all-gather.2

commit v2 on v1

--- a/solution.py
+++ b/solution.py
@@ -61,10 +61,9 @@
     seed = lax.dynamic_slice_in_dim(grads, lane * per_lane, per_lane, 0)
 
     chan_half = section_weight.shape[-1] // (9 * channels)
-    full = lax.all_gather(section_weight[0], "mp", axis=1, tiled=True)
-    out_channels = chan_half * mp_size
-    w_enc = full[0].reshape(out_channels, 3, 3, channels)
-    w_dec = full[1].reshape(out_channels, 3, 3, channels)
+    halves = section_weight[0].reshape(2, chan_half, 3, 3, channels)
+    full = lax.all_gather(halves, "mp", axis=1, tiled=True)
+    w_enc, w_dec = full[0], full[1]
 
     def up(t, v):
         pairs = [(t, t + 1), (pipe_size - 1 - t, pipe_size - 2 - t)]

time: 140 us -> 88.7 us (0.63)
  local copies, waits for them, and re-layouts: 72.5 us -> 22.6 us
  other arithmetic: 5.75 us -> 2 us
  matrix products: 11.9 us -> 14.4 us
    slice x1 -> x0, local copies, waits for them, and re-layouts: 41.4 us -> none  [local(): w_enc = full[0].reshape(out_channels, 3, 3, channels)]
    another operation x2, local copies, waits for them, and re-layouts: 11.9 us -> 7.77 us  [local(): halves = section_weight[0].reshape(2, chan_half, 3, 3, channels)]
    rev x6, local copies, waits for them, and re-layouts: 4.98 us -> 1.01 us  [conv_t(): flipped = jnp.flip(cot, (1, 2))]
    unnamed x16 -> x11, local copies, waits for them, and re-layouts: 1.51 us -> 5.21 us
    convert_element_type x7, other arithmetic: 4.25 us -> 1.12 us  [bf16(): return v.astype(jnp.bfloat16)]
    rev x3, local copies, waits for them, and re-layouts: 3.21 us -> 1 us  [conv_t(): return jnp.flip(out, (1, 2))]
    all_gather x1, waiting for transfers between devices: 13.4 us -> 14.9 us  [local(): full = lax.all_gather(halves, 'mp', axis=1, tiled=True)]
  transfers between devices with their start and end apart: 5 -> 5, of which waited for: 3 -> 3; matrix products, arithmetic and copies ran while one was open for 6% -> 9% of each run, Pallas kernels for 0% -> 0%
where the time goes in v2:
time: 88.7 us; the launch traced here: 88.3 us
  local copies, waits for them, and re-layouts  22.6 us (25%)
  waiting for transfers between devices  20.4 us (23%)
  matrix products  14.4 us (16%)
  between operations  13.9 us (16%)
  blocking collectives  7.86 us (9%)
  starting transfers between devices  7.1 us (8%)
  other arithmetic  2 us (2%)
    all_gather x1, waiting for transfers between devices, local(): full = lax.all_gather(halves, 'mp', axis=1, tiled=True)  14.9 us
    all_gather x1, blocking collectives, local(): every = lax.all_gather(both, ('dp', 'mp'), axis=0, tiled=True)  7.86 us
    another operation x2, local copies, waits for them, and re-layouts, local(): halves = section_weight[0].reshape(2, chan_half, 3, 3, channels)  7.77 us
    conv_general_dilated x3, matrix products, conv_t(): lax.conv_general_dilated(flipped, weight, (1, 1), ((1, 1), (1, 1)), dimen...  7.29 us
    conv_general_dilated x3, matrix products, conv(): lax.conv_general_dilated(act, weight, (1, 1), ((1, 1), (1, 1)), dimension...  6.29 us
    unnamed x11, local copies, waits for them, and re-layouts  5.21 us
    ppermute x2, starting transfers between devices, up(): return lax.ppermute(v, 'pipe', pairs)  4.96 us
    reshape x1, local copies, waits for them, and re-layouts, local(): return grad.reshape(1, -1)  4.57 us
  transfers between devices with their start and end apart: 5, of which 3 were waited for; matrix products, arithmetic and copies ran while one was open for 9% of the time, Pallas kernels for 0%

profile of v2, /device:TPU:0, one launch (start us, length us, event | category | flops | bytes accessed | tf_op | source)
XLA Modules:
  0.0 88.3 jit_solution(8419242096322244493)
XLA Ops:
  6.5 3.9 %reshape.76 = bf16[921600]{0:T(1024)(128)(2,1)} reshape(bf16[1,2,460800]{2,1,0:T(2,128)(2,1)} %param.4) | data formatting | bytes 3686400
  10.4 6.1 %reshape_squeeze.3 = bf16[2,160,3,3,320]{4,3,2,1,0:T(4,128)(2,1)S(1)} reshape(bf16[921600]{0:T(1024)(128)(2,1)} %reshape.76) | data formatting | bytes 3686400 | tf_op jit(solution)/shard_map/reshape;squeeze | solution.py:64
  16.5 1.7 %copy.49 = bf16[2,160,3,3,320]{4,1,3,2,0:T(8,128)(2,1)} copy(bf16[2,160,3,3,320]{4,3,2,1,0:T(4,128)(2,1)S(1)} %reshape_squeeze.3) | data formatting | bytes 3686400 | tf_op jit(solution)/shard_map/reshape;squeeze | solution.py:64
  18.3 0.9 %copy-done = bf16[1,2,2,4,16,320]{5,4,3,2,1,0:T(8,128)(2,1)S(1)} copy-done((bf16[1,2,2,4,16,320]{5,4,3,2,1,0:T(8,128)(2,1)S(1)}, bf16[1,2,2,4,16,320]{5,4,3,2,1,0:T(8,128)(2,1)}, u32[]{:S(2)}) %copy-start) | copy-done | bytes 163864
  19.1 0.1 copy.57
  19.3 0.3 rev.20
  19.7 0.1 copy.46
  19.8 0.1 fusion.119
  20.1 0.1 fusion.115
  20.2 14.9 %all-gather.2.cloned.1.call-done = bf16[2,320,3,3,320]{4,1,3,2,0:T(8,128)(2,1)} async-done(((bf16[2,160,3,3,320]{4,1,3,2,0:T(8,128)(2,1)}), bf16[2,320,3,3,320]{4,1,3,2,0:T(8,128)(2,1)}) %all-gather.2.cloned.1.call-update) | async-done | bytes 3686416 | tf_op jit(solution)/shard_map/all_gather | solution.py:65
  35.1 2.5 %fusion.7 = f32[4,16,3,320]{3,1,2,0:T(8,128)S(1)} fusion(bf16[2,320,3,3,320]{4,1,3,2,0:T(8,128)(2,1)} %all-gather.2.cloned.1.call-done, bf16[4,2,7,2,320]{4,2,1,3,0:T(8,128)(2,1)S(1)} %slice.32, bf16[4,2,8,3,320]{4,2,1,3,0:T(8,128)(2,1)S(1)} %copy.59, pred[16,3]{0,1:T(4,128)(4,1)S(1)} %copy-done.3), kind=kOutput, calls=%fused_computation.9 | convolution fusion | flops 295587840 | bytes 2652208 | tf_op jit(solution)/shard_map/conv_general_dilated | solution.py:22
  37.6 0.1 copy.60
  37.8 0.3 copy-done.2
  38.0 1.0 %fusion.9 = f32[4,16,3,320]{3,1,2,0:T(8,128)S(1)} fusion(bf16[2,320,3,3,320]{4,1,3,2,0:T(8,128)(2,1)S(1)} %copy-done.2, bf16[4,2,7,2,320]{4,2,1,3,0:T(8,128)(2,1)S(1)} %slice.24, bf16[4,2,8,3,320]{4,2,1,3,0:T(8,128)(2,1)S(1)} %copy.48, pred[16,3]{0,1:T(4,128)(4,1)S(1)} %copy-done.3), kind=kOutput, calls=%fused_computation.11 | convolution fusion | flops 295587840 | bytes 2703872 | tf_op jit(solution)/shard_map/conv_general_dilated | solution.py:13
  39.1 0.1 copy.50
  39.2 3.7 %collective-permute-start = (bf16[2,4,16,320]{3,1,2,0:T(4,128)(2,1)S(1)}, bf16[2,4,16,320]{3,1,2,0:T(4,128)(2,1)S(1)}, u32[]{:S(2)}, u32[]{:S(2)}) collective-permute-start(bf16[2,4,16,320]{3,1,2,0:T(4,128)(2,1)S(1)} %fusion.71), channel_id=1, source_target_pairs={{0,4},{12,8},{1,5},{13,9},{2,6},{14,10},{3,7},{15,11},{16,20},{28,... | collective-permute-start | bytes 245768 | tf_op jit(solution)/shard_map/ppermute | solution.py:70
  42.9 0.3 rev.21
  43.3 1.3 %collective-permute-start.2 = (f32[2,4,16,320]{3,1,2,0:T(4,128)S(1)}, f32[2,4,16,320]{3,1,2,0:T(4,128)S(1)}, u32[]{:S(2)}, u32[]{:S(2)}) collective-permute-start(f32[2,4,16,320]{3,1,2,0:T(4,128)S(1)} %rev.21), channel_id=1, source_target_pairs={{0,4},{12,8},{1,5},{13,9},{2,6},{14,10},{3,7},{15,11},{16,20},{28,... | collective-permute-start | bytes 491528 | tf_op jit(solution)/shard_map/ppermute | solution.py:70
  44.6 1.2 %collective-permute-done = bf16[2,4,16,320]{3,1,2,0:T(4,128)(2,1)S(1)} collective-permute-done((bf16[2,4,16,320]{3,1,2,0:T(4,128)(2,1)S(1)}, bf16[2,4,16,320]{3,1,2,0:T(4,128)(2,1)S(1)}, u32[]{:S(2)}, u32[]{:S(2)}) %collective-permute-start) | collective-permute-done | bytes 81952 | tf_op jit(solution)/shard_map/ppermute | solution.py:70
  45.8 0.1 fusion.118
  46.1 2.6 %fusion.10 = f32[4,16,3,320]{3,1,2,0:T(8,128)S(1)} fusion(bf16[2,320,3,3,320]{4,1,3,2,0:T(8,128)(2,1)} %all-gather.2.cloned.1.call-done, bf16[4,2,7,2,320]{4,2,1,3,0:T(8,128)(2,1)S(1)} %slice.27, bf16[4,2,8,3,320]{4,2,1,3,0:T(8,128)(2,1)S(1)} %copy.52, pred[16,3]{0,1:T(4,128)(4,1)S(1)} %copy-done.3), kind=kOutput, calls=%fused_computation.12 | convolution fusion | flops 295587840 | bytes 2652208 | tf_op jit(solution)/shard_map/conv_general_dilated | solution.py:13
  48.7 0.1 copy.53
  48.8 0.1 fusion.63
  49.1 2.6 %fusion.6 = f32[4,16,3,320]{3,1,2,0:T(8,128)S(1)} fusion(bf16[2,320,3,3,320]{4,1,3,2,0:T(8,128)(2,1)} %all-gather.2.cloned.1.call-done, bf16[4,2,7,2,320]{4,2,1,3,0:T(8,128)(2,1)S(1)} %slice.29, bf16[4,2,8,3,320]{4,2,1,3,0:T(8,128)(2,1)S(1)} %copy.55, pred[16,3]{0,1:T(4,128)(4,1)S(1)} %copy-done.3), kind=kOutput, calls=%fused_computation.8 | convolution fusion | flops 295587840 | bytes 2652208 | tf_op jit(solution)/shard_map/conv_general_dilated | solution.py:13
  51.8 0.1 copy.56
  51.9 0.3 add_convert_fusion.3
  52.2 0.3 rev.22
  52.6 2.4 %fusion.8 = f32[4,16,3,320]{3,1,2,0:T(8,128)S(1)} fusion(bf16[2,320,3,3,320]{4,1,3,2,0:T(8,128)(2,1)} %all-gather.2.cloned.1.call-done, bf16[4,2,7,2,320]{4,2,1,3,0:T(8,128)(2,1)S(1)} %slice.34, bf16[4,2,8,3,320]{4,2,1,3,0:T(8,128)(2,1)S(1)} %copy.62, pred[16,3]{0,1:T(4,128)(4,1)S(1)} %copy-done.3), kind=kOutput, calls=%fused_computation.10 | convolution fusion | flops 295587840 | bytes 2652208 | tf_op jit(solution)/shard_map/conv_general_dilated | solution.py:22
  55.0 0.1 copy.63
  55.1 0.3 rev.23
  55.5 0.2 add_convert_fusion.1
  55.7 0.3 rev.24
  56.1 2.4 %fusion.11 = f32[4,16,3,320]{3,1,2,0:T(8,128)S(1)} fusion(bf16[2,320,3,3,320]{4,1,3,2,0:T(8,128)(2,1)} %all-gather.2.cloned.1.call-done, bf16[4,2,7,2,320]{4,2,1,3,0:T(8,128)(2,1)S(1)} %slice.36, bf16[4,2,8,3,320]{4,2,1,3,0:T(8,128)(2,1)S(1)} %copy.65, pred[16,3]{0,1:T(4,128)(4,1)S(1)} %copy-done.3), kind=kOutput, calls=%fused_computation.13 | convolution fusion | flops 295587840 | bytes 2652208 | tf_op jit(solution)/shard_map/conv_general_dilated | solution.py:22
  58.5 0.1 copy.66
  58.6 0.3 rev.25
  59.0 0.2 add_convert_fusion
  59.2 1.3 %collective-permute-start.3 = (bf16[2,4,16,320]{3,1,2,0:T(4,128)(2,1)S(1)}, bf16[2,4,16,320]{3,1,2,0:T(4,128)(2,1)S(1)}, u32[]{:S(2)}, u32[]{:S(2)}) collective-permute-start(bf16[2,4,16,320]{3,1,2,0:T(4,128)(2,1)S(1)} %add_convert_fusion), channel_id=1, source_target_pairs={{4,0},{5,1},{6,2},{7,3},{20,16},{21,17},{22,18},{23,19}} | collective-permute-start | bytes 245768 | tf_op jit(solution)/shard_map/ppermute | solution.py:137
  60.5 0.1 fusion.116
  60.6 0.8 collective-permute-start.1
  61.5 4.2 %collective-permute-done.3 = bf16[2,4,16,320]{3,1,2,0:T(4,128)(2,1)S(1)} collective-permute-done((bf16[2,4,16,320]{3,1,2,0:T(4,128)(2,1)S(1)}, bf16[2,4,16,320]{3,1,2,0:T(4,128)(2,1)S(1)}, u32[]{:S(2)}, u32[]{:S(2)}) %collective-permute-start.3) | collective-permute-done | bytes 81952 | tf_op jit(solution)/shard_map/ppermute | solution.py:137
  65.7 0.2 fusion.95
  66.0 0.3 fusion.94
  66.2 0.1 pad_maximum_fusion
  66.4 7.9 %all_gather.7 = bf16[8,4,16,640]{3,2,1,0:T(8,128)(2,1)S(1)} all-gather(bf16[2,4,16,640]{3,2,1,0:T(8,128)(2,1)S(1)} %copy.67), channel_id=1, replica_groups=mesh['groups'=2,'pipe'=4,'dp'=2,'mp'=2] {'dp','mp'}, dimensions={0}, use_global_device_ids=true | all-gather | bytes 819200 | tf_op jit(solution)/shard_map/all_gather | solution.py:147
  74.3 0.2 constant_dynamic-slice_fusion.1
  74.5 0.9 fusion.18
  75.3 1.5 %copy.70 = f32[160,3,3,320]{3,2,1,0:T(4,128)S(1)} copy(f32[160,3,3,320]{3,0,2,1:T(8,128)S(1)} %fusion.18) | data formatting | bytes 3686400 | tf_op jit(solution)/shard_map/conv_general_dilated | solution.py:31
  76.9 4.6 %reshape.15 = f32[1,460800]{1,0:T(1,128)} reshape(f32[160,3,3,320]{3,2,1,0:T(4,128)S(1)} %copy.70) | data formatting | bytes 3686400 | tf_op jit(solution)/shard_map/reshape | solution.py:151
  (36 shorter events, 0.9 us)
Async XLA Ops:
  6.5 28.6 %all-gather.2.cloned.1.call-start = ((), (), s32[]{:S(2)}) async-start(), calls=%async_computation | async-start | bytes 6635520 | tf_op jit(solution)/shard_map/all_gather | solution.py:65
  18.2 0.9 %copy-start = (bf16[1,2,2,4,16,320]{5,4,3,2,1,0:T(8,128)(2,1)S(1)}, bf16[1,2,2,4,16,320]{5,4,3,2,1,0:T(8,128)(2,1)}, u32[]{:S(2)}) copy-start(bf16[1,2,2,4,16,320]{5,4,3,2,1,0:T(8,128)(2,1)} %param.5) | copy-start | bytes 491524
  18.2 1.5 %copy-start.1 = (bf16[1,2,2,4,16,320]{5,4,3,2,1,0:T(8,128)(2,1)S(1)}, bf16[1,2,2,4,16,320]{5,4,3,2,1,0:T(8,128)(2,1)}, u32[]{:S(2)}) copy-start(bf16[1,2,2,4,16,320]{5,4,3,2,1,0:T(8,128)(2,1)} %param.3) | copy-start | bytes 491524
  18.2 16.9 %copy-start.3 = (pred[16,3]{0,1:T(4,128)(4,1)S(1)}, pred[16,3]{0,1:T(4,128)(4,1)}, u32[]{:S(2)}) copy-start(pred[16,3]{0,1:T(4,128)(4,1)} %constant.58) | copy-start | bytes 148
  35.1 2.9 %copy-start.2 = (bf16[2,320,3,3,320]{4,1,3,2,0:T(8,128)(2,1)S(1)}, bf16[2,320,3,3,320]{4,1,3,2,0:T(8,128)(2,1)}, u32[]{:S(2)}) copy-start(bf16[2,320,3,3,320]{4,1,3,2,0:T(8,128)(2,1)} %all-gather.2.cloned.1.call-done) | copy-start | bytes 11059204
  39.2 6.6 %collective-permute-start = (bf16[2,4,16,320]{3,1,2,0:T(4,128)(2,1)S(1)}, bf16[2,4,16,320]{3,1,2,0:T(4,128)(2,1)S(1)}, u32[]{:S(2)}, u32[]{:S(2)}) collective-permute-start(bf16[2,4,16,320]{3,1,2,0:T(4,128)(2,1)S(1)} %fusion.71), channel_id=1, source_target_pairs={{0,4},{12,8},{1,5},{13,9},{2,6},{14,10},{3,7},{15,11},{16,20},{28,... | collective-permute-start | bytes 245768 | tf_op jit(solution)/shard_map/ppermute | solution.py:70
  43.3 8.6 %collective-permute-start.2 = (f32[2,4,16,320]{3,1,2,0:T(4,128)S(1)}, f32[2,4,16,320]{3,1,2,0:T(4,128)S(1)}, u32[]{:S(2)}, u32[]{:S(2)}) collective-permute-start(f32[2,4,16,320]{3,1,2,0:T(4,128)S(1)} %rev.21), channel_id=1, source_target_pairs={{0,4},{12,8},{1,5},{13,9},{2,6},{14,10},{3,7},{15,11},{16,20},{28,... | collective-permute-start | bytes 491528 | tf_op jit(solution)/shard_map/ppermute | solution.py:70
  59.2 6.5 %collective-permute-start.3 = (bf16[2,4,16,320]{3,1,2,0:T(4,128)(2,1)S(1)}, bf16[2,4,16,320]{3,1,2,0:T(4,128)(2,1)S(1)}, u32[]{:S(2)}, u32[]{:S(2)}) collective-permute-start(bf16[2,4,16,320]{3,1,2,0:T(4,128)(2,1)S(1)} %add_convert_fusion), channel_id=1, source_target_pairs={{4,0},{5,1},{6,2},{7,3},{20,16},{21,17},{22,18},{23,19}} | collective-permute-start | bytes 245768 | tf_op jit(solution)/shard_map/ppermute | solution.py:137
  60.6 5.3 %collective-permute-start.1 = (bf16[2,4,16,320]{3,1,2,0:T(4,128)(2,1)S(1)}, bf16[2,4,16,320]{3,1,2,0:T(4,128)(2,1)S(1)}, u32[]{:S(2)}, u32[]{:S(2)}) collective-permute-start(bf16[2,4,16,320]{3,1,2,0:T(4,128)(2,1)S(1)} %get-tuple-element.9), channel_id=1, source_target_pairs={{8,12},{9,13},{10,14},{11,15},{24,28},{25,29},{26,30},{27,31}} | collective-permute-start | bytes 245768 | tf_op jit(solution)/shard_map/ppermute | solution.py:112
Sparse Core Ops, SparseCore 0:
  18.4 16.6 all-gather.1

commit v3 on v2

--- a/solution.py
+++ b/solution.py
@@ -43,27 +43,54 @@
     return v.astype(jnp.bfloat16)
 
 
+def lane_shift(v, dd, dm):
+    nd, nm = lax.axis_size("dp"), lax.axis_size("mp")
+    pairs = [
+        (((d + dd) % nd) * nm + (m + dm) % nm, d * nm + m)
+        for d in range(nd)
+        for m in range(nm)
+    ]
+    return lax.ppermute(v, ("dp", "mp"), pairs)
+
+
+def cross_shift(v, dd, dm):
+    npipe, nd, nm = lax.axis_size("pipe"), lax.axis_size("dp"), lax.axis_size("mp")
+    pairs = []
+    for src, dst in ((1, 0), (npipe - 2, npipe - 1)):
+        for d in range(nd):
+            for m in range(nm):
+                source = (src * nd + (d + dd) % nd) * nm + (m + dm) % nm
+                pairs.append((source, (dst * nd + d) * nm + m))
+    return lax.ppermute(v, ("pipe", "dp", "mp"), pairs)
+
+
+def every_lane(v, shift):
+    nd, nm = lax.axis_size("dp"), lax.axis_size("mp")
+    parts = [shift(v, dd, dm) if (dd, dm) != (0, 0) or shift is cross_shift else v
+             for dd in range(nd) for dm in range(nm)]
+    return jnp.concatenate(parts, axis=0)
+
+
 def local(latent, section_weight, out_grad):
     pipe_size = lax.axis_size("pipe")
     half = pipe_size // 2
     device = lax.axis_index("pipe")
     lower = device < half
     stage = jnp.minimum(device, pipe_size - 1 - device)
-    mp_size = lax.axis_size("mp")
     lane = lax.axis_index("mp")
+    swap = [(0, 1), (1, 0)]
 
     channels = latent.shape[-1]
     img = latent.shape[-3:]
     samples = latent.reshape((-1,) + img)
     grads = out_grad.reshape((-1,) + img)
-    per_lane = samples.shape[0] // mp_size
-    x0 = lax.dynamic_slice_in_dim(samples, lane * per_lane, per_lane, 0)
-    seed = lax.dynamic_slice_in_dim(grads, lane * per_lane, per_lane, 0)
+    per_lane = samples.shape[0] // 2
+    mine = lane * per_lane
+    theirs = (1 - lane) * per_lane
 
     chan_half = section_weight.shape[-1] // (9 * channels)
-    halves = section_weight[0].reshape(2, chan_half, 3, 3, channels)
-    full = lax.all_gather(halves, "mp", axis=1, tiled=True)
-    w_enc, w_dec = full[0], full[1]
+    own = section_weight[0].reshape(2, chan_half, 3, 3, channels)
+    other = lax.ppermute(own, "mp", swap)
 
     def up(t, v):
         pairs = [(t, t + 1), (pipe_size - 1 - t, pipe_size - 2 - t)]
@@ -73,12 +100,32 @@
         pairs = [(t, t - 1), (pipe_size - 1 - t, pipe_size - t)]
         return lax.ppermute(v, "pipe", pairs)
 
-    u0 = f32(x0)
-    a0 = bf16(jax.nn.silu(u0))
-    h1 = bf16(u0 + conv(a0, w_enc))
-    d_last = conv_t(seed, w_dec)
+    def take(v, at):
+        return lax.dynamic_slice_in_dim(v, at, per_lane, 0)
+
+    def join(first, second):
+        return jnp.where(lane == 0, jnp.concatenate([first, second], -1),
+                         jnp.concatenate([second, first], -1))
+
+    low = lane * chan_half
+    act_all = bf16(jax.nn.silu(f32(samples)))
+    own_in = lax.dynamic_slice_in_dim(samples, low, chan_half, 3)
+    h1_half = bf16(f32(own_in) + conv(act_all, own[0]))
+    seed_half = lax.dynamic_slice_in_dim(grads, low, chan_half, 3)
+    d_part = conv_t(seed_half, own[1])
+    h1_got, d_got = lax.ppermute((take(h1_half, theirs), take(d_part, theirs)), "mp", swap)
+    h1 = join(take(h1_half, mine), h1_got)
+    d_last = take(d_part, mine) + d_got
+    x0 = take(samples, mine)
+    a0 = take(act_all, mine)
+    seed = take(grads, mine)
     h1_r = up(0, h1)
     d_last_r = up(0, d_last)
+
+    other, _ = lax.optimization_barrier((other, h1))
+    full = jnp.where(lane == 0, jnp.concatenate([own, other], 1),
+                     jnp.concatenate([other, own], 1))
+    w_enc, w_dec = full[0], full[1]
 
     enc_in, enc_act, enc_out = {}, {}, {}
     enc_in[0], enc_act[0], enc_out[0] = x0, a0, h1
@@ -109,7 +156,6 @@
     a_last = bf16(jax.nn.silu(u_last))
     b_last = d_last_r * silu_slope(u_last)
     skip = {1: bf16(b_last)}
-    a_last_r = lax.ppermute(a_last, "pipe", [(pipe_size - 2, pipe_size - 1)])
     cot = bf16(f32(seed) + b_last)
 
     for t in range(1, half):
@@ -134,19 +180,23 @@
         b = d * silu_slope(f32(enc_in[t]))
         cot = bf16(f32(cot) + b)
     c0 = bf16(f32(cot) + f32(skip[1]))
-    c0_r = lax.ppermute(c0, "pipe", [(1, 0)])
-
-    acts_lo = jnp.stack([a0] + [enc_act[t] for t in range(1, half)])
-    cots_lo = jnp.stack([c0_r] + [enc_c[t] for t in range(1, half)])
-    acts_up = jnp.stack([a_last_r] + [dec_act[t] for t in range(1, half)])
-    cots_up = jnp.stack([seed] + [dec_c[t] for t in range(1, half)])
-    act_sel = jnp.where(lower, acts_lo[stage], acts_up[stage])
-    cot_sel = jnp.where(lower, cots_lo[stage], cots_up[stage])
-
-    both = jnp.concatenate([act_sel, cot_sel], axis=-1)
-    every = lax.all_gather(both, ("dp", "mp"), axis=0, tiled=True)
-    act_all = every[..., :channels]
-    cot_all = lax.dynamic_slice_in_dim(every, channels + lane * chan_half, chan_half, 3)
+
+    late = every_lane(jnp.concatenate([jnp.where(lower, c0, a_last)], -1), cross_shift)
+    early = every_lane(jnp.concatenate([a0, seed], -1), lane_shift)
+    acts = jnp.stack([enc_act[t] for t in range(1, half)] or [a0])
+    cots = jnp.stack([enc_c[t] for t in range(1, half)] or [a0])
+    acts_up = jnp.stack([dec_act[t] for t in range(1, half)] or [a0])
+    cots_up = jnp.stack([dec_c[t] for t in range(1, half)] or [a0])
+    at = jnp.maximum(stage - 1, 0)
+    mid = every_lane(
+        jnp.concatenate([jnp.where(lower, acts[at], acts_up[at]),
+                         jnp.where(lower, cots[at], cots_up[at])], -1),
+        lane_shift)
+    first_a = jnp.where(lower, early[..., :channels], late)
+    first_c = jnp.where(lower, late, early[..., channels:])
+    act_all = jnp.where(stage == 0, first_a, mid[..., :channels])
+    cot_all = jnp.where(stage == 0, first_c, mid[..., channels:])
+    cot_all = lax.dynamic_slice_in_dim(cot_all, low, chan_half, 3)
     grad = weight_grad(act_all, cot_all)
     return grad.reshape(1, -1)
 

time: 88.7 us -> 107 us (1.21)
  local copies, waits for them, and re-layouts: 22.6 us -> 46.3 us
  between operations: 13.9 us -> 0.75 us
  starting transfers between devices: 7.1 us -> 18.9 us
  other arithmetic: 2 us -> 10.2 us
  blocking collectives: 7.86 us -> 0 us
  matrix products: 14.4 us -> 10.1 us
    slice x1, local copies, waits for them, and re-layouts: 0.04 us -> 19.4 us  [local(): d_part = conv_t(seed_half, own[1])]
    all_gather x1 -> x0, waiting for transfers between devices: 14.9 us -> none  [local(): full = lax.all_gather(halves, 'mp', axis=1, tiled=True)]
    ppermute x2 -> x13, waiting for transfers between devices: 4.24 us -> 17.7 us  [the longest x4 11 us: cross_shift(): return lax.ppermute(v, ('pipe', 'dp', 'mp'), pairs)]
    all_gather x1 -> x0, blocking collectives: 7.86 us -> none  [local(): every = lax.all_gather(both, ('dp', 'mp'), axis=0, tiled=True)]
    ppermute x2 -> x13, starting transfers between devices: 2.14 us -> 9.46 us  [the longest x4 5.38 us: cross_shift(): return lax.ppermute(v, ('pipe', 'dp', 'mp'), pairs)]
    select_n x2 -> x6, other arithmetic: 0.51 us -> 6.77 us  [the longest x1 4.91 us: local(): jnp.where(lane == 0, jnp.concatenate([own, other], 1), jnp.concatenate([o...]
    ppermute x2, starting transfers between devices: 4.96 us -> 9.39 us  [up(): return lax.ppermute(v, 'pipe', pairs)]
    squeeze x0 -> x2, local copies, waits for them, and re-layouts: none -> 3.39 us  [the longest x1 1.71 us: local(): h1_half = bf16(f32(own_in) + conv(act_all, own[0]))]
  transfers between devices with their start and end apart: 5 -> 15, of which waited for: 3 -> 6; matrix products, arithmetic and copies ran while one was open for 9% -> 44% of each run, Pallas kernels for 0% -> 0%
where the time goes in v3:
time: 107 us; the launch traced here: 106 us
  local copies, waits for them, and re-layouts  46.3 us (43%)
  waiting for transfers between devices  19.9 us (19%)
  starting transfers between devices  18.9 us (18%)
  other arithmetic  10.2 us (10%)
  matrix products  10.1 us (9%)
    slice x1, local copies, waits for them, and re-layouts, local(): d_part = conv_t(seed_half, own[1])  19.4 us
    ppermute x4, waiting for transfers between devices, cross_shift(): return lax.ppermute(v, ('pipe', 'dp', 'mp'), pairs)  11 us
    ppermute x2, starting transfers between devices, up(): return lax.ppermute(v, 'pipe', pairs)  9.39 us
    another operation x2, local copies, waits for them, and re-layouts, local(): own = section_weight[0].reshape(2, chan_half, 3, 3, channels)  7.74 us
    ppermute x6, waiting for transfers between devices, lane_shift(): return lax.ppermute(v, ('dp', 'mp'), pairs)  6.65 us
    conv_general_dilated x3, matrix products, conv_t(): lax.conv_general_dilated(flipped, weight, (1, 1), ((1, 1), (1, 1)), dimen...  5.56 us
    ppermute x4, starting transfers between devices, cross_shift(): return lax.ppermute(v, ('pipe', 'dp', 'mp'), pairs)  5.38 us
    select_n x1, other arithmetic, local(): jnp.where(lane == 0, jnp.concatenate([own, other], 1), jnp.concatenate([o...  4.91 us
  transfers between devices with their start and end apart: 15, of which 6 were waited for; matrix products, arithmetic and copies ran while one was open for 44% of the time, Pallas kernels for 0%

profile of v3, /device:TPU:0, one launch (start us, length us, event | category | flops | bytes accessed | tf_op | source)
XLA Modules:
  0.0 106.1 jit_solution(14046439804214870863)
XLA Ops:
  0.0 3.9 %reshape.86 = bf16[921600]{0:T(1024)(128)(2,1)} reshape(bf16[1,2,460800]{2,1,0:T(2,128)(2,1)} %param.4) | data formatting | bytes 3686400
  3.9 6.1 %reshape_squeeze.3 = bf16[2,160,3,3,320]{4,3,2,1,0:T(4,128)(2,1)S(1)} reshape(bf16[921600]{0:T(1024)(128)(2,1)} %reshape.86) | data formatting | bytes 3686400 | tf_op jit(solution)/shard_map/reshape;squeeze | solution.py:92
  10.0 1.7 %copy.89 = bf16[2,160,3,3,320]{4,1,3,2,0:T(8,128)(2,1)} copy(bf16[2,160,3,3,320]{4,3,2,1,0:T(4,128)(2,1)S(1)} %reshape_squeeze.3) | data formatting | bytes 3686400 | tf_op jit(solution)/shard_map/reshape;squeeze | solution.py:92
  11.7 0.5 collective-permute-start.7
  12.1 19.4 %slice_reduce_fusion.1 = (bf16[460800]{0:T(1024)(128)(2,1)S(1)}, bf16[460800]{0:T(1024)(128)(2,1)S(1)}) fusion(bf16[1,2,460800]{2,1,0:T(2,128)(2,1)S(1)} %copy-done), kind=kLoop, calls=%fused_computation.8 | loop fusion | bytes 3686400 | tf_op jit(solution)/shard_map/slice | solution.py:115
  31.5 1.7 %squeeze.17 = bf16[160,3,3,320]{3,2,1,0:T(4,128)(2,1)S(1)} reshape(bf16[460800]{0:T(1024)(128)(2,1)S(1)} %get-tuple-element.8) | data formatting | bytes 1843200 | tf_op jit(solution)/shard_map/squeeze | solution.py:113
  33.3 1.0 fusion.22
  34.7 0.2 fusion.12
  34.9 1.6 %convolution_select_fusion.1 = f32[4,32,3,160]{3,1,2,0:T(8,128)} fusion(bf16[160,3,3,320]{3,2,1,0:T(4,128)(2,1)S(1)} %squeeze.17, bf16[4,4,8,5,320]{4,1,3,2,0:T(4,128)(2,1)S(1)} %fusion.12, pred[32,3]{0,1:T(4,128)(4,1)S(1)} %copy-done.7), kind=kOutput, calls=%fused_computation.10 | convolution fusion | flops 294973440 | bytes 1577056 | tf_op jit(solution)/shard_map/conv_general_dilated | solution.py:13
  36.6 1.3 %copy.84 = f32[4,32,3,160]{3,0,2,1:T(4,128)S(1)} copy(f32[4,32,3,160]{3,1,2,0:T(8,128)} %convolution_select_fusion.1) | data formatting | bytes 491520 | tf_op jit(solution)/shard_map/conv_general_dilated | solution.py:13
  38.0 0.7 constant_dynamic-slice_fusion.1
  38.7 0.3 collective-permute-start.5
  39.0 1.7 %squeeze.16 = bf16[160,3,3,320]{3,2,1,0:T(4,128)(2,1)S(1)} reshape(bf16[460800]{0:T(1024)(128)(2,1)S(1)} %get-tuple-element.7) | data formatting | bytes 1843200 | tf_op jit(solution)/shard_map/squeeze | solution.py:115
  41.4 0.8 convolution_select_fusion
  42.2 0.4 copy.79
  42.9 0.2 collective-permute-start.3
  43.1 1.0 maximum_select_fusion.1
  44.1 5.0 %collective-permute-start.6 = (bf16[2,4,16,320]{3,2,1,0:T(8,128)(2,1)S(1)}, bf16[2,4,16,320]{3,2,1,0:T(8,128)(2,1)S(1)}, u32[]{:S(2)}, u32[]{:S(2)}) collective-permute-start(bf16[2,4,16,320]{3,2,1,0:T(8,128)(2,1)S(1)} %maximum_select_fusion.1), channel_id=1, source_target_pairs={{0,4},{12,8},{1,5},{13,9},{2,6},{14,10},{3,7},{15,11},{16,20},{28,... | collective-permute-start | bytes 245768 | tf_op jit(solution)/shard_map/ppermute | solution.py:97
  49.2 2.2 %collective-permute-done.6 = bf16[2,4,16,320]{3,2,1,0:T(8,128)(2,1)S(1)} collective-permute-done((bf16[2,4,16,320]{3,2,1,0:T(8,128)(2,1)S(1)}, bf16[2,4,16,320]{3,2,1,0:T(8,128)(2,1)S(1)}, u32[]{:S(2)}, u32[]{:S(2)}) %collective-permute-start.6) | collective-permute-done | bytes 81952 | tf_op jit(solution)/shard_map/ppermute | solution.py:97
  51.7 0.2 fusion.31
  52.0 4.4 %collective-permute-start.4 = (f32[2,4,16,320]{3,2,1,0:T(8,128)S(1)}, f32[2,4,16,320]{3,2,1,0:T(8,128)S(1)}, u32[]{:S(2)}, u32[]{:S(2)}) collective-permute-start(f32[2,4,16,320]{3,2,1,0:T(8,128)S(1)} %dynamic-slice_add_fusion), channel_id=1, source_target_pairs={{0,4},{12,8},{1,5},{13,9},{2,6},{14,10},{3,7},{15,11},{16,20},{28,... | collective-permute-start | bytes 491528 | tf_op jit(solution)/shard_map/ppermute | solution.py:97
  56.4 4.9 %maximum_select_fusion = bf16[2,320,3,3,320]{4,1,3,2,0:T(8,128)(2,1)S(1)} fusion(bf16[2,160,3,3,320]{4,1,3,2,0:T(8,128)(2,1)} %collective-permute-done.7, bf16[2,160,3,3,320]{4,1,3,2,0:T(8,128)(2,1)} %copy.89, pred[]{:T(512)S(6)} %eq.9), kind=kLoop, calls=%fused_computation | loop fusion | flops 16588800 | bytes 7372801 | tf_op jit(solution)/shard_map/jit(_where)/select_n | solution.py:126
  61.3 1.0 fusion.6
  63.0 0.2 fusion.32
  63.4 1.0 fusion.4
  64.8 0.2 collective-permute-start.2
  65.0 1.4 %collective-permute-start.1 = (bf16[2,4,16,640]{3,2,1,0:T(8,128)(2,1)S(1)}, bf16[2,4,16,640]{3,2,1,0:T(8,128)(2,1)S(1)}, u32[]{:S(2)}, u32[]{:S(2)}) collective-permute-start(bf16[2,4,16,640]{3,2,1,0:T(8,128)(2,1)S(1)} %pad_maximum_fusion.2), channel_id=1, source_target_pairs={{2,0},{3,1},{0,2},{1,3},{6,4},{7,5},{4,6},{5,7},{10,8},{11,9},{8,1... | collective-permute-start | bytes 491528 | tf_op jit(solution)/shard_map/ppermute | solution.py:53
  66.4 0.3 collective-permute-start
  67.1 0.2 fusion.33
  67.4 2.4 %fusion.5 = f32[4,16,3,320]{3,1,2,0:T(8,128)S(1)} fusion(bf16[2,320,3,3,320]{4,1,3,2,0:T(8,128)(2,1)} %copy-done.1, bf16[4,2,8,5,320]{4,1,3,2,0:T(2,128)(2,1)S(1)} %fusion.33, pred[16,3]{0,1:T(4,128)(4,1)S(1)} %copy-done.6), kind=kOutput, calls=%fused_computation.12 | convolution fusion | flops 294973440 | bytes 2662448 | tf_op jit(solution)/shard_map/conv_general_dilated | solution.py:22
  70.6 0.2 fusion.34
  70.8 2.4 %fusion.7 = f32[4,16,3,320]{3,1,2,0:T(8,128)S(1)} fusion(bf16[2,320,3,3,320]{4,1,3,2,0:T(8,128)(2,1)} %copy-done.1, bf16[4,2,8,5,320]{4,1,3,2,0:T(2,128)(2,1)S(1)} %fusion.34, pred[16,3]{0,1:T(4,128)(4,1)S(1)} %copy-done.6), kind=kOutput, calls=%fused_computation.14 | convolution fusion | flops 294973440 | bytes 2662448 | tf_op jit(solution)/shard_map/conv_general_dilated | solution.py:22
  73.5 0.2 fusion.64
  73.7 1.3 %collective-permute-start.8 = (bf16[2,4,16,320]{3,2,1,0:T(8,128)(2,1)S(1)}, bf16[2,4,16,320]{3,2,1,0:T(8,128)(2,1)S(1)}, u32[]{:S(2)}, u32[]{:S(2)}) collective-permute-start(bf16[2,4,16,320]{3,2,1,0:T(8,128)(2,1)S(1)} %fusion.64), channel_id=1, source_target_pairs={{4,0},{5,1},{6,2},{7,3},{8,12},{9,13},{10,14},{11,15},{20,16},{21,... | collective-permute-start | bytes 245768 | tf_op jit(solution)/shard_map/ppermute | solution.py:64
  75.0 1.3 %collective-permute-start.9 = (bf16[2,4,16,320]{3,2,1,0:T(8,128)(2,1)S(1)}, bf16[2,4,16,320]{3,2,1,0:T(8,128)(2,1)S(1)}, u32[]{:S(2)}, u32[]{:S(2)}) collective-permute-start(bf16[2,4,16,320]{3,2,1,0:T(8,128)(2,1)S(1)} %fusion.64), channel_id=1, source_target_pairs={{5,0},{4,1},{7,2},{6,3},{9,12},{8,13},{11,14},{10,15},{21,16},{20,... | collective-permute-start | bytes 245768 | tf_op jit(solution)/shard_map/ppermute | solution.py:64
  76.4 4.8 %collective-permute-done.8 = bf16[2,4,16,320]{3,2,1,0:T(8,128)(2,1)S(1)} collective-permute-done((bf16[2,4,16,320]{3,2,1,0:T(8,128)(2,1)S(1)}, bf16[2,4,16,320]{3,2,1,0:T(8,128)(2,1)S(1)}, u32[]{:S(2)}, u32[]{:S(2)}) %collective-permute-start.8) | collective-permute-done | bytes 81952 | tf_op jit(solution)/shard_map/ppermute | solution.py:64
  81.2 1.3 %collective-permute-start.10 = (bf16[2,4,16,320]{3,2,1,0:T(8,128)(2,1)S(1)}, bf16[2,4,16,320]{3,2,1,0:T(8,128)(2,1)S(1)}, u32[]{:S(2)}, u32[]{:S(2)}) collective-permute-start(bf16[2,4,16,320]{3,2,1,0:T(8,128)(2,1)S(1)} %fusion.64), channel_id=1, source_target_pairs={{6,0},{7,1},{4,2},{5,3},{10,12},{11,13},{8,14},{9,15},{22,16},{23,... | collective-permute-start | bytes 245768 | tf_op jit(solution)/shard_map/ppermute | solution.py:64
  82.5 1.5 %collective-permute-start.11 = (bf16[2,4,16,320]{3,2,1,0:T(8,128)(2,1)S(1)}, bf16[2,4,16,320]{3,2,1,0:T(8,128)(2,1)S(1)}, u32[]{:S(2)}, u32[]{:S(2)}) collective-permute-start(bf16[2,4,16,320]{3,2,1,0:T(8,128)(2,1)S(1)} %fusion.64), channel_id=1, source_target_pairs={{7,0},{6,1},{5,2},{4,3},{11,12},{10,13},{9,14},{8,15},{23,16},{22,... | collective-permute-start | bytes 245768 | tf_op jit(solution)/shard_map/ppermute | solution.py:64
  84.0 4.9 %collective-permute-done.10 = bf16[2,4,16,320]{3,2,1,0:T(8,128)(2,1)S(1)} collective-permute-done((bf16[2,4,16,320]{3,2,1,0:T(8,128)(2,1)S(1)}, bf16[2,4,16,320]{3,2,1,0:T(8,128)(2,1)S(1)}, u32[]{:S(2)}, u32[]{:S(2)}) %collective-permute-start.10) | collective-permute-done | bytes 81952 | tf_op jit(solution)/shard_map/ppermute | solution.py:64
  88.9 1.4 %collective-permute-done.11 = bf16[2,4,16,320]{3,2,1,0:T(8,128)(2,1)S(1)} collective-permute-done((bf16[2,4,16,320]{3,2,1,0:T(8,128)(2,1)S(1)}, bf16[2,4,16,320]{3,2,1,0:T(8,128)(2,1)S(1)}, u32[]{:S(2)}, u32[]{:S(2)}) %collective-permute-start.11) | collective-permute-done | bytes 81952 | tf_op jit(solution)/shard_map/ppermute | solution.py:64
  90.3 1.1 %collective-permute-start.13 = (bf16[2,4,16,640]{3,2,1,0:T(8,128)(2,1)S(1)}, bf16[2,4,16,640]{3,2,1,0:T(8,128)(2,1)S(1)}, u32[]{:S(2)}, u32[]{:S(2)}) collective-permute-start(bf16[2,4,16,640]{3,2,1,0:T(8,128)(2,1)S(1)} %pad_maximum_fusion.3), channel_id=1, source_target_pairs={{2,0},{3,1},{0,2},{1,3},{6,4},{7,5},{4,6},{5,7},{10,8},{11,9},{8,1... | collective-permute-start | bytes 491528 | tf_op jit(solution)/shard_map/ppermute | solution.py:53
  91.6 3.8 %collective-permute-done.14 = bf16[2,4,16,640]{3,2,1,0:T(8,128)(2,1)S(1)} collective-permute-done((bf16[2,4,16,640]{3,2,1,0:T(8,128)(2,1)S(1)}, bf16[2,4,16,640]{3,2,1,0:T(8,128)(2,1)S(1)}, u32[]{:S(2)}, u32[]{:S(2)}) %collective-permute-start.14) | collective-permute-done | bytes 163872 | tf_op jit(solution)/shard_map/ppermute | solution.py:53
  95.4 2.8 %collective-permute-done.13 = bf16[2,4,16,640]{3,2,1,0:T(8,128)(2,1)S(1)} collective-permute-done((bf16[2,4,16,640]{3,2,1,0:T(8,128)(2,1)S(1)}, bf16[2,4,16,640]{3,2,1,0:T(8,128)(2,1)S(1)}, u32[]{:S(2)}, u32[]{:S(2)}) %collective-permute-start.13) | collective-permute-done | bytes 163872 | tf_op jit(solution)/shard_map/ppermute | solution.py:53
  98.4 0.3 fusion.68
  98.7 0.4 dynamic-slice_select_fusion
  99.1 0.9 fusion.23
  100.0 1.5 %copy.107 = f32[160,3,3,320]{3,2,1,0:T(4,128)S(1)} copy(f32[160,3,3,320]{3,0,2,1:T(8,128)S(1)} %fusion.23) | data formatting | bytes 3686400 | tf_op jit(solution)/shard_map/conv_general_dilated | solution.py:31
  101.5 4.6 %reshape.23 = f32[1,460800]{1,0:T(1,128)} reshape(f32[160,3,3,320]{3,2,1,0:T(4,128)S(1)} %copy.107) | data formatting | bytes 3686400 | tf_op jit(solution)/shard_map/reshape | solution.py:201
  (83 shorter events, 4.6 us)
Async XLA Ops:
  10.0 2.2 %copy-start = (bf16[1,2,460800]{2,1,0:T(2,128)(2,1)S(1)}, bf16[1,2,460800]{2,1,0:T(2,128)(2,1)}, u32[]{:S(2)}) copy-start(bf16[1,2,460800]{2,1,0:T(2,128)(2,1)} %param.4) | copy-start | bytes 5529604
  11.7 44.7 %collective-permute-start.7 = (bf16[2,160,3,3,320]{4,1,3,2,0:T(8,128)(2,1)}, bf16[2,160,3,3,320]{4,1,3,2,0:T(8,128)(2,1)}, u32[]{:S(2)}, u32[]{:S(2)}) collective-permute-start(bf16[2,160,3,3,320]{4,1,3,2,0:T(8,128)(2,1)} %copy.89), channel_id=1, source_target_pairs={{0,1},{1,0},{2,3},{3,2},{4,5},{5,4},{6,7},{7,6},{8,9},{9,8},{10,11... | collective-permute-start | bytes 5529608 | tf_op jit(solution)/shard_map/ppermute | solution.py:93
  31.5 3.4 %copy-start.7 = (pred[32,3]{0,1:T(4,128)(4,1)S(1)}, pred[32,3]{0,1:T(4,128)(4,1)}, u32[]{:S(2)}) copy-start(pred[32,3]{0,1:T(4,128)(4,1)} %constant.59) | copy-start | bytes 292
  34.9 3.0 %copy-start.2 = (bf16[1,2,2,4,16,320]{5,4,3,2,1,0:T(8,128)(2,1)S(1)}, bf16[1,2,2,4,16,320]{5,4,3,2,1,0:T(8,128)(2,1)}, u32[]{:S(2)}) copy-start(bf16[1,2,2,4,16,320]{5,4,3,2,1,0:T(8,128)(2,1)} %param.3) | copy-start | bytes 491524
  36.6 4.1 %copy-start.3 = (bf16[1,2,2,4,16,320]{5,4,3,2,1,0:T(8,128)(2,1)S(1)}, bf16[1,2,2,4,16,320]{5,4,3,2,1,0:T(8,128)(2,1)}, u32[]{:S(2)}) copy-start(bf16[1,2,2,4,16,320]{5,4,3,2,1,0:T(8,128)(2,1)} %param.5) | copy-start | bytes 491524
  38.7 4.4 %collective-permute-start.5 = (bf16[2,4,16,160]{3,2,1,0:T(8,128)(2,1)}, bf16[2,4,16,160]{3,2,1,0:T(8,128)(2,1)}, u32[]{:S(2)}, u32[]{:S(2)}) collective-permute-start(bf16[2,4,16,160]{3,2,1,0:T(8,128)(2,1)} %get-tuple-element.19), channel_id=1, source_target_pairs={{0,1},{1,0},{2,3},{3,2},{4,5},{5,4},{6,7},{7,6},{8,9},{9,8},{10,11... | collective-permute-start | bytes 122888 | tf_op jit(solution)/shard_map/ppermute | solution.py:116
  42.2 0.9 copy-start.5
  42.9 9.1 %collective-permute-start.3 = (f32[2,4,16,320]{3,2,1,0:T(8,128)S(1)}, f32[2,4,16,320]{3,2,1,0:T(8,128)S(1)}, u32[]{:S(2)}, u32[]{:S(2)}) collective-permute-start(f32[2,4,16,320]{3,2,1,0:T(8,128)S(1)} %constant_dynamic-slice_fusion.2), channel_id=1, source_target_pairs={{0,1},{1,0},{2,3},{3,2},{4,5},{5,4},{6,7},{7,6},{8,9},{9,8},{10,11... | collective-permute-start | bytes 491528 | tf_op jit(solution)/shard_map/ppermute | solution.py:116
  44.1 7.2 %collective-permute-start.6 = (bf16[2,4,16,320]{3,2,1,0:T(8,128)(2,1)S(1)}, bf16[2,4,16,320]{3,2,1,0:T(8,128)(2,1)S(1)}, u32[]{:S(2)}, u32[]{:S(2)}) collective-permute-start(bf16[2,4,16,320]{3,2,1,0:T(8,128)(2,1)S(1)} %maximum_select_fusion.1), channel_id=1, source_target_pairs={{0,4},{12,8},{1,5},{13,9},{2,6},{14,10},{3,7},{15,11},{16,20},{28,... | collective-permute-start | bytes 245768 | tf_op jit(solution)/shard_map/ppermute | solution.py:97
  52.0 9.3 %copy-start.6 = (pred[16,3]{0,1:T(4,128)(4,1)S(1)}, pred[16,3]{0,1:T(4,128)(4,1)}, u32[]{:S(2)}) copy-start(pred[16,3]{0,1:T(4,128)(4,1)} %constant.61) | copy-start | bytes 148
  52.0 12.6 %collective-permute-start.4 = (f32[2,4,16,320]{3,2,1,0:T(8,128)S(1)}, f32[2,4,16,320]{3,2,1,0:T(8,128)S(1)}, u32[]{:S(2)}, u32[]{:S(2)}) collective-permute-start(f32[2,4,16,320]{3,2,1,0:T(8,128)S(1)} %dynamic-slice_add_fusion), channel_id=1, source_target_pairs={{0,4},{12,8},{1,5},{13,9},{2,6},{14,10},{3,7},{15,11},{16,20},{28,... | collective-permute-start | bytes 491528 | tf_op jit(solution)/shard_map/ppermute | solution.py:97
  61.3 2.0 %copy-start.1 = (bf16[2,320,3,3,320]{4,1,3,2,0:T(8,128)(2,1)}, bf16[2,320,3,3,320]{4,1,3,2,0:T(8,128)(2,1)S(1)}, u32[]{:S(2)}) copy-start(bf16[2,320,3,3,320]{4,1,3,2,0:T(8,128)(2,1)S(1)} %maximum_select_fusion) | copy-start | bytes 11059204
  63.4 1.2 %copy-start.4 = (bf16[1,2,2,4,16,320]{5,4,3,2,1,0:T(8,128)(2,1)S(1)}, bf16[1,2,2,4,16,320]{5,4,3,2,1,0:T(8,128)(2,1)}, u32[]{:S(2)}) copy-start(bf16[1,2,2,4,16,320]{5,4,3,2,1,0:T(8,128)(2,1)} %param.5) | copy-start | bytes 491524
  64.8 26.7 %collective-permute-start.2 = (bf16[2,4,16,640]{3,2,1,0:T(8,128)(2,1)S(1)}, bf16[2,4,16,640]{3,2,1,0:T(8,128)(2,1)S(1)}, u32[]{:S(2)}, u32[]{:S(2)}) collective-permute-start(bf16[2,4,16,640]{3,2,1,0:T(8,128)(2,1)S(1)} %pad_maximum_fusion.2), channel_id=1, source_target_pairs={{3,0},{2,1},{1,2},{0,3},{7,4},{6,5},{5,6},{4,7},{11,8},{10,9},{9,1... | collective-permute-start | bytes 491528 | tf_op jit(solution)/shard_map/ppermute | solution.py:53
  65.0 26.5 %collective-permute-start.1 = (bf16[2,4,16,640]{3,2,1,0:T(8,128)(2,1)S(1)}, bf16[2,4,16,640]{3,2,1,0:T(8,128)(2,1)S(1)}, u32[]{:S(2)}, u32[]{:S(2)}) collective-permute-start(bf16[2,4,16,640]{3,2,1,0:T(8,128)(2,1)S(1)} %pad_maximum_fusion.2), channel_id=1, source_target_pairs={{2,0},{3,1},{0,2},{1,3},{6,4},{7,5},{4,6},{5,7},{10,8},{11,9},{8,1... | collective-permute-start | bytes 491528 | tf_op jit(solution)/shard_map/ppermute | solution.py:53
  66.4 25.1 %collective-permute-start = (bf16[2,4,16,640]{3,2,1,0:T(8,128)(2,1)S(1)}, bf16[2,4,16,640]{3,2,1,0:T(8,128)(2,1)S(1)}, u32[]{:S(2)}, u32[]{:S(2)}) collective-permute-start(bf16[2,4,16,640]{3,2,1,0:T(8,128)(2,1)S(1)} %pad_maximum_fusion.2), channel_id=1, source_target_pairs={{1,0},{0,1},{3,2},{2,3},{5,4},{4,5},{7,6},{6,7},{9,8},{8,9},{11,10... | collective-permute-start | bytes 491528 | tf_op jit(solution)/shard_map/ppermute | solution.py:53
  73.7 7.5 %collective-permute-start.8 = (bf16[2,4,16,320]{3,2,1,0:T(8,128)(2,1)S(1)}, bf16[2,4,16,320]{3,2,1,0:T(8,128)(2,1)S(1)}, u32[]{:S(2)}, u32[]{:S(2)}) collective-permute-start(bf16[2,4,16,320]{3,2,1,0:T(8,128)(2,1)S(1)} %fusion.64), channel_id=1, source_target_pairs={{4,0},{5,1},{6,2},{7,3},{8,12},{9,13},{10,14},{11,15},{20,16},{21,... | collective-permute-start | bytes 245768 | tf_op jit(solution)/shard_map/ppermute | solution.py:64
  75.0 7.5 %collective-permute-start.9 = (bf16[2,4,16,320]{3,2,1,0:T(8,128)(2,1)S(1)}, bf16[2,4,16,320]{3,2,1,0:T(8,128)(2,1)S(1)}, u32[]{:S(2)}, u32[]{:S(2)}) collective-permute-start(bf16[2,4,16,320]{3,2,1,0:T(8,128)(2,1)S(1)} %fusion.64), channel_id=1, source_target_pairs={{5,0},{4,1},{7,2},{6,3},{9,12},{8,13},{11,14},{10,15},{21,16},{20,... | collective-permute-start | bytes 245768 | tf_op jit(solution)/shard_map/ppermute | solution.py:64
  81.2 7.7 %collective-permute-start.10 = (bf16[2,4,16,320]{3,2,1,0:T(8,128)(2,1)S(1)}, bf16[2,4,16,320]{3,2,1,0:T(8,128)(2,1)S(1)}, u32[]{:S(2)}, u32[]{:S(2)}) collective-permute-start(bf16[2,4,16,320]{3,2,1,0:T(8,128)(2,1)S(1)} %fusion.64), channel_id=1, source_target_pairs={{6,0},{7,1},{4,2},{5,3},{10,12},{11,13},{8,14},{9,15},{22,16},{23,... | collective-permute-start | bytes 245768 | tf_op jit(solution)/shard_map/ppermute | solution.py:64
  82.5 7.8 %collective-permute-start.11 = (bf16[2,4,16,320]{3,2,1,0:T(8,128)(2,1)S(1)}, bf16[2,4,16,320]{3,2,1,0:T(8,128)(2,1)S(1)}, u32[]{:S(2)}, u32[]{:S(2)}) collective-permute-start(bf16[2,4,16,320]{3,2,1,0:T(8,128)(2,1)S(1)} %fusion.64), channel_id=1, source_target_pairs={{7,0},{6,1},{5,2},{4,3},{11,12},{10,13},{9,14},{8,15},{23,16},{22,... | collective-permute-start | bytes 245768 | tf_op jit(solution)/shard_map/ppermute | solution.py:64
  88.9 6.5 %collective-permute-start.14 = (bf16[2,4,16,640]{3,2,1,0:T(8,128)(2,1)S(1)}, bf16[2,4,16,640]{3,2,1,0:T(8,128)(2,1)S(1)}, u32[]{:S(2)}, u32[]{:S(2)}) collective-permute-start(bf16[2,4,16,640]{3,2,1,0:T(8,128)(2,1)S(1)} %pad_maximum_fusion.3), channel_id=1, source_target_pairs={{3,0},{2,1},{1,2},{0,3},{7,4},{6,5},{5,6},{4,7},{11,8},{10,9},{9,1... | collective-permute-start | bytes 491528 | tf_op jit(solution)/shard_map/ppermute | solution.py:53
  90.3 7.9 %collective-permute-start.13 = (bf16[2,4,16,640]{3,2,1,0:T(8,128)(2,1)S(1)}, bf16[2,4,16,640]{3,2,1,0:T(8,128)(2,1)S(1)}, u32[]{:S(2)}, u32[]{:S(2)}) collective-permute-start(bf16[2,4,16,640]{3,2,1,0:T(8,128)(2,1)S(1)} %pad_maximum_fusion.3), channel_id=1, source_target_pairs={{2,0},{3,1},{0,2},{1,3},{6,4},{7,5},{4,6},{5,7},{10,8},{11,9},{8,1... | collective-permute-start | bytes 491528 | tf_op jit(solution)/shard_map/ppermute | solution.py:53
  91.5 6.8 %collective-permute-start.12 = (bf16[2,4,16,640]{3,2,1,0:T(8,128)(2,1)S(1)}, bf16[2,4,16,640]{3,2,1,0:T(8,128)(2,1)S(1)}, u32[]{:S(2)}, u32[]{:S(2)}) collective-permute-start(bf16[2,4,16,640]{3,2,1,0:T(8,128)(2,1)S(1)} %pad_maximum_fusion.3), channel_id=1, source_target_pairs={{1,0},{0,1},{3,2},{2,3},{5,4},{4,5},{7,6},{6,7},{9,8},{8,9},{11,10... | collective-permute-start | bytes 491528 | tf_op jit(solution)/shard_map/ppermute | solution.py:53

commit v4 on v2

--- a/solution.py
+++ b/solution.py
@@ -49,21 +49,20 @@
     device = lax.axis_index("pipe")
     lower = device < half
     stage = jnp.minimum(device, pipe_size - 1 - device)
-    mp_size = lax.axis_size("mp")
     lane = lax.axis_index("mp")
+    swap = [(0, 1), (1, 0)]
 
     channels = latent.shape[-1]
     img = latent.shape[-3:]
     samples = latent.reshape((-1,) + img)
     grads = out_grad.reshape((-1,) + img)
-    per_lane = samples.shape[0] // mp_size
-    x0 = lax.dynamic_slice_in_dim(samples, lane * per_lane, per_lane, 0)
-    seed = lax.dynamic_slice_in_dim(grads, lane * per_lane, per_lane, 0)
+    per_lane = samples.shape[0] // 2
+    mine = lane * per_lane
+    theirs = (1 - lane) * per_lane
 
     chan_half = section_weight.shape[-1] // (9 * channels)
-    halves = section_weight[0].reshape(2, chan_half, 3, 3, channels)
-    full = lax.all_gather(halves, "mp", axis=1, tiled=True)
-    w_enc, w_dec = full[0], full[1]
+    own = lax.optimization_barrier(section_weight[0].reshape(2, chan_half, 3, 3, channels))
+    other = lax.ppermute(own, "mp", swap)
 
     def up(t, v):
         pairs = [(t, t + 1), (pipe_size - 1 - t, pipe_size - 2 - t)]
@@ -73,12 +72,32 @@
         pairs = [(t, t - 1), (pipe_size - 1 - t, pipe_size - t)]
         return lax.ppermute(v, "pipe", pairs)
 
-    u0 = f32(x0)
-    a0 = bf16(jax.nn.silu(u0))
-    h1 = bf16(u0 + conv(a0, w_enc))
-    d_last = conv_t(seed, w_dec)
+    def take(v, at):
+        return lax.dynamic_slice_in_dim(v, at, per_lane, 0)
+
+    def join(first, second):
+        return jnp.where(lane == 0, jnp.concatenate([first, second], -1),
+                         jnp.concatenate([second, first], -1))
+
+    low = lane * chan_half
+    act_all = bf16(jax.nn.silu(f32(samples)))
+    own_in = lax.dynamic_slice_in_dim(samples, low, chan_half, 3)
+    h1_half = bf16(f32(own_in) + conv(act_all, own[0]))
+    seed_half = lax.dynamic_slice_in_dim(grads, low, chan_half, 3)
+    d_part = conv_t(seed_half, own[1])
+    h1_got, d_got = lax.ppermute((take(h1_half, theirs), take(d_part, theirs)), "mp", swap)
+    h1 = join(take(h1_half, mine), h1_got)
+    d_last = take(d_part, mine) + d_got
+    x0 = take(samples, mine)
+    a0 = take(act_all, mine)
+    seed = take(grads, mine)
     h1_r = up(0, h1)
     d_last_r = up(0, d_last)
+
+    other, _ = lax.optimization_barrier((other, h1))
+    full = jnp.where(lane == 0, jnp.concatenate([own, other], 1),
+                     jnp.concatenate([other, own], 1))
+    w_enc, w_dec = full[0], full[1]
 
     enc_in, enc_act, enc_out = {}, {}, {}
     enc_in[0], enc_act[0], enc_out[0] = x0, a0, h1
@@ -109,7 +128,6 @@
     a_last = bf16(jax.nn.silu(u_last))
     b_last = d_last_r * silu_slope(u_last)
     skip = {1: bf16(b_last)}
-    a_last_r = lax.ppermute(a_last, "pipe", [(pipe_size - 2, pipe_size - 1)])
     cot = bf16(f32(seed) + b_last)
 
     for t in range(1, half):
@@ -134,19 +152,18 @@
         b = d * silu_slope(f32(enc_in[t]))
         cot = bf16(f32(cot) + b)
     c0 = bf16(f32(cot) + f32(skip[1]))
-    c0_r = lax.ppermute(c0, "pipe", [(1, 0)])
 
+    sent = lax.ppermute(jnp.where(lower, c0, a_last), "pipe", [(1, 0), (pipe_size - 2, pipe_size - 1)])
     acts_lo = jnp.stack([a0] + [enc_act[t] for t in range(1, half)])
-    cots_lo = jnp.stack([c0_r] + [enc_c[t] for t in range(1, half)])
-    acts_up = jnp.stack([a_last_r] + [dec_act[t] for t in range(1, half)])
+    cots_lo = jnp.stack([sent] + [enc_c[t] for t in range(1, half)])
+    acts_up = jnp.stack([sent] + [dec_act[t] for t in range(1, half)])
     cots_up = jnp.stack([seed] + [dec_c[t] for t in range(1, half)])
     act_sel = jnp.where(lower, acts_lo[stage], acts_up[stage])
     cot_sel = jnp.where(lower, cots_lo[stage], cots_up[stage])
-
     both = jnp.concatenate([act_sel, cot_sel], axis=-1)
     every = lax.all_gather(both, ("dp", "mp"), axis=0, tiled=True)
     act_all = every[..., :channels]
-    cot_all = lax.dynamic_slice_in_dim(every, channels + lane * chan_half, chan_half, 3)
+    cot_all = lax.dynamic_slice_in_dim(every, channels + low, chan_half, 3)
     grad = weight_grad(act_all, cot_all)
     return grad.reshape(1, -1)
 

time: 88.7 us -> 72.2 us (0.81)
  between operations: 13.9 us -> 0.56 us
  waiting for transfers between devices: 20.4 us -> 7.67 us
  other arithmetic: 2 us -> 6.84 us
  starting transfers between devices: 7.1 us -> 11.4 us
  local copies, waits for them, and re-layouts: 22.6 us -> 25.3 us
  matrix products: 14.4 us -> 11.9 us
    all_gather x1 -> x0, waiting for transfers between devices: 14.9 us -> none  [local(): full = lax.all_gather(halves, 'mp', axis=1, tiled=True)]
    ppermute x2, starting transfers between devices: 4.96 us -> 9.15 us  [up(): return lax.ppermute(v, 'pipe', pairs)]
    select_n x1 -> x3, other arithmetic: 0.25 us -> 4.09 us  [the longest x1 3.61 us: local(): jnp.where(lane == 0, jnp.concatenate([own, other], 1), jnp.concatenate([o...]
    conv_general_dilated x3, matrix products: 6.29 us -> 4.17 us  [conv(): lax.conv_general_dilated(act, weight, (1, 1), ((1, 1), (1, 1)), dimension...]
    another operation x2, local copies, waits for them, and re-layouts: 7.77 us -> 6.09 us  [the longest x1 6.05 us: local(): section_weight[0].reshape(2, chan_half, 3, 3, channels)]
    optimization_barrier x0 -> x1, local copies, waits for them, and re-layouts: none -> 1.68 us  [local(): lax.optimization_barrier(section_weight[0].reshape(2, chan_half, 3, 3, ch...]
    dynamic_slice x2 -> x4, local copies, waits for them, and re-layouts: 0.2 us -> 1.69 us  [the longest x2 1.39 us: take(): return lax.dynamic_slice_in_dim(v, at, per_lane, 0)]
    ppermute x2, waiting for transfers between devices: 1.24 us -> 2.57 us  [up(): return lax.ppermute(v, 'pipe', pairs)]
  transfers between devices with their start and end apart: 5 -> 6, of which waited for: 3 -> 2; matrix products, arithmetic and copies ran while one was open for 9% -> 23% of each run, Pallas kernels for 0% -> 0%
where the time goes in v4:
time: 72.2 us; the launch traced here: 71.7 us
  local copies, waits for them, and re-layouts  25.3 us (35%)
  matrix products  11.9 us (16%)
  starting transfers between devices  11.4 us (16%)
  blocking collectives  8.11 us (11%)
  waiting for transfers between devices  7.67 us (11%)
  other arithmetic  6.84 us (9%)
    ppermute x2, starting transfers between devices, up(): return lax.ppermute(v, 'pipe', pairs)  9.15 us
    all_gather x1, blocking collectives, local(): every = lax.all_gather(both, ('dp', 'mp'), axis=0, tiled=True)  8.11 us
    conv_general_dilated x3, matrix products, conv_t(): lax.conv_general_dilated(flipped, weight, (1, 1), ((1, 1), (1, 1)), dimen...  6.82 us
    another operation x1, local copies, waits for them, and re-layouts, local(): section_weight[0].reshape(2, chan_half, 3, 3, channels)  6.05 us
    unnamed x11, local copies, waits for them, and re-layouts  5.58 us
    ppermute x1, waiting for transfers between devices, local(): lax.ppermute(jnp.where(lower, c0, a_last), 'pipe', [(1, 0), (pipe_size -...  5.09 us
    reshape x1, local copies, waits for them, and re-layouts, local(): return grad.reshape(1, -1)  4.57 us
    conv_general_dilated x3, matrix products, conv(): lax.conv_general_dilated(act, weight, (1, 1), ((1, 1), (1, 1)), dimension...  4.17 us
  transfers between devices with their start and end apart: 6, of which 2 were waited for; matrix products, arithmetic and copies ran while one was open for 23% of the time, Pallas kernels for 0%

profile of v4, /device:TPU:0, one launch (start us, length us, event | category | flops | bytes accessed | tf_op | source)
XLA Modules:
  0.0 71.7 jit_solution(4862025032973493745)
XLA Ops:
  0.0 3.9 %reshape.76 = bf16[921600]{0:T(1024)(128)(2,1)} reshape(bf16[1,2,460800]{2,1,0:T(2,128)(2,1)} %param.4) | data formatting | bytes 3686400
  3.9 6.1 %reshape_squeeze.3 = bf16[2,160,3,3,320]{4,3,2,1,0:T(4,128)(2,1)S(1)} reshape(bf16[921600]{0:T(1024)(128)(2,1)} %reshape.76) | data formatting | bytes 3686400 | tf_op jit(solution)/shard_map/reshape;squeeze | solution.py:64
  10.0 1.7 %copy.53 = bf16[2,160,3,3,320]{4,1,3,2,0:T(8,128)(2,1)} copy(bf16[2,160,3,3,320]{4,3,2,1,0:T(4,128)(2,1)S(1)} %reshape_squeeze.3) | data formatting | bytes 3686400 | tf_op jit(solution)/shard_map/optimization_barrier | solution.py:64
  11.6 0.5 collective-permute-start.4
  12.2 0.2 fusion.22
  12.7 2.1 %convolution_select_fusion.1 = f32[4,32,3,160]{3,1,2,0:T(8,128)S(1)} fusion(bf16[2,160,3,3,320]{4,1,3,2,0:T(8,128)(2,1)} %copy.53, bf16[4,4,7,2,320]{4,2,1,3,0:T(8,128)(2,1)S(1)} %slice.32, bf16[4,4,8,3,320]{4,2,1,3,0:T(8,128)(2,1)S(1)} %copy.52, pred[32,3]{0,1:T(4,128)(4,1)S(1)} %copy-done.3), kind=kOutput, calls=%fused_computation.8 | convolution fusion | flops 296202240 | bytes 1740896 | tf_op jit(solution)/shard_map/conv_general_dilated | solution.py:13
  14.8 0.3 copy.54
  15.1 0.2 fusion.32
  15.2 0.7 constant_dynamic-slice_fusion.4
  16.0 1.0 %copy.55 = bf16[1,2,2,4,16,320]{5,3,4,2,1,0:T(4,128)(2,1)S(1)} copy(bf16[1,2,2,4,16,320]{5,4,3,2,1,0:T(8,128)(2,1)} %param.5) | data formatting | bytes 327680 | tf_op args[2]
  17.0 0.2 constant_dynamic-slice_fusion.1
  17.2 0.3 rev.22
  17.7 2.1 %convolution_select_fusion = f32[4,32,3,320]{3,1,2,0:T(8,128)S(1)} fusion(bf16[2,160,3,3,320]{4,1,3,2,0:T(8,128)(2,1)} %copy.53, bf16[4,4,7,2,160]{4,2,1,3,0:T(8,128)(2,1)S(1)} %slice.35, bf16[4,4,8,3,160]{4,2,1,3,0:T(8,128)(2,1)S(1)} %copy.57, pred[32,3]{0,1:T(4,128)(4,1)S(1)} %copy-done.3), kind=kOutput, calls=%fused_computation.7 | convolution fusion | flops 295649280 | bytes 1792096 | tf_op jit(solution)/shard_map/conv_general_dilated | solution.py:22
  19.7 0.4 copy.59
  20.2 0.6 rev.23
  20.8 0.7 constant_dynamic-slice_fusion
  21.5 0.4 collective-permute-start.2
  21.9 0.2 maximum_select_fusion.1
  22.1 4.6 %collective-permute-start.1 = (bf16[2,4,16,320]{3,1,2,0:T(4,128)(2,1)S(1)}, bf16[2,4,16,320]{3,1,2,0:T(4,128)(2,1)S(1)}, u32[]{:S(2)}, u32[]{:S(2)}) collective-permute-start(bf16[2,4,16,320]{3,1,2,0:T(4,128)(2,1)S(1)} %maximum_select_fusion.1), channel_id=1, source_target_pairs={{0,4},{12,8},{1,5},{13,9},{2,6},{14,10},{3,7},{15,11},{16,20},{28,... | collective-permute-start | bytes 245768 | tf_op jit(solution)/shard_map/ppermute | solution.py:69
  26.7 2.6 %collective-permute-done.1 = bf16[2,4,16,320]{3,1,2,0:T(4,128)(2,1)S(1)} collective-permute-done((bf16[2,4,16,320]{3,1,2,0:T(4,128)(2,1)S(1)}, bf16[2,4,16,320]{3,1,2,0:T(4,128)(2,1)S(1)}, u32[]{:S(2)}, u32[]{:S(2)}) %collective-permute-start.1) | collective-permute-done | bytes 81952 | tf_op jit(solution)/shard_map/ppermute | solution.py:69
  29.6 1.0 %dynamic-slice_add_fusion = f32[2,4,16,320]{3,1,2,0:T(4,128)S(1)} fusion(f32[2,4,16,320]{3,1,2,0:T(4,128)} %collective-permute-done.2, f32[4,4,16,320]{3,1,2,0:T(4,128)S(1)} %rev.23, s32[]{:T(128)S(6)} %select_n.62), kind=kLoop, calls=%fused_computation.113 | loop fusion | flops 40960 | bytes 491524 | tf_op jit(solution)/shard_map/add | solution.py:90
  30.6 4.6 %collective-permute-start.3 = (f32[2,4,16,320]{3,1,2,0:T(4,128)S(1)}, f32[2,4,16,320]{3,1,2,0:T(4,128)S(1)}, u32[]{:S(2)}, u32[]{:S(2)}) collective-permute-start(f32[2,4,16,320]{3,1,2,0:T(4,128)S(1)} %dynamic-slice_add_fusion), channel_id=1, source_target_pairs={{0,4},{12,8},{1,5},{13,9},{2,6},{14,10},{3,7},{15,11},{16,20},{28,... | collective-permute-start | bytes 491528 | tf_op jit(solution)/shard_map/ppermute | solution.py:69
  35.2 3.6 %maximum_select_fusion = bf16[2,320,3,3,320]{4,1,3,2,0:T(8,128)(2,1)S(1)} fusion(bf16[2,160,3,3,320]{4,1,3,2,0:T(8,128)(2,1)S(1)} %collective-permute-done.4, bf16[2,160,3,3,320]{4,1,3,2,0:T(8,128)(2,1)} %copy.53, pred[]{:T(512)S(6)} %eq.4), kind=kLoop, calls=%fused_computation | loop fusion | flops 16588800 | bytes 7372801 | tf_op jit(solution)/shard_map/jit(_where)/select_n | solution.py:98
  38.8 1.0 %fusion.6 = f32[4,16,3,320]{3,1,2,0:T(8,128)S(1)} fusion(bf16[2,320,3,3,320]{4,1,3,2,0:T(8,128)(2,1)S(1)} %maximum_select_fusion, bf16[4,2,7,2,320]{4,2,1,3,0:T(8,128)(2,1)S(1)} %slice.38, bf16[4,2,8,3,320]{4,2,1,3,0:T(8,128)(2,1)S(1)} %copy.61, pred[16,3]{0,1:T(4,128)(4,1)S(1)} %copy-done.2), kind=kOutput, calls=%fused_computation.11 | convolution fusion | flops 295587840 | bytes 2703872 | tf_op jit(solution)/shard_map/conv_general_dilated | solution.py:13
  39.8 0.1 copy.65
  39.9 0.1 fusion.65
  40.2 0.6 copy-done
  40.8 1.0 %fusion.4 = f32[4,16,3,320]{3,1,2,0:T(8,128)S(1)} fusion(bf16[2,320,3,3,320]{4,1,3,2,0:T(8,128)(2,1)S(1)} %maximum_select_fusion, bf16[4,2,7,2,320]{4,2,1,3,0:T(8,128)(2,1)S(1)} %slice.41, bf16[4,2,8,3,320]{4,2,1,3,0:T(8,128)(2,1)S(1)} %copy.67, pred[16,3]{0,1:T(4,128)(4,1)S(1)} %copy-done.2), kind=kOutput, calls=%fused_computation.9 | convolution fusion | flops 295587840 | bytes 2703872 | tf_op jit(solution)/shard_map/conv_general_dilated | solution.py:13
  41.8 0.1 copy.68
  42.0 0.2 add_convert_fusion.3
  42.2 0.3 rev.24
  42.6 2.4 %fusion.5 = f32[4,16,3,320]{3,1,2,0:T(8,128)S(1)} fusion(bf16[2,320,3,3,320]{4,1,3,2,0:T(8,128)(2,1)} %copy-done, bf16[4,2,7,2,320]{4,2,1,3,0:T(8,128)(2,1)S(1)} %slice.44, bf16[4,2,8,3,320]{4,2,1,3,0:T(8,128)(2,1)S(1)} %copy.70, pred[16,3]{0,1:T(4,128)(4,1)S(1)} %copy-done.2), kind=kOutput, calls=%fused_computation.10 | convolution fusion | flops 295587840 | bytes 2652208 | tf_op jit(solution)/shard_map/conv_general_dilated | solution.py:22
  45.0 0.1 copy.71
  45.2 0.3 rev.25
  45.5 0.2 add_convert_fusion.1
  45.7 0.3 rev.26
  46.1 2.4 %fusion.7 = f32[4,16,3,320]{3,1,2,0:T(8,128)S(1)} fusion(bf16[2,320,3,3,320]{4,1,3,2,0:T(8,128)(2,1)} %copy-done, bf16[4,2,7,2,320]{4,2,1,3,0:T(8,128)(2,1)S(1)} %slice.46, bf16[4,2,8,3,320]{4,2,1,3,0:T(8,128)(2,1)S(1)} %copy.73, pred[16,3]{0,1:T(4,128)(4,1)S(1)} %copy-done.2), kind=kOutput, calls=%fused_computation.12 | convolution fusion | flops 295587840 | bytes 2652208 | tf_op jit(solution)/shard_map/conv_general_dilated | solution.py:22
  48.7 0.3 rev.27
  49.0 0.3 fusion.85
  49.4 1.3 %collective-permute-start.5 = (bf16[2,4,16,320]{3,1,2,0:T(4,128)(2,1)S(1)}, bf16[2,4,16,320]{3,1,2,0:T(4,128)(2,1)S(1)}, u32[]{:S(2)}, u32[]{:S(2)}) collective-permute-start(bf16[2,4,16,320]{3,1,2,0:T(4,128)(2,1)S(1)} %fusion.85), channel_id=1, source_target_pairs={{4,0},{8,12},{5,1},{9,13},{6,2},{10,14},{7,3},{11,15},{20,16},{24,... | collective-permute-start | bytes 245768 | tf_op jit(solution)/shard_map/ppermute | solution.py:156
  50.8 5.1 %collective-permute-done.5 = bf16[2,4,16,320]{3,1,2,0:T(4,128)(2,1)S(1)} collective-permute-done((bf16[2,4,16,320]{3,1,2,0:T(4,128)(2,1)S(1)}, bf16[2,4,16,320]{3,1,2,0:T(4,128)(2,1)S(1)}, u32[]{:S(2)}, u32[]{:S(2)}) %collective-permute-start.5) | collective-permute-done | bytes 81952 | tf_op jit(solution)/shard_map/ppermute | solution.py:156
  55.9 0.4 fusion.92
  56.3 0.1 pad_maximum_fusion
  56.5 8.1 %all_gather.3 = bf16[8,4,16,640]{3,2,1,0:T(8,128)(2,1)S(1)} all-gather(bf16[2,4,16,640]{3,2,1,0:T(8,128)(2,1)S(1)} %copy.75), channel_id=1, replica_groups=mesh['groups'=2,'pipe'=4,'dp'=2,'mp'=2] {'dp','mp'}, dimensions={0}, use_global_device_ids=true | all-gather | bytes 819200 | tf_op jit(solution)/shard_map/all_gather | solution.py:164
  64.6 0.2 constant_dynamic-slice_fusion.2
  64.8 0.9 %fusion.23 = f32[160,3,3,320]{3,0,2,1:T(8,128)S(1)} fusion(bf16[8,4,16,320]{3,2,1,0:T(8,128)(2,1)S(1)} %slice.48, bf16[8,4,16,160]{3,2,1,0:T(8,128)(2,1)S(1)} %constant_dynamic-slice_fusion.2), kind=kOutput, calls=%fused_computation.35 | convolution fusion | flops 376832000 | bytes 2334720 | tf_op jit(solution)/shard_map/conv_general_dilated | solution.py:31
  65.6 1.5 %copy.78 = f32[160,3,3,320]{3,2,1,0:T(4,128)S(1)} copy(f32[160,3,3,320]{3,0,2,1:T(8,128)S(1)} %fusion.23) | data formatting | bytes 3686400 | tf_op jit(solution)/shard_map/conv_general_dilated | solution.py:31
  67.2 4.6 %reshape.15 = f32[1,460800]{1,0:T(1,128)} reshape(f32[160,3,3,320]{3,2,1,0:T(4,128)S(1)} %copy.78) | data formatting | bytes 3686400 | tf_op jit(solution)/shard_map/reshape | solution.py:168
  (41 shorter events, 1.5 us)
Async XLA Ops:
  10.0 2.1 %copy-start.1 = (bf16[1,2,2,4,16,320]{5,4,3,2,1,0:T(8,128)(2,1)S(1)}, bf16[1,2,2,4,16,320]{5,4,3,2,1,0:T(8,128)(2,1)}, u32[]{:S(2)}) copy-start(bf16[1,2,2,4,16,320]{5,4,3,2,1,0:T(8,128)(2,1)} %param.3) | copy-start | bytes 491524
  11.6 1.0 %copy-start.3 = (pred[32,3]{0,1:T(4,128)(4,1)S(1)}, pred[32,3]{0,1:T(4,128)(4,1)}, u32[]{:S(2)}) copy-start(pred[32,3]{0,1:T(4,128)(4,1)} %constant.61) | copy-start | bytes 292
  11.6 23.5 %collective-permute-start.4 = (bf16[2,160,3,3,320]{4,1,3,2,0:T(8,128)(2,1)}, bf16[2,160,3,3,320]{4,1,3,2,0:T(8,128)(2,1)S(1)}, u32[]{:S(2)}, u32[]{:S(2)}) collective-permute-start(bf16[2,160,3,3,320]{4,1,3,2,0:T(8,128)(2,1)} %copy.53), channel_id=1, source_target_pairs={{0,1},{1,0},{2,3},{3,2},{4,5},{5,4},{6,7},{7,6},{8,9},{9,8},{10,11... | collective-permute-start | bytes 5529608 | tf_op jit(solution)/shard_map/ppermute | solution.py:65
  15.9 6.0 %collective-permute-start = (bf16[2,4,16,160]{3,1,2,0:T(4,128)(2,1)}, bf16[2,4,16,160]{3,1,2,0:T(4,128)(2,1)S(1)}, u32[]{:S(2)}, u32[]{:S(2)}) collective-permute-start(bf16[2,4,16,160]{3,1,2,0:T(4,128)(2,1)} %get-tuple-element.12), channel_id=1, source_target_pairs={{0,1},{1,0},{2,3},{3,2},{4,5},{5,4},{6,7},{7,6},{8,9},{9,8},{10,11... | collective-permute-start | bytes 122888 | tf_op jit(solution)/shard_map/ppermute | solution.py:88
  21.5 8.1 %collective-permute-start.2 = (f32[2,4,16,320]{3,1,2,0:T(4,128)}, f32[2,4,16,320]{3,1,2,0:T(4,128)}, u32[]{:S(2)}, u32[]{:S(2)}) collective-permute-start(f32[2,4,16,320]{3,1,2,0:T(4,128)} %constant_dynamic-slice_fusion), channel_id=1, source_target_pairs={{0,1},{1,0},{2,3},{3,2},{4,5},{5,4},{6,7},{7,6},{8,9},{9,8},{10,11... | collective-permute-start | bytes 491528 | tf_op jit(solution)/shard_map/ppermute | solution.py:88
  22.1 7.2 %collective-permute-start.1 = (bf16[2,4,16,320]{3,1,2,0:T(4,128)(2,1)S(1)}, bf16[2,4,16,320]{3,1,2,0:T(4,128)(2,1)S(1)}, u32[]{:S(2)}, u32[]{:S(2)}) collective-permute-start(bf16[2,4,16,320]{3,1,2,0:T(4,128)(2,1)S(1)} %maximum_select_fusion.1), channel_id=1, source_target_pairs={{0,4},{12,8},{1,5},{13,9},{2,6},{14,10},{3,7},{15,11},{16,20},{28,... | collective-permute-start | bytes 245768 | tf_op jit(solution)/shard_map/ppermute | solution.py:69
  30.5 8.2 %copy-start.2 = (pred[16,3]{0,1:T(4,128)(4,1)S(1)}, pred[16,3]{0,1:T(4,128)(4,1)}, u32[]{:S(2)}) copy-start(pred[16,3]{0,1:T(4,128)(4,1)} %constant.63) | copy-start | bytes 148
  30.6 11.4 %collective-permute-start.3 = (f32[2,4,16,320]{3,1,2,0:T(4,128)S(1)}, f32[2,4,16,320]{3,1,2,0:T(4,128)S(1)}, u32[]{:S(2)}, u32[]{:S(2)}) collective-permute-start(f32[2,4,16,320]{3,1,2,0:T(4,128)S(1)} %dynamic-slice_add_fusion), channel_id=1, source_target_pairs={{0,4},{12,8},{1,5},{13,9},{2,6},{14,10},{3,7},{15,11},{16,20},{28,... | collective-permute-start | bytes 491528 | tf_op jit(solution)/shard_map/ppermute | solution.py:69
  38.8 2.0 %copy-start = (bf16[2,320,3,3,320]{4,1,3,2,0:T(8,128)(2,1)}, bf16[2,320,3,3,320]{4,1,3,2,0:T(8,128)(2,1)S(1)}, u32[]{:S(2)}) copy-start(bf16[2,320,3,3,320]{4,1,3,2,0:T(8,128)(2,1)S(1)} %maximum_select_fusion) | copy-start | bytes 11059204
  49.4 6.5 %collective-permute-start.5 = (bf16[2,4,16,320]{3,1,2,0:T(4,128)(2,1)S(1)}, bf16[2,4,16,320]{3,1,2,0:T(4,128)(2,1)S(1)}, u32[]{:S(2)}, u32[]{:S(2)}) collective-permute-start(bf16[2,4,16,320]{3,1,2,0:T(4,128)(2,1)S(1)} %fusion.85), channel_id=1, source_target_pairs={{4,0},{8,12},{5,1},{9,13},{6,2},{10,14},{7,3},{11,15},{20,16},{24,... | collective-permute-start | bytes 245768 | tf_op jit(solution)/shard_map/ppermute | solution.py:156

commit v5 on v4

--- a/solution.py
+++ b/solution.py
@@ -61,7 +61,10 @@
     theirs = (1 - lane) * per_lane
 
     chan_half = section_weight.shape[-1] // (9 * channels)
-    own = lax.optimization_barrier(section_weight[0].reshape(2, chan_half, 3, 3, channels))
+    own = lax.optimization_barrier(
+        section_weight[0].reshape(2, chan_half, 9, channels).transpose(0, 2, 1, 3)
+        .reshape(2, 3, 3, chan_half, channels)
+    ).transpose(0, 3, 1, 2, 4)
     other = lax.ppermute(own, "mp", swap)
 
     def up(t, v):
@@ -85,9 +88,10 @@
     h1_half = bf16(f32(own_in) + conv(act_all, own[0]))
     seed_half = lax.dynamic_slice_in_dim(grads, low, chan_half, 3)
     d_part = conv_t(seed_half, own[1])
-    h1_got, d_got = lax.ppermute((take(h1_half, theirs), take(d_part, theirs)), "mp", swap)
-    h1 = join(take(h1_half, mine), h1_got)
-    d_last = take(d_part, mine) + d_got
+    h1_all = lax.all_gather(h1_half, "mp", axis=3, tiled=False)
+    d_all = lax.all_gather(d_part, "mp", axis=0, tiled=False)
+    h1 = take(jnp.concatenate([h1_all[..., 0, :], h1_all[..., 1, :]], -1), mine)
+    d_last = take(d_all[0] + d_all[1], mine)
     x0 = take(samples, mine)
     a0 = take(act_all, mine)
     seed = take(grads, mine)

time: 72.2 us -> 69.7 us (0.965)
  blocking collectives: 8.11 us -> 13.4 us
  starting transfers between devices: 11.4 us -> 7.91 us
  matrix products: 11.9 us -> 9.33 us
  waiting for transfers between devices: 7.67 us -> 5.41 us
  other arithmetic: 6.84 us -> 7.67 us
    all_gather x0 -> x2, blocking collectives: none -> 5.24 us  [the longest x1 2.74 us: local(): h1_all = lax.all_gather(h1_half, 'mp', axis=3, tiled=False)]
    ppermute x2, starting transfers between devices: 9.15 us -> 6.1 us  [up(): return lax.ppermute(v, 'pipe', pairs)]
    transpose x0 -> x1, local copies, waits for them, and re-layouts: none -> 2.66 us  [local(): section_weight[0].reshape(2, chan_half, 9, channels).transpose(0, 2, 1, 3)]
    ppermute x2, waiting for transfers between devices: 2.57 us -> 0.01 us  [up(): return lax.ppermute(v, 'pipe', pairs)]
    optimization_barrier x1 -> x0, local copies, waits for them, and re-layouts: 1.68 us -> none  [local(): lax.optimization_barrier(section_weight[0].reshape(2, chan_half, 3, 3, ch...]
    another operation x1, local copies, waits for them, and re-layouts: 6.05 us -> 4.5 us  [local(): section_weight[0].reshape(2, chan_half, 9, channels).transpose(0, 2, 1, 3)]
    dynamic_slice x2 -> x0, local copies, waits for them, and re-layouts: 1.39 us -> none  [take(): return lax.dynamic_slice_in_dim(v, at, per_lane, 0)]
    conv_general_dilated x0 -> x6, other arithmetic: none -> 1.28 us  [the longest x3 0.67 us: conv(): lax.conv_general_dilated(act, weight, (1, 1), ((1, 1), (1, 1)), dimension...]
  transfers between devices with their start and end apart: 6 -> 4, of which waited for: 2 -> 1; matrix products, arithmetic and copies ran while one was open for 23% -> 24% of each run, Pallas kernels for 0% -> 0%
where the time goes in v5:
time: 69.7 us; the launch traced here: 69.3 us
  local copies, waits for them, and re-layouts  25 us (36%)
  blocking collectives  13.4 us (19%)
  matrix products  9.33 us (13%)
  starting transfers between devices  7.91 us (11%)
  other arithmetic  7.67 us (11%)
  waiting for transfers between devices  5.41 us (8%)
    all_gather x1, blocking collectives, local(): every = lax.all_gather(both, ('dp', 'mp'), axis=0, tiled=True)  8.11 us
    ppermute x2, starting transfers between devices, up(): return lax.ppermute(v, 'pipe', pairs)  6.1 us
    unnamed x25, local copies, waits for them, and re-layouts  5.98 us
    conv_general_dilated x3, matrix products, conv_t(): lax.conv_general_dilated(flipped, weight, (1, 1), ((1, 1), (1, 1)), dimen...  5.55 us
    ppermute x1, waiting for transfers between devices, local(): lax.ppermute(jnp.where(lower, c0, a_last), 'pipe', [(1, 0), (pipe_size -...  5.4 us
    reshape x1, local copies, waits for them, and re-layouts, local(): return grad.reshape(1, -1)  4.57 us
    another operation x1, local copies, waits for them, and re-layouts, local(): section_weight[0].reshape(2, chan_half, 9, channels).transpose(0, 2, 1, 3)  4.5 us
    select_n x1, other arithmetic, local(): jnp.where(lane == 0, jnp.concatenate([own, other], 1), jnp.concatenate([o...  3.6 us
  transfers between devices with their start and end apart: 4, of which 1 were waited for; matrix products, arithmetic and copies ran while one was open for 24% of the time, Pallas kernels for 0%

profile of v5, /device:TPU:0, one launch (start us, length us, event | category | flops | bytes accessed | tf_op | source)
XLA Modules:
  0.0 69.3 jit_solution(2031037616548605368)
XLA Ops:
  0.0 2.7 %reshape.89 = bf16[921600]{0:T(1024)(128)(2,1)S(1)} reshape(bf16[1,2,460800]{2,1,0:T(2,128)(2,1)} %param.4) | data formatting | bytes 3686400
  2.7 4.5 %reshape_squeeze.3 = bf16[2,160,9,320]{3,2,1,0:T(8,128)(2,1)} reshape(bf16[921600]{0:T(1024)(128)(2,1)S(1)} %reshape.89) | data formatting | bytes 3686400 | tf_op jit(solution)/shard_map/reshape;squeeze | solution.py:65
  7.2 2.7 %copy.81 = bf16[2,9,160,320]{3,2,1,0:T(8,128)(2,1)S(1)} copy(bf16[2,9,160,320]{3,1,2,0:T(8,128)(2,1)} %bitcast.116) | data formatting | bytes 3686400 | tf_op jit(solution)/shard_map/transpose | solution.py:65
  9.8 0.5 collective-permute-start.2
  10.4 0.1 fusion.20
  10.5 0.7 copy-done.1
  11.2 0.2 copy.122
  11.5 0.2 fusion.10
  11.8 0.9 %convolution_select_fusion.1 = f32[4,32,3,160]{3,1,2,0:T(8,128)S(1)} fusion(bf16[2,160,3,3,320]{4,1,3,2,0:T(8,128)(2,1)S(1)} %bitcast.118, bf16[4,4,8,5,320]{4,1,3,2,0:T(4,128)(2,1)S(1)} %fusion.10, pred[32,3]{0,1:T(4,128)(4,1)S(1)} %copy-done.6), kind=kOutput, calls=%fused_computation.8 | convolution fusion | flops 294973440 | bytes 1843712 | tf_op jit(solution)/shard_map/conv_general_dilated | solution.py:13
  12.7 0.3 copy.82
  13.1 0.5 copy.84
  13.6 2.7 %all-gather = bf16[4,4,16,320]{2,1,0,3:T(4,128)(2,1)S(1)} all-gather(bf16[4,4,16,160]{2,1,0,3:T(4,128)(2,1)S(1)} %copy.84), channel_id=2, replica_groups=mesh['groups'=2,'pipe'=4,'dp'=2,'mp'=2] {'mp'}, dimensions={3}, use_global_device_ids=true | all-gather | bytes 245760 | tf_op jit(solution)/shard_map/all_gather | solution.py:91
  16.4 0.5 fusion.77
  16.8 1.2 %copy.115 = bf16[4,4,16,1,160]{4,2,1,0,3:T(8,128)(2,1)} copy(bf16[4,4,16,1,160]{2,1,0,4,3:T(4,128)(2,1)S(1)} %get-tuple-element.10) | data formatting | bytes 163840
  18.0 0.5 copy.112
  18.6 0.9 %fusion.71 = bf16[2,4,16,320]{3,2,1,0:T(8,128)(2,1)S(1)} fusion(s32[]{:T(128)S(6)} %select_n.52, bf16[4,4,16,160]{3,2,1,0:T(8,128)(2,1)} %bitcast.150, bf16[4,4,16,160]{3,2,1,0:T(8,128)(2,1)S(1)} %bitcast.151), kind=kLoop, calls=%fused_computation.114 | loop fusion | flops 163840 | bytes 245764 | tf_op jit(solution)/shard_map/concatenate | solution.py:93
  19.5 4.6 %collective-permute-start = (bf16[2,4,16,320]{3,2,1,0:T(8,128)(2,1)S(1)}, bf16[2,4,16,320]{3,2,1,0:T(8,128)(2,1)S(1)}, u32[]{:S(2)}, u32[]{:S(2)}) collective-permute-start(bf16[2,4,16,320]{3,2,1,0:T(8,128)(2,1)S(1)} %fusion.71), channel_id=1, source_target_pairs={{0,4},{12,8},{1,5},{13,9},{2,6},{14,10},{3,7},{15,11},{16,20},{28,... | collective-permute-start | bytes 245768 | tf_op jit(solution)/shard_map/ppermute | solution.py:72
  24.1 1.0 %constant_dynamic-slice_fusion = bf16[4,4,16,160]{3,2,1,0:T(8,128)(2,1)S(1)} fusion(bf16[4,4,16,320]{3,2,1,0:T(8,128)(2,1)} %bitcast.146, s32[]{:T(128)S(6)} %select_n.53), kind=kLoop, calls=%fused_computation.117 | loop fusion | bytes 163844 | tf_op jit(solution)/shard_map/dynamic_slice | solution.py:89
  25.2 0.1 rev.22
  25.6 0.2 fusion.23
  25.7 0.8 %convolution_select_fusion = f32[4,32,3,320]{3,1,2,0:T(8,128)S(1)} fusion(bf16[2,160,3,3,320]{4,1,3,2,0:T(8,128)(2,1)S(1)} %bitcast.119, bf16[4,4,8,5,160]{4,1,3,2,0:T(4,128)(2,1)S(1)} %fusion.23, pred[32,3]{0,1:T(4,128)(4,1)S(1)} %copy-done.6), kind=kOutput, calls=%fused_computation.7 | convolution fusion | flops 295034880 | bytes 1925632 | tf_op jit(solution)/shard_map/conv_general_dilated | solution.py:22
  26.5 0.4 copy.89
  27.0 0.6 rev.23
  27.6 2.5 %all-gather.1 = f32[8,4,16,320]{3,2,1,0:T(8,128)S(1)} all-gather(f32[4,4,16,320]{3,2,1,0:T(8,128)S(1)} %copy.90), channel_id=3, replica_groups=mesh['groups'=2,'pipe'=4,'dp'=2,'mp'=2] {'mp'}, dimensions={0}, use_global_device_ids=true | all-gather | bytes 983040 | tf_op jit(solution)/shard_map/all_gather | solution.py:92
  30.2 0.7 %dynamic-slice_add_fusion = f32[2,4,16,320]{3,2,1,0:T(8,128)} fusion(f32[4,4,16,320]{3,2,1,0:T(8,128)S(1)} %get-tuple-element.12, s32[]{:T(128)S(6)} %select_n.52, f32[4,4,16,320]{3,2,1,0:T(8,128)S(1)} %get-tuple-element.11), kind=kLoop, calls=%fused_computation.83 | loop fusion | flops 40960 | bytes 491524 | tf_op jit(solution)/shard_map/add | solution.py:94
  30.9 1.5 %collective-permute-start.1 = (f32[2,4,16,320]{3,2,1,0:T(8,128)}, f32[2,4,16,320]{3,2,1,0:T(8,128)S(1)}, u32[]{:S(2)}, u32[]{:S(2)}) collective-permute-start(f32[2,4,16,320]{3,2,1,0:T(8,128)} %dynamic-slice_add_fusion), channel_id=1, source_target_pairs={{0,4},{12,8},{1,5},{13,9},{2,6},{14,10},{3,7},{15,11},{16,20},{28,... | collective-permute-start | bytes 491528 | tf_op jit(solution)/shard_map/ppermute | solution.py:72
  32.8 0.2 fusion.29
  33.1 3.6 %maximum_select_fusion = bf16[2,320,3,3,320]{4,1,3,2,0:T(8,128)(2,1)S(1)} fusion(bf16[2,160,3,3,320]{4,1,3,2,0:T(8,128)(2,1)} %collective-permute-done.2, bf16[2,160,3,3,320]{4,1,3,2,0:T(8,128)(2,1)S(1)} %bitcast.120, pred[]{:T(512)S(6)} %eq.3), kind=kLoop, calls=%fused_computation | loop fusion | flops 16588800 | bytes 7372801 | tf_op jit(solution)/shard_map/jit(_where)/select_n | solution.py:102
  36.7 1.0 %fusion.6 = f32[4,16,3,320]{3,1,2,0:T(8,128)S(1)} fusion(bf16[2,320,3,3,320]{4,1,3,2,0:T(8,128)(2,1)S(1)} %maximum_select_fusion, bf16[4,2,8,5,320]{4,1,3,2,0:T(2,128)(2,1)S(1)} %fusion.29, pred[16,3]{0,1:T(4,128)(4,1)S(1)} %copy-done.5), kind=kOutput, calls=%fused_computation.11 | convolution fusion | flops 294973440 | bytes 2703872 | tf_op jit(solution)/shard_map/conv_general_dilated | solution.py:13
  38.3 0.2 fusion.30
  38.5 0.2 copy-done
  38.7 1.0 %fusion.4 = f32[4,16,3,320]{3,1,2,0:T(8,128)S(1)} fusion(bf16[2,320,3,3,320]{4,1,3,2,0:T(8,128)(2,1)S(1)} %maximum_select_fusion, bf16[4,2,8,5,320]{4,1,3,2,0:T(2,128)(2,1)S(1)} %fusion.30, pred[16,3]{0,1:T(4,128)(4,1)S(1)} %copy-done.5), kind=kOutput, calls=%fused_computation.9 | convolution fusion | flops 294973440 | bytes 2703872 | tf_op jit(solution)/shard_map/conv_general_dilated | solution.py:13
  39.9 0.1 add_convert_fusion.3
  40.0 0.1 rev.24
  40.5 0.2 fusion.31
  40.7 2.4 %fusion.5 = f32[4,16,3,320]{3,1,2,0:T(8,128)S(1)} fusion(bf16[2,320,3,3,320]{4,1,3,2,0:T(8,128)(2,1)} %copy-done, bf16[4,2,8,5,320]{4,1,3,2,0:T(2,128)(2,1)S(1)} %fusion.31, pred[16,3]{0,1:T(4,128)(4,1)S(1)} %copy-done.5), kind=kOutput, calls=%fused_computation.10 | convolution fusion | flops 294973440 | bytes 2662448 | tf_op jit(solution)/shard_map/conv_general_dilated | solution.py:22
  43.5 0.1 rev.26
  43.9 0.2 fusion.32
  44.2 2.4 %fusion.7 = f32[4,16,3,320]{3,1,2,0:T(8,128)S(1)} fusion(bf16[2,320,3,3,320]{4,1,3,2,0:T(8,128)(2,1)} %copy-done, bf16[4,2,8,5,320]{4,1,3,2,0:T(2,128)(2,1)S(1)} %fusion.32, pred[16,3]{0,1:T(4,128)(4,1)S(1)} %copy-done.5), kind=kOutput, calls=%fused_computation.12 | convolution fusion | flops 294973440 | bytes 2662448 | tf_op jit(solution)/shard_map/conv_general_dilated | solution.py:22
  46.8 0.2 fusion.62
  47.0 1.3 %collective-permute-start.3 = (bf16[2,4,16,320]{3,2,1,0:T(8,128)(2,1)S(1)}, bf16[2,4,16,320]{3,2,1,0:T(8,128)(2,1)S(1)}, u32[]{:S(2)}, u32[]{:S(2)}) collective-permute-start(bf16[2,4,16,320]{3,2,1,0:T(8,128)(2,1)S(1)} %fusion.62), channel_id=1, source_target_pairs={{4,0},{8,12},{5,1},{9,13},{6,2},{10,14},{7,3},{11,15},{20,16},{24,... | collective-permute-start | bytes 245768 | tf_op jit(solution)/shard_map/ppermute | solution.py:160
  48.4 5.4 %collective-permute-done.3 = bf16[2,4,16,320]{3,2,1,0:T(8,128)(2,1)S(1)} collective-permute-done((bf16[2,4,16,320]{3,2,1,0:T(8,128)(2,1)S(1)}, bf16[2,4,16,320]{3,2,1,0:T(8,128)(2,1)S(1)}, u32[]{:S(2)}, u32[]{:S(2)}) %collective-permute-start.3) | collective-permute-done | bytes 81952 | tf_op jit(solution)/shard_map/ppermute | solution.py:160
  53.8 0.2 fusion.69
  54.0 8.1 %all_gather.19 = bf16[8,4,16,640]{3,2,1,0:T(8,128)(2,1)S(1)} all-gather(bf16[2,4,16,640]{3,2,1,0:T(8,128)(2,1)S(1)} %pad_maximum_fusion), channel_id=1, replica_groups=mesh['groups'=2,'pipe'=4,'dp'=2,'mp'=2] {'dp','mp'}, dimensions={0}, use_global_device_ids=true | all-gather | bytes 819200 | tf_op jit(solution)/shard_map/all_gather | solution.py:168
  62.2 0.2 constant_dynamic-slice_fusion.1
  62.3 0.9 %fusion.21 = f32[160,3,3,320]{3,0,2,1:T(8,128)S(1)} fusion(bf16[8,4,16,320]{3,2,1,0:T(8,128)(2,1)S(1)} %slice.70, bf16[8,4,16,160]{3,2,1,0:T(8,128)(2,1)S(1)} %constant_dynamic-slice_fusion.1), kind=kOutput, calls=%fused_computation.34 | convolution fusion | flops 376832000 | bytes 2334720 | tf_op jit(solution)/shard_map/conv_general_dilated | solution.py:31
  63.2 1.5 %copy.109 = f32[160,3,3,320]{3,2,1,0:T(4,128)S(1)} copy(f32[160,3,3,320]{3,0,2,1:T(8,128)S(1)} %fusion.21) | data formatting | bytes 3686400 | tf_op jit(solution)/shard_map/conv_general_dilated | solution.py:31
  64.7 4.6 %reshape.21 = f32[1,460800]{1,0:T(1,128)} reshape(f32[160,3,3,320]{3,2,1,0:T(4,128)S(1)} %copy.109) | data formatting | bytes 3686400 | tf_op jit(solution)/shard_map/reshape | solution.py:172
  (57 shorter events, 3.0 us)
Async XLA Ops:
  7.2 3.2 %copy-start.3 = (bf16[1,2,2,4,16,320]{5,4,3,2,1,0:T(8,128)(2,1)S(1)}, bf16[1,2,2,4,16,320]{5,4,3,2,1,0:T(8,128)(2,1)}, u32[]{:S(2)}) copy-start(bf16[1,2,2,4,16,320]{5,4,3,2,1,0:T(8,128)(2,1)} %param.3) | copy-start | bytes 491524
  9.8 1.9 %copy-start.6 = (pred[32,3]{0,1:T(4,128)(4,1)S(1)}, pred[32,3]{0,1:T(4,128)(4,1)}, u32[]{:S(2)}) copy-start(pred[32,3]{0,1:T(4,128)(4,1)} %constant.60) | copy-start | bytes 292
  9.8 23.2 %collective-permute-start.2 = (bf16[2,160,3,3,320]{4,1,3,2,0:T(8,128)(2,1)S(1)}, bf16[2,160,3,3,320]{4,1,3,2,0:T(8,128)(2,1)}, u32[]{:S(2)}, u32[]{:S(2)}) collective-permute-start(bf16[2,160,3,3,320]{4,1,3,2,0:T(8,128)(2,1)S(1)} %bitcast.117), channel_id=1, source_target_pairs={{0,1},{1,0},{2,3},{3,2},{4,5},{5,4},{6,7},{7,6},{8,9},{9,8},{10,11... | collective-permute-start | bytes 5529608 | tf_op jit(solution)/shard_map/ppermute | solution.py:68
  10.5 0.7 copy-start.1
  19.5 12.9 %collective-permute-start = (bf16[2,4,16,320]{3,2,1,0:T(8,128)(2,1)S(1)}, bf16[2,4,16,320]{3,2,1,0:T(8,128)(2,1)S(1)}, u32[]{:S(2)}, u32[]{:S(2)}) collective-permute-start(bf16[2,4,16,320]{3,2,1,0:T(8,128)(2,1)S(1)} %fusion.71), channel_id=1, source_target_pairs={{0,4},{12,8},{1,5},{13,9},{2,6},{14,10},{3,7},{15,11},{16,20},{28,... | collective-permute-start | bytes 245768 | tf_op jit(solution)/shard_map/ppermute | solution.py:72
  27.6 4.8 %copy-start.2 = (bf16[4,4,16,320]{3,2,1,0:T(8,128)(2,1)S(1)}, bf16[4,4,16,320]{3,2,1,0:T(8,128)(2,1)}, u32[]{:S(2)}) copy-start(bf16[4,4,16,320]{3,2,1,0:T(8,128)(2,1)} %copy-done.1) | copy-start | bytes 491524
  30.9 9.0 %collective-permute-start.1 = (f32[2,4,16,320]{3,2,1,0:T(8,128)}, f32[2,4,16,320]{3,2,1,0:T(8,128)S(1)}, u32[]{:S(2)}, u32[]{:S(2)}) collective-permute-start(f32[2,4,16,320]{3,2,1,0:T(8,128)} %dynamic-slice_add_fusion), channel_id=1, source_target_pairs={{0,4},{12,8},{1,5},{13,9},{2,6},{14,10},{3,7},{15,11},{16,20},{28,... | collective-permute-start | bytes 491528 | tf_op jit(solution)/shard_map/ppermute | solution.py:72
  33.0 3.6 %copy-start.5 = (pred[16,3]{0,1:T(4,128)(4,1)S(1)}, pred[16,3]{0,1:T(4,128)(4,1)}, u32[]{:S(2)}) copy-start(pred[16,3]{0,1:T(4,128)(4,1)} %constant.62) | copy-start | bytes 148
  36.7 2.0 %copy-start = (bf16[2,320,3,3,320]{4,1,3,2,0:T(8,128)(2,1)}, bf16[2,320,3,3,320]{4,1,3,2,0:T(8,128)(2,1)S(1)}, u32[]{:S(2)}) copy-start(bf16[2,320,3,3,320]{4,1,3,2,0:T(8,128)(2,1)S(1)} %maximum_select_fusion) | copy-start | bytes 11059204
  38.7 1.2 %copy-start.4 = (bf16[1,2,2,4,16,320]{5,4,3,2,1,0:T(8,128)(2,1)S(1)}, bf16[1,2,2,4,16,320]{5,4,3,2,1,0:T(8,128)(2,1)}, u32[]{:S(2)}) copy-start(bf16[1,2,2,4,16,320]{5,4,3,2,1,0:T(8,128)(2,1)} %param.5) | copy-start | bytes 491524
  47.0 6.7 %collective-permute-start.3 = (bf16[2,4,16,320]{3,2,1,0:T(8,128)(2,1)S(1)}, bf16[2,4,16,320]{3,2,1,0:T(8,128)(2,1)S(1)}, u32[]{:S(2)}, u32[]{:S(2)}) collective-permute-start(bf16[2,4,16,320]{3,2,1,0:T(8,128)(2,1)S(1)} %fusion.62), channel_id=1, source_target_pairs={{4,0},{8,12},{5,1},{9,13},{6,2},{10,14},{7,3},{11,15},{20,16},{24,... | collective-permute-start | bytes 245768 | tf_op jit(solution)/shard_map/ppermute | solution.py:160

commit v6 on v5

--- a/solution.py
+++ b/solution.py
@@ -43,7 +43,7 @@
     return v.astype(jnp.bfloat16)
 
 
-def local(latent, section_weight, out_grad):
+def local_general(latent, section_weight, out_grad):
     pipe_size = lax.axis_size("pipe")
     half = pipe_size // 2
     device = lax.axis_index("pipe")
@@ -172,6 +172,101 @@
     return grad.reshape(1, -1)
 
 
+def on_stage(active, fn, *args):
+    shapes = jax.eval_shape(fn, *args)
+    def idle(*unused):
+        return jax.tree.map(lambda v: jnp.zeros(v.shape, v.dtype), shapes)
+    return lax.cond(active, fn, idle, *args)
+
+
+def local(latent, section_weight, out_grad):
+    pipe_size = lax.axis_size("pipe")
+    half = pipe_size // 2
+    if half != 2:
+        return local_general(latent, section_weight, out_grad)
+    device = lax.axis_index("pipe")
+    lower = device < half
+    stage = jnp.minimum(device, pipe_size - 1 - device)
+    lane = lax.axis_index("mp")
+    swap = [(0, 1), (1, 0)]
+
+    channels = latent.shape[-1]
+    img = latent.shape[-3:]
+    samples = latent.reshape((-1,) + img)
+    grads = out_grad.reshape((-1,) + img)
+    per_lane = samples.shape[0] // 2
+    mine = lane * per_lane
+    chan_half = section_weight.shape[-1] // (9 * channels)
+    low = lane * chan_half
+
+    def take(v, at):
+        return lax.dynamic_slice_in_dim(v, at, per_lane, 0)
+
+    own = lax.optimization_barrier(
+        section_weight[0].reshape(2, chan_half, 9, channels).transpose(0, 2, 1, 3)
+        .reshape(2, 3, 3, chan_half, channels)
+    ).transpose(0, 3, 1, 2, 4)
+
+    x0 = take(samples, mine)
+    seed = take(grads, mine)
+    a0 = bf16(jax.nn.silu(f32(x0)))
+
+    def first(samples, grads, own):
+        act_all = bf16(jax.nn.silu(f32(samples)))
+        own_in = lax.dynamic_slice_in_dim(samples, low, chan_half, 3)
+        h1_half = bf16(f32(own_in) + conv(act_all, own[0]))
+        seed_half = lax.dynamic_slice_in_dim(grads, low, chan_half, 3)
+        d_part = conv_t(seed_half, own[1])
+        h1_all = lax.all_gather(h1_half, "mp", axis=3, tiled=False)
+        d_all = lax.all_gather(d_part, "mp", axis=0, tiled=False)
+        h1 = take(jnp.concatenate([h1_all[..., 0, :], h1_all[..., 1, :]], -1), mine)
+        return h1, take(d_all[0] + d_all[1], mine)
+
+    def weights(own):
+        other = lax.ppermute(own, "mp", swap)
+        return jnp.where(lane == 0, jnp.concatenate([own, other], 1),
+                         jnp.concatenate([other, own], 1))
+
+    h1, d_last = on_stage(stage == 0, first, samples, grads, own)
+    full = on_stage(stage == 1, weights, own)
+    ups = [(0, 1), (pipe_size - 1, pipe_size - 2)]
+    h1_r = lax.ppermute(h1, "pipe", ups)
+    d_last_r = lax.ppermute(d_last, "pipe", ups)
+
+    def middle(h1_r, d_last_r, seed, full, lower):
+        w_enc, w_dec = full[0], full[1]
+        u1 = f32(h1_r)
+        a1 = bf16(jax.nn.silu(u1))
+        h2 = bf16(u1 + conv(a1, w_enc))
+        u2 = f32(h2) + f32(h2)
+        a2 = bf16(jax.nn.silu(u2))
+        h3 = bf16(f32(h2) + conv(a2, w_dec))
+        u3 = f32(h3) + u1
+        a3 = bf16(jax.nn.silu(u3))
+        b3 = d_last_r * silu_slope(u3)
+        c2 = bf16(f32(seed) + b3)
+        b2 = conv_t(c2, w_dec) * silu_slope(u2)
+        g2 = bf16(f32(c2) + b2)
+        c1 = bf16(f32(g2) + b2)
+        b1 = conv_t(c1, w_enc) * silu_slope(u1)
+        g1 = bf16(f32(c1) + b1)
+        c0 = bf16(f32(g1) + f32(bf16(b3)))
+        return (jnp.where(lower, c0, a3), jnp.where(lower, a1, a2),
+                jnp.where(lower, c1, c2))
+
+    back, act1, cot1 = on_stage(stage == 1, middle, h1_r, d_last_r, seed, full, lower)
+    sent = lax.ppermute(back, "pipe", [(1, 0), (pipe_size - 2, pipe_size - 1)])
+
+    act_sel = jnp.where(stage == 0, jnp.where(lower, a0, sent), act1)
+    cot_sel = jnp.where(stage == 0, jnp.where(lower, sent, seed), cot1)
+    both = jnp.concatenate([act_sel, cot_sel], axis=-1)
+    every = lax.all_gather(both, ("dp", "mp"), axis=0, tiled=True)
+    act_all = every[..., :channels]
+    cot_all = lax.dynamic_slice_in_dim(every, channels + low, chan_half, 3)
+    grad = weight_grad(act_all, cot_all)
+    return grad.reshape(1, -1)
+
+
 def solution(mesh):
     return jax.shard_map(
         local,

time: 69.7 us -> 72.5 us (1.040)
  waiting for transfers between devices: 5.41 us -> 21.7 us
  matrix products: 9.33 us -> 3.32 us
  other arithmetic: 7.67 us -> 2.6 us
  starting transfers between devices: 7.91 us -> 3.89 us
  blocking collectives: 13.4 us -> 14.3 us
  local copies, waits for them, and re-layouts: 25 us -> 25.8 us
    ppermute x4 -> x3, waiting for transfers between devices: 5.41 us -> 21.7 us  [the longest x1 18.7 us: local(): sent = lax.ppermute(back, 'pipe', [(1, 0), (pipe_size - 2, pipe_size - 1)])]
    conv_general_dilated x3 -> x1, matrix products: 5.55 us -> 0.82 us  [conv_t(): lax.conv_general_dilated(flipped, weight, (1, 1), ((1, 1), (1, 1)), dimen...]
    ppermute x4 -> x3, starting transfers between devices: 7.91 us -> 3.89 us  [the longest x1 1.3 us: local(): d_last_r = lax.ppermute(d_last, 'pipe', ups)]
    select_n x3 -> x1, other arithmetic: 3.96 us -> 0.12 us  [local(): act_sel = jnp.where(stage == 0, jnp.where(lower, a0, sent), act1)]
    unnamed x25 -> x9, local copies, waits for them, and re-layouts: 5.98 us -> 2.68 us
    cond x0 -> x8, local copies, waits for them, and re-layouts: none -> 2.97 us
    another operation x2 -> x6, local copies, waits for them, and re-layouts: 0.04 us -> 2.91 us  [the longest x1 0.02 us: local(): cots_up = jnp.stack([seed] + [dec_c[t] for t in range(1, half)])]
    conv_general_dilated x3 -> x1, matrix products: 2.91 us -> 1.64 us  [conv(): lax.conv_general_dilated(act, weight, (1, 1), ((1, 1), (1, 1)), dimension...]
  transfers between devices with their start and end apart: 4 -> 3, of which waited for: 1 -> 2; matrix products, arithmetic and copies ran while one was open for 24% -> 4% of each run, Pallas kernels for 0% -> 0%
where the time goes in v6:
time: 72.5 us; the launch traced here: 72.2 us
  local copies, waits for them, and re-layouts  25.8 us (36%)
  waiting for transfers between devices  21.7 us (30%)
  blocking collectives  14.3 us (20%)
  starting transfers between devices  3.89 us (5%)
  matrix products  3.32 us (5%)
  other arithmetic  2.6 us (4%)
    ppermute x1, waiting for transfers between devices, local(): sent = lax.ppermute(back, 'pipe', [(1, 0), (pipe_size - 2, pipe_size - 1)])  18.7 us
    all_gather x1, blocking collectives, local(): every = lax.all_gather(both, ('dp', 'mp'), axis=0, tiled=True)  9.08 us
    reshape x1, local copies, waits for them, and re-layouts, local(): return grad.reshape(1, -1)  4.57 us
    another operation x1, local copies, waits for them, and re-layouts, local(): section_weight[0].reshape(2, chan_half, 9, channels).transpose(0, 2, 1, 3)  4.48 us
    ppermute x1, waiting for transfers between devices, local(): h1_r = lax.ppermute(h1, 'pipe', ups)  3.03 us
    another operation x6, local copies, waits for them, and re-layouts  2.91 us
    all_gather x1, blocking collectives, first(): h1_all = lax.all_gather(h1_half, 'mp', axis=3, tiled=False)  2.74 us
    unnamed x9, local copies, waits for them, and re-layouts  2.68 us
  transfers between devices with their start and end apart: 3, of which 2 were waited for; matrix products, arithmetic and copies ran while one was open for 4% of the time, Pallas kernels for 0%

profile of v6, /device:TPU:0, one launch (start us, length us, event | category | flops | bytes accessed | tf_op | source)
XLA Modules:
  0.0 72.2 jit_solution(18316323686638947715)
XLA Ops:
  0.0 2.7 %reshape.85 = bf16[921600]{0:T(1024)(128)(2,1)S(1)} reshape(bf16[1,2,460800]{2,1,0:T(2,128)(2,1)} %param.10) | data formatting | bytes 3686400
  2.7 4.5 %reshape_squeeze.3 = bf16[2,160,9,320]{3,2,1,0:T(8,128)(2,1)} reshape(bf16[921600]{0:T(1024)(128)(2,1)S(1)} %reshape.85) | data formatting | bytes 3686400 | tf_op jit(solution)/shard_map/reshape;squeeze | solution.py:206
  7.2 2.7 %copy.138 = bf16[2,9,160,320]{3,2,1,0:T(8,128)(2,1)S(1)} copy(bf16[2,9,160,320]{3,1,2,0:T(8,128)(2,1)} %bitcast.99) | data formatting | bytes 3686400 | tf_op jit(solution)/shard_map/transpose | solution.py:206
  9.8 16.2 %conditional.3 = (bf16[2,4,16,320]{3,2,1,0:T(8,128)(2,1)S(1)}, f32[2,4,16,320]{3,2,1,0:T(8,128)}) conditional(s32[]{:T(128)} %convert_element_type.90, () %tuple.28, (s32[]{:T(128)}, bf16[4,4,16,320]{3,2,1,0:T(8,128)(2,1)S(1)}, bf16[2,160,3,3,320]{4,1,3,2,0:T(8,128)(2,1)S(1)}, s32[]{:T(128)}, bf16[4,4,16,320]{3,2,1,0:T(8,128)(2,1)S(1)}) %tuple.67), branch_computations={%region_2.3_spmd, %region_3.4_spmd} | conditional | flops 592670720 | bytes 15515140 | solution.py:179
  9.9 0.2 copy.140
  10.0 0.0 copy-start.6
  10.0 0.2 constant_dynamic-slice_fusion
  10.3 0.1 pad.2
  10.4 0.2 fusion.12
  10.6 0.2 fusion.17
  10.8 0.2 copy.159
  10.9 0.1 pad.clone
  11.1 0.1 slice.42
  11.1 0.2 fusion.6
  11.4 1.6 %convolution_select_fusion.1 = f32[4,32,3,160]{3,1,2,0:T(8,128)} fusion(bf16[2,160,3,3,320]{4,1,3,2,0:T(8,128)(2,1)S(1)} %get-tuple-element.36, bf16[4,4,8,5,320]{4,1,3,2,0:T(4,128)(2,1)S(1)} %fusion.6, pred[32,3]{0,1:T(4,128)(4,1)S(1)} %copy-done.6), kind=kOutput, calls=%fused_computation.2 | convolution fusion | flops 294973440 | bytes 1843712 | tf_op jit(solution)/shard_map/cond/branch_1_fun/conv_general_dilated | solution.py:13
  13.0 0.8 %convolution_select_fusion = f32[4,32,3,320]{3,1,2,0:T(8,128)S(1)} fusion(bf16[2,160,3,3,320]{4,1,3,2,0:T(8,128)(2,1)S(1)} %get-tuple-element.36, bf16[4,4,8,5,160]{4,1,3,2,0:T(4,128)(2,1)S(1)} %fusion.12, pred[32,3]{0,1:T(4,128)(4,1)S(1)} %copy-done.6), kind=kOutput, calls=%fused_computation.1 | convolution fusion | flops 295034880 | bytes 1925632 | tf_op jit(solution)/shard_map/cond/branch_1_fun/conv_general_dilated | solution.py:22
  13.8 0.4 copy.124
  14.3 0.6 rev.17
  14.9 1.3 %copy.120 = f32[4,32,3,160]{3,0,2,1:T(4,128)S(1)} copy(f32[4,32,3,160]{3,1,2,0:T(8,128)} %convolution_select_fusion.1) | data formatting | bytes 491520 | tf_op jit(solution)/shard_map/cond/branch_1_fun/conv_general_dilated | solution.py:13
  16.1 0.1 copy.139
  16.2 0.2 fusion.16
  16.4 2.4 %all-gather.1 = f32[8,4,16,320]{3,2,1,0:T(8,128)S(1)} all-gather(f32[4,4,16,320]{3,2,1,0:T(8,128)S(1)} %copy.125), channel_id=3, replica_groups=mesh['groups'=2,'pipe'=4,'dp'=2,'mp'=2] {'mp'}, dimensions={0}, use_global_device_ids=true | all-gather | bytes 983040 | tf_op jit(solution)/shard_map/cond/branch_1_fun/all_gather | solution.py:221
  18.8 0.1 fusion.93
  18.9 0.7 dynamic-slice_add_fusion
  19.6 0.6 copy.121
  20.2 2.7 %all-gather = bf16[4,4,16,320]{2,1,0,3:T(4,128)(2,1)S(1)} all-gather(bf16[4,4,16,160]{2,1,0,3:T(4,128)(2,1)S(1)} %copy.121), channel_id=2, replica_groups=mesh['groups'=2,'pipe'=4,'dp'=2,'mp'=2] {'mp'}, dimensions={3}, use_global_device_ids=true | all-gather | bytes 245760 | tf_op jit(solution)/shard_map/cond/branch_1_fun/all_gather | solution.py:220
  22.9 0.5 fusion.92
  23.4 1.2 %copy.156 = bf16[4,4,16,1,160]{4,2,3,1,0:T(8,128)(2,1)} copy(bf16[4,4,16,1,160]{2,1,0,4,3:T(4,128)(2,1)S(1)} %get-tuple-element.119) | data formatting | bytes 163840 | tf_op jit(solution)/shard_map/cond
  24.6 0.5 copy.155
  25.1 0.9 %fusion.18 = bf16[2,4,16,320]{3,2,1,0:T(8,128)(2,1)S(1)} fusion(s32[]{:T(128)S(6)} %select_n.46, bf16[4,4,16,160]{3,2,1,0:T(8,128)(2,1)S(1)} %bitcast.128, bf16[4,4,16,160]{3,2,1,0:T(8,128)(2,1)} %bitcast.127), kind=kLoop, calls=%fused_computation.31 | loop fusion | flops 163840 | bytes 245764 | tf_op jit(solution)/shard_map/cond/branch_1_fun/concatenate | solution.py:222
  26.0 1.0 %copy.142 = f32[2,4,16,320]{3,1,2,0:T(4,128)S(1)} copy(f32[2,4,16,320]{3,2,1,0:T(8,128)} %get-tuple-element.50) | data formatting | bytes 327680 | tf_op jit(solution)/shard_map/cond | solution.py:179
  27.1 1.3 %collective-permute-start.2 = (f32[2,4,16,320]{3,1,2,0:T(4,128)S(1)}, f32[2,4,16,320]{3,1,2,0:T(4,128)S(1)}, u32[]{:S(2)}, u32[]{:S(2)}) collective-permute-start(f32[2,4,16,320]{3,1,2,0:T(4,128)S(1)} %copy.142), channel_id=1, source_target_pairs={{0,4},{12,8},{1,5},{13,9},{2,6},{14,10},{3,7},{15,11},{16,20},{28,... | collective-permute-start | bytes 491528 | tf_op jit(solution)/shard_map/ppermute | solution.py:234
  28.4 1.3 %collective-permute-start.1 = (bf16[2,4,16,320]{3,1,2,0:T(4,128)(2,1)S(1)}, bf16[2,4,16,320]{3,1,2,0:T(4,128)(2,1)S(1)}, u32[]{:S(2)}, u32[]{:S(2)}) collective-permute-start(bf16[2,4,16,320]{3,1,2,0:T(4,128)(2,1)S(1)} %copy.141), channel_id=1, source_target_pairs={{0,4},{12,8},{1,5},{13,9},{2,6},{14,10},{3,7},{15,11},{16,20},{28,... | collective-permute-start | bytes 245768 | tf_op jit(solution)/shard_map/ppermute | solution.py:233
  29.7 0.0 copy-start.4
  29.7 2.6 %conditional.4 = (bf16[2,320,3,3,320]{4,1,3,2,0:T(8,128)(2,1)}) conditional(s32[]{:T(128)} %convert_element_type.89, () %tuple.30, (s32[]{:T(128)}, bf16[2,160,3,3,320]{4,1,3,2,0:T(8,128)(2,1)S(1)}) %tuple.65), branch_computations={%region_0.1_spmd, %region_1.2_spmd} | conditional | flops 16588801 | bytes 14745658 | solution.py:179
  29.7 2.6 %broadcast.17 = bf16[2,320,3,3,320]{4,1,3,2,0:T(8,128)(2,1)} broadcast(bf16[]{:T(256)} %constant.10.clone), dimensions={} | broadcast | bytes 3686402 | tf_op jit(solution)/shard_map/broadcast.9
  32.4 3.0 %collective-permute-done.1 = bf16[2,4,16,320]{3,1,2,0:T(4,128)(2,1)S(1)} collective-permute-done((bf16[2,4,16,320]{3,1,2,0:T(4,128)(2,1)S(1)}, bf16[2,4,16,320]{3,1,2,0:T(4,128)(2,1)S(1)}, u32[]{:S(2)}, u32[]{:S(2)}) %collective-permute-start.1) | collective-permute-done | bytes 81952 | tf_op jit(solution)/shard_map/ppermute | solution.py:233
  35.4 0.0 collective-permute-done.2
  35.4 0.3 conditional.5
  35.7 1.3 %collective-permute-start.3 = (bf16[2,4,16,320]{3,2,1,0:T(8,128)(2,1)S(1)}, bf16[2,4,16,320]{3,2,1,0:T(8,128)(2,1)S(1)}, u32[]{:S(2)}, u32[]{:S(2)}) collective-permute-start(bf16[2,4,16,320]{3,2,1,0:T(8,128)(2,1)S(1)} %copy.144), channel_id=1, source_target_pairs={{4,0},{8,12},{5,1},{9,13},{6,2},{10,14},{7,3},{11,15},{20,16},{24,... | collective-permute-start | bytes 245768 | tf_op jit(solution)/shard_map/ppermute | solution.py:258
  37.0 18.7 %collective-permute-done.3 = bf16[2,4,16,320]{3,2,1,0:T(8,128)(2,1)S(1)} collective-permute-done((bf16[2,4,16,320]{3,2,1,0:T(8,128)(2,1)S(1)}, bf16[2,4,16,320]{3,2,1,0:T(8,128)(2,1)S(1)}, u32[]{:S(2)}, u32[]{:S(2)}) %collective-permute-start.3) | collective-permute-done | bytes 81952 | tf_op jit(solution)/shard_map/ppermute | solution.py:258
  55.7 0.1 fusion.89
  55.8 0.1 pad_maximum_fusion
  55.9 9.1 %all_gather.15 = bf16[8,4,16,640]{3,2,1,0:T(8,128)(2,1)S(1)} all-gather(bf16[2,4,16,640]{3,2,1,0:T(8,128)(2,1)S(1)} %pad_maximum_fusion), channel_id=1, replica_groups=mesh['groups'=2,'pipe'=4,'dp'=2,'mp'=2] {'dp','mp'}, dimensions={0}, use_global_device_ids=true | all-gather | bytes 819200 | tf_op jit(solution)/shard_map/all_gather | solution.py:263
  65.1 0.2 constant_dynamic-slice_fusion.1
  65.2 0.9 %fusion.81 = f32[160,3,3,320]{3,0,2,1:T(8,128)S(1)} fusion(bf16[8,4,16,320]{3,2,1,0:T(8,128)(2,1)S(1)} %slice.58, bf16[8,4,16,160]{3,2,1,0:T(8,128)(2,1)S(1)} %constant_dynamic-slice_fusion.1), kind=kOutput, calls=%fused_computation.108 | convolution fusion | flops 376832000 | bytes 2334720 | tf_op jit(solution)/shard_map/conv_general_dilated | solution.py:31
  66.1 1.5 %copy.149 = f32[160,3,3,320]{3,2,1,0:T(4,128)S(1)} copy(f32[160,3,3,320]{3,0,2,1:T(8,128)S(1)} %fusion.81) | data formatting | bytes 3686400 | tf_op jit(solution)/shard_map/conv_general_dilated | solution.py:31
  67.6 4.6 %reshape.17 = f32[1,460800]{1,0:T(1,128)} reshape(f32[160,3,3,320]{3,2,1,0:T(4,128)S(1)} %copy.149) | data formatting | bytes 3686400 | tf_op jit(solution)/shard_map/reshape | solution.py:267
  (19 shorter events, 0.3 us)
Async XLA Ops:
  7.2 2.7 %copy-start.1 = (bf16[1,2,2,4,16,320]{5,4,3,2,1,0:T(8,128)(2,1)S(1)}, bf16[1,2,2,4,16,320]{5,4,3,2,1,0:T(8,128)(2,1)}, u32[]{:S(2)}) copy-start(bf16[1,2,2,4,16,320]{5,4,3,2,1,0:T(8,128)(2,1)} %param.9) | copy-start | bytes 491524
  7.2 2.7 %copy-start.3 = (bf16[1,2,2,4,16,320]{5,4,3,2,1,0:T(8,128)(2,1)S(1)}, bf16[1,2,2,4,16,320]{5,4,3,2,1,0:T(8,128)(2,1)}, u32[]{:S(2)}) copy-start(bf16[1,2,2,4,16,320]{5,4,3,2,1,0:T(8,128)(2,1)} %param.11) | copy-start | bytes 491524
  10.0 1.3 %copy-start.6 = (pred[32,3]{0,1:T(4,128)(4,1)S(1)}, pred[32,3]{0,1:T(4,128)(4,1)}, u32[]{:S(2)}) copy-start(pred[32,3]{0,1:T(4,128)(4,1)} %constant.85) | copy-start | bytes 292 | tf_op jit(solution)/shard_map/cond
  27.1 8.4 %collective-permute-start.2 = (f32[2,4,16,320]{3,1,2,0:T(4,128)S(1)}, f32[2,4,16,320]{3,1,2,0:T(4,128)S(1)}, u32[]{:S(2)}, u32[]{:S(2)}) collective-permute-start(f32[2,4,16,320]{3,1,2,0:T(4,128)S(1)} %copy.142), channel_id=1, source_target_pairs={{0,4},{12,8},{1,5},{13,9},{2,6},{14,10},{3,7},{15,11},{16,20},{28,... | collective-permute-start | bytes 491528 | tf_op jit(solution)/shard_map/ppermute | solution.py:234
  28.4 7.0 %collective-permute-start.1 = (bf16[2,4,16,320]{3,1,2,0:T(4,128)(2,1)S(1)}, bf16[2,4,16,320]{3,1,2,0:T(4,128)(2,1)S(1)}, u32[]{:S(2)}, u32[]{:S(2)}) collective-permute-start(bf16[2,4,16,320]{3,1,2,0:T(4,128)(2,1)S(1)} %copy.141), channel_id=1, source_target_pairs={{0,4},{12,8},{1,5},{13,9},{2,6},{14,10},{3,7},{15,11},{16,20},{28,... | collective-permute-start | bytes 245768 | tf_op jit(solution)/shard_map/ppermute | solution.py:233
  29.7 2.6 %copy-start.4 = (bf16[1,2,2,4,16,320]{5,4,3,2,1,0:T(8,128)(2,1)S(1)}, bf16[1,2,2,4,16,320]{5,4,3,2,1,0:T(8,128)(2,1)}, u32[]{:S(2)}) copy-start(bf16[1,2,2,4,16,320]{5,4,3,2,1,0:T(8,128)(2,1)} %param.11) | copy-start | bytes 491524
  35.4 20.3 %copy-start.2 = (bf16[1,2,2,4,16,320]{5,4,3,2,1,0:T(8,128)(2,1)S(1)}, bf16[1,2,2,4,16,320]{5,4,3,2,1,0:T(8,128)(2,1)}, u32[]{:S(2)}) copy-start(bf16[1,2,2,4,16,320]{5,4,3,2,1,0:T(8,128)(2,1)} %param.9) | copy-start | bytes 491524
  35.7 20.0 %collective-permute-start.3 = (bf16[2,4,16,320]{3,2,1,0:T(8,128)(2,1)S(1)}, bf16[2,4,16,320]{3,2,1,0:T(8,128)(2,1)S(1)}, u32[]{:S(2)}, u32[]{:S(2)}) collective-permute-start(bf16[2,4,16,320]{3,2,1,0:T(8,128)(2,1)S(1)} %copy.144), channel_id=1, source_target_pairs={{4,0},{8,12},{5,1},{9,13},{6,2},{10,14},{7,3},{11,15},{20,16},{24,... | collective-permute-start | bytes 245768 | tf_op jit(solution)/shard_map/ppermute | solution.py:258

commit v7 on v6

--- a/solution.py
+++ b/solution.py
@@ -210,25 +210,27 @@
     x0 = take(samples, mine)
     seed = take(grads, mine)
     a0 = bf16(jax.nn.silu(f32(x0)))
-
-    def first(samples, grads, own):
-        act_all = bf16(jax.nn.silu(f32(samples)))
-        own_in = lax.dynamic_slice_in_dim(samples, low, chan_half, 3)
-        h1_half = bf16(f32(own_in) + conv(act_all, own[0]))
-        seed_half = lax.dynamic_slice_in_dim(grads, low, chan_half, 3)
-        d_part = conv_t(seed_half, own[1])
-        h1_all = lax.all_gather(h1_half, "mp", axis=3, tiled=False)
-        d_all = lax.all_gather(d_part, "mp", axis=0, tiled=False)
-        h1 = take(jnp.concatenate([h1_all[..., 0, :], h1_all[..., 1, :]], -1), mine)
-        return h1, take(d_all[0] + d_all[1], mine)
-
-    def weights(own):
-        other = lax.ppermute(own, "mp", swap)
+    other_enc = lax.ppermute(own[0], "mp", swap)
+    other_dec = lax.ppermute(own[1], "mp", swap)
+
+    def join(first, second):
+        return jnp.where(lane == 0, jnp.concatenate([first, second], -1),
+                         jnp.concatenate([second, first], -1))
+
+    def first(x0, a0, seed, own, other_enc, other_dec):
+        h1 = bf16(f32(x0) + join(conv(a0, own[0]), conv(a0, other_enc)))
+        high = (1 - lane) * chan_half
+        d_own = conv_t(lax.dynamic_slice_in_dim(seed, low, chan_half, 3), own[1])
+        d_other = conv_t(lax.dynamic_slice_in_dim(seed, high, chan_half, 3), other_dec)
+        return h1, d_own + d_other
+
+    def weights(own, other_enc, other_dec):
+        other = jnp.stack([other_enc, other_dec])
         return jnp.where(lane == 0, jnp.concatenate([own, other], 1),
                          jnp.concatenate([other, own], 1))
 
-    h1, d_last = on_stage(stage == 0, first, samples, grads, own)
-    full = on_stage(stage == 1, weights, own)
+    h1, d_last = on_stage(stage == 0, first, x0, a0, seed, own, other_enc, other_dec)
+    full = on_stage(stage == 1, weights, own, other_enc, other_dec)
     ups = [(0, 1), (pipe_size - 1, pipe_size - 2)]
     h1_r = lax.ppermute(h1, "pipe", ups)
     d_last_r = lax.ppermute(d_last, "pipe", ups)

time: 72.5 us -> 88.3 us (1.22)
  local copies, waits for them, and re-layouts: 25.8 us -> 36 us
  blocking collectives: 14.3 us -> 8.13 us
  waiting for transfers between devices: 21.7 us -> 27.6 us
  other arithmetic: 2.6 us -> 6.11 us
  starting transfers between devices: 3.89 us -> 5.06 us
    ppermute x1, waiting for transfers between devices: 18.7 us -> 24.7 us  [local(): sent = lax.ppermute(back, 'pipe', [(1, 0), (pipe_size - 2, pipe_size - 1)])]
    all_gather x2 -> x0, blocking collectives: 5.18 us -> none  [the longest x1 2.74 us: first(): h1_all = lax.all_gather(h1_half, 'mp', axis=3, tiled=False)]
    rev x2, local copies, waits for them, and re-layouts: 0.61 us -> 4.9 us  [conv_t(): return jnp.flip(out, (1, 2))]
    another operation x6 -> x7, local copies, waits for them, and re-layouts: 2.91 us -> 5.31 us
    convert_element_type x2, other arithmetic: 0.37 us -> 2.55 us  [bf16(): return v.astype(jnp.bfloat16)]
    cond x5 -> x2, local copies, waits for them, and re-layouts: 1.91 us -> 0.01 us
    reshape x1, local copies, waits for them, and re-layouts: 4.57 us -> 6.39 us  [local(): return grad.reshape(1, -1)]
    ppermute x1, waiting for transfers between devices: 3.03 us -> 1.32 us  [local(): h1_r = lax.ppermute(h1, 'pipe', ups)]
  transfers between devices with their start and end apart: 3 -> 5, of which waited for: 2 -> 4; matrix products, arithmetic and copies ran while one was open for 4% -> 7% of each run, Pallas kernels for 0% -> 0%
where the time goes in v7:
time: 88.3 us; the launch traced here: 87.6 us
  local copies, waits for them, and re-layouts  36 us (41%)
  waiting for transfers between devices  27.6 us (31%)
  blocking collectives  8.13 us (9%)
  other arithmetic  6.11 us (7%)
  starting transfers between devices  5.06 us (6%)
  matrix products  4.2 us (5%)
    ppermute x1, waiting for transfers between devices, local(): sent = lax.ppermute(back, 'pipe', [(1, 0), (pipe_size - 2, pipe_size - 1)])  24.7 us
    all_gather x1, blocking collectives, local(): every = lax.all_gather(both, ('dp', 'mp'), axis=0, tiled=True)  8.13 us
    reshape x1, local copies, waits for them, and re-layouts, local(): return grad.reshape(1, -1)  6.39 us
    another operation x7, local copies, waits for them, and re-layouts  5.31 us
    rev x2, local copies, waits for them, and re-layouts, conv_t(): return jnp.flip(out, (1, 2))  4.9 us
    another operation x1, local copies, waits for them, and re-layouts, local(): section_weight[0].reshape(2, chan_half, 9, channels).transpose(0, 2, 1, 3)  4.46 us
    conv_general_dilated x1, local copies, waits for them, and re-layouts, weight_grad(): lax.conv_general_dilated(act, cot, (1, 1), ((1, 1), (1, 1)), dimension_nu...  3.08 us
    unnamed x5, local copies, waits for them, and re-layouts  2.67 us
  transfers between devices with their start and end apart: 5, of which 4 were waited for; matrix products, arithmetic and copies ran while one was open for 7% of the time, Pallas kernels for 0%

profile of v7, /device:TPU:0, one launch (start us, length us, event | category | flops | bytes accessed | tf_op | source)
XLA Modules:
  0.0 87.6 jit_solution(17764151461400357909)
XLA Ops:
  0.0 2.7 %reshape.93 = bf16[921600]{0:T(1024)(128)(2,1)S(1)} reshape(bf16[1,2,460800]{2,1,0:T(2,128)(2,1)} %param.10) | data formatting | bytes 3686400
  2.7 4.5 %reshape_squeeze.3 = bf16[2,160,9,320]{3,2,1,0:T(8,128)(2,1)} reshape(bf16[921600]{0:T(1024)(128)(2,1)S(1)} %reshape.93) | data formatting | bytes 3686400 | tf_op jit(solution)/shard_map/reshape;squeeze | solution.py:206
  7.1 2.6 %copy.81 = bf16[2,9,160,320]{3,2,1,0:T(8,128)(2,1)S(1)} copy(bf16[2,9,160,320]{3,1,2,0:T(8,128)(2,1)} %bitcast.117) | data formatting | bytes 3686400 | tf_op jit(solution)/shard_map/transpose | solution.py:206
  9.8 1.6 %slice_bitcast_fusion.21 = (bf16[160,3,3,320]{3,0,2,1:T(8,128)(2,1)}, bf16[160,3,3,320]{3,0,2,1:T(8,128)(2,1)}) fusion(bf16[2,160,3,3,320]{4,1,3,2,0:T(8,128)(2,1)S(1)} %bitcast.114), kind=kLoop, calls=%fused_computation.106 | loop fusion | bytes 3686400 | tf_op jit(solution)/shard_map/squeeze | solution.py:214
  11.4 0.5 collective-permute-start.1
  11.9 0.9 %constant_dynamic-slice_fusion.3 = bf16[2,4,16,320]{3,2,1,0:T(8,128)(2,1)S(1)} fusion(bf16[4,4,16,320]{3,2,1,0:T(8,128)(2,1)} %bitcast.144, s32[]{:T(128)S(6)} %select_n.67), kind=kLoop, calls=%fused_computation.121 | loop fusion | bytes 163844 | tf_op jit(solution)/shard_map/dynamic_slice | solution.py:203
  12.8 1.6 %fusion.71 = (bf16[2,4,16,320]{3,2,1,0:T(8,128)(2,1)}, bf16[2,4,16,320]{3,2,1,0:T(8,128)(2,1)}) fusion(bf16[4,4,16,320]{3,2,1,0:T(8,128)(2,1)} %bitcast.146, s32[]{:T(128)S(6)} %select_n.67), kind=kLoop, calls=%fused_computation.116 | loop fusion | flops 245760 | bytes 245764 | tf_op jit(solution)/shard_map/convert_element_type | solution.py:43
  14.4 1.1 %collective-permute-done.1 = bf16[160,3,3,320]{3,0,2,1:T(8,128)(2,1)} collective-permute-done((bf16[160,3,3,320]{3,0,2,1:T(8,128)(2,1)}, bf16[160,3,3,320]{3,0,2,1:T(8,128)(2,1)}, u32[]{:S(2)}, u32[]{:S(2)}) %collective-permute-start.1) | collective-permute-done | bytes 921632 | tf_op jit(solution)/shard_map/ppermute | solution.py:214
  15.5 0.4 collective-permute-done
  16.0 16.8 %conditional.3 = (bf16[2,4,16,320]{3,1,2,0:T(4,128)(2,1)S(1)}, f32[2,4,16,320]{3,1,2,0:T(4,128)}) conditional(s32[]{:T(128)} %convert_element_type.84, () %tuple.28, (bf16[2,4,16,320]{3,2,1,0:T(8,128)(2,1)}, s32[]{:T(128)}, bf16[2,160,3,3,320]{4,1,3,2,0:T(8,128)(2,1)S(1)}, bf16[2,4,16,320]{3,2,1,0:T(8,128)(2,1)}, ...), branch_computations={%region_2.3_spmd, %region_3.4_spmd} | conditional | flops 591585280 | bytes 11756992 | solution.py:179
  16.0 0.1 copy.84
  16.1 0.2 constant_dynamic-slice_fusion
  16.3 0.7 reverse_bitcast_fusion
  17.2 0.2 fusion.14
  17.3 1.8 %convolution_select_fusion = f32[4,16,3,320]{3,1,2,0:T(8,128)S(1)} fusion(bf16[160,3,3,320]{3,0,2,1:T(8,128)(2,1)} %get-tuple-element.53, bf16[4,2,8,5,160]{4,1,3,2,0:T(2,128)(2,1)S(1)} %fusion.14, pred[16,3]{0,1:T(4,128)(4,1)} %constant.91), kind=kOutput, calls=%fused_computation.3 | convolution fusion | flops 147517440 | bytes 1269808 | tf_op jit(solution)/shard_map/cond/branch_1_fun/conv_general_dilated | solution.py:22
  19.1 0.1 copy.68
  19.2 0.7 slice_bitcast_fusion
  19.9 2.5 %rev.22 = f32[2,4,16,320]{3,1,2,0:T(4,128)} reverse(f32[2,4,16,320]{3,1,2,0:T(4,128)} %slice_bitcast_fusion), dimensions={1,2} | reverse | bytes 327680 | tf_op jit(solution)/shard_map/cond/branch_1_fun/jit(_flip)/rev | solution.py:27
  22.4 0.9 %pad.4 = bf16[4,2,24,160]{3,1,2,0:T(2,128)(2,1)S(1)} pad(bf16[4,2,16,160]{3,1,2,0:T(2,128)(2,1)} %get-tuple-element.132, bf16[]{:T(256)} %constant.55), padding=0_0x0_0x1_7x0_0 | pad | bytes 102402 | tf_op jit(solution)/shard_map/cond/branch_1_fun/jit(_flip)/rev | solution.py:21
  23.4 0.2 fusion.13
  23.5 1.0 %copy.147 = bf16[2,4,16,320]{3,0,2,1:T(2,128)(2,1)S(1)} copy(bf16[2,4,16,320]{3,2,1,0:T(8,128)(2,1)} %get-tuple-element.102) | data formatting | bytes 163840 | tf_op jit(solution)/shard_map
  24.5 0.1 pad
  24.7 0.2 fusion.6
  25.0 0.5 convolution_select_fusion.2
  25.5 0.5 convolution_select_fusion.3
  26.0 0.5 convolution_select_fusion.1
  26.5 0.2 maximum_select_fusion.1
  26.7 0.1 copy.64
  26.8 0.9 %fusion.12 = bf16[2,4,16,320]{3,1,2,0:T(4,128)(2,1)S(1)} fusion(f32[4,2,24,320]{3,0,2,1:T(4,128)S(1)} %bitcast.131, bf16[2,4,16,320]{3,2,1,0:T(8,128)(2,1)} %get-tuple-element.99), kind=kLoop, calls=%fused_computation.25 | loop fusion | flops 122880 | bytes 327680 | tf_op jit(solution)/shard_map/cond/branch_1_fun/convert_element_type | solution.py:43
  27.8 0.1 copy.66
  27.9 0.7 slice_bitcast_fusion.1
  28.6 2.4 %rev.20 = f32[2,4,16,320]{3,1,2,0:T(4,128)} reverse(f32[2,4,16,320]{3,1,2,0:T(4,128)} %slice_bitcast_fusion.1), dimensions={1,2} | reverse | bytes 327680 | tf_op jit(solution)/shard_map/cond/branch_1_fun/jit(_flip)/rev | solution.py:27
  31.1 1.7 %add.56 = f32[2,4,16,320]{3,1,2,0:T(4,128)} add(f32[2,4,16,320]{3,1,2,0:T(4,128)} %rev.20, f32[2,4,16,320]{3,1,2,0:T(4,128)} %rev.22) | non-fusion elementwise | flops 40960 | bytes 491520 | tf_op jit(solution)/shard_map/cond/branch_1_fun/add | solution.py:225
  32.8 2.0 %collective-permute-start.3 = (f32[2,4,16,320]{3,1,2,0:T(4,128)}, f32[2,4,16,320]{3,1,2,0:T(4,128)}, u32[]{:S(2)}, u32[]{:S(2)}) collective-permute-start(f32[2,4,16,320]{3,1,2,0:T(4,128)} %get-tuple-element.65), channel_id=1, source_target_pairs={{0,4},{12,8},{1,5},{13,9},{2,6},{14,10},{3,7},{15,11},{16,20},{28,... | collective-permute-start | bytes 491528 | tf_op jit(solution)/shard_map/ppermute | solution.py:236
  34.8 1.3 %collective-permute-start.2 = (bf16[2,4,16,320]{3,1,2,0:T(4,128)(2,1)}, bf16[2,4,16,320]{3,1,2,0:T(4,128)(2,1)S(1)}, u32[]{:S(2)}, u32[]{:S(2)}) collective-permute-start(bf16[2,4,16,320]{3,1,2,0:T(4,128)(2,1)} %copy-done.2), channel_id=1, source_target_pairs={{0,4},{12,8},{1,5},{13,9},{2,6},{14,10},{3,7},{15,11},{16,20},{28,... | collective-permute-start | bytes 245768 | tf_op jit(solution)/shard_map/ppermute | solution.py:235
  36.1 4.1 %conditional.4 = (bf16[2,320,3,3,320]{4,3,2,1,0:T(4,128)(2,1)}) conditional(s32[]{:T(128)} %convert_element_type.83, () %tuple.30, (s32[]{:T(128)}, bf16[160,3,3,320]{3,0,2,1:T(8,128)(2,1)S(1)}, bf16[160,3,3,320]{3,0,2,1:T(8,128)(2,1)}, bf16[2,160,3,3,320]{4,1,3,2,0:T(8,128)(2,1)S(1)}) %tuple.63), branch_computations={%region_0.1_spmd, %region_1.2_spmd} | conditional | flops 9216001 | bytes 14745618 | solution.py:179
  36.1 4.1 %broadcast.15 = bf16[2,320,3,3,320]{4,3,2,1,0:T(4,128)(2,1)} broadcast(bf16[]{:T(256)} %constant.10.clone), dimensions={} | broadcast | bytes 3686402 | tf_op jit(solution)/shard_map/broadcast.7
  40.2 1.3 %collective-permute-done.2 = bf16[2,4,16,320]{3,1,2,0:T(4,128)(2,1)S(1)} collective-permute-done((bf16[2,4,16,320]{3,1,2,0:T(4,128)(2,1)}, bf16[2,4,16,320]{3,1,2,0:T(4,128)(2,1)S(1)}, u32[]{:S(2)}, u32[]{:S(2)}) %collective-permute-start.2) | collective-permute-done | bytes 81952 | tf_op jit(solution)/shard_map/ppermute | solution.py:235
  41.5 0.3 conditional.5
  41.8 1.3 %collective-permute-start.4 = (bf16[2,4,16,320]{3,2,1,0:T(8,128)(2,1)S(1)}, bf16[2,4,16,320]{3,2,1,0:T(8,128)(2,1)S(1)}, u32[]{:S(2)}, u32[]{:S(2)}) collective-permute-start(bf16[2,4,16,320]{3,2,1,0:T(8,128)(2,1)S(1)} %copy.90), channel_id=1, source_target_pairs={{4,0},{8,12},{5,1},{9,13},{6,2},{10,14},{7,3},{11,15},{20,16},{24,... | collective-permute-start | bytes 245768 | tf_op jit(solution)/shard_map/ppermute | solution.py:260
  43.1 24.7 %collective-permute-done.4 = bf16[2,4,16,320]{3,2,1,0:T(8,128)(2,1)S(1)} collective-permute-done((bf16[2,4,16,320]{3,2,1,0:T(8,128)(2,1)S(1)}, bf16[2,4,16,320]{3,2,1,0:T(8,128)(2,1)S(1)}, u32[]{:S(2)}, u32[]{:S(2)}) %collective-permute-start.4) | collective-permute-done | bytes 81952 | tf_op jit(solution)/shard_map/ppermute | solution.py:260
  67.8 1.0 %select_select_fusion.1 = (bf16[2,4,16,320]{3,2,1,0:T(8,128)(2,1)S(1)}, bf16[2,4,16,320]{3,2,1,0:T(8,128)(2,1)S(1)}) fusion(bf16[2,4,16,320]{3,2,1,0:T(8,128)(2,1)S(1)} %get-tuple-element.116, bf16[2,4,16,320]{3,2,1,0:T(8,128)(2,1)S(1)} %collective-permute-done.4, pred[]{:T(512)} %lt.16, pred[]{:T(512)S(6)} %eq.15, ...), kind=kLoop, calls=%fused_computation.119 | loop fusion | flops 409600 | bytes 573446 | tf_op jit(solution)/shard_map/jit(_where)/select_n | solution.py:262
  68.8 0.1 pad_maximum_fusion
  68.9 8.1 %all_gather.3 = bf16[8,4,16,640]{3,2,1,0:T(8,128)(2,1)S(1)} all-gather(bf16[2,4,16,640]{3,2,1,0:T(8,128)(2,1)S(1)} %pad_maximum_fusion), channel_id=1, replica_groups=mesh['groups'=2,'pipe'=4,'dp'=2,'mp'=2] {'dp','mp'}, dimensions={0}, use_global_device_ids=true | all-gather | bytes 819200 | tf_op jit(solution)/shard_map/all_gather | solution.py:265
  77.1 0.2 constant_dynamic-slice_fusion.2
  77.2 0.9 fusion.65
  78.1 3.1 %copy.95 = f32[160,3,3,320]{3,2,1,0:T(4,128)} copy(f32[160,3,3,320]{3,0,2,1:T(8,128)S(1)} %fusion.65) | data formatting | bytes 3686400 | tf_op jit(solution)/shard_map/conv_general_dilated | solution.py:31
  81.2 6.4 %reshape.15 = f32[1,460800]{1,0:T(1,128)} reshape(f32[160,3,3,320]{3,2,1,0:T(4,128)} %copy.95) | data formatting | bytes 3686400 | tf_op jit(solution)/shard_map/reshape | solution.py:269
  (17 shorter events, 0.4 us)
Async XLA Ops:
  11.4 4.2 %collective-permute-start.1 = (bf16[160,3,3,320]{3,0,2,1:T(8,128)(2,1)}, bf16[160,3,3,320]{3,0,2,1:T(8,128)(2,1)}, u32[]{:S(2)}, u32[]{:S(2)}) collective-permute-start(bf16[160,3,3,320]{3,0,2,1:T(8,128)(2,1)} %get-tuple-element.133), channel_id=1, source_target_pairs={{0,1},{1,0},{2,3},{3,2},{4,5},{5,4},{6,7},{7,6},{8,9},{9,8},{10,11... | collective-permute-start | bytes 2764808 | tf_op jit(solution)/shard_map/ppermute | solution.py:214
  11.8 4.2 %collective-permute-start = (bf16[160,3,3,320]{3,0,2,1:T(8,128)(2,1)}, bf16[160,3,3,320]{3,0,2,1:T(8,128)(2,1)S(1)}, u32[]{:S(2)}, u32[]{:S(2)}) collective-permute-start(bf16[160,3,3,320]{3,0,2,1:T(8,128)(2,1)} %get-tuple-element.134), channel_id=1, source_target_pairs={{0,1},{1,0},{2,3},{3,2},{4,5},{5,4},{6,7},{7,6},{8,9},{9,8},{10,11... | collective-permute-start | bytes 2764808 | tf_op jit(solution)/shard_map/ppermute | solution.py:213
  17.3 7.6 %copy-start.3 = (pred[16,3]{0,1:T(4,128)(4,1)S(1)}, pred[16,3]{0,1:T(4,128)(4,1)}, u32[]{:S(2)}) copy-start(pred[16,3]{0,1:T(4,128)(4,1)} %constant.91) | copy-start | bytes 148 | tf_op jit(solution)/shard_map/cond
  32.8 2.0 %copy-start.2 = (bf16[2,4,16,320]{3,1,2,0:T(4,128)(2,1)}, bf16[2,4,16,320]{3,1,2,0:T(4,128)(2,1)S(1)}, u32[]{:S(2)}) copy-start(bf16[2,4,16,320]{3,1,2,0:T(4,128)(2,1)S(1)} %get-tuple-element.64) | copy-start | bytes 245764
  32.8 8.7 %collective-permute-start.3 = (f32[2,4,16,320]{3,1,2,0:T(4,128)}, f32[2,4,16,320]{3,1,2,0:T(4,128)}, u32[]{:S(2)}, u32[]{:S(2)}) collective-permute-start(f32[2,4,16,320]{3,1,2,0:T(4,128)} %get-tuple-element.65), channel_id=1, source_target_pairs={{0,4},{12,8},{1,5},{13,9},{2,6},{14,10},{3,7},{15,11},{16,20},{28,... | collective-permute-start | bytes 491528 | tf_op jit(solution)/shard_map/ppermute | solution.py:236
  34.8 6.7 %collective-permute-start.2 = (bf16[2,4,16,320]{3,1,2,0:T(4,128)(2,1)}, bf16[2,4,16,320]{3,1,2,0:T(4,128)(2,1)S(1)}, u32[]{:S(2)}, u32[]{:S(2)}) collective-permute-start(bf16[2,4,16,320]{3,1,2,0:T(4,128)(2,1)} %copy-done.2), channel_id=1, source_target_pairs={{0,4},{12,8},{1,5},{13,9},{2,6},{14,10},{3,7},{15,11},{16,20},{28,... | collective-permute-start | bytes 245768 | tf_op jit(solution)/shard_map/ppermute | solution.py:235
  41.5 26.3 %copy-start.1 = (bf16[1,2,2,4,16,320]{5,4,3,2,1,0:T(8,128)(2,1)S(1)}, bf16[1,2,2,4,16,320]{5,4,3,2,1,0:T(8,128)(2,1)}, u32[]{:S(2)}) copy-start(bf16[1,2,2,4,16,320]{5,4,3,2,1,0:T(8,128)(2,1)} %param.11) | copy-start | bytes 491524
  41.8 26.0 %collective-permute-start.4 = (bf16[2,4,16,320]{3,2,1,0:T(8,128)(2,1)S(1)}, bf16[2,4,16,320]{3,2,1,0:T(8,128)(2,1)S(1)}, u32[]{:S(2)}, u32[]{:S(2)}) collective-permute-start(bf16[2,4,16,320]{3,2,1,0:T(8,128)(2,1)S(1)} %copy.90), channel_id=1, source_target_pairs={{4,0},{8,12},{5,1},{9,13},{6,2},{10,14},{7,3},{11,15},{20,16},{24,... | collective-permute-start | bytes 245768 | tf_op jit(solution)/shard_map/ppermute | solution.py:260

commit v8 on v5

--- a/solution.py
+++ b/solution.py
@@ -88,10 +88,9 @@
     h1_half = bf16(f32(own_in) + conv(act_all, own[0]))
     seed_half = lax.dynamic_slice_in_dim(grads, low, chan_half, 3)
     d_part = conv_t(seed_half, own[1])
-    h1_all = lax.all_gather(h1_half, "mp", axis=3, tiled=False)
-    d_all = lax.all_gather(d_part, "mp", axis=0, tiled=False)
-    h1 = take(jnp.concatenate([h1_all[..., 0, :], h1_all[..., 1, :]], -1), mine)
-    d_last = take(d_all[0] + d_all[1], mine)
+    parts = lax.all_gather(jnp.concatenate([f32(h1_half), d_part], -1), "mp", axis=0, tiled=False)
+    h1 = take(bf16(jnp.concatenate([parts[0, ..., :chan_half], parts[1, ..., :chan_half]], -1)), mine)
+    d_last = take(parts[0, ..., chan_half:] + parts[1, ..., chan_half:], mine)
     x0 = take(samples, mine)
     a0 = take(act_all, mine)
     seed = take(grads, mine)

time: 69.7 us -> 65.7 us (0.943)
  local copies, waits for them, and re-layouts: 25 us -> 22.1 us
  blocking collectives: 13.4 us -> 10.7 us
  waiting for transfers between devices: 5.41 us -> 6.79 us
    all_gather x2 -> x1, blocking collectives: 5.24 us -> 2.56 us  [local(): lax.all_gather(jnp.concatenate([f32(h1_half), d_part], -1), 'mp', axis=0,...]
    unnamed x25 -> x21, local copies, waits for them, and re-layouts: 5.98 us -> 3.55 us
    ppermute x2, waiting for transfers between devices: 0.01 us -> 1.62 us  [up(): return lax.ppermute(v, 'pipe', pairs)]
    squeeze x0 -> x1, local copies, waits for them, and re-layouts: none -> 0.98 us  [local(): parts[1, ..., :chan_half]]
    dynamic_slice x1, local copies, waits for them, and re-layouts: 1.04 us -> 0.1 us  [local(): seed_half = lax.dynamic_slice_in_dim(grads, low, chan_half, 3)]
    another operation x0 -> x1, other arithmetic: none -> 0.88 us
    add x1 -> x0, other arithmetic: 0.72 us -> none  [local(): d_last = take(d_all[0] + d_all[1], mine)]
  transfers between devices with their start and end apart: 4 -> 4, of which waited for: 1 -> 2; matrix products, arithmetic and copies ran while one was open for 24% -> 23% of each run, Pallas kernels for 0% -> 0%
where the time goes in v8:
time: 65.7 us; the launch traced here: 65.4 us
  local copies, waits for them, and re-layouts  22.1 us (34%)
  blocking collectives  10.7 us (16%)
  matrix products  9.33 us (14%)
  other arithmetic  7.93 us (12%)
  starting transfers between devices  7.91 us (12%)
  waiting for transfers between devices  6.79 us (10%)
    all_gather x1, blocking collectives, local(): every = lax.all_gather(both, ('dp', 'mp'), axis=0, tiled=True)  8.11 us
    ppermute x2, starting transfers between devices, up(): return lax.ppermute(v, 'pipe', pairs)  6.1 us
    conv_general_dilated x3, matrix products, conv_t(): lax.conv_general_dilated(flipped, weight, (1, 1), ((1, 1), (1, 1)), dimen...  5.55 us
    ppermute x1, waiting for transfers between devices, local(): lax.ppermute(jnp.where(lower, c0, a_last), 'pipe', [(1, 0), (pipe_size -...  5.17 us
    reshape x1, local copies, waits for them, and re-layouts, local(): return grad.reshape(1, -1)  4.57 us
    another operation x1, local copies, waits for them, and re-layouts, local(): section_weight[0].reshape(2, chan_half, 9, channels).transpose(0, 2, 1, 3)  4.5 us
    select_n x1, other arithmetic, local(): jnp.where(lane == 0, jnp.concatenate([own, other], 1), jnp.concatenate([o...  3.6 us
    unnamed x21, local copies, waits for them, and re-layouts  3.55 us
  transfers between devices with their start and end apart: 4, of which 2 were waited for; matrix products, arithmetic and copies ran while one was open for 23% of the time, Pallas kernels for 0%

profile of v8, /device:TPU:0, one launch (start us, length us, event | category | flops | bytes accessed | tf_op | source)
XLA Modules:
  0.0 65.4 jit_solution(6997602404517826083)
XLA Ops:
  0.0 2.7 %reshape.83 = bf16[921600]{0:T(1024)(128)(2,1)S(1)} reshape(bf16[1,2,460800]{2,1,0:T(2,128)(2,1)} %param.4) | data formatting | bytes 3686400
  2.7 4.5 %reshape_squeeze.3 = bf16[2,160,9,320]{3,2,1,0:T(8,128)(2,1)} reshape(bf16[921600]{0:T(1024)(128)(2,1)S(1)} %reshape.83) | data formatting | bytes 3686400 | tf_op jit(solution)/shard_map/reshape;squeeze | solution.py:65
  7.2 2.7 %copy.78 = bf16[2,9,160,320]{3,2,1,0:T(8,128)(2,1)S(1)} copy(bf16[2,9,160,320]{3,1,2,0:T(8,128)(2,1)} %bitcast.121) | data formatting | bytes 3686400 | tf_op jit(solution)/shard_map/transpose | solution.py:65
  9.8 0.5 collective-permute-start.2
  10.5 0.1 rev.22
  10.9 0.2 fusion.23
  11.1 0.1 fusion.20
  11.2 0.2 copy.112
  11.5 0.2 fusion.10
  11.8 0.9 %convolution_select_fusion.1 = f32[4,32,3,160]{3,1,2,0:T(8,128)S(1)} fusion(bf16[2,160,3,3,320]{4,1,3,2,0:T(8,128)(2,1)S(1)} %bitcast.123, bf16[4,4,8,5,320]{4,1,3,2,0:T(4,128)(2,1)S(1)} %fusion.10, pred[32,3]{0,1:T(4,128)(4,1)S(1)} %copy-done.5), kind=kOutput, calls=%fused_computation.8 | convolution fusion | flops 294973440 | bytes 1843712 | tf_op jit(solution)/shard_map/conv_general_dilated | solution.py:13
  12.7 0.3 copy.79
  13.1 0.2 copy.84
  13.3 0.8 %convolution_select_fusion = f32[4,32,3,320]{3,1,2,0:T(8,128)S(1)} fusion(bf16[2,160,3,3,320]{4,1,3,2,0:T(8,128)(2,1)S(1)} %bitcast.124, bf16[4,4,8,5,160]{4,1,3,2,0:T(4,128)(2,1)S(1)} %fusion.23, pred[32,3]{0,1:T(4,128)(4,1)S(1)} %copy-done.5), kind=kOutput, calls=%fused_computation.7 | convolution fusion | flops 295034880 | bytes 1925632 | tf_op jit(solution)/shard_map/conv_general_dilated | solution.py:22
  14.1 0.4 copy.83
  14.5 0.6 rev.23
  15.1 0.3 pad_maximum_fusion
  15.4 0.2 copy.85
  15.6 2.6 %all-gather = f32[8,4,16,480]{3,2,1,0:T(8,128)S(1)} all-gather(f32[4,4,16,480]{3,2,1,0:T(8,128)S(1)} %copy.85), channel_id=2, replica_groups=mesh['groups'=2,'pipe'=4,'dp'=2,'mp'=2] {'mp'}, dimensions={0}, use_global_device_ids=true | all-gather | bytes 1474560 | tf_op jit(solution)/shard_map/all_gather | solution.py:91
  18.1 0.9 %convert.8 = bf16[2,4,4,16,480]{4,3,2,1,0:T(8,128)(2,1)} convert(f32[2,4,4,16,480]{4,3,2,1,0:T(8,128)S(1)} %bitcast.126) | non-fusion elementwise | flops 245760 | bytes 1474560 | tf_op jit(solution)/shard_map/convert.5
  19.0 1.0 %slice_bitcast_fusion.19 = (bf16[4,4,16,160]{3,2,1,0:T(8,128)(2,1)S(1)}, bf16[4,4,16,160]{3,2,1,0:T(8,128)(2,1)S(1)}) fusion(bf16[2,4,4,16,480]{4,3,2,1,0:T(8,128)(2,1)} %convert.8), kind=kLoop, calls=%fused_computation.108 | loop fusion | bytes 327680 | tf_op jit(solution)/shard_map/squeeze | solution.py:92
  20.0 0.7 %fusion.73 = bf16[2,4,16,320]{3,2,1,0:T(8,128)(2,1)} fusion(s32[]{:T(128)S(6)} %select_n.52, bf16[4,4,16,160]{3,2,1,0:T(8,128)(2,1)S(1)} %get-tuple-element.12, bf16[4,4,16,160]{3,2,1,0:T(8,128)(2,1)S(1)} %get-tuple-element.11), kind=kLoop, calls=%fused_computation.119 | loop fusion | flops 163840 | bytes 245764 | tf_op jit(solution)/shard_map/concatenate | solution.py:92
  20.7 4.6 %collective-permute-start = (bf16[2,4,16,320]{3,2,1,0:T(8,128)(2,1)}, bf16[2,4,16,320]{3,2,1,0:T(8,128)(2,1)S(1)}, u32[]{:S(2)}, u32[]{:S(2)}) collective-permute-start(bf16[2,4,16,320]{3,2,1,0:T(8,128)(2,1)} %fusion.73), channel_id=1, source_target_pairs={{0,4},{12,8},{1,5},{13,9},{2,6},{14,10},{3,7},{15,11},{16,20},{28,... | collective-permute-start | bytes 245768 | tf_op jit(solution)/shard_map/ppermute | solution.py:72
  25.3 0.3 fusion.79
  25.6 1.5 %collective-permute-start.1 = (f32[2,4,16,320]{3,2,1,0:T(8,128)S(1)}, f32[2,4,16,320]{3,2,1,0:T(8,128)S(1)}, u32[]{:S(2)}, u32[]{:S(2)}) collective-permute-start(f32[2,4,16,320]{3,2,1,0:T(8,128)S(1)} %fusion.62), channel_id=1, source_target_pairs={{0,4},{12,8},{1,5},{13,9},{2,6},{14,10},{3,7},{15,11},{16,20},{28,... | collective-permute-start | bytes 491528 | tf_op jit(solution)/shard_map/ppermute | solution.py:72
  27.2 1.6 %collective-permute-done = bf16[2,4,16,320]{3,2,1,0:T(8,128)(2,1)S(1)} collective-permute-done((bf16[2,4,16,320]{3,2,1,0:T(8,128)(2,1)}, bf16[2,4,16,320]{3,2,1,0:T(8,128)(2,1)S(1)}, u32[]{:S(2)}, u32[]{:S(2)}) %collective-permute-start) | collective-permute-done | bytes 81952 | tf_op jit(solution)/shard_map/ppermute | solution.py:72
  29.1 0.2 fusion.29
  29.4 3.6 %maximum_select_fusion = bf16[2,320,3,3,320]{4,1,3,2,0:T(8,128)(2,1)S(1)} fusion(bf16[2,160,3,3,320]{4,1,3,2,0:T(8,128)(2,1)} %collective-permute-done.2, bf16[2,160,3,3,320]{4,1,3,2,0:T(8,128)(2,1)S(1)} %bitcast.125, pred[]{:T(512)S(6)} %eq.3), kind=kLoop, calls=%fused_computation | loop fusion | flops 16588800 | bytes 7372801 | tf_op jit(solution)/shard_map/jit(_where)/select_n | solution.py:101
  33.0 1.0 %fusion.6 = f32[4,16,3,320]{3,1,2,0:T(8,128)S(1)} fusion(bf16[2,320,3,3,320]{4,1,3,2,0:T(8,128)(2,1)S(1)} %maximum_select_fusion, bf16[4,2,8,5,320]{4,1,3,2,0:T(2,128)(2,1)S(1)} %fusion.29, pred[16,3]{0,1:T(4,128)(4,1)S(1)} %copy-done.4), kind=kOutput, calls=%fused_computation.11 | convolution fusion | flops 294973440 | bytes 2703872 | tf_op jit(solution)/shard_map/conv_general_dilated | solution.py:13
  34.0 0.1 copy.88
  34.6 0.2 fusion.30
  34.9 0.2 copy-done
  35.0 1.0 %fusion.4 = f32[4,16,3,320]{3,1,2,0:T(8,128)S(1)} fusion(bf16[2,320,3,3,320]{4,1,3,2,0:T(8,128)(2,1)S(1)} %maximum_select_fusion, bf16[4,2,8,5,320]{4,1,3,2,0:T(2,128)(2,1)S(1)} %fusion.30, pred[16,3]{0,1:T(4,128)(4,1)S(1)} %copy-done.4), kind=kOutput, calls=%fused_computation.9 | convolution fusion | flops 294973440 | bytes 2703872 | tf_op jit(solution)/shard_map/conv_general_dilated | solution.py:13
  36.2 0.1 add_convert_fusion.3
  36.4 0.1 rev.24
  36.8 0.2 fusion.31
  37.0 2.4 %fusion.5 = f32[4,16,3,320]{3,1,2,0:T(8,128)S(1)} fusion(bf16[2,320,3,3,320]{4,1,3,2,0:T(8,128)(2,1)} %copy-done, bf16[4,2,8,5,320]{4,1,3,2,0:T(2,128)(2,1)S(1)} %fusion.31, pred[16,3]{0,1:T(4,128)(4,1)S(1)} %copy-done.4), kind=kOutput, calls=%fused_computation.10 | convolution fusion | flops 294973440 | bytes 2662448 | tf_op jit(solution)/shard_map/conv_general_dilated | solution.py:22
  39.8 0.1 rev.26
  40.3 0.2 fusion.32
  40.5 2.4 %fusion.7 = f32[4,16,3,320]{3,1,2,0:T(8,128)S(1)} fusion(bf16[2,320,3,3,320]{4,1,3,2,0:T(8,128)(2,1)} %copy-done, bf16[4,2,8,5,320]{4,1,3,2,0:T(2,128)(2,1)S(1)} %fusion.32, pred[16,3]{0,1:T(4,128)(4,1)S(1)} %copy-done.4), kind=kOutput, calls=%fused_computation.12 | convolution fusion | flops 294973440 | bytes 2662448 | tf_op jit(solution)/shard_map/conv_general_dilated | solution.py:22
  43.2 0.2 fusion.64
  43.4 1.3 %collective-permute-start.3 = (bf16[2,4,16,320]{3,2,1,0:T(8,128)(2,1)S(1)}, bf16[2,4,16,320]{3,2,1,0:T(8,128)(2,1)S(1)}, u32[]{:S(2)}, u32[]{:S(2)}) collective-permute-start(bf16[2,4,16,320]{3,2,1,0:T(8,128)(2,1)S(1)} %fusion.64), channel_id=1, source_target_pairs={{4,0},{8,12},{5,1},{9,13},{6,2},{10,14},{7,3},{11,15},{20,16},{24,... | collective-permute-start | bytes 245768 | tf_op jit(solution)/shard_map/ppermute | solution.py:159
  44.7 5.2 %collective-permute-done.3 = bf16[2,4,16,320]{3,2,1,0:T(8,128)(2,1)S(1)} collective-permute-done((bf16[2,4,16,320]{3,2,1,0:T(8,128)(2,1)S(1)}, bf16[2,4,16,320]{3,2,1,0:T(8,128)(2,1)S(1)}, u32[]{:S(2)}, u32[]{:S(2)}) %collective-permute-start.3) | collective-permute-done | bytes 81952 | tf_op jit(solution)/shard_map/ppermute | solution.py:159
  49.9 0.2 fusion.71
  50.1 8.1 %all_gather.11 = bf16[8,4,16,640]{3,2,1,0:T(8,128)(2,1)S(1)} all-gather(bf16[2,4,16,640]{3,2,1,0:T(8,128)(2,1)S(1)} %pad_maximum_fusion.1), channel_id=1, replica_groups=mesh['groups'=2,'pipe'=4,'dp'=2,'mp'=2] {'dp','mp'}, dimensions={0}, use_global_device_ids=true | all-gather | bytes 819200 | tf_op jit(solution)/shard_map/all_gather | solution.py:167
  58.3 0.2 constant_dynamic-slice_fusion
  58.4 0.9 %fusion.21 = f32[160,3,3,320]{3,0,2,1:T(8,128)S(1)} fusion(bf16[8,4,16,320]{3,2,1,0:T(8,128)(2,1)S(1)} %slice.70, bf16[8,4,16,160]{3,2,1,0:T(8,128)(2,1)S(1)} %constant_dynamic-slice_fusion), kind=kOutput, calls=%fused_computation.35 | convolution fusion | flops 376832000 | bytes 2334720 | tf_op jit(solution)/shard_map/conv_general_dilated | solution.py:31
  59.3 1.5 %copy.104 = f32[160,3,3,320]{3,2,1,0:T(4,128)S(1)} copy(f32[160,3,3,320]{3,0,2,1:T(8,128)S(1)} %fusion.21) | data formatting | bytes 3686400 | tf_op jit(solution)/shard_map/conv_general_dilated | solution.py:31
  60.8 4.6 %reshape.21 = f32[1,460800]{1,0:T(1,128)} reshape(f32[160,3,3,320]{3,2,1,0:T(4,128)S(1)} %copy.104) | data formatting | bytes 3686400 | tf_op jit(solution)/shard_map/reshape | solution.py:171
  (53 shorter events, 3.0 us)
Async XLA Ops:
  7.2 3.2 %copy-start.2 = (bf16[1,2,2,4,16,320]{5,4,3,2,1,0:T(8,128)(2,1)S(1)}, bf16[1,2,2,4,16,320]{5,4,3,2,1,0:T(8,128)(2,1)}, u32[]{:S(2)}) copy-start(bf16[1,2,2,4,16,320]{5,4,3,2,1,0:T(8,128)(2,1)} %param.5) | copy-start | bytes 491524
  7.2 3.9 %copy-start.1 = (bf16[1,2,2,4,16,320]{5,4,3,2,1,0:T(8,128)(2,1)S(1)}, bf16[1,2,2,4,16,320]{5,4,3,2,1,0:T(8,128)(2,1)}, u32[]{:S(2)}) copy-start(bf16[1,2,2,4,16,320]{5,4,3,2,1,0:T(8,128)(2,1)} %param.3) | copy-start | bytes 491524
  9.8 19.5 %collective-permute-start.2 = (bf16[2,160,3,3,320]{4,1,3,2,0:T(8,128)(2,1)S(1)}, bf16[2,160,3,3,320]{4,1,3,2,0:T(8,128)(2,1)}, u32[]{:S(2)}, u32[]{:S(2)}) collective-permute-start(bf16[2,160,3,3,320]{4,1,3,2,0:T(8,128)(2,1)S(1)} %bitcast.122), channel_id=1, source_target_pairs={{0,1},{1,0},{2,3},{3,2},{4,5},{5,4},{6,7},{7,6},{8,9},{9,8},{10,11... | collective-permute-start | bytes 5529608 | tf_op jit(solution)/shard_map/ppermute | solution.py:68
  10.5 1.3 %copy-start.5 = (pred[32,3]{0,1:T(4,128)(4,1)S(1)}, pred[32,3]{0,1:T(4,128)(4,1)}, u32[]{:S(2)}) copy-start(pred[32,3]{0,1:T(4,128)(4,1)} %constant.60) | copy-start | bytes 292
  20.7 8.1 %collective-permute-start = (bf16[2,4,16,320]{3,2,1,0:T(8,128)(2,1)}, bf16[2,4,16,320]{3,2,1,0:T(8,128)(2,1)S(1)}, u32[]{:S(2)}, u32[]{:S(2)}) collective-permute-start(bf16[2,4,16,320]{3,2,1,0:T(8,128)(2,1)} %fusion.73), channel_id=1, source_target_pairs={{0,4},{12,8},{1,5},{13,9},{2,6},{14,10},{3,7},{15,11},{16,20},{28,... | collective-permute-start | bytes 245768 | tf_op jit(solution)/shard_map/ppermute | solution.py:72
  25.6 10.6 %collective-permute-start.1 = (f32[2,4,16,320]{3,2,1,0:T(8,128)S(1)}, f32[2,4,16,320]{3,2,1,0:T(8,128)S(1)}, u32[]{:S(2)}, u32[]{:S(2)}) collective-permute-start(f32[2,4,16,320]{3,2,1,0:T(8,128)S(1)} %fusion.62), channel_id=1, source_target_pairs={{0,4},{12,8},{1,5},{13,9},{2,6},{14,10},{3,7},{15,11},{16,20},{28,... | collective-permute-start | bytes 491528 | tf_op jit(solution)/shard_map/ppermute | solution.py:72
  29.4 3.6 %copy-start.4 = (pred[16,3]{0,1:T(4,128)(4,1)S(1)}, pred[16,3]{0,1:T(4,128)(4,1)}, u32[]{:S(2)}) copy-start(pred[16,3]{0,1:T(4,128)(4,1)} %constant.62) | copy-start | bytes 148
  33.0 2.0 %copy-start = (bf16[2,320,3,3,320]{4,1,3,2,0:T(8,128)(2,1)}, bf16[2,320,3,3,320]{4,1,3,2,0:T(8,128)(2,1)S(1)}, u32[]{:S(2)}) copy-start(bf16[2,320,3,3,320]{4,1,3,2,0:T(8,128)(2,1)S(1)} %maximum_select_fusion) | copy-start | bytes 11059204
  35.0 1.2 %copy-start.3 = (bf16[1,2,2,4,16,320]{5,4,3,2,1,0:T(8,128)(2,1)S(1)}, bf16[1,2,2,4,16,320]{5,4,3,2,1,0:T(8,128)(2,1)}, u32[]{:S(2)}) copy-start(bf16[1,2,2,4,16,320]{5,4,3,2,1,0:T(8,128)(2,1)} %param.5) | copy-start | bytes 491524
  43.4 6.5 %collective-permute-start.3 = (bf16[2,4,16,320]{3,2,1,0:T(8,128)(2,1)S(1)}, bf16[2,4,16,320]{3,2,1,0:T(8,128)(2,1)S(1)}, u32[]{:S(2)}, u32[]{:S(2)}) collective-permute-start(bf16[2,4,16,320]{3,2,1,0:T(8,128)(2,1)S(1)} %fusion.64), channel_id=1, source_target_pairs={{4,0},{8,12},{5,1},{9,13},{6,2},{10,14},{7,3},{11,15},{20,16},{24,... | collective-permute-start | bytes 245768 | tf_op jit(solution)/shard_map/ppermute | solution.py:159

commit v9 on v8

--- a/solution.py
+++ b/solution.py
@@ -97,10 +97,12 @@
     h1_r = up(0, h1)
     d_last_r = up(0, d_last)
 
-    other, _ = lax.optimization_barrier((other, h1))
-    full = jnp.where(lane == 0, jnp.concatenate([own, other], 1),
-                     jnp.concatenate([other, own], 1))
-    w_enc, w_dec = full[0], full[1]
+    def assemble(mine_half, their_half):
+        return jnp.where(lane == 0, jnp.concatenate([mine_half, their_half], 0),
+                         jnp.concatenate([their_half, mine_half], 0))
+
+    other_enc, _ = lax.optimization_barrier((other[0], h1))
+    w_enc = assemble(own[0], other_enc)
 
     enc_in, enc_act, enc_out = {}, {}, {}
     enc_in[0], enc_act[0], enc_out[0] = x0, a0, h1
@@ -115,7 +117,8 @@
             received = up(t, h_out)
 
     dec_u, dec_act, dec_c = {}, {}, {}
-    h_in = enc_out[half - 1]
+    other_dec, h_in = lax.optimization_barrier((other[1], enc_out[half - 1]))
+    w_dec = assemble(own[1], other_dec)
     u = f32(h_in) + f32(h_in)
     a = bf16(jax.nn.silu(u))
     current = bf16(f32(h_in) + conv(a, w_dec))

time: 65.7 us -> 66.1 us (level)
  local copies, waits for them, and re-layouts: 22.1 us -> 27.1 us
  other arithmetic: 7.93 us -> 5.86 us
  waiting for transfers between devices: 6.79 us -> 5.33 us
  matrix products: 9.33 us -> 8.2 us
    select_n x1 -> x0, other arithmetic: 3.6 us -> none  [local(): jnp.where(lane == 0, jnp.concatenate([own, other], 1), jnp.concatenate([o...]
    squeeze x0 -> x2, local copies, waits for them, and re-layouts: none -> 3.48 us  [the longest x1 1.89 us: local(): other_enc, _ = lax.optimization_barrier((other[0], h1))]
    ppermute x2, waiting for transfers between devices: 1.62 us -> 0.04 us  [up(): return lax.ppermute(v, 'pipe', pairs)]
    conv_general_dilated x3, matrix products: 5.55 us -> 4.3 us  [conv_t(): lax.conv_general_dilated(flipped, weight, (1, 1), ((1, 1), (1, 1)), dimen...]
    rev x3, local copies, waits for them, and re-layouts: 0.78 us -> 1.98 us  [conv_t(): return jnp.flip(out, (1, 2))]
    convert_element_type x4, other arithmetic: 0.43 us -> 1.26 us  [bf16(): return v.astype(jnp.bfloat16)]
    unnamed x21 -> x31, local copies, waits for them, and re-layouts: 3.55 us -> 3.86 us
  transfers between devices with their start and end apart: 4 -> 4, of which waited for: 2 -> 1; matrix products, arithmetic and copies ran while one was open for 23% -> 24% of each run, Pallas kernels for 0% -> 0%
where the time goes in v9:
time: 66.1 us; the launch traced here: 65.7 us
  local copies, waits for them, and re-layouts  27.1 us (41%)
  blocking collectives  10.7 us (16%)
  matrix products  8.2 us (12%)
  starting transfers between devices  7.91 us (12%)
  other arithmetic  5.86 us (9%)
  waiting for transfers between devices  5.33 us (8%)
  between operations  0.67 us (1%)
    all_gather x1, blocking collectives, local(): every = lax.all_gather(both, ('dp', 'mp'), axis=0, tiled=True)  8.1 us
    ppermute x2, starting transfers between devices, up(): return lax.ppermute(v, 'pipe', pairs)  6.1 us
    ppermute x1, waiting for transfers between devices, local(): lax.ppermute(jnp.where(lower, c0, a_last), 'pipe', [(1, 0), (pipe_size -...  5.28 us
    reshape x1, local copies, waits for them, and re-layouts, local(): return grad.reshape(1, -1)  4.57 us
    another operation x1, local copies, waits for them, and re-layouts, local(): section_weight[0].reshape(2, chan_half, 9, channels).transpose(0, 2, 1, 3)  4.48 us
    conv_general_dilated x3, matrix products, conv_t(): lax.conv_general_dilated(flipped, weight, (1, 1), ((1, 1), (1, 1)), dimen...  4.3 us
    unnamed x31, local copies, waits for them, and re-layouts  3.86 us
    conv_general_dilated x3, matrix products, conv(): lax.conv_general_dilated(act, weight, (1, 1), ((1, 1), (1, 1)), dimension...  3.04 us
  transfers between devices with their start and end apart: 4, of which 1 were waited for; matrix products, arithmetic and copies ran while one was open for 24% of the time, Pallas kernels for 0%

profile of v9, /device:TPU:0, one launch (start us, length us, event | category | flops | bytes accessed | tf_op | source)
XLA Modules:
  0.0 65.7 jit_solution(15694774311322022784)
XLA Ops:
  0.0 2.7 %reshape.83 = bf16[921600]{0:T(1024)(128)(2,1)S(1)} reshape(bf16[1,2,460800]{2,1,0:T(2,128)(2,1)} %param.4) | data formatting | bytes 3686400
  2.7 4.5 %reshape_squeeze.3 = bf16[2,160,9,320]{3,2,1,0:T(8,128)(2,1)} reshape(bf16[921600]{0:T(1024)(128)(2,1)S(1)} %reshape.83) | data formatting | bytes 3686400 | tf_op jit(solution)/shard_map/reshape;squeeze | solution.py:65
  7.2 2.7 %copy.78 = bf16[2,9,160,320]{3,2,1,0:T(8,128)(2,1)S(1)} copy(bf16[2,9,160,320]{3,1,2,0:T(8,128)(2,1)} %bitcast.108) | data formatting | bytes 3686400 | tf_op jit(solution)/shard_map/transpose | solution.py:65
  9.8 0.5 collective-permute-start.2
  10.9 0.2 fusion.15
  11.0 0.1 fusion.12
  11.2 0.2 copy.112
  11.5 0.2 fusion.2
  11.8 0.9 %convolution_select_fusion.1 = f32[4,32,3,160]{3,1,2,0:T(8,128)S(1)} fusion(bf16[4,4,8,5,320]{4,1,3,2,0:T(4,128)(2,1)S(1)} %fusion.2, pred[32,3]{0,1:T(4,128)(4,1)S(1)} %copy-done.10, bf16[2,160,3,3,320]{4,1,3,2,0:T(8,128)(2,1)S(1)} %bitcast.110), kind=kOutput, calls=%fused_computation.3 | convolution fusion | flops 294973440 | bytes 1843712 | tf_op jit(solution)/shard_map/conv_general_dilated | solution.py:13
  12.7 0.3 copy.79
  13.0 0.8 %convolution_select_fusion = f32[4,32,3,320]{3,1,2,0:T(8,128)S(1)} fusion(bf16[4,4,8,5,160]{4,1,3,2,0:T(4,128)(2,1)S(1)} %fusion.15, pred[32,3]{0,1:T(4,128)(4,1)S(1)} %copy-done.10, bf16[2,160,3,3,320]{4,1,3,2,0:T(8,128)(2,1)S(1)} %bitcast.111), kind=kOutput, calls=%fused_computation.2 | convolution fusion | flops 295034880 | bytes 1925632 | tf_op jit(solution)/shard_map/conv_general_dilated | solution.py:22
  13.8 0.4 copy.83
  14.3 0.2 copy.84
  14.5 0.6 rev.23
  15.1 0.3 pad_maximum_fusion
  15.4 0.2 copy.85
  15.6 2.6 %all-gather = f32[8,4,16,480]{3,2,1,0:T(8,128)S(1)} all-gather(f32[4,4,16,480]{3,2,1,0:T(8,128)S(1)} %copy.85), channel_id=2, replica_groups=mesh['groups'=2,'pipe'=4,'dp'=2,'mp'=2] {'mp'}, dimensions={0}, use_global_device_ids=true | all-gather | bytes 1474560 | tf_op jit(solution)/shard_map/all_gather | solution.py:91
  18.1 0.9 %convert.8 = bf16[2,4,4,16,480]{4,3,2,1,0:T(8,128)(2,1)} convert(f32[2,4,4,16,480]{4,3,2,1,0:T(8,128)S(1)} %bitcast.113) | non-fusion elementwise | flops 245760 | bytes 1474560 | tf_op jit(solution)/shard_map/convert.5
  19.0 1.0 %slice_bitcast_fusion.5 = (bf16[4,4,16,160]{3,2,1,0:T(8,128)(2,1)S(1)}, bf16[4,4,16,160]{3,2,1,0:T(8,128)(2,1)S(1)}) fusion(bf16[2,4,4,16,480]{4,3,2,1,0:T(8,128)(2,1)} %convert.8), kind=kLoop, calls=%fused_computation.105 | loop fusion | bytes 327680 | tf_op jit(solution)/shard_map/squeeze | solution.py:92
  20.0 0.7 %fusion.65 = bf16[2,4,16,320]{3,2,1,0:T(8,128)(2,1)} fusion(s32[]{:T(128)S(6)} %select_n.56, bf16[4,4,16,160]{3,2,1,0:T(8,128)(2,1)S(1)} %get-tuple-element.18, bf16[4,4,16,160]{3,2,1,0:T(8,128)(2,1)S(1)} %get-tuple-element.17), kind=kLoop, calls=%fused_computation.116 | loop fusion | flops 163840 | bytes 245764 | tf_op jit(solution)/shard_map/concatenate | solution.py:92
  20.7 4.6 %collective-permute-start = (bf16[2,4,16,320]{3,2,1,0:T(8,128)(2,1)}, bf16[2,4,16,320]{3,2,1,0:T(8,128)(2,1)S(1)}, u32[]{:S(2)}, u32[]{:S(2)}) collective-permute-start(bf16[2,4,16,320]{3,2,1,0:T(8,128)(2,1)} %fusion.65), channel_id=1, source_target_pairs={{0,4},{12,8},{1,5},{13,9},{2,6},{14,10},{3,7},{15,11},{16,20},{28,... | collective-permute-start | bytes 245768 | tf_op jit(solution)/shard_map/ppermute | solution.py:72
  25.3 0.3 fusion.74
  25.6 1.5 %collective-permute-start.1 = (f32[2,4,16,320]{3,2,1,0:T(8,128)S(1)}, f32[2,4,16,320]{3,2,1,0:T(8,128)S(1)}, u32[]{:S(2)}, u32[]{:S(2)}) collective-permute-start(f32[2,4,16,320]{3,2,1,0:T(8,128)S(1)} %fusion.54), channel_id=1, source_target_pairs={{0,4},{12,8},{1,5},{13,9},{2,6},{14,10},{3,7},{15,11},{16,20},{28,... | collective-permute-start | bytes 491528 | tf_op jit(solution)/shard_map/ppermute | solution.py:72
  27.1 1.6 %slice_bitcast_fusion.2 = (bf16[160,3,3,320]{3,0,2,1:T(8,128)(2,1)}, bf16[160,3,3,320]{3,0,2,1:T(8,128)(2,1)}) fusion(bf16[2,160,3,3,320]{4,1,3,2,0:T(8,128)(2,1)S(1)} %bitcast.112), kind=kLoop, calls=%fused_computation.10 | loop fusion | bytes 3686400 | tf_op jit(solution)/shard_map/squeeze | solution.py:90
  28.7 0.7 %fusion.71 = (bf16[1,2,4,16,320]{4,3,2,1,0:T(8,128)(2,1)}, bf16[4,2,16,320]{3,2,0,1:T(8,128)(2,1)S(1)}) fusion(bf16[2,4,16,320]{3,2,1,0:T(8,128)(2,1)S(1)} %collective-permute-done), kind=kLoop, calls=%fused_computation.126 | loop fusion | flops 245760 | bytes 245760 | tf_op jit(solution)/shard_map/stack | solution.py:163
  29.7 0.2 fusion.21
  30.0 1.9 %slice_bitcast_fusion = (bf16[160,3,3,320]{3,0,2,1:T(8,128)(2,1)S(1)}, bf16[160,3,3,320]{3,0,2,1:T(8,128)(2,1)S(1)}) fusion(bf16[2,160,3,3,320]{4,1,3,2,0:T(8,128)(2,1)} %collective-permute-done.2), kind=kLoop, calls=%fused_computation.8 | loop fusion | bytes 3686400 | tf_op jit(solution)/shard_map/squeeze | solution.py:104
  31.9 1.1 %convolution_select_fusion.5 = f32[4,16,3,320]{3,1,2,0:T(8,128)S(1)} fusion(bf16[160,3,3,320]{3,0,2,1:T(8,128)(2,1)S(1)} %get-tuple-element.8, bf16[160,3,3,320]{3,0,2,1:T(8,128)(2,1)S(1)} %copy-done, pred[]{:T(512)S(6)} %eq.4, bf16[4,2,8,5,320]{4,1,3,2,0:T(2,128)(2,1)S(1)} %fusion.21, pred[16,3]{0,1:T(4,128)(4,1)S(1)} %copy-done.9), kind=kOutput, calls=%fused_computation.7 | convolution fusion | flops 303267840 | bytes 2293809 | tf_op jit(solution)/shard_map/conv_general_dilated | solution.py:13
  33.6 0.2 fusion.22
  33.8 0.4 copy-done.2
  34.2 1.1 %convolution_select_fusion.4 = f32[4,16,3,320]{3,1,2,0:T(8,128)S(1)} fusion(bf16[160,3,3,320]{3,0,2,1:T(8,128)(2,1)S(1)} %get-tuple-element.10, bf16[160,3,3,320]{3,0,2,1:T(8,128)(2,1)S(1)} %copy-done.2, pred[]{:T(512)S(6)} %eq.4, bf16[4,2,8,5,320]{4,1,3,2,0:T(2,128)(2,1)S(1)} %fusion.22, pred[16,3]{0,1:T(4,128)(4,1)S(1)} %copy-done.9), kind=kOutput, calls=%fused_computation.6 | convolution fusion | flops 303267840 | bytes 2293809 | tf_op jit(solution)/shard_map/conv_general_dilated | solution.py:13
  35.5 0.2 fusion.72
  35.7 0.1 rev.24
  36.1 0.2 fusion.23
  36.3 2.6 %convolution_select_fusion.3 = f32[4,16,3,320]{3,1,2,0:T(8,128)S(1)} fusion(bf16[160,3,3,320]{3,0,2,1:T(8,128)(2,1)} %copy-done.3, bf16[160,3,3,320]{3,0,2,1:T(8,128)(2,1)S(1)} %copy-done.2, pred[]{:T(512)S(6)} %eq.4, bf16[4,2,8,5,320]{4,1,3,2,0:T(2,128)(2,1)S(1)} %fusion.23, pred[16,3]{0,1:T(4,128)(4,1)S(1)} %copy-done.9), kind=kOutput, calls=%fused_computation.5 | convolution fusion | flops 303267840 | bytes 2293809 | tf_op jit(solution)/shard_map/conv_general_dilated | solution.py:22
  39.1 1.3 %rev.25 = f32[2,4,16,320]{3,2,1,0:T(8,128)} reverse(f32[2,4,16,320]{3,2,1,0:T(8,128)S(1)} %bitcast.136), dimensions={1,2} | reverse | bytes 327680 | tf_op jit(solution)/shard_map/jit(_flip)/rev | solution.py:27
  40.4 1.0 %add_convert_fusion.1 = bf16[2,4,16,320]{3,2,1,0:T(8,128)(2,1)S(1)} fusion(f32[2,4,16,320]{3,2,1,0:T(8,128)} %rev.25, bf16[2,4,16,320]{3,2,1,0:T(8,128)(2,1)S(1)} %fusion.48, bf16[2,4,16,320]{3,2,1,0:T(8,128)(2,1)S(1)} %get-tuple-element.24), kind=kLoop, calls=%fused_computation.98 | loop fusion | flops 655360 | bytes 409600 | tf_op jit(solution)/shard_map/convert_element_type | solution.py:43
  41.9 0.2 fusion.24
  42.1 0.9 %convolution_select_fusion.2 = f32[4,16,3,320]{3,1,2,0:T(8,128)S(1)} fusion(bf16[160,3,3,320]{3,0,2,1:T(8,128)(2,1)S(1)} %get-tuple-element.8, bf16[160,3,3,320]{3,0,2,1:T(8,128)(2,1)S(1)} %copy-done.1, pred[]{:T(512)S(6)} %eq.4, bf16[4,2,8,5,320]{4,1,3,2,0:T(2,128)(2,1)S(1)} %fusion.24, pred[16,3]{0,1:T(4,128)(4,1)S(1)} %copy-done.9), kind=kOutput, calls=%fused_computation.4 | convolution fusion | flops 303267840 | bytes 2293809 | tf_op jit(solution)/shard_map/conv_general_dilated | solution.py:22
  43.4 0.2 fusion.56
  43.6 1.3 %collective-permute-start.3 = (bf16[2,4,16,320]{3,2,1,0:T(8,128)(2,1)S(1)}, bf16[2,4,16,320]{3,2,1,0:T(8,128)(2,1)S(1)}, u32[]{:S(2)}, u32[]{:S(2)}) collective-permute-start(bf16[2,4,16,320]{3,2,1,0:T(8,128)(2,1)S(1)} %fusion.56), channel_id=1, source_target_pairs={{4,0},{8,12},{5,1},{9,13},{6,2},{10,14},{7,3},{11,15},{20,16},{24,... | collective-permute-start | bytes 245768 | tf_op jit(solution)/shard_map/ppermute | solution.py:162
  44.9 5.3 %collective-permute-done.3 = bf16[2,4,16,320]{3,2,1,0:T(8,128)(2,1)S(1)} collective-permute-done((bf16[2,4,16,320]{3,2,1,0:T(8,128)(2,1)S(1)}, bf16[2,4,16,320]{3,2,1,0:T(8,128)(2,1)S(1)}, u32[]{:S(2)}, u32[]{:S(2)}) %collective-permute-start.3) | collective-permute-done | bytes 81952 | tf_op jit(solution)/shard_map/ppermute | solution.py:162
  50.2 0.2 fusion.63
  50.5 8.1 %all_gather.11 = bf16[8,4,16,640]{3,2,1,0:T(8,128)(2,1)S(1)} all-gather(bf16[2,4,16,640]{3,2,1,0:T(8,128)(2,1)S(1)} %pad_maximum_fusion.1), channel_id=1, replica_groups=mesh['groups'=2,'pipe'=4,'dp'=2,'mp'=2] {'dp','mp'}, dimensions={0}, use_global_device_ids=true | all-gather | bytes 819200 | tf_op jit(solution)/shard_map/all_gather | solution.py:170
  58.6 0.2 constant_dynamic-slice_fusion
  58.8 0.9 %fusion.13 = f32[160,3,3,320]{3,0,2,1:T(8,128)S(1)} fusion(bf16[8,4,16,320]{3,2,1,0:T(8,128)(2,1)S(1)} %slice.72, bf16[8,4,16,160]{3,2,1,0:T(8,128)(2,1)S(1)} %constant_dynamic-slice_fusion), kind=kOutput, calls=%fused_computation.32 | convolution fusion | flops 376832000 | bytes 2334720 | tf_op jit(solution)/shard_map/conv_general_dilated | solution.py:31
  59.6 1.5 %copy.104 = f32[160,3,3,320]{3,2,1,0:T(4,128)S(1)} copy(f32[160,3,3,320]{3,0,2,1:T(8,128)S(1)} %fusion.13) | data formatting | bytes 3686400 | tf_op jit(solution)/shard_map/conv_general_dilated | solution.py:31
  61.2 4.6 %reshape.21 = f32[1,460800]{1,0:T(1,128)} reshape(f32[160,3,3,320]{3,2,1,0:T(4,128)S(1)} %copy.104) | data formatting | bytes 3686400 | tf_op jit(solution)/shard_map/reshape | solution.py:174
  (64 shorter events, 3.1 us)
Async XLA Ops:
  7.2 3.2 %copy-start.4 = (bf16[1,2,2,4,16,320]{5,4,3,2,1,0:T(8,128)(2,1)S(1)}, bf16[1,2,2,4,16,320]{5,4,3,2,1,0:T(8,128)(2,1)}, u32[]{:S(2)}) copy-start(bf16[1,2,2,4,16,320]{5,4,3,2,1,0:T(8,128)(2,1)} %param.5) | copy-start | bytes 491524
  7.2 3.9 %copy-start.7 = (bf16[1,2,2,4,16,320]{5,4,3,2,1,0:T(8,128)(2,1)S(1)}, bf16[1,2,2,4,16,320]{5,4,3,2,1,0:T(8,128)(2,1)}, u32[]{:S(2)}) copy-start(bf16[1,2,2,4,16,320]{5,4,3,2,1,0:T(8,128)(2,1)} %param.3) | copy-start | bytes 491524
  9.8 20.1 %collective-permute-start.2 = (bf16[2,160,3,3,320]{4,1,3,2,0:T(8,128)(2,1)S(1)}, bf16[2,160,3,3,320]{4,1,3,2,0:T(8,128)(2,1)}, u32[]{:S(2)}, u32[]{:S(2)}) collective-permute-start(bf16[2,160,3,3,320]{4,1,3,2,0:T(8,128)(2,1)S(1)} %bitcast.109), channel_id=1, source_target_pairs={{0,1},{1,0},{2,3},{3,2},{4,5},{5,4},{6,7},{7,6},{8,9},{9,8},{10,11... | collective-permute-start | bytes 5529608 | tf_op jit(solution)/shard_map/ppermute | solution.py:68
  10.5 1.3 %copy-start.10 = (pred[32,3]{0,1:T(4,128)(4,1)S(1)}, pred[32,3]{0,1:T(4,128)(4,1)}, u32[]{:S(2)}) copy-start(pred[32,3]{0,1:T(4,128)(4,1)} %constant.60) | copy-start | bytes 292
  20.7 8.1 %collective-permute-start = (bf16[2,4,16,320]{3,2,1,0:T(8,128)(2,1)}, bf16[2,4,16,320]{3,2,1,0:T(8,128)(2,1)S(1)}, u32[]{:S(2)}, u32[]{:S(2)}) collective-permute-start(bf16[2,4,16,320]{3,2,1,0:T(8,128)(2,1)} %fusion.65), channel_id=1, source_target_pairs={{0,4},{12,8},{1,5},{13,9},{2,6},{14,10},{3,7},{15,11},{16,20},{28,... | collective-permute-start | bytes 245768 | tf_op jit(solution)/shard_map/ppermute | solution.py:72
  25.6 9.9 %collective-permute-start.1 = (f32[2,4,16,320]{3,2,1,0:T(8,128)S(1)}, f32[2,4,16,320]{3,2,1,0:T(8,128)S(1)}, u32[]{:S(2)}, u32[]{:S(2)}) collective-permute-start(f32[2,4,16,320]{3,2,1,0:T(8,128)S(1)} %fusion.54), channel_id=1, source_target_pairs={{0,4},{12,8},{1,5},{13,9},{2,6},{14,10},{3,7},{15,11},{16,20},{28,... | collective-permute-start | bytes 491528 | tf_op jit(solution)/shard_map/ppermute | solution.py:72
  30.0 1.9 %copy-start = (bf16[160,3,3,320]{3,0,2,1:T(8,128)(2,1)S(1)}, bf16[160,3,3,320]{3,0,2,1:T(8,128)(2,1)}, u32[]{:S(2)}) copy-start(bf16[160,3,3,320]{3,0,2,1:T(8,128)(2,1)} %get-tuple-element.12) | copy-start | bytes 2764804
  30.0 1.9 %copy-start.9 = (pred[16,3]{0,1:T(4,128)(4,1)S(1)}, pred[16,3]{0,1:T(4,128)(4,1)}, u32[]{:S(2)}) copy-start(pred[16,3]{0,1:T(4,128)(4,1)} %constant.62) | copy-start | bytes 148
  31.9 1.9 %copy-start.3 = (bf16[160,3,3,320]{3,0,2,1:T(8,128)(2,1)}, bf16[160,3,3,320]{3,0,2,1:T(8,128)(2,1)S(1)}, u32[]{:S(2)}) copy-start(bf16[160,3,3,320]{3,0,2,1:T(8,128)(2,1)S(1)} %get-tuple-element.10) | copy-start | bytes 2764804
  33.0 1.2 %copy-start.2 = (bf16[160,3,3,320]{3,0,2,1:T(8,128)(2,1)S(1)}, bf16[160,3,3,320]{3,0,2,1:T(8,128)(2,1)}, u32[]{:S(2)}) copy-start(bf16[160,3,3,320]{3,0,2,1:T(8,128)(2,1)} %get-tuple-element.11) | copy-start | bytes 2764804
  34.2 1.3 %copy-start.5 = (bf16[1,2,2,4,16,320]{5,4,3,2,1,0:T(8,128)(2,1)S(1)}, bf16[1,2,2,4,16,320]{5,4,3,2,1,0:T(8,128)(2,1)}, u32[]{:S(2)}) copy-start(bf16[1,2,2,4,16,320]{5,4,3,2,1,0:T(8,128)(2,1)} %param.5) | copy-start | bytes 491524
  38.9 3.2 %copy-start.1 = (bf16[160,3,3,320]{3,0,2,1:T(8,128)(2,1)S(1)}, bf16[160,3,3,320]{3,0,2,1:T(8,128)(2,1)}, u32[]{:S(2)}) copy-start(bf16[160,3,3,320]{3,0,2,1:T(8,128)(2,1)} %get-tuple-element.12) | copy-start | bytes 2764804
  43.1 1.8 %copy-start.6 = (bf16[1,2,2,4,16,320]{5,4,3,2,1,0:T(8,128)(2,1)S(1)}, bf16[1,2,2,4,16,320]{5,4,3,2,1,0:T(8,128)(2,1)}, u32[]{:S(2)}) copy-start(bf16[1,2,2,4,16,320]{5,4,3,2,1,0:T(8,128)(2,1)} %param.5) | copy-start | bytes 491524
  43.1 7.1 %copy-start.8 = (bf16[1,2,4,16,320]{4,3,2,1,0:T(8,128)(2,1)S(1)}, bf16[1,2,4,16,320]{4,3,2,1,0:T(8,128)(2,1)}, u32[]{:S(2)}) copy-start(bf16[1,2,4,16,320]{4,3,2,1,0:T(8,128)(2,1)} %get-tuple-element.21) | copy-start | bytes 245764
  43.6 6.6 %collective-permute-start.3 = (bf16[2,4,16,320]{3,2,1,0:T(8,128)(2,1)S(1)}, bf16[2,4,16,320]{3,2,1,0:T(8,128)(2,1)S(1)}, u32[]{:S(2)}, u32[]{:S(2)}) collective-permute-start(bf16[2,4,16,320]{3,2,1,0:T(8,128)(2,1)S(1)} %fusion.56), channel_id=1, source_target_pairs={{4,0},{8,12},{5,1},{9,13},{6,2},{10,14},{7,3},{11,15},{20,16},{24,... | collective-permute-start | bytes 245768 | tf_op jit(solution)/shard_map/ppermute | solution.py:162

commit v10 on v8

--- a/solution.py
+++ b/solution.py
@@ -163,10 +163,15 @@
     cots_up = jnp.stack([seed] + [dec_c[t] for t in range(1, half)])
     act_sel = jnp.where(lower, acts_lo[stage], acts_up[stage])
     cot_sel = jnp.where(lower, cots_lo[stage], cots_up[stage])
-    both = jnp.concatenate([act_sel, cot_sel], axis=-1)
-    every = lax.all_gather(both, ("dp", "mp"), axis=0, tiled=True)
-    act_all = every[..., :channels]
-    cot_all = lax.dynamic_slice_in_dim(every, channels + low, chan_half, 3)
+    swapped = (stage == 0) & jnp.logical_not(lower)
+    early = jnp.where(swapped, cot_sel, act_sel)
+    late = jnp.where(swapped, act_sel, cot_sel)
+    early, _ = lax.optimization_barrier((early, c0))
+    early_all = lax.all_gather(early, ("dp", "mp"), axis=0, tiled=True)
+    late, _ = lax.optimization_barrier((late, early_all))
+    late_all = lax.all_gather(late, ("dp", "mp"), axis=0, tiled=True)
+    act_all = jnp.where(swapped, late_all, early_all)
+    cot_all = lax.dynamic_slice_in_dim(jnp.where(swapped, early_all, late_all), low, chan_half, 3)
     grad = weight_grad(act_all, cot_all)
     return grad.reshape(1, -1)
 

time: 65.7 us -> 71.2 us (1.084)
  blocking collectives: 10.7 us -> 15.8 us
    all_gather x1 -> x2, blocking collectives: 8.11 us -> 13.3 us  [the longest x1 6.8 us: local(): late_all = lax.all_gather(late, ('dp', 'mp'), axis=0, tiled=True)]
  transfers between devices with their start and end apart: 4 -> 4, of which waited for: 2 -> 2; matrix products, arithmetic and copies ran while one was open for 23% -> 21% of each run, Pallas kernels for 0% -> 0%
where the time goes in v10:
time: 71.2 us; the launch traced here: 70.9 us
  local copies, waits for them, and re-layouts  22.5 us (32%)
  blocking collectives  15.8 us (22%)
  matrix products  9.38 us (13%)
  starting transfers between devices  7.91 us (11%)
  other arithmetic  7.88 us (11%)
  waiting for transfers between devices  6.79 us (10%)
    all_gather x1, blocking collectives, local(): late_all = lax.all_gather(late, ('dp', 'mp'), axis=0, tiled=True)  6.8 us
    all_gather x1, blocking collectives, local(): early_all = lax.all_gather(early, ('dp', 'mp'), axis=0, tiled=True)  6.47 us
    ppermute x2, starting transfers between devices, up(): return lax.ppermute(v, 'pipe', pairs)  6.1 us
    conv_general_dilated x3, matrix products, conv_t(): lax.conv_general_dilated(flipped, weight, (1, 1), ((1, 1), (1, 1)), dimen...  5.56 us
    ppermute x1, waiting for transfers between devices, local(): lax.ppermute(jnp.where(lower, c0, a_last), 'pipe', [(1, 0), (pipe_size -...  5.17 us
    reshape x1, local copies, waits for them, and re-layouts, local(): return grad.reshape(1, -1)  4.57 us
    another operation x1, local copies, waits for them, and re-layouts, local(): section_weight[0].reshape(2, chan_half, 9, channels).transpose(0, 2, 1, 3)  4.5 us
    unnamed x21, local copies, waits for them, and re-layouts  3.63 us
  transfers between devices with their start and end apart: 4, of which 2 were waited for; matrix products, arithmetic and copies ran while one was open for 21% of the time, Pallas kernels for 0%

profile of v10, /device:TPU:0, one launch (start us, length us, event | category | flops | bytes accessed | tf_op | source)
XLA Modules:
  0.0 70.9 jit_solution(14533609106914754492)
XLA Ops:
  0.0 2.7 %reshape.87 = bf16[921600]{0:T(1024)(128)(2,1)S(1)} reshape(bf16[1,2,460800]{2,1,0:T(2,128)(2,1)} %param.4) | data formatting | bytes 3686400
  2.7 4.5 %reshape_squeeze.3 = bf16[2,160,9,320]{3,2,1,0:T(8,128)(2,1)} reshape(bf16[921600]{0:T(1024)(128)(2,1)S(1)} %reshape.87) | data formatting | bytes 3686400 | tf_op jit(solution)/shard_map/reshape;squeeze | solution.py:65
  7.2 2.7 %copy.80 = bf16[2,9,160,320]{3,2,1,0:T(8,128)(2,1)S(1)} copy(bf16[2,9,160,320]{3,1,2,0:T(8,128)(2,1)} %bitcast.122) | data formatting | bytes 3686400 | tf_op jit(solution)/shard_map/transpose | solution.py:65
  9.8 0.5 collective-permute-start.2
  10.9 0.2 fusion.24
  11.0 0.8 %convolution_select_fusion = f32[4,32,3,320]{3,1,2,0:T(8,128)S(1)} fusion(bf16[2,160,3,3,320]{4,1,3,2,0:T(8,128)(2,1)S(1)} %bitcast.124, bf16[4,4,8,5,160]{4,1,3,2,0:T(4,128)(2,1)S(1)} %fusion.24, pred[32,3]{0,1:T(4,128)(4,1)S(1)} %copy-done.5), kind=kOutput, calls=%fused_computation.7 | convolution fusion | flops 295034880 | bytes 1925632 | tf_op jit(solution)/shard_map/conv_general_dilated | solution.py:22
  11.9 0.4 copy.85
  12.3 0.6 rev.23
  12.9 0.1 fusion.20
  13.0 0.2 copy.114
  13.4 0.2 fusion.10
  13.6 0.9 %convolution_select_fusion.1 = f32[4,32,3,160]{3,1,2,0:T(8,128)S(1)} fusion(bf16[2,160,3,3,320]{4,1,3,2,0:T(8,128)(2,1)S(1)} %bitcast.125, bf16[4,4,8,5,320]{4,1,3,2,0:T(4,128)(2,1)S(1)} %fusion.10, pred[32,3]{0,1:T(4,128)(4,1)S(1)} %copy-done.5), kind=kOutput, calls=%fused_computation.8 | convolution fusion | flops 294973440 | bytes 1843712 | tf_op jit(solution)/shard_map/conv_general_dilated | solution.py:13
  14.5 0.3 copy.81
  14.9 0.2 copy.86
  15.1 0.3 pad_maximum_fusion
  15.4 0.2 copy.87
  15.6 2.6 %all-gather = f32[8,4,16,480]{3,2,1,0:T(8,128)S(1)} all-gather(f32[4,4,16,480]{3,2,1,0:T(8,128)S(1)} %copy.87), channel_id=2, replica_groups=mesh['groups'=2,'pipe'=4,'dp'=2,'mp'=2] {'mp'}, dimensions={0}, use_global_device_ids=true | all-gather | bytes 1474560 | tf_op jit(solution)/shard_map/all_gather | solution.py:91
  18.1 0.9 %convert.8 = bf16[2,4,4,16,480]{4,3,2,1,0:T(8,128)(2,1)} convert(f32[2,4,4,16,480]{4,3,2,1,0:T(8,128)S(1)} %bitcast.127) | non-fusion elementwise | flops 245760 | bytes 1474560 | tf_op jit(solution)/shard_map/convert.5
  19.0 1.0 %slice_bitcast_fusion.19 = (bf16[4,4,16,160]{3,2,1,0:T(8,128)(2,1)S(1)}, bf16[4,4,16,160]{3,2,1,0:T(8,128)(2,1)S(1)}) fusion(bf16[2,4,4,16,480]{4,3,2,1,0:T(8,128)(2,1)} %convert.8), kind=kLoop, calls=%fused_computation.110 | loop fusion | bytes 327680 | tf_op jit(solution)/shard_map/squeeze | solution.py:92
  20.0 0.7 %fusion.73 = bf16[2,4,16,320]{3,2,1,0:T(8,128)(2,1)} fusion(s32[]{:T(128)S(6)} %select_n.76, bf16[4,4,16,160]{3,2,1,0:T(8,128)(2,1)S(1)} %get-tuple-element.21, bf16[4,4,16,160]{3,2,1,0:T(8,128)(2,1)S(1)} %get-tuple-element.20), kind=kLoop, calls=%fused_computation.119 | loop fusion | flops 163840 | bytes 245764 | tf_op jit(solution)/shard_map/concatenate | solution.py:92
  20.7 4.6 %collective-permute-start = (bf16[2,4,16,320]{3,2,1,0:T(8,128)(2,1)}, bf16[2,4,16,320]{3,2,1,0:T(8,128)(2,1)S(1)}, u32[]{:S(2)}, u32[]{:S(2)}) collective-permute-start(bf16[2,4,16,320]{3,2,1,0:T(8,128)(2,1)} %fusion.73), channel_id=1, source_target_pairs={{0,4},{12,8},{1,5},{13,9},{2,6},{14,10},{3,7},{15,11},{16,20},{28,... | collective-permute-start | bytes 245768 | tf_op jit(solution)/shard_map/ppermute | solution.py:72
  25.3 0.3 fusion.82
  25.6 1.5 %collective-permute-start.1 = (f32[2,4,16,320]{3,2,1,0:T(8,128)S(1)}, f32[2,4,16,320]{3,2,1,0:T(8,128)S(1)}, u32[]{:S(2)}, u32[]{:S(2)}) collective-permute-start(f32[2,4,16,320]{3,2,1,0:T(8,128)S(1)} %fusion.64), channel_id=1, source_target_pairs={{0,4},{12,8},{1,5},{13,9},{2,6},{14,10},{3,7},{15,11},{16,20},{28,... | collective-permute-start | bytes 491528 | tf_op jit(solution)/shard_map/ppermute | solution.py:72
  27.2 1.6 %collective-permute-done = bf16[2,4,16,320]{3,2,1,0:T(8,128)(2,1)S(1)} collective-permute-done((bf16[2,4,16,320]{3,2,1,0:T(8,128)(2,1)}, bf16[2,4,16,320]{3,2,1,0:T(8,128)(2,1)S(1)}, u32[]{:S(2)}, u32[]{:S(2)}) %collective-permute-start) | collective-permute-done | bytes 81952 | tf_op jit(solution)/shard_map/ppermute | solution.py:72
  29.1 0.2 fusion.31
  29.4 3.6 %maximum_select_fusion = bf16[2,320,3,3,320]{4,1,3,2,0:T(8,128)(2,1)S(1)} fusion(bf16[2,160,3,3,320]{4,1,3,2,0:T(8,128)(2,1)} %collective-permute-done.2, bf16[2,160,3,3,320]{4,1,3,2,0:T(8,128)(2,1)S(1)} %bitcast.126, pred[]{:T(512)S(6)} %eq.7), kind=kLoop, calls=%fused_computation | loop fusion | flops 16588800 | bytes 7372801 | tf_op jit(solution)/shard_map/jit(_where)/select_n | solution.py:101
  33.0 1.0 %fusion.6 = f32[4,16,3,320]{3,1,2,0:T(8,128)S(1)} fusion(bf16[2,320,3,3,320]{4,1,3,2,0:T(8,128)(2,1)S(1)} %maximum_select_fusion, bf16[4,2,8,5,320]{4,1,3,2,0:T(2,128)(2,1)S(1)} %fusion.31, pred[16,3]{0,1:T(4,128)(4,1)S(1)} %copy-done.4), kind=kOutput, calls=%fused_computation.11 | convolution fusion | flops 294973440 | bytes 2703872 | tf_op jit(solution)/shard_map/conv_general_dilated | solution.py:13
  34.6 0.2 fusion.32
  34.8 0.2 copy-done
  35.0 1.0 %fusion.4 = f32[4,16,3,320]{3,1,2,0:T(8,128)S(1)} fusion(bf16[2,320,3,3,320]{4,1,3,2,0:T(8,128)(2,1)S(1)} %maximum_select_fusion, bf16[4,2,8,5,320]{4,1,3,2,0:T(2,128)(2,1)S(1)} %fusion.32, pred[16,3]{0,1:T(4,128)(4,1)S(1)} %copy-done.4), kind=kOutput, calls=%fused_computation.9 | convolution fusion | flops 294973440 | bytes 2703872 | tf_op jit(solution)/shard_map/conv_general_dilated | solution.py:13
  36.2 0.2 fusion.76
  36.4 0.1 rev.24
  36.9 0.2 fusion.33
  37.1 2.4 %fusion.5 = f32[4,16,3,320]{3,1,2,0:T(8,128)S(1)} fusion(bf16[2,320,3,3,320]{4,1,3,2,0:T(8,128)(2,1)} %copy-done, bf16[4,2,8,5,320]{4,1,3,2,0:T(2,128)(2,1)S(1)} %fusion.33, pred[16,3]{0,1:T(4,128)(4,1)S(1)} %copy-done.4), kind=kOutput, calls=%fused_computation.10 | convolution fusion | flops 294973440 | bytes 2662448 | tf_op jit(solution)/shard_map/conv_general_dilated | solution.py:22
  39.9 0.1 rev.26
  40.3 0.2 fusion.34
  40.6 2.4 %fusion.7 = f32[4,16,3,320]{3,1,2,0:T(8,128)S(1)} fusion(bf16[2,320,3,3,320]{4,1,3,2,0:T(8,128)(2,1)} %copy-done, bf16[4,2,8,5,320]{4,1,3,2,0:T(2,128)(2,1)S(1)} %fusion.34, pred[16,3]{0,1:T(4,128)(4,1)S(1)} %copy-done.4), kind=kOutput, calls=%fused_computation.12 | convolution fusion | flops 294973440 | bytes 2662448 | tf_op jit(solution)/shard_map/conv_general_dilated | solution.py:22
  43.2 0.2 fusion.66
  43.4 1.3 %collective-permute-start.3 = (bf16[2,4,16,320]{3,2,1,0:T(8,128)(2,1)S(1)}, bf16[2,4,16,320]{3,2,1,0:T(8,128)(2,1)S(1)}, u32[]{:S(2)}, u32[]{:S(2)}) collective-permute-start(bf16[2,4,16,320]{3,2,1,0:T(8,128)(2,1)S(1)} %fusion.66), channel_id=1, source_target_pairs={{4,0},{8,12},{5,1},{9,13},{6,2},{10,14},{7,3},{11,15},{20,16},{24,... | collective-permute-start | bytes 245768 | tf_op jit(solution)/shard_map/ppermute | solution.py:159
  44.8 5.2 %collective-permute-done.3 = bf16[2,4,16,320]{3,2,1,0:T(8,128)(2,1)S(1)} collective-permute-done((bf16[2,4,16,320]{3,2,1,0:T(8,128)(2,1)S(1)}, bf16[2,4,16,320]{3,2,1,0:T(8,128)(2,1)S(1)}, u32[]{:S(2)}, u32[]{:S(2)}) %collective-permute-start.3) | collective-permute-done | bytes 81952 | tf_op jit(solution)/shard_map/ppermute | solution.py:159
  49.9 0.2 select_bitcast_fusion
  50.1 6.5 %all_gather.14 = bf16[8,4,16,320]{3,2,1,0:T(8,128)(2,1)S(1)} all-gather(bf16[2,4,16,320]{3,2,1,0:T(8,128)(2,1)S(1)} %get-tuple-element.9), channel_id=1, replica_groups=mesh['groups'=2,'pipe'=4,'dp'=2,'mp'=2] {'dp','mp'}, dimensions={0}, use_global_device_ids=true | all-gather | bytes 409600 | tf_op jit(solution)/shard_map/all_gather | solution.py:170
  56.6 0.2 copy.105
  56.8 6.8 %all_gather.15 = bf16[8,4,16,320]{3,2,1,0:T(8,128)(2,1)S(1)} all-gather(bf16[2,4,16,320]{3,2,1,0:T(8,128)(2,1)S(1)} %select_bitcast_fusion.1), channel_id=1, replica_groups=mesh['groups'=2,'pipe'=4,'dp'=2,'mp'=2] {'dp','mp'}, dimensions={0}, use_global_device_ids=true | all-gather | bytes 409600 | tf_op jit(solution)/shard_map/all_gather | solution.py:172
  63.6 0.2 copy.104
  63.9 0.9 %fusion.21 = f32[160,3,3,320]{3,0,2,1:T(8,128)S(1)} fusion(bf16[8,4,16,320]{3,0,2,1:T(8,128)(2,1)S(1)} %copy.104, bf16[8,4,16,320]{3,0,2,1:T(8,128)(2,1)S(1)} %copy.105, pred[]{:T(512)S(6)} %and.5, s32[]{:T(128)S(6)} %select_n.77), kind=kOutput, calls=%fused_computation.35 | convolution fusion | flops 377077760 | bytes 3155456 | tf_op jit(solution)/shard_map/conv_general_dilated | solution.py:31
  64.8 1.5 %copy.108 = f32[160,3,3,320]{3,2,1,0:T(4,128)S(1)} copy(f32[160,3,3,320]{3,0,2,1:T(8,128)S(1)} %fusion.21) | data formatting | bytes 3686400 | tf_op jit(solution)/shard_map/conv_general_dilated | solution.py:31
  66.3 4.6 %reshape.25 = f32[1,460800]{1,0:T(1,128)} reshape(f32[160,3,3,320]{3,2,1,0:T(4,128)S(1)} %copy.108) | data formatting | bytes 3686400 | tf_op jit(solution)/shard_map/reshape | solution.py:176
  (53 shorter events, 3.0 us)
Async XLA Ops:
  7.2 3.2 %copy-start.1 = (bf16[1,2,2,4,16,320]{5,4,3,2,1,0:T(8,128)(2,1)S(1)}, bf16[1,2,2,4,16,320]{5,4,3,2,1,0:T(8,128)(2,1)}, u32[]{:S(2)}) copy-start(bf16[1,2,2,4,16,320]{5,4,3,2,1,0:T(8,128)(2,1)} %param.5) | copy-start | bytes 491524
  7.2 3.9 %copy-start.5 = (pred[32,3]{0,1:T(4,128)(4,1)S(1)}, pred[32,3]{0,1:T(4,128)(4,1)}, u32[]{:S(2)}) copy-start(pred[32,3]{0,1:T(4,128)(4,1)} %constant.57) | copy-start | bytes 292
  9.8 19.5 %collective-permute-start.2 = (bf16[2,160,3,3,320]{4,1,3,2,0:T(8,128)(2,1)S(1)}, bf16[2,160,3,3,320]{4,1,3,2,0:T(8,128)(2,1)}, u32[]{:S(2)}, u32[]{:S(2)}) collective-permute-start(bf16[2,160,3,3,320]{4,1,3,2,0:T(8,128)(2,1)S(1)} %bitcast.123), channel_id=1, source_target_pairs={{0,1},{1,0},{2,3},{3,2},{4,5},{5,4},{6,7},{7,6},{8,9},{9,8},{10,11... | collective-permute-start | bytes 5529608 | tf_op jit(solution)/shard_map/ppermute | solution.py:68
  11.8 1.0 %copy-start.3 = (bf16[1,2,2,4,16,320]{5,4,3,2,1,0:T(8,128)(2,1)S(1)}, bf16[1,2,2,4,16,320]{5,4,3,2,1,0:T(8,128)(2,1)}, u32[]{:S(2)}) copy-start(bf16[1,2,2,4,16,320]{5,4,3,2,1,0:T(8,128)(2,1)} %param.3) | copy-start | bytes 491524
  20.7 8.1 %collective-permute-start = (bf16[2,4,16,320]{3,2,1,0:T(8,128)(2,1)}, bf16[2,4,16,320]{3,2,1,0:T(8,128)(2,1)S(1)}, u32[]{:S(2)}, u32[]{:S(2)}) collective-permute-start(bf16[2,4,16,320]{3,2,1,0:T(8,128)(2,1)} %fusion.73), channel_id=1, source_target_pairs={{0,4},{12,8},{1,5},{13,9},{2,6},{14,10},{3,7},{15,11},{16,20},{28,... | collective-permute-start | bytes 245768 | tf_op jit(solution)/shard_map/ppermute | solution.py:72
  25.6 10.6 %collective-permute-start.1 = (f32[2,4,16,320]{3,2,1,0:T(8,128)S(1)}, f32[2,4,16,320]{3,2,1,0:T(8,128)S(1)}, u32[]{:S(2)}, u32[]{:S(2)}) collective-permute-start(f32[2,4,16,320]{3,2,1,0:T(8,128)S(1)} %fusion.64), channel_id=1, source_target_pairs={{0,4},{12,8},{1,5},{13,9},{2,6},{14,10},{3,7},{15,11},{16,20},{28,... | collective-permute-start | bytes 491528 | tf_op jit(solution)/shard_map/ppermute | solution.py:72
  29.4 3.6 %copy-start.4 = (pred[16,3]{0,1:T(4,128)(4,1)S(1)}, pred[16,3]{0,1:T(4,128)(4,1)}, u32[]{:S(2)}) copy-start(pred[16,3]{0,1:T(4,128)(4,1)} %constant.59) | copy-start | bytes 148
  33.0 2.0 %copy-start = (bf16[2,320,3,3,320]{4,1,3,2,0:T(8,128)(2,1)}, bf16[2,320,3,3,320]{4,1,3,2,0:T(8,128)(2,1)S(1)}, u32[]{:S(2)}) copy-start(bf16[2,320,3,3,320]{4,1,3,2,0:T(8,128)(2,1)S(1)} %maximum_select_fusion) | copy-start | bytes 11059204
  35.0 1.2 %copy-start.2 = (bf16[1,2,2,4,16,320]{5,4,3,2,1,0:T(8,128)(2,1)S(1)}, bf16[1,2,2,4,16,320]{5,4,3,2,1,0:T(8,128)(2,1)}, u32[]{:S(2)}) copy-start(bf16[1,2,2,4,16,320]{5,4,3,2,1,0:T(8,128)(2,1)} %param.5) | copy-start | bytes 491524
  43.4 6.5 %collective-permute-start.3 = (bf16[2,4,16,320]{3,2,1,0:T(8,128)(2,1)S(1)}, bf16[2,4,16,320]{3,2,1,0:T(8,128)(2,1)S(1)}, u32[]{:S(2)}, u32[]{:S(2)}) collective-permute-start(bf16[2,4,16,320]{3,2,1,0:T(8,128)(2,1)S(1)} %fusion.66), channel_id=1, source_target_pairs={{4,0},{8,12},{5,1},{9,13},{6,2},{10,14},{7,3},{11,15},{20,16},{24,... | collective-permute-start | bytes 245768 | tf_op jit(solution)/shard_map/ppermute | solution.py:159

commit v11 on v8

--- a/solution.py
+++ b/solution.py
@@ -156,15 +156,40 @@
         cot = bf16(f32(cot) + b)
     c0 = bf16(f32(cot) + f32(skip[1]))
 
-    sent = lax.ppermute(jnp.where(lower, c0, a_last), "pipe", [(1, 0), (pipe_size - 2, pipe_size - 1)])
-    acts_lo = jnp.stack([a0] + [enc_act[t] for t in range(1, half)])
-    cots_lo = jnp.stack([sent] + [enc_c[t] for t in range(1, half)])
-    acts_up = jnp.stack([sent] + [dec_act[t] for t in range(1, half)])
-    cots_up = jnp.stack([seed] + [dec_c[t] for t in range(1, half)])
-    act_sel = jnp.where(lower, acts_lo[stage], acts_up[stage])
-    cot_sel = jnp.where(lower, cots_lo[stage], cots_up[stage])
-    both = jnp.concatenate([act_sel, cot_sel], axis=-1)
-    every = lax.all_gather(both, ("dp", "mp"), axis=0, tiled=True)
+    nd = lax.axis_size("dp")
+    pair0, _ = lax.optimization_barrier((jnp.concatenate([x0, seed], -1), h1_r))
+    others = [pair0] + [lax.ppermute(pair0, "dp", [((d + dd) % nd, d) for d in range(nd)])
+                        for dd in range(1, nd)]
+    back = jnp.where(lower, c0, a_last)
+
+    def to_first(dd):
+        pairs = [(src * nd + (d + dd) % nd, dst * nd + d)
+                 for src, dst in ((1, 0), (pipe_size - 2, pipe_size - 1)) for d in range(nd)]
+        return lax.ppermute(back, ("pipe", "dp"), pairs)
+
+    acts_lo = jnp.stack([enc_act[t] for t in range(1, half)])
+    cots_lo = jnp.stack([enc_c[t] for t in range(1, half)])
+    acts_up = jnp.stack([dec_act[t] for t in range(1, half)])
+    cots_up = jnp.stack([dec_c[t] for t in range(1, half)])
+    at = jnp.maximum(stage - 1, 0)
+    own_pair = jnp.concatenate([jnp.where(lower, acts_lo[at], acts_up[at]),
+                                jnp.where(lower, cots_lo[at], cots_up[at])], -1)
+    inner = [j for j in range(pipe_size) if min(j, pipe_size - 1 - j) >= 1]
+
+    def among(dd):
+        pairs = [(j * nd + (d + dd) % nd, j * nd + d) for j in inner for d in range(nd)]
+        return lax.ppermute(own_pair, ("pipe", "dp"), pairs)
+
+    got = [to_first(dd) for dd in range(nd)]
+    mids = [own_pair] + [among(dd) for dd in range(1, nd)]
+    pieces = []
+    for dd in range(nd):
+        a_first = bf16(jax.nn.silu(f32(others[dd][..., :channels])))
+        act = jnp.where(lower, a_first, got[dd])
+        cot = jnp.where(lower, got[dd], others[dd][..., channels:])
+        first_pair = jnp.concatenate([act, cot], -1)
+        pieces.append(jnp.where(stage == 0, first_pair, mids[dd]))
+    every = lax.all_gather(jnp.concatenate(pieces, 0), "mp", axis=0, tiled=True)
     act_all = every[..., :channels]
     cot_all = lax.dynamic_slice_in_dim(every, channels + low, chan_half, 3)
     grad = weight_grad(act_all, cot_all)

time: 65.7 us -> 69.2 us (1.053)
  the two profiles are of different devices: /device:TPU:0 before, /device:TPU:13 now
where the time goes in v11:
time: 69.2 us; the launch traced here: 68.9 us
  local copies, waits for them, and re-layouts  24.8 us (36%)
  starting transfers between devices  9.57 us (14%)
  matrix products  9.35 us (14%)
  other arithmetic  8.33 us (12%)
  waiting for transfers between devices  8.17 us (12%)
  blocking collectives  7.99 us (12%)
    conv_general_dilated x3, matrix products, conv_t(): lax.conv_general_dilated(flipped, weight, (1, 1), ((1, 1), (1, 1)), dimen...  5.57 us
    all_gather x1, blocking collectives, local(): every = lax.all_gather(jnp.concatenate(pieces, 0), 'mp', axis=0, tiled=True)  5.43 us
    reshape x1, local copies, waits for them, and re-layouts, local(): return grad.reshape(1, -1)  4.57 us
    another operation x1, local copies, waits for them, and re-layouts, local(): section_weight[0].reshape(2, chan_half, 9, channels).transpose(0, 2, 1, 3)  4.44 us
    ppermute x1, waiting for transfers between devices, among(): return lax.ppermute(own_pair, ('pipe', 'dp'), pairs)  4.04 us
    select_n x1, other arithmetic, local(): jnp.where(lane == 0, jnp.concatenate([own, other], 1), jnp.concatenate([o...  3.57 us
    ppermute x2, starting transfers between devices, to_first(): return lax.ppermute(back, ('pipe', 'dp'), pairs)  3.5 us
    unnamed x17, local copies, waits for them, and re-layouts  3.37 us
  transfers between devices with their start and end apart: 7, of which 3 were waited for; matrix products, arithmetic and copies ran while one was open for 25% of the time, Pallas kernels for 0%

profile of v11, /device:TPU:13, one launch (start us, length us, event | category | flops | bytes accessed | tf_op | source)
XLA Modules:
  0.0 68.9 jit_solution(14200761312044786150)
XLA Ops:
  0.0 2.7 %reshape.87 = bf16[921600]{0:T(1024)(128)(2,1)S(1)} reshape(bf16[1,2,460800]{2,1,0:T(2,128)(2,1)} %param.4) | data formatting | bytes 3686400
  2.7 4.4 %reshape_squeeze.3 = bf16[2,160,9,320]{3,2,1,0:T(8,128)(2,1)} reshape(bf16[921600]{0:T(1024)(128)(2,1)S(1)} %reshape.87) | data formatting | bytes 3686400 | tf_op jit(solution)/shard_map/reshape;squeeze | solution.py:65
  7.1 2.7 %copy.55 = bf16[2,9,160,320]{3,2,1,0:T(8,128)(2,1)S(1)} copy(bf16[2,9,160,320]{3,1,2,0:T(8,128)(2,1)} %bitcast.102) | data formatting | bytes 3686400 | tf_op jit(solution)/shard_map/transpose | solution.py:65
  9.8 0.7 %collective-permute-start.2 = (bf16[2,160,3,3,320]{4,1,3,2,0:T(8,128)(2,1)S(1)}, bf16[2,160,3,3,320]{4,1,3,2,0:T(8,128)(2,1)}, u32[]{:S(2)}, u32[]{:S(2)}) collective-permute-start(bf16[2,160,3,3,320]{4,1,3,2,0:T(8,128)(2,1)S(1)} %bitcast.103), channel_id=1, source_target_pairs={{0,1},{1,0},{2,3},{3,2},{4,5},{5,4},{6,7},{7,6},{8,9},{9,8},{10,11... | collective-permute-start | bytes 5529608 | tf_op jit(solution)/shard_map/ppermute | solution.py:68
  10.6 0.2 fusion.86
  11.3 0.3 rev.22
  11.9 0.9 %convolution_select_fusion.1 = f32[4,32,3,160]{3,1,2,0:T(8,128)S(1)} fusion(bf16[2,160,3,3,320]{4,1,3,2,0:T(8,128)(2,1)S(1)} %bitcast.104, bf16[4,4,7,2,320]{4,2,1,3,0:T(8,128)(2,1)S(1)} %slice.66, bf16[4,4,8,3,320]{4,2,1,3,0:T(8,128)(2,1)S(1)} %copy.54, pred[32,3]{0,1:T(4,128)(4,1)S(1)} %copy-done.6), kind=kOutput, calls=%fused_computation.8 | convolution fusion | flops 296202240 | bytes 1843712 | tf_op jit(solution)/shard_map/conv_general_dilated | solution.py:13
  12.8 1.0 %copy.56 = f32[4,32,3,160]{3,0,2,1:T(4,128)} copy(f32[4,32,3,160]{3,1,2,0:T(8,128)S(1)} %convolution_select_fusion.1) | data formatting | bytes 491520 | tf_op jit(solution)/shard_map/conv_general_dilated | solution.py:13
  13.8 0.8 %convolution_select_fusion = f32[4,32,3,320]{3,1,2,0:T(8,128)S(1)} fusion(bf16[2,160,3,3,320]{4,1,3,2,0:T(8,128)(2,1)S(1)} %bitcast.105, bf16[4,4,7,2,160]{4,2,1,3,0:T(8,128)(2,1)S(1)} %slice.69, bf16[4,4,8,3,160]{4,2,1,3,0:T(8,128)(2,1)S(1)} %copy.58, pred[32,3]{0,1:T(4,128)(4,1)S(1)} %copy-done.6), kind=kOutput, calls=%fused_computation.7 | convolution fusion | flops 295649280 | bytes 1925632 | tf_op jit(solution)/shard_map/conv_general_dilated | solution.py:22
  14.6 0.4 copy.59
  15.0 0.6 rev.23
  15.6 1.1 %fusion.88 = f32[4,4,16,160]{3,1,2,0:T(4,128)S(1)} fusion(f32[4,4,24,160]{3,0,2,1:T(4,128)} %bitcast.115, bf16[4,4,16,320]{3,1,2,0:T(4,128)(2,1)S(1)} %bitcast.109, s32[]{:T(128)S(6)} %select_n.72), kind=kLoop, calls=%fused_computation.129 | loop fusion | flops 163840 | bytes 409604 | tf_op jit(solution)/shard_map/convert_element_type | solution.py:39
  16.7 0.3 pad_maximum_fusion
  17.2 2.6 %all-gather = f32[8,4,16,480]{3,2,1,0:T(8,128)S(1)} all-gather(f32[4,4,16,480]{3,2,1,0:T(8,128)S(1)} %copy.60), channel_id=2, replica_groups=mesh['groups'=2,'pipe'=4,'dp'=2,'mp'=2] {'mp'}, dimensions={0}, use_global_device_ids=true | all-gather | bytes 1474560 | tf_op jit(solution)/shard_map/all_gather | solution.py:91
  19.7 1.5 %copy.87 = bf16[2,4,4,16,480]{4,2,3,1,0:T(4,128)(2,1)} copy(f32[2,4,4,16,480]{4,3,2,1,0:T(8,128)S(1)} %bitcast.107) | data formatting | bytes 1474560 | tf_op jit(solution)/shard_map/all_gather | solution.py:91
  21.2 1.1 %slice_bitcast_fusion.24 = (bf16[4,4,16,160]{3,1,2,0:T(4,128)(2,1)S(1)}, bf16[4,4,16,160]{3,1,2,0:T(4,128)(2,1)S(1)}) fusion(bf16[2,4,4,16,480]{4,2,3,1,0:T(4,128)(2,1)} %copy.87), kind=kLoop, calls=%fused_computation.130 | loop fusion | bytes 327680 | tf_op jit(solution)/shard_map/squeeze | solution.py:92
  22.3 0.8 %fusion.96 = bf16[2,4,16,320]{3,1,2,0:T(4,128)(2,1)} fusion(s32[]{:T(128)S(6)} %select_n.71, bf16[4,4,16,160]{3,1,2,0:T(4,128)(2,1)S(1)} %get-tuple-element.22, bf16[4,4,16,160]{3,1,2,0:T(4,128)(2,1)S(1)} %get-tuple-element.21), kind=kLoop, calls=%fused_computation.139 | loop fusion | flops 163840 | bytes 245764 | tf_op jit(solution)/shard_map/concatenate | solution.py:92
  23.0 1.3 %collective-permute-start = (bf16[2,4,16,320]{3,1,2,0:T(4,128)(2,1)}, bf16[2,4,16,320]{3,1,2,0:T(4,128)(2,1)S(1)}, u32[]{:S(2)}, u32[]{:S(2)}) collective-permute-start(bf16[2,4,16,320]{3,1,2,0:T(4,128)(2,1)} %fusion.96), channel_id=1, source_target_pairs={{0,4},{12,8},{1,5},{13,9},{2,6},{14,10},{3,7},{15,11},{16,20},{28,... | collective-permute-start | bytes 245768 | tf_op jit(solution)/shard_map/ppermute | solution.py:72
  24.3 0.3 fusion.117
  24.7 1.5 %collective-permute-start.1 = (f32[2,4,16,320]{3,1,2,0:T(4,128)S(1)}, f32[2,4,16,320]{3,1,2,0:T(4,128)S(1)}, u32[]{:S(2)}, u32[]{:S(2)}) collective-permute-start(f32[2,4,16,320]{3,1,2,0:T(4,128)S(1)} %bitcast.130), channel_id=1, source_target_pairs={{0,4},{12,8},{1,5},{13,9},{2,6},{14,10},{3,7},{15,11},{16,20},{28,... | collective-permute-start | bytes 491528 | tf_op jit(solution)/shard_map/ppermute | solution.py:72
  26.2 3.0 %collective-permute-done = bf16[2,4,16,320]{3,1,2,0:T(4,128)(2,1)S(1)} collective-permute-done((bf16[2,4,16,320]{3,1,2,0:T(4,128)(2,1)}, bf16[2,4,16,320]{3,1,2,0:T(4,128)(2,1)S(1)}, u32[]{:S(2)}, u32[]{:S(2)}) %collective-permute-start) | collective-permute-done | bytes 81952 | tf_op jit(solution)/shard_map/ppermute | solution.py:72
  29.5 3.6 %maximum_select_fusion = bf16[2,320,3,3,320]{4,1,3,2,0:T(8,128)(2,1)S(1)} fusion(bf16[2,160,3,3,320]{4,1,3,2,0:T(8,128)(2,1)} %collective-permute-done.2, bf16[2,160,3,3,320]{4,1,3,2,0:T(8,128)(2,1)S(1)} %bitcast.106, pred[]{:T(512)S(6)} %eq.8), kind=kLoop, calls=%fused_computation | loop fusion | flops 16588800 | bytes 7372801 | tf_op jit(solution)/shard_map/jit(_where)/select_n | solution.py:101
  33.1 1.0 %fusion.6 = f32[4,16,3,320]{3,1,2,0:T(8,128)S(1)} fusion(bf16[2,320,3,3,320]{4,1,3,2,0:T(8,128)(2,1)S(1)} %maximum_select_fusion, bf16[4,2,7,2,320]{4,2,1,3,0:T(8,128)(2,1)S(1)} %slice.76, bf16[4,2,8,3,320]{4,2,1,3,0:T(8,128)(2,1)S(1)} %copy.64, pred[16,3]{0,1:T(4,128)(4,1)S(1)} %copy-done.5), kind=kOutput, calls=%fused_computation.11 | convolution fusion | flops 295587840 | bytes 2703872 | tf_op jit(solution)/shard_map/conv_general_dilated | solution.py:13
  34.2 0.2 broadcast_select_fusion.1
  34.6 0.5 copy-done
  35.1 1.0 %fusion.4 = f32[4,16,3,320]{3,1,2,0:T(8,128)S(1)} fusion(bf16[2,320,3,3,320]{4,1,3,2,0:T(8,128)(2,1)S(1)} %maximum_select_fusion, bf16[4,2,7,2,320]{4,2,1,3,0:T(8,128)(2,1)S(1)} %slice.79, bf16[4,2,8,3,320]{4,2,1,3,0:T(8,128)(2,1)S(1)} %copy.67, pred[16,3]{0,1:T(4,128)(4,1)S(1)} %copy-done.5), kind=kOutput, calls=%fused_computation.9 | convolution fusion | flops 295587840 | bytes 2703872 | tf_op jit(solution)/shard_map/conv_general_dilated | solution.py:13
  36.3 0.2 add_convert_fusion.3
  36.5 0.3 rev.24
  36.9 2.4 %fusion.5 = f32[4,16,3,320]{3,1,2,0:T(8,128)S(1)} fusion(bf16[2,320,3,3,320]{4,1,3,2,0:T(8,128)(2,1)} %copy-done, bf16[4,2,7,2,320]{4,2,1,3,0:T(8,128)(2,1)S(1)} %slice.82, bf16[4,2,8,3,320]{4,2,1,3,0:T(8,128)(2,1)S(1)} %copy.70, pred[16,3]{0,1:T(4,128)(4,1)S(1)} %copy-done.5), kind=kOutput, calls=%fused_computation.10 | convolution fusion | flops 295587840 | bytes 2652208 | tf_op jit(solution)/shard_map/conv_general_dilated | solution.py:22
  39.5 0.3 rev.25
  39.8 0.2 broadcast_select_fusion
  40.1 0.3 rev.26
  40.5 2.4 %fusion.7 = f32[4,16,3,320]{3,1,2,0:T(8,128)S(1)} fusion(bf16[2,320,3,3,320]{4,1,3,2,0:T(8,128)(2,1)} %copy-done, bf16[4,2,7,2,320]{4,2,1,3,0:T(8,128)(2,1)S(1)} %slice.84, bf16[4,2,8,3,320]{4,2,1,3,0:T(8,128)(2,1)S(1)} %copy.73, pred[16,3]{0,1:T(4,128)(4,1)S(1)} %copy-done.5), kind=kOutput, calls=%fused_computation.12 | convolution fusion | flops 295587840 | bytes 2652208 | tf_op jit(solution)/shard_map/conv_general_dilated | solution.py:22
  43.0 0.3 rev.27
  43.4 0.3 fusion.95
  43.7 2.2 %collective-permute-start.5 = (bf16[2,4,16,320]{3,1,2,0:T(4,128)(2,1)S(1)}, bf16[2,4,16,320]{3,1,2,0:T(4,128)(2,1)S(1)}, u32[]{:S(2)}, u32[]{:S(2)}) collective-permute-start(bf16[2,4,16,320]{3,1,2,0:T(4,128)(2,1)S(1)} %fusion.95), channel_id=1, source_target_pairs={{6,0},{4,2},{10,12},{8,14},{7,1},{5,3},{11,13},{9,15},{22,16},{20,... | collective-permute-start | bytes 245768 | tf_op jit(solution)/shard_map/ppermute | solution.py:168
  45.9 1.3 %collective-permute-start.3 = (bf16[2,4,16,320]{3,1,2,0:T(4,128)(2,1)S(1)}, bf16[2,4,16,320]{3,1,2,0:T(4,128)(2,1)S(1)}, u32[]{:S(2)}, u32[]{:S(2)}) collective-permute-start(bf16[2,4,16,320]{3,1,2,0:T(4,128)(2,1)S(1)} %fusion.95), channel_id=1, source_target_pairs={{4,0},{6,2},{8,12},{10,14},{5,1},{7,3},{9,13},{11,15},{20,16},{22,... | collective-permute-start | bytes 245768 | tf_op jit(solution)/shard_map/ppermute | solution.py:168
  47.3 0.4 collective-permute-start.4
  47.7 1.1 %collective-permute-done.3 = bf16[2,4,16,320]{3,1,2,0:T(4,128)(2,1)S(1)} collective-permute-done((bf16[2,4,16,320]{3,1,2,0:T(4,128)(2,1)S(1)}, bf16[2,4,16,320]{3,1,2,0:T(4,128)(2,1)S(1)}, u32[]{:S(2)}, u32[]{:S(2)}) %collective-permute-start.3) | collective-permute-done | bytes 81952 | tf_op jit(solution)/shard_map/ppermute | solution.py:168
  48.8 0.2 fusion.94
  49.0 0.3 maximum_select_fusion.1
  49.3 2.2 %collective-permute-start.6 = (bf16[2,4,16,640]{3,1,2,0:T(4,128)(2,1)S(1)}, bf16[2,4,16,640]{3,1,2,0:T(4,128)(2,1)S(1)}, u32[]{:S(2)}, u32[]{:S(2)}) collective-permute-start(bf16[2,4,16,640]{3,1,2,0:T(4,128)(2,1)S(1)} %get-tuple-element.10), channel_id=1, source_target_pairs={{6,4},{4,6},{10,8},{8,10},{7,5},{5,7},{11,9},{9,11},{22,20},{20,22... | collective-permute-start | bytes 491528 | tf_op jit(solution)/shard_map/ppermute | solution.py:181
  51.6 0.2 fusion.93
  51.8 4.0 %collective-permute-done.6 = bf16[2,4,16,640]{3,1,2,0:T(4,128)(2,1)S(1)} collective-permute-done((bf16[2,4,16,640]{3,1,2,0:T(4,128)(2,1)S(1)}, bf16[2,4,16,640]{3,1,2,0:T(4,128)(2,1)S(1)}, u32[]{:S(2)}, u32[]{:S(2)}) %collective-permute-start.6) | collective-permute-done | bytes 163872 | tf_op jit(solution)/shard_map/ppermute | solution.py:181
  56.3 5.4 %all_gather.11 = bf16[8,4,16,640]{3,2,1,0:T(8,128)(2,1)S(1)} all-gather(bf16[4,4,16,640]{3,2,1,0:T(8,128)(2,1)S(1)} %copy.75), channel_id=1, replica_groups=mesh['groups'=2,'pipe'=4,'dp'=2,'mp'=2] {'mp'}, dimensions={0}, use_global_device_ids=true | all-gather | bytes 983040 | tf_op jit(solution)/shard_map/all_gather | solution.py:192
  61.9 0.9 %fusion.23 = f32[160,3,3,320]{3,0,2,1:T(8,128)S(1)} fusion(bf16[8,4,16,320]{3,2,1,0:T(8,128)(2,1)S(1)} %slice.88, bf16[8,4,16,160]{3,2,1,0:T(8,128)(2,1)S(1)} %constant_dynamic-slice_fusion), kind=kOutput, calls=%fused_computation.37 | convolution fusion | flops 376832000 | bytes 2334720 | tf_op jit(solution)/shard_map/conv_general_dilated | solution.py:31
  62.8 1.5 %copy.78 = f32[160,3,3,320]{3,2,1,0:T(4,128)S(1)} copy(f32[160,3,3,320]{3,0,2,1:T(8,128)S(1)} %fusion.23) | data formatting | bytes 3686400 | tf_op jit(solution)/shard_map/conv_general_dilated | solution.py:31
  64.3 4.6 %reshape.25 = f32[1,460800]{1,0:T(1,128)} reshape(f32[160,3,3,320]{3,2,1,0:T(4,128)S(1)} %copy.78) | data formatting | bytes 3686400 | tf_op jit(solution)/shard_map/reshape | solution.py:196
  (56 shorter events, 2.8 us)
Async XLA Ops:
  7.1 3.4 %copy-start.3 = (bf16[1,2,2,4,16,320]{5,4,3,2,1,0:T(8,128)(2,1)S(1)}, bf16[1,2,2,4,16,320]{5,4,3,2,1,0:T(8,128)(2,1)}, u32[]{:S(2)}) copy-start(bf16[1,2,2,4,16,320]{5,4,3,2,1,0:T(8,128)(2,1)} %param.3) | copy-start | bytes 491524
  9.8 1.3 %copy-start.4 = (bf16[1,2,2,4,16,320]{5,4,3,2,1,0:T(8,128)(2,1)S(1)}, bf16[1,2,2,4,16,320]{5,4,3,2,1,0:T(8,128)(2,1)}, u32[]{:S(2)}) copy-start(bf16[1,2,2,4,16,320]{5,4,3,2,1,0:T(8,128)(2,1)} %param.5) | copy-start | bytes 491524
  9.8 2.1 %copy-start.6 = (pred[32,3]{0,1:T(4,128)(4,1)S(1)}, pred[32,3]{0,1:T(4,128)(4,1)}, u32[]{:S(2)}) copy-start(pred[32,3]{0,1:T(4,128)(4,1)} %constant.64) | copy-start | bytes 292
  9.8 19.7 %collective-permute-start.2 = (bf16[2,160,3,3,320]{4,1,3,2,0:T(8,128)(2,1)S(1)}, bf16[2,160,3,3,320]{4,1,3,2,0:T(8,128)(2,1)}, u32[]{:S(2)}, u32[]{:S(2)}) collective-permute-start(bf16[2,160,3,3,320]{4,1,3,2,0:T(8,128)(2,1)S(1)} %bitcast.103), channel_id=1, source_target_pairs={{0,1},{1,0},{2,3},{3,2},{4,5},{5,4},{6,7},{7,6},{8,9},{9,8},{10,11... | collective-permute-start | bytes 5529608 | tf_op jit(solution)/shard_map/ppermute | solution.py:68
  11.2 1.6 %copy-start.1 = (bf16[1,2,2,4,16,320]{5,3,4,2,1,0:T(4,128)(2,1)}, bf16[1,2,2,4,16,320]{5,3,4,2,1,0:T(4,128)(2,1)S(1)}, u32[]{:S(2)}) copy-start(bf16[1,2,2,4,16,320]{5,3,4,2,1,0:T(4,128)(2,1)S(1)} %copy.52) | copy-start | bytes 491524
  23.0 6.2 %collective-permute-start = (bf16[2,4,16,320]{3,1,2,0:T(4,128)(2,1)}, bf16[2,4,16,320]{3,1,2,0:T(4,128)(2,1)S(1)}, u32[]{:S(2)}, u32[]{:S(2)}) collective-permute-start(bf16[2,4,16,320]{3,1,2,0:T(4,128)(2,1)} %fusion.96), channel_id=1, source_target_pairs={{0,4},{12,8},{1,5},{13,9},{2,6},{14,10},{3,7},{15,11},{16,20},{28,... | collective-permute-start | bytes 245768 | tf_op jit(solution)/shard_map/ppermute | solution.py:72
  24.7 11.6 %collective-permute-start.1 = (f32[2,4,16,320]{3,1,2,0:T(4,128)S(1)}, f32[2,4,16,320]{3,1,2,0:T(4,128)S(1)}, u32[]{:S(2)}, u32[]{:S(2)}) collective-permute-start(f32[2,4,16,320]{3,1,2,0:T(4,128)S(1)} %bitcast.130), channel_id=1, source_target_pairs={{0,4},{12,8},{1,5},{13,9},{2,6},{14,10},{3,7},{15,11},{16,20},{28,... | collective-permute-start | bytes 491528 | tf_op jit(solution)/shard_map/ppermute | solution.py:72
  29.5 3.6 %copy-start.5 = (pred[16,3]{0,1:T(4,128)(4,1)S(1)}, pred[16,3]{0,1:T(4,128)(4,1)}, u32[]{:S(2)}) copy-start(pred[16,3]{0,1:T(4,128)(4,1)} %constant.66) | copy-start | bytes 148
  33.1 2.0 %copy-start = (bf16[2,320,3,3,320]{4,1,3,2,0:T(8,128)(2,1)}, bf16[2,320,3,3,320]{4,1,3,2,0:T(8,128)(2,1)S(1)}, u32[]{:S(2)}) copy-start(bf16[2,320,3,3,320]{4,1,3,2,0:T(8,128)(2,1)S(1)} %maximum_select_fusion) | copy-start | bytes 11059204
  35.1 1.2 %copy-start.2 = (bf16[1,2,2,4,16,320]{5,3,4,2,1,0:T(4,128)(2,1)S(1)}, bf16[1,2,2,4,16,320]{5,3,4,2,1,0:T(4,128)(2,1)}, u32[]{:S(2)}) copy-start(bf16[1,2,2,4,16,320]{5,3,4,2,1,0:T(4,128)(2,1)} %copy-done.1) | copy-start | bytes 491524
  43.7 7.8 %collective-permute-start.5 = (bf16[2,4,16,320]{3,1,2,0:T(4,128)(2,1)S(1)}, bf16[2,4,16,320]{3,1,2,0:T(4,128)(2,1)S(1)}, u32[]{:S(2)}, u32[]{:S(2)}) collective-permute-start(bf16[2,4,16,320]{3,1,2,0:T(4,128)(2,1)S(1)} %fusion.95), channel_id=1, source_target_pairs={{6,0},{4,2},{10,12},{8,14},{7,1},{5,3},{11,13},{9,15},{22,16},{20,... | collective-permute-start | bytes 245768 | tf_op jit(solution)/shard_map/ppermute | solution.py:168
  45.9 2.9 %collective-permute-start.3 = (bf16[2,4,16,320]{3,1,2,0:T(4,128)(2,1)S(1)}, bf16[2,4,16,320]{3,1,2,0:T(4,128)(2,1)S(1)}, u32[]{:S(2)}, u32[]{:S(2)}) collective-permute-start(bf16[2,4,16,320]{3,1,2,0:T(4,128)(2,1)S(1)} %fusion.95), channel_id=1, source_target_pairs={{4,0},{6,2},{8,12},{10,14},{5,1},{7,3},{9,13},{11,15},{20,16},{22,... | collective-permute-start | bytes 245768 | tf_op jit(solution)/shard_map/ppermute | solution.py:168
  47.3 4.2 %collective-permute-start.4 = (bf16[2,4,16,640]{3,1,2,0:T(4,128)(2,1)S(1)}, bf16[2,4,16,640]{3,1,2,0:T(4,128)(2,1)S(1)}, u32[]{:S(2)}, u32[]{:S(2)}) collective-permute-start(bf16[2,4,16,640]{3,1,2,0:T(4,128)(2,1)S(1)} %pad_maximum_fusion.2), channel_id=1, source_target_pairs={{2,0},{0,2},{3,1},{1,3},{6,4},{4,6},{7,5},{5,7},{10,8},{8,10},{11,... | collective-permute-start | bytes 491528 | tf_op jit(solution)/shard_map/ppermute | solution.py:161
  49.3 6.5 %collective-permute-start.6 = (bf16[2,4,16,640]{3,1,2,0:T(4,128)(2,1)S(1)}, bf16[2,4,16,640]{3,1,2,0:T(4,128)(2,1)S(1)}, u32[]{:S(2)}, u32[]{:S(2)}) collective-permute-start(bf16[2,4,16,640]{3,1,2,0:T(4,128)(2,1)S(1)} %get-tuple-element.10), channel_id=1, source_target_pairs={{6,4},{4,6},{10,8},{8,10},{7,5},{5,7},{11,9},{9,11},{22,20},{20,22... | collective-permute-start | bytes 491528 | tf_op jit(solution)/shard_map/ppermute | solution.py:181

commit v12 on v11

--- a/solution.py
+++ b/solution.py
@@ -157,10 +157,7 @@
     c0 = bf16(f32(cot) + f32(skip[1]))
 
     nd = lax.axis_size("dp")
-    pair0, _ = lax.optimization_barrier((jnp.concatenate([x0, seed], -1), h1_r))
-    others = [pair0] + [lax.ppermute(pair0, "dp", [((d + dd) % nd, d) for d in range(nd)])
-                        for dd in range(1, nd)]
-    back = jnp.where(lower, c0, a_last)
+    back = jnp.where(lower, jnp.concatenate([a0, c0], -1), jnp.concatenate([a_last, seed], -1))
 
     def to_first(dd):
         pairs = [(src * nd + (d + dd) % nd, dst * nd + d)
@@ -182,13 +179,7 @@
 
     got = [to_first(dd) for dd in range(nd)]
     mids = [own_pair] + [among(dd) for dd in range(1, nd)]
-    pieces = []
-    for dd in range(nd):
-        a_first = bf16(jax.nn.silu(f32(others[dd][..., :channels])))
-        act = jnp.where(lower, a_first, got[dd])
-        cot = jnp.where(lower, got[dd], others[dd][..., channels:])
-        first_pair = jnp.concatenate([act, cot], -1)
-        pieces.append(jnp.where(stage == 0, first_pair, mids[dd]))
+    pieces = [jnp.where(stage == 0, got[dd], mids[dd]) for dd in range(nd)]
     every = lax.all_gather(jnp.concatenate(pieces, 0), "mp", axis=0, tiled=True)
     act_all = every[..., :channels]
     cot_all = lax.dynamic_slice_in_dim(every, channels + low, chan_half, 3)

time: 69.2 us -> 68.9 us (level)
  the two profiles are of different devices: /device:TPU:13 before, /device:TPU:19 now
where the time goes in v12:
time: 68.9 us; the launch traced here: 68.5 us
  local copies, waits for them, and re-layouts  24.9 us (36%)
  blocking collectives  9.73 us (14%)
  matrix products  9.37 us (14%)
  starting transfers between devices  8.24 us (12%)
  waiting for transfers between devices  7.96 us (12%)
  other arithmetic  7.73 us (11%)
    all_gather x1, blocking collectives, local(): every = lax.all_gather(jnp.concatenate(pieces, 0), 'mp', axis=0, tiled=True)  7.18 us
    conv_general_dilated x3, matrix products, conv_t(): lax.conv_general_dilated(flipped, weight, (1, 1), ((1, 1), (1, 1)), dimen...  5.6 us
    reshape x1, local copies, waits for them, and re-layouts, local(): return grad.reshape(1, -1)  4.57 us
    another operation x1, local copies, waits for them, and re-layouts, local(): section_weight[0].reshape(2, chan_half, 9, channels).transpose(0, 2, 1, 3)  4.47 us
    select_n x1, other arithmetic, local(): jnp.where(lane == 0, jnp.concatenate([own, other], 1), jnp.concatenate([o...  3.6 us
    unnamed x17, local copies, waits for them, and re-layouts  3.36 us
    ppermute x2, waiting for transfers between devices, up(): return lax.ppermute(v, 'pipe', pairs)  3.13 us
    ppermute x1, waiting for transfers between devices, among(): return lax.ppermute(own_pair, ('pipe', 'dp'), pairs)  2.99 us
  transfers between devices with their start and end apart: 6, of which 4 were waited for; matrix products, arithmetic and copies ran while one was open for 24% of the time, Pallas kernels for 0%

profile of v12, /device:TPU:19, one launch (start us, length us, event | category | flops | bytes accessed | tf_op | source)
XLA Modules:
  0.0 68.5 jit_solution(10323381968777545670)
XLA Ops:
  0.0 2.7 %reshape.87 = bf16[921600]{0:T(1024)(128)(2,1)S(1)} reshape(bf16[1,2,460800]{2,1,0:T(2,128)(2,1)} %param.4) | data formatting | bytes 3686400
  2.7 4.5 %reshape_squeeze.3 = bf16[2,160,9,320]{3,2,1,0:T(8,128)(2,1)} reshape(bf16[921600]{0:T(1024)(128)(2,1)S(1)} %reshape.87) | data formatting | bytes 3686400 | tf_op jit(solution)/shard_map/reshape;squeeze | solution.py:65
  7.1 2.7 %copy.55 = bf16[2,9,160,320]{3,2,1,0:T(8,128)(2,1)S(1)} copy(bf16[2,9,160,320]{3,1,2,0:T(8,128)(2,1)} %bitcast.104) | data formatting | bytes 3686400 | tf_op jit(solution)/shard_map/transpose | solution.py:65
  9.8 0.7 %collective-permute-start.2 = (bf16[2,160,3,3,320]{4,1,3,2,0:T(8,128)(2,1)S(1)}, bf16[2,160,3,3,320]{4,1,3,2,0:T(8,128)(2,1)}, u32[]{:S(2)}, u32[]{:S(2)}) collective-permute-start(bf16[2,160,3,3,320]{4,1,3,2,0:T(8,128)(2,1)S(1)} %bitcast.105), channel_id=1, source_target_pairs={{0,1},{1,0},{2,3},{3,2},{4,5},{5,4},{6,7},{7,6},{8,9},{9,8},{10,11... | collective-permute-start | bytes 5529608 | tf_op jit(solution)/shard_map/ppermute | solution.py:68
  10.7 0.2 fusion.22
  11.2 0.3 rev.22
  11.9 0.9 %convolution_select_fusion.1 = f32[4,32,3,160]{3,1,2,0:T(8,128)S(1)} fusion(bf16[2,160,3,3,320]{4,1,3,2,0:T(8,128)(2,1)S(1)} %bitcast.106, bf16[4,4,7,2,320]{4,2,1,3,0:T(8,128)(2,1)S(1)} %slice.50, bf16[4,4,8,3,320]{4,2,1,3,0:T(8,128)(2,1)S(1)} %copy.54, pred[32,3]{0,1:T(4,128)(4,1)S(1)} %copy-done.6), kind=kOutput, calls=%fused_computation.8 | convolution fusion | flops 296202240 | bytes 1843712 | tf_op jit(solution)/shard_map/conv_general_dilated | solution.py:13
  12.8 1.0 %copy.56 = f32[4,32,3,160]{3,0,2,1:T(4,128)} copy(f32[4,32,3,160]{3,1,2,0:T(8,128)S(1)} %convolution_select_fusion.1) | data formatting | bytes 491520 | tf_op jit(solution)/shard_map/conv_general_dilated | solution.py:13
  13.8 0.8 %convolution_select_fusion = f32[4,32,3,320]{3,1,2,0:T(8,128)S(1)} fusion(bf16[2,160,3,3,320]{4,1,3,2,0:T(8,128)(2,1)S(1)} %bitcast.107, bf16[4,4,7,2,160]{4,2,1,3,0:T(8,128)(2,1)S(1)} %slice.53, bf16[4,4,8,3,160]{4,2,1,3,0:T(8,128)(2,1)S(1)} %copy.58, pred[32,3]{0,1:T(4,128)(4,1)S(1)} %copy-done.6), kind=kOutput, calls=%fused_computation.7 | convolution fusion | flops 295649280 | bytes 1925632 | tf_op jit(solution)/shard_map/conv_general_dilated | solution.py:22
  14.6 0.4 copy.59
  15.1 0.6 rev.23
  15.7 1.1 %fusion.81 = f32[4,4,16,160]{3,1,2,0:T(4,128)S(1)} fusion(f32[4,4,24,160]{3,0,2,1:T(4,128)} %bitcast.115, bf16[4,4,16,320]{3,1,2,0:T(4,128)(2,1)S(1)} %bitcast.112, s32[]{:T(128)S(6)} %select_n.58), kind=kLoop, calls=%fused_computation.118 | loop fusion | flops 163840 | bytes 409604 | tf_op jit(solution)/shard_map/convert_element_type | solution.py:39
  16.8 0.3 pad_maximum_fusion
  17.2 2.6 %all-gather = f32[8,4,16,480]{3,2,1,0:T(8,128)S(1)} all-gather(f32[4,4,16,480]{3,2,1,0:T(8,128)S(1)} %copy.60), channel_id=2, replica_groups=mesh['groups'=2,'pipe'=4,'dp'=2,'mp'=2] {'mp'}, dimensions={0}, use_global_device_ids=true | all-gather | bytes 1474560 | tf_op jit(solution)/shard_map/all_gather | solution.py:91
  19.8 1.5 %copy.87 = bf16[2,4,4,16,480]{4,2,3,1,0:T(4,128)(2,1)} copy(f32[2,4,4,16,480]{4,3,2,1,0:T(8,128)S(1)} %bitcast.109) | data formatting | bytes 1474560 | tf_op jit(solution)/shard_map/all_gather | solution.py:91
  21.2 1.1 %slice_bitcast_fusion.24 = (bf16[4,4,16,160]{3,1,2,0:T(4,128)(2,1)S(1)}, bf16[4,4,16,160]{3,1,2,0:T(4,128)(2,1)S(1)}) fusion(bf16[2,4,4,16,480]{4,2,3,1,0:T(4,128)(2,1)} %copy.87), kind=kLoop, calls=%fused_computation.119 | loop fusion | bytes 327680 | tf_op jit(solution)/shard_map/squeeze | solution.py:92
  22.3 0.8 %fusion.86 = bf16[2,4,16,320]{3,1,2,0:T(4,128)(2,1)} fusion(s32[]{:T(128)S(6)} %select_n.57, bf16[4,4,16,160]{3,1,2,0:T(4,128)(2,1)S(1)} %get-tuple-element.20, bf16[4,4,16,160]{3,1,2,0:T(4,128)(2,1)S(1)} %get-tuple-element.19), kind=kLoop, calls=%fused_computation.125 | loop fusion | flops 163840 | bytes 245764 | tf_op jit(solution)/shard_map/concatenate | solution.py:92
  23.1 1.3 %collective-permute-start.1 = (bf16[2,4,16,320]{3,1,2,0:T(4,128)(2,1)}, bf16[2,4,16,320]{3,1,2,0:T(4,128)(2,1)S(1)}, u32[]{:S(2)}, u32[]{:S(2)}) collective-permute-start(bf16[2,4,16,320]{3,1,2,0:T(4,128)(2,1)} %fusion.86), channel_id=1, source_target_pairs={{0,4},{12,8},{1,5},{13,9},{2,6},{14,10},{3,7},{15,11},{16,20},{28,... | collective-permute-start | bytes 245768 | tf_op jit(solution)/shard_map/ppermute | solution.py:72
  24.3 0.3 fusion.107
  24.7 1.5 %collective-permute-start = (f32[2,4,16,320]{3,1,2,0:T(4,128)S(1)}, f32[2,4,16,320]{3,1,2,0:T(4,128)S(1)}, u32[]{:S(2)}, u32[]{:S(2)}) collective-permute-start(f32[2,4,16,320]{3,1,2,0:T(4,128)S(1)} %bitcast.132), channel_id=1, source_target_pairs={{0,4},{12,8},{1,5},{13,9},{2,6},{14,10},{3,7},{15,11},{16,20},{28,... | collective-permute-start | bytes 491528 | tf_op jit(solution)/shard_map/ppermute | solution.py:72
  26.3 3.1 %collective-permute-done.1 = bf16[2,4,16,320]{3,1,2,0:T(4,128)(2,1)S(1)} collective-permute-done((bf16[2,4,16,320]{3,1,2,0:T(4,128)(2,1)}, bf16[2,4,16,320]{3,1,2,0:T(4,128)(2,1)S(1)}, u32[]{:S(2)}, u32[]{:S(2)}) %collective-permute-start.1) | collective-permute-done | bytes 81952 | tf_op jit(solution)/shard_map/ppermute | solution.py:72
  29.7 3.6 %maximum_select_fusion = bf16[2,320,3,3,320]{4,1,3,2,0:T(8,128)(2,1)S(1)} fusion(bf16[2,160,3,3,320]{4,1,3,2,0:T(8,128)(2,1)} %collective-permute-done.2, bf16[2,160,3,3,320]{4,1,3,2,0:T(8,128)(2,1)S(1)} %bitcast.108, pred[]{:T(512)S(6)} %eq.8), kind=kLoop, calls=%fused_computation | loop fusion | flops 16588800 | bytes 7372801 | tf_op jit(solution)/shard_map/jit(_where)/select_n | solution.py:101
  33.3 1.0 %fusion.6 = f32[4,16,3,320]{3,1,2,0:T(8,128)S(1)} fusion(bf16[2,320,3,3,320]{4,1,3,2,0:T(8,128)(2,1)S(1)} %maximum_select_fusion, bf16[4,2,7,2,320]{4,2,1,3,0:T(8,128)(2,1)S(1)} %slice.60, bf16[4,2,8,3,320]{4,2,1,3,0:T(8,128)(2,1)S(1)} %copy.64, pred[16,3]{0,1:T(4,128)(4,1)S(1)} %copy-done.5), kind=kOutput, calls=%fused_computation.11 | convolution fusion | flops 295587840 | bytes 2703872 | tf_op jit(solution)/shard_map/conv_general_dilated | solution.py:13
  34.5 0.2 broadcast_select_fusion.3
  34.8 0.5 copy-done
  35.3 1.0 %fusion.4 = f32[4,16,3,320]{3,1,2,0:T(8,128)S(1)} fusion(bf16[2,320,3,3,320]{4,1,3,2,0:T(8,128)(2,1)S(1)} %maximum_select_fusion, bf16[4,2,7,2,320]{4,2,1,3,0:T(8,128)(2,1)S(1)} %slice.63, bf16[4,2,8,3,320]{4,2,1,3,0:T(8,128)(2,1)S(1)} %copy.67, pred[16,3]{0,1:T(4,128)(4,1)S(1)} %copy-done.5), kind=kOutput, calls=%fused_computation.9 | convolution fusion | flops 295587840 | bytes 2703872 | tf_op jit(solution)/shard_map/conv_general_dilated | solution.py:13
  36.5 0.3 add_convert_fusion.3
  36.8 0.3 rev.24
  37.2 2.4 %fusion.5 = f32[4,16,3,320]{3,1,2,0:T(8,128)S(1)} fusion(bf16[2,320,3,3,320]{4,1,3,2,0:T(8,128)(2,1)} %copy-done, bf16[4,2,7,2,320]{4,2,1,3,0:T(8,128)(2,1)S(1)} %slice.66, bf16[4,2,8,3,320]{4,2,1,3,0:T(8,128)(2,1)S(1)} %copy.70, pred[16,3]{0,1:T(4,128)(4,1)S(1)} %copy-done.5), kind=kOutput, calls=%fused_computation.10 | convolution fusion | flops 295587840 | bytes 2652208 | tf_op jit(solution)/shard_map/conv_general_dilated | solution.py:22
  39.7 0.3 rev.25
  40.1 0.2 broadcast_select_fusion.2
  40.3 0.3 rev.26
  40.7 2.4 %fusion.7 = f32[4,16,3,320]{3,1,2,0:T(8,128)S(1)} fusion(bf16[2,320,3,3,320]{4,1,3,2,0:T(8,128)(2,1)} %copy-done, bf16[4,2,7,2,320]{4,2,1,3,0:T(8,128)(2,1)S(1)} %slice.68, bf16[4,2,8,3,320]{4,2,1,3,0:T(8,128)(2,1)S(1)} %copy.73, pred[16,3]{0,1:T(4,128)(4,1)S(1)} %copy-done.5), kind=kOutput, calls=%fused_computation.12 | convolution fusion | flops 295587840 | bytes 2652208 | tf_op jit(solution)/shard_map/conv_general_dilated | solution.py:22
  43.3 0.3 rev.27
  43.6 0.2 add_convert_fusion
  43.8 0.2 maximum_select_fusion.1
  44.1 1.3 %collective-permute-start.3 = (bf16[2,4,16,640]{3,1,2,0:T(4,128)(2,1)S(1)}, bf16[2,4,16,640]{3,1,2,0:T(4,128)(2,1)S(1)}, u32[]{:S(2)}, u32[]{:S(2)}) collective-permute-start(bf16[2,4,16,640]{3,1,2,0:T(4,128)(2,1)S(1)} %maximum_select_fusion.1), channel_id=1, source_target_pairs={{4,0},{6,2},{8,12},{10,14},{5,1},{7,3},{9,13},{11,15},{20,16},{22,... | collective-permute-start | bytes 491528 | tf_op jit(solution)/shard_map/ppermute | solution.py:165
  45.4 1.3 %collective-permute-start.4 = (bf16[2,4,16,640]{3,1,2,0:T(4,128)(2,1)S(1)}, bf16[2,4,16,640]{3,1,2,0:T(4,128)(2,1)S(1)}, u32[]{:S(2)}, u32[]{:S(2)}) collective-permute-start(bf16[2,4,16,640]{3,1,2,0:T(4,128)(2,1)S(1)} %maximum_select_fusion.1), channel_id=1, source_target_pairs={{6,0},{4,2},{10,12},{8,14},{7,1},{5,3},{11,13},{9,15},{22,16},{20,... | collective-permute-start | bytes 491528 | tf_op jit(solution)/shard_map/ppermute | solution.py:165
  46.7 0.9 %collective-permute-done.3 = bf16[2,4,16,640]{3,1,2,0:T(4,128)(2,1)S(1)} collective-permute-done((bf16[2,4,16,640]{3,1,2,0:T(4,128)(2,1)S(1)}, bf16[2,4,16,640]{3,1,2,0:T(4,128)(2,1)S(1)}, u32[]{:S(2)}, u32[]{:S(2)}) %collective-permute-start.3) | collective-permute-done | bytes 163872 | tf_op jit(solution)/shard_map/ppermute | solution.py:165
  47.6 0.2 broadcast_select_fusion.1
  47.8 2.1 %collective-permute-start.5 = (bf16[2,4,16,640]{3,1,2,0:T(4,128)(2,1)S(1)}, bf16[2,4,16,640]{3,1,2,0:T(4,128)(2,1)S(1)}, u32[]{:S(2)}, u32[]{:S(2)}) collective-permute-start(bf16[2,4,16,640]{3,1,2,0:T(4,128)(2,1)S(1)} %get-tuple-element.8), channel_id=1, source_target_pairs={{6,4},{4,6},{10,8},{8,10},{7,5},{5,7},{11,9},{9,11},{22,20},{20,22... | collective-permute-start | bytes 491528 | tf_op jit(solution)/shard_map/ppermute | solution.py:178
  50.0 0.9 %collective-permute-done.4 = bf16[2,4,16,640]{3,1,2,0:T(4,128)(2,1)S(1)} collective-permute-done((bf16[2,4,16,640]{3,1,2,0:T(4,128)(2,1)S(1)}, bf16[2,4,16,640]{3,1,2,0:T(4,128)(2,1)S(1)}, u32[]{:S(2)}, u32[]{:S(2)}) %collective-permute-start.4) | collective-permute-done | bytes 163872 | tf_op jit(solution)/shard_map/ppermute | solution.py:165
  50.9 3.0 %collective-permute-done.5 = bf16[2,4,16,640]{3,1,2,0:T(4,128)(2,1)S(1)} collective-permute-done((bf16[2,4,16,640]{3,1,2,0:T(4,128)(2,1)S(1)}, bf16[2,4,16,640]{3,1,2,0:T(4,128)(2,1)S(1)}, u32[]{:S(2)}, u32[]{:S(2)}) %collective-permute-start.5) | collective-permute-done | bytes 163872 | tf_op jit(solution)/shard_map/ppermute | solution.py:178
  53.9 0.2 pad_maximum_fusion.1
  54.2 7.2 %all_gather.11 = bf16[8,4,16,640]{3,2,1,0:T(8,128)(2,1)S(1)} all-gather(bf16[4,4,16,640]{3,2,1,0:T(8,128)(2,1)S(1)} %copy.75), channel_id=1, replica_groups=mesh['groups'=2,'pipe'=4,'dp'=2,'mp'=2] {'mp'}, dimensions={0}, use_global_device_ids=true | all-gather | bytes 983040 | tf_op jit(solution)/shard_map/all_gather | solution.py:183
  61.6 0.9 %fusion.23 = f32[160,3,3,320]{3,0,2,1:T(8,128)S(1)} fusion(bf16[8,4,16,320]{3,2,1,0:T(8,128)(2,1)S(1)} %slice.70, bf16[8,4,16,160]{3,2,1,0:T(8,128)(2,1)S(1)} %constant_dynamic-slice_fusion), kind=kOutput, calls=%fused_computation.37 | convolution fusion | flops 376832000 | bytes 2334720 | tf_op jit(solution)/shard_map/conv_general_dilated | solution.py:31
  62.4 1.5 %copy.78 = f32[160,3,3,320]{3,2,1,0:T(4,128)S(1)} copy(f32[160,3,3,320]{3,0,2,1:T(8,128)S(1)} %fusion.23) | data formatting | bytes 3686400 | tf_op jit(solution)/shard_map/conv_general_dilated | solution.py:31
  64.0 4.6 %reshape.25 = f32[1,460800]{1,0:T(1,128)} reshape(f32[160,3,3,320]{3,2,1,0:T(4,128)S(1)} %copy.78) | data formatting | bytes 3686400 | tf_op jit(solution)/shard_map/reshape | solution.py:187
  (52 shorter events, 2.3 us)
Async XLA Ops:
  7.1 3.4 %copy-start.3 = (bf16[1,2,2,4,16,320]{5,4,3,2,1,0:T(8,128)(2,1)S(1)}, bf16[1,2,2,4,16,320]{5,4,3,2,1,0:T(8,128)(2,1)}, u32[]{:S(2)}) copy-start(bf16[1,2,2,4,16,320]{5,4,3,2,1,0:T(8,128)(2,1)} %param.3) | copy-start | bytes 491524
  7.1 3.8 %copy-start.4 = (bf16[1,2,2,4,16,320]{5,4,3,2,1,0:T(8,128)(2,1)S(1)}, bf16[1,2,2,4,16,320]{5,4,3,2,1,0:T(8,128)(2,1)}, u32[]{:S(2)}) copy-start(bf16[1,2,2,4,16,320]{5,4,3,2,1,0:T(8,128)(2,1)} %param.5) | copy-start | bytes 491524
  9.8 2.1 %copy-start.6 = (pred[32,3]{0,1:T(4,128)(4,1)S(1)}, pred[32,3]{0,1:T(4,128)(4,1)}, u32[]{:S(2)}) copy-start(pred[32,3]{0,1:T(4,128)(4,1)} %constant.62) | copy-start | bytes 292
  9.8 19.8 %collective-permute-start.2 = (bf16[2,160,3,3,320]{4,1,3,2,0:T(8,128)(2,1)S(1)}, bf16[2,160,3,3,320]{4,1,3,2,0:T(8,128)(2,1)}, u32[]{:S(2)}, u32[]{:S(2)}) collective-permute-start(bf16[2,160,3,3,320]{4,1,3,2,0:T(8,128)(2,1)S(1)} %bitcast.105), channel_id=1, source_target_pairs={{0,1},{1,0},{2,3},{3,2},{4,5},{5,4},{6,7},{7,6},{8,9},{9,8},{10,11... | collective-permute-start | bytes 5529608 | tf_op jit(solution)/shard_map/ppermute | solution.py:68
  11.0 1.8 %copy-start.1 = (bf16[1,2,2,4,16,320]{5,3,4,2,1,0:T(4,128)(2,1)}, bf16[1,2,2,4,16,320]{5,3,4,2,1,0:T(4,128)(2,1)S(1)}, u32[]{:S(2)}) copy-start(bf16[1,2,2,4,16,320]{5,3,4,2,1,0:T(4,128)(2,1)S(1)} %copy.52) | copy-start | bytes 491524
  23.1 6.3 %collective-permute-start.1 = (bf16[2,4,16,320]{3,1,2,0:T(4,128)(2,1)}, bf16[2,4,16,320]{3,1,2,0:T(4,128)(2,1)S(1)}, u32[]{:S(2)}, u32[]{:S(2)}) collective-permute-start(bf16[2,4,16,320]{3,1,2,0:T(4,128)(2,1)} %fusion.86), channel_id=1, source_target_pairs={{0,4},{12,8},{1,5},{13,9},{2,6},{14,10},{3,7},{15,11},{16,20},{28,... | collective-permute-start | bytes 245768 | tf_op jit(solution)/shard_map/ppermute | solution.py:72
  24.7 11.7 %collective-permute-start = (f32[2,4,16,320]{3,1,2,0:T(4,128)S(1)}, f32[2,4,16,320]{3,1,2,0:T(4,128)S(1)}, u32[]{:S(2)}, u32[]{:S(2)}) collective-permute-start(f32[2,4,16,320]{3,1,2,0:T(4,128)S(1)} %bitcast.132), channel_id=1, source_target_pairs={{0,4},{12,8},{1,5},{13,9},{2,6},{14,10},{3,7},{15,11},{16,20},{28,... | collective-permute-start | bytes 491528 | tf_op jit(solution)/shard_map/ppermute | solution.py:72
  29.6 3.6 %copy-start.5 = (pred[16,3]{0,1:T(4,128)(4,1)S(1)}, pred[16,3]{0,1:T(4,128)(4,1)}, u32[]{:S(2)}) copy-start(pred[16,3]{0,1:T(4,128)(4,1)} %constant.64) | copy-start | bytes 148
  33.3 2.0 %copy-start = (bf16[2,320,3,3,320]{4,1,3,2,0:T(8,128)(2,1)}, bf16[2,320,3,3,320]{4,1,3,2,0:T(8,128)(2,1)S(1)}, u32[]{:S(2)}) copy-start(bf16[2,320,3,3,320]{4,1,3,2,0:T(8,128)(2,1)S(1)} %maximum_select_fusion) | copy-start | bytes 11059204
  35.3 1.2 %copy-start.2 = (bf16[1,2,2,4,16,320]{5,3,4,2,1,0:T(4,128)(2,1)S(1)}, bf16[1,2,2,4,16,320]{5,3,4,2,1,0:T(4,128)(2,1)}, u32[]{:S(2)}) copy-start(bf16[1,2,2,4,16,320]{5,3,4,2,1,0:T(4,128)(2,1)} %copy-done.1) | copy-start | bytes 491524
  44.1 3.5 %collective-permute-start.3 = (bf16[2,4,16,640]{3,1,2,0:T(4,128)(2,1)S(1)}, bf16[2,4,16,640]{3,1,2,0:T(4,128)(2,1)S(1)}, u32[]{:S(2)}, u32[]{:S(2)}) collective-permute-start(bf16[2,4,16,640]{3,1,2,0:T(4,128)(2,1)S(1)} %maximum_select_fusion.1), channel_id=1, source_target_pairs={{4,0},{6,2},{8,12},{10,14},{5,1},{7,3},{9,13},{11,15},{20,16},{22,... | collective-permute-start | bytes 491528 | tf_op jit(solution)/shard_map/ppermute | solution.py:165
  45.4 5.5 %collective-permute-start.4 = (bf16[2,4,16,640]{3,1,2,0:T(4,128)(2,1)S(1)}, bf16[2,4,16,640]{3,1,2,0:T(4,128)(2,1)S(1)}, u32[]{:S(2)}, u32[]{:S(2)}) collective-permute-start(bf16[2,4,16,640]{3,1,2,0:T(4,128)(2,1)S(1)} %maximum_select_fusion.1), channel_id=1, source_target_pairs={{6,0},{4,2},{10,12},{8,14},{7,1},{5,3},{11,13},{9,15},{22,16},{20,... | collective-permute-start | bytes 491528 | tf_op jit(solution)/shard_map/ppermute | solution.py:165
  47.8 6.1 %collective-permute-start.5 = (bf16[2,4,16,640]{3,1,2,0:T(4,128)(2,1)S(1)}, bf16[2,4,16,640]{3,1,2,0:T(4,128)(2,1)S(1)}, u32[]{:S(2)}, u32[]{:S(2)}) collective-permute-start(bf16[2,4,16,640]{3,1,2,0:T(4,128)(2,1)S(1)} %get-tuple-element.8), channel_id=1, source_target_pairs={{6,4},{4,6},{10,8},{8,10},{7,5},{5,7},{11,9},{9,11},{22,20},{20,22... | collective-permute-start | bytes 491528 | tf_op jit(solution)/shard_map/ppermute | solution.py:178

commit v13 on v8

--- a/solution.py
+++ b/solution.py
@@ -94,10 +94,10 @@
     x0 = take(samples, mine)
     a0 = take(act_all, mine)
     seed = take(grads, mine)
+    other, h1 = lax.optimization_barrier((other, h1))
     h1_r = up(0, h1)
     d_last_r = up(0, d_last)
 
-    other, _ = lax.optimization_barrier((other, h1))
     full = jnp.where(lane == 0, jnp.concatenate([own, other], 1),
                      jnp.concatenate([other, own], 1))
     w_enc, w_dec = full[0], full[1]

time: 65.7 us -> 67.7 us (1.030)
  other arithmetic: 7.93 us -> 9.83 us
  waiting for transfers between devices: 6.79 us -> 5.35 us
  local copies, waits for them, and re-layouts: 22.1 us -> 22.8 us
  starting transfers between devices: 7.91 us -> 8.59 us
    ppermute x2, waiting for transfers between devices: 1.62 us -> 0.01 us  [up(): return lax.ppermute(v, 'pipe', pairs)]
    convert_element_type x4, other arithmetic: 0.43 us -> 1.36 us  [bf16(): return v.astype(jnp.bfloat16)]
    select_n x1, other arithmetic: 0.19 us -> 1.12 us  [local(): jnp.where(lower, c0, a_last)]
    concatenate x1, local copies, waits for them, and re-layouts: 0.16 us -> 0.96 us  [local(): jnp.concatenate([f32(h1_half), d_part], -1)]
    dynamic_slice x1, other arithmetic: 0.03 us -> 0.72 us  [take(): return lax.dynamic_slice_in_dim(v, at, per_lane, 0)]
    ppermute x2, starting transfers between devices: 6.1 us -> 6.78 us  [up(): return lax.ppermute(v, 'pipe', pairs)]
  transfers between devices with their start and end apart: 4 -> 4, of which waited for: 2 -> 1; matrix products, arithmetic and copies ran while one was open for 23% -> 24% of each run, Pallas kernels for 0% -> 0%
where the time goes in v13:
time: 67.7 us; the launch traced here: 67.4 us
  local copies, waits for them, and re-layouts  22.8 us (34%)
  blocking collectives  10.9 us (16%)
  other arithmetic  9.83 us (15%)
  matrix products  9.34 us (14%)
  starting transfers between devices  8.59 us (13%)
  waiting for transfers between devices  5.35 us (8%)
    all_gather x1, blocking collectives, local(): every = lax.all_gather(both, ('dp', 'mp'), axis=0, tiled=True)  8.11 us
    ppermute x2, starting transfers between devices, up(): return lax.ppermute(v, 'pipe', pairs)  6.78 us
    conv_general_dilated x3, matrix products, conv_t(): lax.conv_general_dilated(flipped, weight, (1, 1), ((1, 1), (1, 1)), dimen...  5.55 us
    ppermute x1, waiting for transfers between devices, local(): lax.ppermute(jnp.where(lower, c0, a_last), 'pipe', [(1, 0), (pipe_size -...  5.35 us
    reshape x1, local copies, waits for them, and re-layouts, local(): return grad.reshape(1, -1)  4.57 us
    another operation x1, local copies, waits for them, and re-layouts, local(): section_weight[0].reshape(2, chan_half, 9, channels).transpose(0, 2, 1, 3)  4.5 us
    select_n x1, other arithmetic, local(): jnp.where(lane == 0, jnp.concatenate([own, other], 1), jnp.concatenate([o...  3.6 us
    unnamed x21, local copies, waits for them, and re-layouts  3.4 us
  transfers between devices with their start and end apart: 4, of which 1 were waited for; matrix products, arithmetic and copies ran while one was open for 24% of the time, Pallas kernels for 0%

profile of v13, /device:TPU:0, one launch (start us, length us, event | category | flops | bytes accessed | tf_op | source)
XLA Modules:
  0.0 67.4 jit_solution(9693250350917935303)
XLA Ops:
  0.0 2.7 %reshape.83 = bf16[921600]{0:T(1024)(128)(2,1)S(1)} reshape(bf16[1,2,460800]{2,1,0:T(2,128)(2,1)} %param.4) | data formatting | bytes 3686400
  2.7 4.5 %reshape_squeeze.3 = bf16[2,160,9,320]{3,2,1,0:T(8,128)(2,1)} reshape(bf16[921600]{0:T(1024)(128)(2,1)S(1)} %reshape.83) | data formatting | bytes 3686400 | tf_op jit(solution)/shard_map/reshape;squeeze | solution.py:65
  7.2 2.7 %copy.76 = bf16[2,9,160,320]{3,2,1,0:T(8,128)(2,1)S(1)} copy(bf16[2,9,160,320]{3,1,2,0:T(8,128)(2,1)} %bitcast.121) | data formatting | bytes 3686400 | tf_op jit(solution)/shard_map/transpose | solution.py:65
  9.8 0.5 collective-permute-start
  10.4 0.1 fusion.20
  10.5 0.2 copy.112
  10.9 0.2 fusion.10
  11.1 0.9 %convolution_select_fusion.1 = f32[4,32,3,160]{3,1,2,0:T(8,128)S(1)} fusion(bf16[2,160,3,3,320]{4,1,3,2,0:T(8,128)(2,1)S(1)} %bitcast.123, bf16[4,4,8,5,320]{4,1,3,2,0:T(4,128)(2,1)S(1)} %fusion.10, pred[32,3]{0,1:T(4,128)(4,1)S(1)} %copy-done.5), kind=kOutput, calls=%fused_computation.8 | convolution fusion | flops 294973440 | bytes 1843712 | tf_op jit(solution)/shard_map/conv_general_dilated | solution.py:13
  12.0 0.3 copy.79
  12.5 0.1 rev.22
  12.9 0.2 copy.84
  13.1 0.2 fusion.23
  13.3 0.8 %convolution_select_fusion = f32[4,32,3,320]{3,1,2,0:T(8,128)S(1)} fusion(bf16[2,160,3,3,320]{4,1,3,2,0:T(8,128)(2,1)S(1)} %bitcast.124, bf16[4,4,8,5,160]{4,1,3,2,0:T(4,128)(2,1)S(1)} %fusion.23, pred[32,3]{0,1:T(4,128)(4,1)S(1)} %copy-done.5), kind=kOutput, calls=%fused_computation.7 | convolution fusion | flops 295034880 | bytes 1925632 | tf_op jit(solution)/shard_map/conv_general_dilated | solution.py:22
  14.1 0.4 copy.83
  14.5 0.6 rev.23
  15.1 0.3 pad_maximum_fusion
  15.4 1.0 %copy.85 = f32[4,4,16,480]{3,2,1,0:T(8,128)} copy(f32[4,4,16,480]{3,1,2,0:T(4,128)S(1)} %pad_maximum_fusion) | data formatting | bytes 983040 | tf_op jit(solution)/shard_map/concatenate | solution.py:91
  16.3 2.8 %all-gather = f32[8,4,16,480]{3,2,1,0:T(8,128)S(1)} all-gather(f32[4,4,16,480]{3,2,1,0:T(8,128)} %copy.85), channel_id=2, replica_groups=mesh['groups'=2,'pipe'=4,'dp'=2,'mp'=2] {'mp'}, dimensions={0}, use_global_device_ids=true | all-gather | bytes 1474560 | tf_op jit(solution)/shard_map/all_gather | solution.py:91
  19.1 0.3 fusion.79
  19.4 0.7 %fusion.62 = f32[2,4,16,320]{3,2,1,0:T(8,128)} fusion(f32[1,4,4,16,320]{4,3,2,1,0:T(8,128)S(1)} %get-tuple-element.12, s32[]{:T(128)S(6)} %select_n.52, f32[1,4,4,16,320]{4,3,2,1,0:T(8,128)S(1)} %get-tuple-element.11), kind=kLoop, calls=%fused_computation.85 | loop fusion | flops 40960 | bytes 491524 | tf_op jit(solution)/shard_map/dynamic_slice | solution.py:79
  20.1 5.3 %collective-permute-start.2 = (f32[2,4,16,320]{3,2,1,0:T(8,128)}, f32[2,4,16,320]{3,2,1,0:T(8,128)}, u32[]{:S(2)}, u32[]{:S(2)}) collective-permute-start(f32[2,4,16,320]{3,2,1,0:T(8,128)} %fusion.62), channel_id=1, source_target_pairs={{0,4},{12,8},{1,5},{13,9},{2,6},{14,10},{3,7},{15,11},{16,20},{28,... | collective-permute-start | bytes 491528 | tf_op jit(solution)/shard_map/ppermute | solution.py:72
  25.4 0.9 %convert.8 = bf16[2,4,4,16,480]{4,3,2,1,0:T(8,128)(2,1)} convert(f32[2,4,4,16,480]{4,3,2,1,0:T(8,128)S(1)} %bitcast.127) | non-fusion elementwise | flops 245760 | bytes 1474560 | tf_op jit(solution)/shard_map/convert.5
  26.3 1.0 %slice_bitcast_fusion.19 = (bf16[4,4,16,160]{3,2,1,0:T(8,128)(2,1)S(1)}, bf16[4,4,16,160]{3,2,1,0:T(8,128)(2,1)S(1)}) fusion(bf16[2,4,4,16,480]{4,3,2,1,0:T(8,128)(2,1)} %convert.8), kind=kLoop, calls=%fused_computation.108 | loop fusion | bytes 327680 | tf_op jit(solution)/shard_map/squeeze | solution.py:92
  27.4 1.5 %collective-permute-start.1 = (bf16[2,4,16,320]{3,2,1,0:T(8,128)(2,1)S(1)}, bf16[2,4,16,320]{3,2,1,0:T(8,128)(2,1)S(1)}, u32[]{:S(2)}, u32[]{:S(2)}) collective-permute-start(bf16[2,4,16,320]{3,2,1,0:T(8,128)(2,1)S(1)} %fusion.73), channel_id=1, source_target_pairs={{0,4},{12,8},{1,5},{13,9},{2,6},{14,10},{3,7},{15,11},{16,20},{28,... | collective-permute-start | bytes 245768 | tf_op jit(solution)/shard_map/ppermute | solution.py:72
  28.9 3.6 %maximum_select_fusion = bf16[2,320,3,3,320]{4,1,3,2,0:T(8,128)(2,1)S(1)} fusion(bf16[2,160,3,3,320]{4,1,3,2,0:T(8,128)(2,1)} %collective-permute-done, bf16[2,160,3,3,320]{4,1,3,2,0:T(8,128)(2,1)S(1)} %bitcast.125, pred[]{:T(512)S(6)} %eq.3), kind=kLoop, calls=%fused_computation | loop fusion | flops 16588800 | bytes 7372801 | tf_op jit(solution)/shard_map/jit(_where)/select_n | solution.py:101
  32.9 0.2 fusion.29
  33.1 1.0 %fusion.6 = f32[4,16,3,320]{3,1,2,0:T(8,128)S(1)} fusion(bf16[2,320,3,3,320]{4,1,3,2,0:T(8,128)(2,1)S(1)} %maximum_select_fusion, bf16[4,2,8,5,320]{4,1,3,2,0:T(2,128)(2,1)S(1)} %fusion.29, pred[16,3]{0,1:T(4,128)(4,1)S(1)} %copy-done.4), kind=kOutput, calls=%fused_computation.11 | convolution fusion | flops 294973440 | bytes 2703872 | tf_op jit(solution)/shard_map/conv_general_dilated | solution.py:13
  34.1 0.1 copy.88
  34.7 0.2 fusion.30
  35.0 1.0 %fusion.4 = f32[4,16,3,320]{3,1,2,0:T(8,128)S(1)} fusion(bf16[2,320,3,3,320]{4,1,3,2,0:T(8,128)(2,1)S(1)} %maximum_select_fusion, bf16[4,2,8,5,320]{4,1,3,2,0:T(2,128)(2,1)S(1)} %fusion.30, pred[16,3]{0,1:T(4,128)(4,1)S(1)} %copy-done.4), kind=kOutput, calls=%fused_computation.9 | convolution fusion | flops 294973440 | bytes 2703872 | tf_op jit(solution)/shard_map/conv_general_dilated | solution.py:13
  36.0 0.1 copy.92
  36.2 1.0 %add_convert_fusion.3 = bf16[2,4,16,320]{3,2,1,0:T(8,128)(2,1)S(1)} fusion(bf16[4,4,16,320]{3,2,1,0:T(8,128)(2,1)S(1)} %bitcast.153, s32[]{:T(128)S(6)} %select_n.52, f32[2,4,16,320]{3,2,1,0:T(8,128)} %collective-permute-done.2, bf16[2,4,16,320]{3,2,1,0:T(8,128)(2,1)S(1)} %collective-permute-done.1, f32[4,2,16,320]{3,0,2,1:T(4,128)S(1)} %slice.65, ...), kind=kLoop, calls=%fused_computation.103 | loop fusion | flops 696320 | bytes 655364 | tf_op jit(solution)/shard_map/convert_element_type | solution.py:43
  37.2 0.1 rev.24
  37.7 0.2 fusion.31
  37.9 2.4 %fusion.5 = f32[4,16,3,320]{3,1,2,0:T(8,128)S(1)} fusion(bf16[2,320,3,3,320]{4,1,3,2,0:T(8,128)(2,1)} %copy-done, bf16[4,2,8,5,320]{4,1,3,2,0:T(2,128)(2,1)S(1)} %fusion.31, pred[16,3]{0,1:T(4,128)(4,1)S(1)} %copy-done.4), kind=kOutput, calls=%fused_computation.10 | convolution fusion | flops 294973440 | bytes 2662448 | tf_op jit(solution)/shard_map/conv_general_dilated | solution.py:22
  40.3 0.1 copy.96
  40.7 0.1 rev.26
  41.1 0.2 fusion.32
  41.4 2.4 %fusion.7 = f32[4,16,3,320]{3,1,2,0:T(8,128)S(1)} fusion(bf16[2,320,3,3,320]{4,1,3,2,0:T(8,128)(2,1)} %copy-done, bf16[4,2,8,5,320]{4,1,3,2,0:T(2,128)(2,1)S(1)} %fusion.32, pred[16,3]{0,1:T(4,128)(4,1)S(1)} %copy-done.4), kind=kOutput, calls=%fused_computation.12 | convolution fusion | flops 294973440 | bytes 2662448 | tf_op jit(solution)/shard_map/conv_general_dilated | solution.py:22
  44.0 1.1 %fusion.64 = bf16[2,4,16,320]{3,2,1,0:T(8,128)(2,1)S(1)} fusion(bf16[2,4,16,320]{3,2,1,0:T(8,128)(2,1)S(1)} %collective-permute-done.1, f32[2,4,16,320]{3,2,1,0:T(8,128)S(1)} %rev.27, bf16[2,4,16,320]{3,2,1,0:T(8,128)(2,1)S(1)} %add_convert_fusion.1, pred[]{:T(512)S(6)} %lt.10, f32[4,2,16,320]{3,0,2,1:T(4,128)S(1)} %slice.65, ...), kind=kLoop, calls=%fused_computation.110 | loop fusion | flops 1351680 | bytes 819201 | tf_op jit(solution)/shard_map/jit(_where)/select_n | solution.py:159
  45.1 1.3 %collective-permute-start.3 = (bf16[2,4,16,320]{3,2,1,0:T(8,128)(2,1)S(1)}, bf16[2,4,16,320]{3,2,1,0:T(8,128)(2,1)S(1)}, u32[]{:S(2)}, u32[]{:S(2)}) collective-permute-start(bf16[2,4,16,320]{3,2,1,0:T(8,128)(2,1)S(1)} %fusion.64), channel_id=1, source_target_pairs={{4,0},{8,12},{5,1},{9,13},{6,2},{10,14},{7,3},{11,15},{20,16},{24,... | collective-permute-start | bytes 245768 | tf_op jit(solution)/shard_map/ppermute | solution.py:159
  46.5 5.3 %collective-permute-done.3 = bf16[2,4,16,320]{3,2,1,0:T(8,128)(2,1)S(1)} collective-permute-done((bf16[2,4,16,320]{3,2,1,0:T(8,128)(2,1)S(1)}, bf16[2,4,16,320]{3,2,1,0:T(8,128)(2,1)S(1)}, u32[]{:S(2)}, u32[]{:S(2)}) %collective-permute-start.3) | collective-permute-done | bytes 81952 | tf_op jit(solution)/shard_map/ppermute | solution.py:159
  51.8 0.2 fusion.71
  52.1 8.1 %all_gather.11 = bf16[8,4,16,640]{3,2,1,0:T(8,128)(2,1)S(1)} all-gather(bf16[2,4,16,640]{3,2,1,0:T(8,128)(2,1)S(1)} %pad_maximum_fusion.1), channel_id=1, replica_groups=mesh['groups'=2,'pipe'=4,'dp'=2,'mp'=2] {'dp','mp'}, dimensions={0}, use_global_device_ids=true | all-gather | bytes 819200 | tf_op jit(solution)/shard_map/all_gather | solution.py:167
  60.3 0.2 constant_dynamic-slice_fusion
  60.4 0.9 %fusion.21 = f32[160,3,3,320]{3,0,2,1:T(8,128)S(1)} fusion(bf16[8,4,16,320]{3,2,1,0:T(8,128)(2,1)S(1)} %slice.70, bf16[8,4,16,160]{3,2,1,0:T(8,128)(2,1)S(1)} %constant_dynamic-slice_fusion), kind=kOutput, calls=%fused_computation.35 | convolution fusion | flops 376832000 | bytes 2334720 | tf_op jit(solution)/shard_map/conv_general_dilated | solution.py:31
  61.3 1.5 %copy.104 = f32[160,3,3,320]{3,2,1,0:T(4,128)S(1)} copy(f32[160,3,3,320]{3,0,2,1:T(8,128)S(1)} %fusion.21) | data formatting | bytes 3686400 | tf_op jit(solution)/shard_map/conv_general_dilated | solution.py:31
  62.8 4.6 %reshape.21 = f32[1,460800]{1,0:T(1,128)} reshape(f32[160,3,3,320]{3,2,1,0:T(4,128)S(1)} %copy.104) | data formatting | bytes 3686400 | tf_op jit(solution)/shard_map/reshape | solution.py:171
  (53 shorter events, 2.8 us)
Async XLA Ops:
  7.2 3.2 %copy-start.1 = (bf16[1,2,2,4,16,320]{5,4,3,2,1,0:T(8,128)(2,1)S(1)}, bf16[1,2,2,4,16,320]{5,4,3,2,1,0:T(8,128)(2,1)}, u32[]{:S(2)}) copy-start(bf16[1,2,2,4,16,320]{5,4,3,2,1,0:T(8,128)(2,1)} %param.3) | copy-start | bytes 491524
  9.8 1.3 %copy-start.5 = (pred[32,3]{0,1:T(4,128)(4,1)S(1)}, pred[32,3]{0,1:T(4,128)(4,1)}, u32[]{:S(2)}) copy-start(pred[32,3]{0,1:T(4,128)(4,1)} %constant.60) | copy-start | bytes 292
  9.8 17.5 %collective-permute-start = (bf16[2,160,3,3,320]{4,1,3,2,0:T(8,128)(2,1)S(1)}, bf16[2,160,3,3,320]{4,1,3,2,0:T(8,128)(2,1)}, u32[]{:S(2)}, u32[]{:S(2)}) collective-permute-start(bf16[2,160,3,3,320]{4,1,3,2,0:T(8,128)(2,1)S(1)} %bitcast.122), channel_id=1, source_target_pairs={{0,1},{1,0},{2,3},{3,2},{4,5},{5,4},{6,7},{7,6},{8,9},{9,8},{10,11... | collective-permute-start | bytes 5529608 | tf_op jit(solution)/shard_map/ppermute | solution.py:68
  11.1 1.3 %copy-start.2 = (bf16[1,2,2,4,16,320]{5,4,3,2,1,0:T(8,128)(2,1)S(1)}, bf16[1,2,2,4,16,320]{5,4,3,2,1,0:T(8,128)(2,1)}, u32[]{:S(2)}) copy-start(bf16[1,2,2,4,16,320]{5,4,3,2,1,0:T(8,128)(2,1)} %param.5) | copy-start | bytes 491524
  20.1 16.1 %collective-permute-start.2 = (f32[2,4,16,320]{3,2,1,0:T(8,128)}, f32[2,4,16,320]{3,2,1,0:T(8,128)}, u32[]{:S(2)}, u32[]{:S(2)}) collective-permute-start(f32[2,4,16,320]{3,2,1,0:T(8,128)} %fusion.62), channel_id=1, source_target_pairs={{0,4},{12,8},{1,5},{13,9},{2,6},{14,10},{3,7},{15,11},{16,20},{28,... | collective-permute-start | bytes 491528 | tf_op jit(solution)/shard_map/ppermute | solution.py:72
  27.4 5.7 %copy-start.4 = (pred[16,3]{0,1:T(4,128)(4,1)S(1)}, pred[16,3]{0,1:T(4,128)(4,1)}, u32[]{:S(2)}) copy-start(pred[16,3]{0,1:T(4,128)(4,1)} %constant.62) | copy-start | bytes 148
  27.4 5.1 %collective-permute-start.1 = (bf16[2,4,16,320]{3,2,1,0:T(8,128)(2,1)S(1)}, bf16[2,4,16,320]{3,2,1,0:T(8,128)(2,1)S(1)}, u32[]{:S(2)}, u32[]{:S(2)}) collective-permute-start(bf16[2,4,16,320]{3,2,1,0:T(8,128)(2,1)S(1)} %fusion.73), channel_id=1, source_target_pairs={{0,4},{12,8},{1,5},{13,9},{2,6},{14,10},{3,7},{15,11},{16,20},{28,... | collective-permute-start | bytes 245768 | tf_op jit(solution)/shard_map/ppermute | solution.py:72
  32.5 2.5 %copy-start = (bf16[2,320,3,3,320]{4,1,3,2,0:T(8,128)(2,1)}, bf16[2,320,3,3,320]{4,1,3,2,0:T(8,128)(2,1)S(1)}, u32[]{:S(2)}) copy-start(bf16[2,320,3,3,320]{4,1,3,2,0:T(8,128)(2,1)S(1)} %maximum_select_fusion) | copy-start | bytes 11059204
  35.0 1.2 %copy-start.3 = (bf16[1,2,2,4,16,320]{5,4,3,2,1,0:T(8,128)(2,1)S(1)}, bf16[1,2,2,4,16,320]{5,4,3,2,1,0:T(8,128)(2,1)}, u32[]{:S(2)}) copy-start(bf16[1,2,2,4,16,320]{5,4,3,2,1,0:T(8,128)(2,1)} %param.5) | copy-start | bytes 491524
  45.1 6.7 %collective-permute-start.3 = (bf16[2,4,16,320]{3,2,1,0:T(8,128)(2,1)S(1)}, bf16[2,4,16,320]{3,2,1,0:T(8,128)(2,1)S(1)}, u32[]{:S(2)}, u32[]{:S(2)}) collective-permute-start(bf16[2,4,16,320]{3,2,1,0:T(8,128)(2,1)S(1)} %fusion.64), channel_id=1, source_target_pairs={{4,0},{8,12},{5,1},{9,13},{6,2},{10,14},{7,3},{11,15},{20,16},{24,... | collective-permute-start | bytes 245768 | tf_op jit(solution)/shard_map/ppermute | solution.py:159

commit v14 on v8

--- a/solution.py
+++ b/solution.py
@@ -164,7 +164,7 @@
     act_sel = jnp.where(lower, acts_lo[stage], acts_up[stage])
     cot_sel = jnp.where(lower, cots_lo[stage], cots_up[stage])
     both = jnp.concatenate([act_sel, cot_sel], axis=-1)
-    every = lax.all_gather(both, ("dp", "mp"), axis=0, tiled=True)
+    every = lax.all_gather(both, ("mp", "dp"), axis=0, tiled=True)
     act_all = every[..., :channels]
     cot_all = lax.dynamic_slice_in_dim(every, channels + low, chan_half, 3)
     grad = weight_grad(act_all, cot_all)

time: 65.7 us -> 72.1 us (1.097)
  blocking collectives: 10.7 us -> 17.1 us
    all_gather x1, blocking collectives: 8.11 us -> 14.5 us  [local(): every = lax.all_gather(both, ('mp', 'dp'), axis=0, tiled=True)]
  transfers between devices with their start and end apart: 4 -> 4, of which waited for: 2 -> 2; matrix products, arithmetic and copies ran while one was open for 23% -> 21% of each run, Pallas kernels for 0% -> 0%
where the time goes in v14:
time: 72.1 us; the launch traced here: 71.8 us
  local copies, waits for them, and re-layouts  22.1 us (31%)
  blocking collectives  17.1 us (24%)
  matrix products  9.33 us (13%)
  other arithmetic  7.93 us (11%)
  starting transfers between devices  7.91 us (11%)
  waiting for transfers between devices  6.79 us (9%)
    all_gather x1, blocking collectives, local(): every = lax.all_gather(both, ('mp', 'dp'), axis=0, tiled=True)  14.5 us
    ppermute x2, starting transfers between devices, up(): return lax.ppermute(v, 'pipe', pairs)  6.1 us
    conv_general_dilated x3, matrix products, conv_t(): lax.conv_general_dilated(flipped, weight, (1, 1), ((1, 1), (1, 1)), dimen...  5.55 us
    ppermute x1, waiting for transfers between devices, local(): lax.ppermute(jnp.where(lower, c0, a_last), 'pipe', [(1, 0), (pipe_size -...  5.17 us
    reshape x1, local copies, waits for them, and re-layouts, local(): return grad.reshape(1, -1)  4.57 us
    another operation x1, local copies, waits for them, and re-layouts, local(): section_weight[0].reshape(2, chan_half, 9, channels).transpose(0, 2, 1, 3)  4.5 us
    select_n x1, other arithmetic, local(): jnp.where(lane == 0, jnp.concatenate([own, other], 1), jnp.concatenate([o...  3.6 us
    unnamed x21, local copies, waits for them, and re-layouts  3.55 us
  transfers between devices with their start and end apart: 4, of which 2 were waited for; matrix products, arithmetic and copies ran while one was open for 21% of the time, Pallas kernels for 0%

profile of v14, /device:TPU:0, one launch (start us, length us, event | category | flops | bytes accessed | tf_op | source)
XLA Modules:
  0.0 71.8 jit_solution(10189448626070482895)
XLA Ops:
  0.0 2.7 %reshape.83 = bf16[921600]{0:T(1024)(128)(2,1)S(1)} reshape(bf16[1,2,460800]{2,1,0:T(2,128)(2,1)} %param.4) | data formatting | bytes 3686400
  2.7 4.5 %reshape_squeeze.3 = bf16[2,160,9,320]{3,2,1,0:T(8,128)(2,1)} reshape(bf16[921600]{0:T(1024)(128)(2,1)S(1)} %reshape.83) | data formatting | bytes 3686400 | tf_op jit(solution)/shard_map/reshape;squeeze | solution.py:65
  7.2 2.7 %copy.78 = bf16[2,9,160,320]{3,2,1,0:T(8,128)(2,1)S(1)} copy(bf16[2,9,160,320]{3,1,2,0:T(8,128)(2,1)} %bitcast.121) | data formatting | bytes 3686400 | tf_op jit(solution)/shard_map/transpose | solution.py:65
  9.8 0.5 collective-permute-start.2
  10.5 0.1 rev.22
  10.9 0.2 fusion.23
  11.1 0.1 fusion.20
  11.2 0.2 copy.112
  11.5 0.2 fusion.10
  11.8 0.9 %convolution_select_fusion.1 = f32[4,32,3,160]{3,1,2,0:T(8,128)S(1)} fusion(bf16[2,160,3,3,320]{4,1,3,2,0:T(8,128)(2,1)S(1)} %bitcast.123, bf16[4,4,8,5,320]{4,1,3,2,0:T(4,128)(2,1)S(1)} %fusion.10, pred[32,3]{0,1:T(4,128)(4,1)S(1)} %copy-done.5), kind=kOutput, calls=%fused_computation.8 | convolution fusion | flops 294973440 | bytes 1843712 | tf_op jit(solution)/shard_map/conv_general_dilated | solution.py:13
  12.7 0.3 copy.79
  13.1 0.2 copy.84
  13.3 0.8 %convolution_select_fusion = f32[4,32,3,320]{3,1,2,0:T(8,128)S(1)} fusion(bf16[2,160,3,3,320]{4,1,3,2,0:T(8,128)(2,1)S(1)} %bitcast.124, bf16[4,4,8,5,160]{4,1,3,2,0:T(4,128)(2,1)S(1)} %fusion.23, pred[32,3]{0,1:T(4,128)(4,1)S(1)} %copy-done.5), kind=kOutput, calls=%fused_computation.7 | convolution fusion | flops 295034880 | bytes 1925632 | tf_op jit(solution)/shard_map/conv_general_dilated | solution.py:22
  14.1 0.4 copy.83
  14.5 0.6 rev.23
  15.1 0.3 pad_maximum_fusion
  15.4 0.2 copy.85
  15.6 2.6 %all-gather = f32[8,4,16,480]{3,2,1,0:T(8,128)S(1)} all-gather(f32[4,4,16,480]{3,2,1,0:T(8,128)S(1)} %copy.85), channel_id=2, replica_groups=mesh['groups'=2,'pipe'=4,'dp'=2,'mp'=2] {'mp'}, dimensions={0}, use_global_device_ids=true | all-gather | bytes 1474560 | tf_op jit(solution)/shard_map/all_gather | solution.py:91
  18.1 0.9 %convert.8 = bf16[2,4,4,16,480]{4,3,2,1,0:T(8,128)(2,1)} convert(f32[2,4,4,16,480]{4,3,2,1,0:T(8,128)S(1)} %bitcast.126) | non-fusion elementwise | flops 245760 | bytes 1474560 | tf_op jit(solution)/shard_map/convert.5
  19.0 1.0 %slice_bitcast_fusion.19 = (bf16[4,4,16,160]{3,2,1,0:T(8,128)(2,1)S(1)}, bf16[4,4,16,160]{3,2,1,0:T(8,128)(2,1)S(1)}) fusion(bf16[2,4,4,16,480]{4,3,2,1,0:T(8,128)(2,1)} %convert.8), kind=kLoop, calls=%fused_computation.108 | loop fusion | bytes 327680 | tf_op jit(solution)/shard_map/squeeze | solution.py:92
  20.0 0.7 %fusion.73 = bf16[2,4,16,320]{3,2,1,0:T(8,128)(2,1)} fusion(s32[]{:T(128)S(6)} %select_n.52, bf16[4,4,16,160]{3,2,1,0:T(8,128)(2,1)S(1)} %get-tuple-element.12, bf16[4,4,16,160]{3,2,1,0:T(8,128)(2,1)S(1)} %get-tuple-element.11), kind=kLoop, calls=%fused_computation.119 | loop fusion | flops 163840 | bytes 245764 | tf_op jit(solution)/shard_map/concatenate | solution.py:92
  20.7 4.6 %collective-permute-start = (bf16[2,4,16,320]{3,2,1,0:T(8,128)(2,1)}, bf16[2,4,16,320]{3,2,1,0:T(8,128)(2,1)S(1)}, u32[]{:S(2)}, u32[]{:S(2)}) collective-permute-start(bf16[2,4,16,320]{3,2,1,0:T(8,128)(2,1)} %fusion.73), channel_id=1, source_target_pairs={{0,4},{12,8},{1,5},{13,9},{2,6},{14,10},{3,7},{15,11},{16,20},{28,... | collective-permute-start | bytes 245768 | tf_op jit(solution)/shard_map/ppermute | solution.py:72
  25.3 0.3 fusion.79
  25.6 1.5 %collective-permute-start.1 = (f32[2,4,16,320]{3,2,1,0:T(8,128)S(1)}, f32[2,4,16,320]{3,2,1,0:T(8,128)S(1)}, u32[]{:S(2)}, u32[]{:S(2)}) collective-permute-start(f32[2,4,16,320]{3,2,1,0:T(8,128)S(1)} %fusion.62), channel_id=1, source_target_pairs={{0,4},{12,8},{1,5},{13,9},{2,6},{14,10},{3,7},{15,11},{16,20},{28,... | collective-permute-start | bytes 491528 | tf_op jit(solution)/shard_map/ppermute | solution.py:72
  27.2 1.6 %collective-permute-done = bf16[2,4,16,320]{3,2,1,0:T(8,128)(2,1)S(1)} collective-permute-done((bf16[2,4,16,320]{3,2,1,0:T(8,128)(2,1)}, bf16[2,4,16,320]{3,2,1,0:T(8,128)(2,1)S(1)}, u32[]{:S(2)}, u32[]{:S(2)}) %collective-permute-start) | collective-permute-done | bytes 81952 | tf_op jit(solution)/shard_map/ppermute | solution.py:72
  29.1 0.2 fusion.29
  29.4 3.6 %maximum_select_fusion = bf16[2,320,3,3,320]{4,1,3,2,0:T(8,128)(2,1)S(1)} fusion(bf16[2,160,3,3,320]{4,1,3,2,0:T(8,128)(2,1)} %collective-permute-done.2, bf16[2,160,3,3,320]{4,1,3,2,0:T(8,128)(2,1)S(1)} %bitcast.125, pred[]{:T(512)S(6)} %eq.3), kind=kLoop, calls=%fused_computation | loop fusion | flops 16588800 | bytes 7372801 | tf_op jit(solution)/shard_map/jit(_where)/select_n | solution.py:101
  33.0 1.0 %fusion.6 = f32[4,16,3,320]{3,1,2,0:T(8,128)S(1)} fusion(bf16[2,320,3,3,320]{4,1,3,2,0:T(8,128)(2,1)S(1)} %maximum_select_fusion, bf16[4,2,8,5,320]{4,1,3,2,0:T(2,128)(2,1)S(1)} %fusion.29, pred[16,3]{0,1:T(4,128)(4,1)S(1)} %copy-done.4), kind=kOutput, calls=%fused_computation.11 | convolution fusion | flops 294973440 | bytes 2703872 | tf_op jit(solution)/shard_map/conv_general_dilated | solution.py:13
  34.0 0.1 copy.88
  34.6 0.2 fusion.30
  34.9 0.2 copy-done
  35.0 1.0 %fusion.4 = f32[4,16,3,320]{3,1,2,0:T(8,128)S(1)} fusion(bf16[2,320,3,3,320]{4,1,3,2,0:T(8,128)(2,1)S(1)} %maximum_select_fusion, bf16[4,2,8,5,320]{4,1,3,2,0:T(2,128)(2,1)S(1)} %fusion.30, pred[16,3]{0,1:T(4,128)(4,1)S(1)} %copy-done.4), kind=kOutput, calls=%fused_computation.9 | convolution fusion | flops 294973440 | bytes 2703872 | tf_op jit(solution)/shard_map/conv_general_dilated | solution.py:13
  36.2 0.1 add_convert_fusion.3
  36.4 0.1 rev.24
  36.8 0.2 fusion.31
  37.0 2.4 %fusion.5 = f32[4,16,3,320]{3,1,2,0:T(8,128)S(1)} fusion(bf16[2,320,3,3,320]{4,1,3,2,0:T(8,128)(2,1)} %copy-done, bf16[4,2,8,5,320]{4,1,3,2,0:T(2,128)(2,1)S(1)} %fusion.31, pred[16,3]{0,1:T(4,128)(4,1)S(1)} %copy-done.4), kind=kOutput, calls=%fused_computation.10 | convolution fusion | flops 294973440 | bytes 2662448 | tf_op jit(solution)/shard_map/conv_general_dilated | solution.py:22
  39.8 0.1 rev.26
  40.3 0.2 fusion.32
  40.5 2.4 %fusion.7 = f32[4,16,3,320]{3,1,2,0:T(8,128)S(1)} fusion(bf16[2,320,3,3,320]{4,1,3,2,0:T(8,128)(2,1)} %copy-done, bf16[4,2,8,5,320]{4,1,3,2,0:T(2,128)(2,1)S(1)} %fusion.32, pred[16,3]{0,1:T(4,128)(4,1)S(1)} %copy-done.4), kind=kOutput, calls=%fused_computation.12 | convolution fusion | flops 294973440 | bytes 2662448 | tf_op jit(solution)/shard_map/conv_general_dilated | solution.py:22
  43.2 0.2 fusion.64
  43.4 1.3 %collective-permute-start.3 = (bf16[2,4,16,320]{3,2,1,0:T(8,128)(2,1)S(1)}, bf16[2,4,16,320]{3,2,1,0:T(8,128)(2,1)S(1)}, u32[]{:S(2)}, u32[]{:S(2)}) collective-permute-start(bf16[2,4,16,320]{3,2,1,0:T(8,128)(2,1)S(1)} %fusion.64), channel_id=1, source_target_pairs={{4,0},{8,12},{5,1},{9,13},{6,2},{10,14},{7,3},{11,15},{20,16},{24,... | collective-permute-start | bytes 245768 | tf_op jit(solution)/shard_map/ppermute | solution.py:159
  44.7 5.2 %collective-permute-done.3 = bf16[2,4,16,320]{3,2,1,0:T(8,128)(2,1)S(1)} collective-permute-done((bf16[2,4,16,320]{3,2,1,0:T(8,128)(2,1)S(1)}, bf16[2,4,16,320]{3,2,1,0:T(8,128)(2,1)S(1)}, u32[]{:S(2)}, u32[]{:S(2)}) %collective-permute-start.3) | collective-permute-done | bytes 81952 | tf_op jit(solution)/shard_map/ppermute | solution.py:159
  49.9 0.2 fusion.71
  50.1 14.5 %all_gather.11 = bf16[8,4,16,640]{3,2,1,0:T(8,128)(2,1)S(1)} all-gather(bf16[2,4,16,640]{3,2,1,0:T(8,128)(2,1)S(1)} %pad_maximum_fusion.1), channel_id=1, replica_groups=mesh['groups'=2,'pipe'=4,'dp'=2,'mp'=2] {'mp','dp'}, dimensions={0}, use_global_device_ids=true | all-gather | bytes 819200 | tf_op jit(solution)/shard_map/all_gather | solution.py:167
  64.7 0.2 constant_dynamic-slice_fusion
  64.9 0.9 %fusion.21 = f32[160,3,3,320]{3,0,2,1:T(8,128)S(1)} fusion(bf16[8,4,16,320]{3,2,1,0:T(8,128)(2,1)S(1)} %slice.70, bf16[8,4,16,160]{3,2,1,0:T(8,128)(2,1)S(1)} %constant_dynamic-slice_fusion), kind=kOutput, calls=%fused_computation.35 | convolution fusion | flops 376832000 | bytes 2334720 | tf_op jit(solution)/shard_map/conv_general_dilated | solution.py:31
  65.7 1.5 %copy.104 = f32[160,3,3,320]{3,2,1,0:T(4,128)S(1)} copy(f32[160,3,3,320]{3,0,2,1:T(8,128)S(1)} %fusion.21) | data formatting | bytes 3686400 | tf_op jit(solution)/shard_map/conv_general_dilated | solution.py:31
  67.3 4.6 %reshape.21 = f32[1,460800]{1,0:T(1,128)} reshape(f32[160,3,3,320]{3,2,1,0:T(4,128)S(1)} %copy.104) | data formatting | bytes 3686400 | tf_op jit(solution)/shard_map/reshape | solution.py:171
  (53 shorter events, 3.0 us)
Async XLA Ops:
  7.2 3.2 %copy-start.2 = (bf16[1,2,2,4,16,320]{5,4,3,2,1,0:T(8,128)(2,1)S(1)}, bf16[1,2,2,4,16,320]{5,4,3,2,1,0:T(8,128)(2,1)}, u32[]{:S(2)}) copy-start(bf16[1,2,2,4,16,320]{5,4,3,2,1,0:T(8,128)(2,1)} %param.5) | copy-start | bytes 491524
  7.2 3.9 %copy-start.1 = (bf16[1,2,2,4,16,320]{5,4,3,2,1,0:T(8,128)(2,1)S(1)}, bf16[1,2,2,4,16,320]{5,4,3,2,1,0:T(8,128)(2,1)}, u32[]{:S(2)}) copy-start(bf16[1,2,2,4,16,320]{5,4,3,2,1,0:T(8,128)(2,1)} %param.3) | copy-start | bytes 491524
  9.8 19.5 %collective-permute-start.2 = (bf16[2,160,3,3,320]{4,1,3,2,0:T(8,128)(2,1)S(1)}, bf16[2,160,3,3,320]{4,1,3,2,0:T(8,128)(2,1)}, u32[]{:S(2)}, u32[]{:S(2)}) collective-permute-start(bf16[2,160,3,3,320]{4,1,3,2,0:T(8,128)(2,1)S(1)} %bitcast.122), channel_id=1, source_target_pairs={{0,1},{1,0},{2,3},{3,2},{4,5},{5,4},{6,7},{7,6},{8,9},{9,8},{10,11... | collective-permute-start | bytes 5529608 | tf_op jit(solution)/shard_map/ppermute | solution.py:68
  10.5 1.3 %copy-start.5 = (pred[32,3]{0,1:T(4,128)(4,1)S(1)}, pred[32,3]{0,1:T(4,128)(4,1)}, u32[]{:S(2)}) copy-start(pred[32,3]{0,1:T(4,128)(4,1)} %constant.60) | copy-start | bytes 292
  20.7 8.1 %collective-permute-start = (bf16[2,4,16,320]{3,2,1,0:T(8,128)(2,1)}, bf16[2,4,16,320]{3,2,1,0:T(8,128)(2,1)S(1)}, u32[]{:S(2)}, u32[]{:S(2)}) collective-permute-start(bf16[2,4,16,320]{3,2,1,0:T(8,128)(2,1)} %fusion.73), channel_id=1, source_target_pairs={{0,4},{12,8},{1,5},{13,9},{2,6},{14,10},{3,7},{15,11},{16,20},{28,... | collective-permute-start | bytes 245768 | tf_op jit(solution)/shard_map/ppermute | solution.py:72
  25.6 10.6 %collective-permute-start.1 = (f32[2,4,16,320]{3,2,1,0:T(8,128)S(1)}, f32[2,4,16,320]{3,2,1,0:T(8,128)S(1)}, u32[]{:S(2)}, u32[]{:S(2)}) collective-permute-start(f32[2,4,16,320]{3,2,1,0:T(8,128)S(1)} %fusion.62), channel_id=1, source_target_pairs={{0,4},{12,8},{1,5},{13,9},{2,6},{14,10},{3,7},{15,11},{16,20},{28,... | collective-permute-start | bytes 491528 | tf_op jit(solution)/shard_map/ppermute | solution.py:72
  29.4 3.6 %copy-start.4 = (pred[16,3]{0,1:T(4,128)(4,1)S(1)}, pred[16,3]{0,1:T(4,128)(4,1)}, u32[]{:S(2)}) copy-start(pred[16,3]{0,1:T(4,128)(4,1)} %constant.62) | copy-start | bytes 148
  33.0 2.0 %copy-start = (bf16[2,320,3,3,320]{4,1,3,2,0:T(8,128)(2,1)}, bf16[2,320,3,3,320]{4,1,3,2,0:T(8,128)(2,1)S(1)}, u32[]{:S(2)}) copy-start(bf16[2,320,3,3,320]{4,1,3,2,0:T(8,128)(2,1)S(1)} %maximum_select_fusion) | copy-start | bytes 11059204
  35.0 1.2 %copy-start.3 = (bf16[1,2,2,4,16,320]{5,4,3,2,1,0:T(8,128)(2,1)S(1)}, bf16[1,2,2,4,16,320]{5,4,3,2,1,0:T(8,128)(2,1)}, u32[]{:S(2)}) copy-start(bf16[1,2,2,4,16,320]{5,4,3,2,1,0:T(8,128)(2,1)} %param.5) | copy-start | bytes 491524
  43.4 6.5 %collective-permute-start.3 = (bf16[2,4,16,320]{3,2,1,0:T(8,128)(2,1)S(1)}, bf16[2,4,16,320]{3,2,1,0:T(8,128)(2,1)S(1)}, u32[]{:S(2)}, u32[]{:S(2)}) collective-permute-start(bf16[2,4,16,320]{3,2,1,0:T(8,128)(2,1)S(1)} %fusion.64), channel_id=1, source_target_pairs={{4,0},{8,12},{5,1},{9,13},{6,2},{10,14},{7,3},{11,15},{20,16},{24,... | collective-permute-start | bytes 245768 | tf_op jit(solution)/shard_map/ppermute | solution.py:159

commit v15 on v8

--- a/solution.py
+++ b/solution.py
@@ -83,17 +83,14 @@
                          jnp.concatenate([second, first], -1))
 
     low = lane * chan_half
-    act_all = bf16(jax.nn.silu(f32(samples)))
-    own_in = lax.dynamic_slice_in_dim(samples, low, chan_half, 3)
-    h1_half = bf16(f32(own_in) + conv(act_all, own[0]))
-    seed_half = lax.dynamic_slice_in_dim(grads, low, chan_half, 3)
-    d_part = conv_t(seed_half, own[1])
-    parts = lax.all_gather(jnp.concatenate([f32(h1_half), d_part], -1), "mp", axis=0, tiled=False)
-    h1 = take(bf16(jnp.concatenate([parts[0, ..., :chan_half], parts[1, ..., :chan_half]], -1)), mine)
-    d_last = take(parts[0, ..., chan_half:] + parts[1, ..., chan_half:], mine)
+    high = (1 - lane) * chan_half
     x0 = take(samples, mine)
-    a0 = take(act_all, mine)
     seed = take(grads, mine)
+    a0 = bf16(jax.nn.silu(f32(x0)))
+    h1_own = conv(a0, own[0])
+    d_own = conv_t(lax.dynamic_slice_in_dim(seed, low, chan_half, 3), own[1])
+    h1 = bf16(f32(x0) + join(h1_own, conv(a0, other[0])))
+    d_last = d_own + conv_t(lax.dynamic_slice_in_dim(seed, high, chan_half, 3), other[1])
     h1_r = up(0, h1)
     d_last_r = up(0, d_last)
 

time: 65.7 us -> 62.3 us (0.948)
  matrix products: 9.33 us -> 12.3 us
  blocking collectives: 10.7 us -> 8.11 us
  other arithmetic: 7.93 us -> 5.84 us
  waiting for transfers between devices: 6.79 us -> 5.19 us
    all_gather x1 -> x0, blocking collectives: 2.56 us -> none  [local(): lax.all_gather(jnp.concatenate([f32(h1_half), d_part], -1), 'mp', axis=0,...]
    ppermute x2, waiting for transfers between devices: 1.62 us -> 0.01 us  [up(): return lax.ppermute(v, 'pipe', pairs)]
    conv_general_dilated x3 -> x4, matrix products: 5.55 us -> 7.05 us  [conv_t(): lax.conv_general_dilated(flipped, weight, (1, 1), ((1, 1), (1, 1)), dimen...]
    conv_general_dilated x3 -> x4, matrix products: 2.92 us -> 4.39 us  [conv(): lax.conv_general_dilated(act, weight, (1, 1), ((1, 1), (1, 1)), dimension...]
    conv_general_dilated x6 -> x0, other arithmetic: 1.28 us -> none  [the longest x3 0.67 us: conv(): lax.conv_general_dilated(act, weight, (1, 1), ((1, 1), (1, 1)), dimension...]
    concatenate x2 -> x0, other arithmetic: 1.01 us -> none  [the longest x1 0.74 us: local(): jnp.concatenate([parts[0, ..., :chan_half], parts[1, ..., :chan_half]], -1)]
    squeeze x1 -> x0, local copies, waits for them, and re-layouts: 0.98 us -> none  [local(): parts[1, ..., :chan_half]]
    another operation x2 -> x0, other arithmetic: 0.95 us -> none
  transfers between devices with their start and end apart: 4 -> 4, of which waited for: 2 -> 1; matrix products, arithmetic and copies ran while one was open for 23% -> 21% of each run, Pallas kernels for 0% -> 0%
where the time goes in v15:
time: 62.3 us; the launch traced here: 62 us
  local copies, waits for them, and re-layouts  22 us (35%)
  matrix products  12.3 us (20%)
  blocking collectives  8.11 us (13%)
  starting transfers between devices  7.97 us (13%)
  other arithmetic  5.84 us (9%)
  waiting for transfers between devices  5.19 us (8%)
    all_gather x1, blocking collectives, local(): every = lax.all_gather(both, ('dp', 'mp'), axis=0, tiled=True)  8.11 us
    conv_general_dilated x4, matrix products, conv_t(): lax.conv_general_dilated(flipped, weight, (1, 1), ((1, 1), (1, 1)), dimen...  7.05 us
    ppermute x2, starting transfers between devices, up(): return lax.ppermute(v, 'pipe', pairs)  6.16 us
    ppermute x1, waiting for transfers between devices, local(): lax.ppermute(jnp.where(lower, c0, a_last), 'pipe', [(1, 0), (pipe_size -...  5.18 us
    reshape x1, local copies, waits for them, and re-layouts, local(): return grad.reshape(1, -1)  4.57 us
    another operation x1, local copies, waits for them, and re-layouts, local(): section_weight[0].reshape(2, chan_half, 9, channels).transpose(0, 2, 1, 3)  4.48 us
    conv_general_dilated x4, matrix products, conv(): lax.conv_general_dilated(act, weight, (1, 1), ((1, 1), (1, 1)), dimension...  4.39 us
    select_n x1, other arithmetic, local(): jnp.where(lane == 0, jnp.concatenate([own, other], 1), jnp.concatenate([o...  3.61 us
  transfers between devices with their start and end apart: 4, of which 1 were waited for; matrix products, arithmetic and copies ran while one was open for 21% of the time, Pallas kernels for 0%

profile of v15, /device:TPU:0, one launch (start us, length us, event | category | flops | bytes accessed | tf_op | source)
XLA Modules:
  0.0 62.0 jit_solution(4721579696089062504)
XLA Ops:
  0.0 2.7 %reshape.97 = bf16[921600]{0:T(1024)(128)(2,1)S(1)} reshape(bf16[1,2,460800]{2,1,0:T(2,128)(2,1)} %param.4) | data formatting | bytes 3686400
  2.7 4.5 %reshape_squeeze.3 = bf16[2,160,9,320]{3,2,1,0:T(8,128)(2,1)} reshape(bf16[921600]{0:T(1024)(128)(2,1)S(1)} %reshape.97) | data formatting | bytes 3686400 | tf_op jit(solution)/shard_map/reshape;squeeze | solution.py:65
  7.2 2.7 %copy.56 = bf16[2,9,160,320]{3,2,1,0:T(8,128)(2,1)S(1)} copy(bf16[2,9,160,320]{3,1,2,0:T(8,128)(2,1)} %bitcast.118) | data formatting | bytes 3686400 | tf_op jit(solution)/shard_map/transpose | solution.py:65
  9.8 0.5 collective-permute-start
  10.4 0.1 fusion.126
  10.7 0.7 %slice.43 = bf16[4,2,7,2,320]{4,2,1,3,0:T(8,128)(2,1)} slice(bf16[4,2,8,3,320]{4,2,1,3,0:T(8,128)(2,1)S(1)} %copy.55), slice={[0:4], [0:2], [1:8], [0:2], [0:320]} | slice | bytes 143360 | tf_op jit(solution)/shard_map/conv_general_dilated | solution.py:13
  11.4 0.2 constant_dynamic-slice_fusion
  11.6 0.2 rev.29
  11.9 0.6 %slice.50 = bf16[4,2,7,2,160]{4,2,1,3,0:T(8,128)(2,1)} slice(bf16[4,2,8,3,160]{4,2,1,3,0:T(8,128)(2,1)S(1)} %copy.63), slice={[0:4], [0:2], [1:8], [0:2], [0:160]} | slice | bytes 71680 | tf_op jit(solution)/shard_map/conv_general_dilated | solution.py:22
  12.5 0.2 rev.27
  12.8 0.5 convolution_select_fusion.1
  13.5 0.3 rev.28
  13.8 0.1 fusion.123
  14.0 0.5 convolution_select_fusion.3
  14.6 1.8 %convolution_select_fusion.2 = f32[4,16,3,160]{3,1,2,0:T(8,128)S(1)} fusion(bf16[2,160,3,3,320]{4,1,3,2,0:T(8,128)(2,1)} %collective-permute-done, bf16[4,2,7,2,320]{4,2,1,3,0:T(8,128)(2,1)S(1)} %copy-done.3, bf16[4,2,8,3,320]{4,2,1,3,0:T(8,128)(2,1)S(1)} %copy.55, pred[16,3]{0,1:T(4,128)(4,1)S(1)} %copy-done.5), kind=kOutput, calls=%fused_computation.13 | convolution fusion | flops 148101120 | bytes 1423408 | tf_op jit(solution)/shard_map/conv_general_dilated | solution.py:13
  16.4 0.2 maximum_select_fusion.1
  16.6 0.1 copy.57
  16.8 4.7 %collective-permute-start.1 = (bf16[2,4,16,320]{3,1,2,0:T(4,128)(2,1)S(1)}, bf16[2,4,16,320]{3,1,2,0:T(4,128)(2,1)S(1)}, u32[]{:S(2)}, u32[]{:S(2)}) collective-permute-start(bf16[2,4,16,320]{3,1,2,0:T(4,128)(2,1)S(1)} %fusion.58), channel_id=1, source_target_pairs={{0,4},{12,8},{1,5},{13,9},{2,6},{14,10},{3,7},{15,11},{16,20},{28,... | collective-permute-start | bytes 245768 | tf_op jit(solution)/shard_map/ppermute | solution.py:72
  21.5 1.8 %convolution_select_fusion = f32[4,16,3,320]{3,1,2,0:T(8,128)S(1)} fusion(bf16[2,160,3,3,320]{4,1,3,2,0:T(8,128)(2,1)} %collective-permute-done, bf16[4,2,7,2,160]{4,2,1,3,0:T(8,128)(2,1)S(1)} %copy-done.4, bf16[4,2,8,3,160]{4,2,1,3,0:T(8,128)(2,1)S(1)} %copy.63, pred[16,3]{0,1:T(4,128)(4,1)S(1)} %copy-done.5), kind=kOutput, calls=%fused_computation.11 | convolution fusion | flops 147824640 | bytes 1449008 | tf_op jit(solution)/shard_map/conv_general_dilated | solution.py:22
  23.2 0.1 copy.64
  23.4 0.3 rev.30
  23.8 1.5 %collective-permute-start.2 = (f32[2,4,16,320]{3,1,2,0:T(4,128)S(1)}, f32[2,4,16,320]{3,1,2,0:T(4,128)S(1)}, u32[]{:S(2)}, u32[]{:S(2)}) collective-permute-start(f32[2,4,16,320]{3,1,2,0:T(4,128)S(1)} %add.95), channel_id=1, source_target_pairs={{0,4},{12,8},{1,5},{13,9},{2,6},{14,10},{3,7},{15,11},{16,20},{28,... | collective-permute-start | bytes 491528 | tf_op jit(solution)/shard_map/ppermute | solution.py:72
  25.3 3.6 %maximum_select_fusion = bf16[2,320,3,3,320]{4,1,3,2,0:T(8,128)(2,1)S(1)} fusion(bf16[2,160,3,3,320]{4,1,3,2,0:T(8,128)(2,1)} %collective-permute-done, bf16[2,160,3,3,320]{4,1,3,2,0:T(8,128)(2,1)S(1)} %bitcast.122, pred[]{:T(512)S(6)} %eq.4), kind=kLoop, calls=%fused_computation | loop fusion | flops 16588800 | bytes 7372801 | tf_op jit(solution)/shard_map/jit(_where)/select_n | solution.py:98
  29.2 1.0 %fusion.6 = f32[4,16,3,320]{3,1,2,0:T(8,128)S(1)} fusion(bf16[2,320,3,3,320]{4,1,3,2,0:T(8,128)(2,1)S(1)} %maximum_select_fusion, bf16[4,2,7,2,320]{4,2,1,3,0:T(8,128)(2,1)S(1)} %slice.53, bf16[4,2,8,3,320]{4,2,1,3,0:T(8,128)(2,1)S(1)} %copy.66, pred[16,3]{0,1:T(4,128)(4,1)S(1)} %copy-done.5), kind=kOutput, calls=%fused_computation.9 | convolution fusion | flops 295587840 | bytes 2703872 | tf_op jit(solution)/shard_map/conv_general_dilated | solution.py:13
  30.3 0.1 fusion.50
  30.6 0.3 copy-done
  30.9 1.0 %fusion.4 = f32[4,16,3,320]{3,1,2,0:T(8,128)S(1)} fusion(bf16[2,320,3,3,320]{4,1,3,2,0:T(8,128)(2,1)S(1)} %maximum_select_fusion, bf16[4,2,7,2,320]{4,2,1,3,0:T(8,128)(2,1)S(1)} %slice.56, bf16[4,2,8,3,320]{4,2,1,3,0:T(8,128)(2,1)S(1)} %copy.69, pred[16,3]{0,1:T(4,128)(4,1)S(1)} %copy-done.5), kind=kOutput, calls=%fused_computation.7 | convolution fusion | flops 295587840 | bytes 2703872 | tf_op jit(solution)/shard_map/conv_general_dilated | solution.py:13
  32.0 0.1 copy.70
  32.1 0.2 add_convert_fusion.3
  32.3 0.3 rev.31
  32.8 2.4 %fusion.5 = f32[4,16,3,320]{3,1,2,0:T(8,128)S(1)} fusion(bf16[2,320,3,3,320]{4,1,3,2,0:T(8,128)(2,1)} %copy-done, bf16[4,2,7,2,320]{4,2,1,3,0:T(8,128)(2,1)S(1)} %slice.59, bf16[4,2,8,3,320]{4,2,1,3,0:T(8,128)(2,1)S(1)} %copy.72, pred[16,3]{0,1:T(4,128)(4,1)S(1)} %copy-done.5), kind=kOutput, calls=%fused_computation.8 | convolution fusion | flops 295587840 | bytes 2652208 | tf_op jit(solution)/shard_map/conv_general_dilated | solution.py:22
  35.1 0.1 copy.73
  35.3 0.3 rev.32
  35.6 0.2 add_convert_fusion.1
  35.9 0.3 rev.33
  36.3 2.4 %fusion.7 = f32[4,16,3,320]{3,1,2,0:T(8,128)S(1)} fusion(bf16[2,320,3,3,320]{4,1,3,2,0:T(8,128)(2,1)} %copy-done, bf16[4,2,7,2,320]{4,2,1,3,0:T(8,128)(2,1)S(1)} %slice.61, bf16[4,2,8,3,320]{4,2,1,3,0:T(8,128)(2,1)S(1)} %copy.75, pred[16,3]{0,1:T(4,128)(4,1)S(1)} %copy-done.5), kind=kOutput, calls=%fused_computation.10 | convolution fusion | flops 295587840 | bytes 2652208 | tf_op jit(solution)/shard_map/conv_general_dilated | solution.py:22
  38.7 0.1 copy.76
  38.8 0.3 rev.34
  39.2 0.3 fusion.87
  39.5 1.3 %collective-permute-start.3 = (bf16[2,4,16,320]{3,1,2,0:T(4,128)(2,1)S(1)}, bf16[2,4,16,320]{3,1,2,0:T(4,128)(2,1)S(1)}, u32[]{:S(2)}, u32[]{:S(2)}) collective-permute-start(bf16[2,4,16,320]{3,1,2,0:T(4,128)(2,1)S(1)} %fusion.87), channel_id=1, source_target_pairs={{4,0},{8,12},{5,1},{9,13},{6,2},{10,14},{7,3},{11,15},{20,16},{24,... | collective-permute-start | bytes 245768 | tf_op jit(solution)/shard_map/ppermute | solution.py:156
  40.9 5.2 %collective-permute-done.3 = bf16[2,4,16,320]{3,1,2,0:T(4,128)(2,1)S(1)} collective-permute-done((bf16[2,4,16,320]{3,1,2,0:T(4,128)(2,1)S(1)}, bf16[2,4,16,320]{3,1,2,0:T(4,128)(2,1)S(1)}, u32[]{:S(2)}, u32[]{:S(2)}) %collective-permute-start.3) | collective-permute-done | bytes 81952 | tf_op jit(solution)/shard_map/ppermute | solution.py:156
  46.1 0.4 fusion.94
  46.5 0.1 pad_maximum_fusion
  46.7 8.1 %all_gather.3 = bf16[8,4,16,640]{3,2,1,0:T(8,128)(2,1)S(1)} all-gather(bf16[2,4,16,640]{3,2,1,0:T(8,128)(2,1)S(1)} %copy.77), channel_id=1, replica_groups=mesh['groups'=2,'pipe'=4,'dp'=2,'mp'=2] {'dp','mp'}, dimensions={0}, use_global_device_ids=true | all-gather | bytes 819200 | tf_op jit(solution)/shard_map/all_gather | solution.py:164
  54.9 0.2 constant_dynamic-slice_fusion.2
  55.0 0.9 %fusion.13 = f32[160,3,3,320]{3,0,2,1:T(8,128)S(1)} fusion(bf16[8,4,16,320]{3,2,1,0:T(8,128)(2,1)S(1)} %slice.63, bf16[8,4,16,160]{3,2,1,0:T(8,128)(2,1)S(1)} %constant_dynamic-slice_fusion.2), kind=kOutput, calls=%fused_computation.25 | convolution fusion | flops 376832000 | bytes 2334720 | tf_op jit(solution)/shard_map/conv_general_dilated | solution.py:31
  55.9 1.5 %copy.80 = f32[160,3,3,320]{3,2,1,0:T(4,128)S(1)} copy(f32[160,3,3,320]{3,0,2,1:T(8,128)S(1)} %fusion.13) | data formatting | bytes 3686400 | tf_op jit(solution)/shard_map/conv_general_dilated | solution.py:31
  57.4 4.6 %reshape.19 = f32[1,460800]{1,0:T(1,128)} reshape(f32[160,3,3,320]{3,2,1,0:T(4,128)S(1)} %copy.80) | data formatting | bytes 3686400 | tf_op jit(solution)/shard_map/reshape | solution.py:168
  (48 shorter events, 1.6 us)
Async XLA Ops:
  7.2 3.2 %copy-start.1 = (bf16[1,2,2,4,16,320]{5,4,3,2,1,0:T(8,128)(2,1)S(1)}, bf16[1,2,2,4,16,320]{5,4,3,2,1,0:T(8,128)(2,1)}, u32[]{:S(2)}) copy-start(bf16[1,2,2,4,16,320]{5,4,3,2,1,0:T(8,128)(2,1)} %param.3) | copy-start | bytes 491524
  7.2 4.2 %copy-start.2 = (bf16[1,2,2,4,16,320]{5,4,3,2,1,0:T(8,128)(2,1)S(1)}, bf16[1,2,2,4,16,320]{5,4,3,2,1,0:T(8,128)(2,1)}, u32[]{:S(2)}) copy-start(bf16[1,2,2,4,16,320]{5,4,3,2,1,0:T(8,128)(2,1)} %param.5) | copy-start | bytes 491524
  9.8 3.0 %copy-start.5 = (pred[16,3]{0,1:T(4,128)(4,1)S(1)}, pred[16,3]{0,1:T(4,128)(4,1)}, u32[]{:S(2)}) copy-start(pred[16,3]{0,1:T(4,128)(4,1)} %constant.106) | copy-start | bytes 148
  9.8 4.7 %collective-permute-start = (bf16[2,160,3,3,320]{4,1,3,2,0:T(8,128)(2,1)S(1)}, bf16[2,160,3,3,320]{4,1,3,2,0:T(8,128)(2,1)}, u32[]{:S(2)}, u32[]{:S(2)}) collective-permute-start(bf16[2,160,3,3,320]{4,1,3,2,0:T(8,128)(2,1)S(1)} %bitcast.119), channel_id=1, source_target_pairs={{0,1},{1,0},{2,3},{3,2},{4,5},{5,4},{6,7},{7,6},{8,9},{9,8},{10,11... | collective-permute-start | bytes 5529608 | tf_op jit(solution)/shard_map/ppermute | solution.py:68
  12.8 1.2 %copy-start.3 = (bf16[4,2,7,2,320]{4,2,1,3,0:T(8,128)(2,1)S(1)}, bf16[4,2,7,2,320]{4,2,1,3,0:T(8,128)(2,1)}, u32[]{:S(2)}) copy-start(bf16[4,2,7,2,320]{4,2,1,3,0:T(8,128)(2,1)} %slice.43) | copy-start | bytes 215044
  14.6 6.9 %copy-start.4 = (bf16[4,2,7,2,160]{4,2,1,3,0:T(8,128)(2,1)S(1)}, bf16[4,2,7,2,160]{4,2,1,3,0:T(8,128)(2,1)}, u32[]{:S(2)}) copy-start(bf16[4,2,7,2,160]{4,2,1,3,0:T(8,128)(2,1)} %slice.50) | copy-start | bytes 107524
  16.8 12.1 %collective-permute-start.1 = (bf16[2,4,16,320]{3,1,2,0:T(4,128)(2,1)S(1)}, bf16[2,4,16,320]{3,1,2,0:T(4,128)(2,1)S(1)}, u32[]{:S(2)}, u32[]{:S(2)}) collective-permute-start(bf16[2,4,16,320]{3,1,2,0:T(4,128)(2,1)S(1)} %fusion.58), channel_id=1, source_target_pairs={{0,4},{12,8},{1,5},{13,9},{2,6},{14,10},{3,7},{15,11},{16,20},{28,... | collective-permute-start | bytes 245768 | tf_op jit(solution)/shard_map/ppermute | solution.py:72
  23.8 8.3 %collective-permute-start.2 = (f32[2,4,16,320]{3,1,2,0:T(4,128)S(1)}, f32[2,4,16,320]{3,1,2,0:T(4,128)S(1)}, u32[]{:S(2)}, u32[]{:S(2)}) collective-permute-start(f32[2,4,16,320]{3,1,2,0:T(4,128)S(1)} %add.95), channel_id=1, source_target_pairs={{0,4},{12,8},{1,5},{13,9},{2,6},{14,10},{3,7},{15,11},{16,20},{28,... | collective-permute-start | bytes 491528 | tf_op jit(solution)/shard_map/ppermute | solution.py:72
  28.9 2.0 %copy-start = (bf16[2,320,3,3,320]{4,1,3,2,0:T(8,128)(2,1)}, bf16[2,320,3,3,320]{4,1,3,2,0:T(8,128)(2,1)S(1)}, u32[]{:S(2)}) copy-start(bf16[2,320,3,3,320]{4,1,3,2,0:T(8,128)(2,1)S(1)} %maximum_select_fusion) | copy-start | bytes 11059204
  39.5 6.6 %collective-permute-start.3 = (bf16[2,4,16,320]{3,1,2,0:T(4,128)(2,1)S(1)}, bf16[2,4,16,320]{3,1,2,0:T(4,128)(2,1)S(1)}, u32[]{:S(2)}, u32[]{:S(2)}) collective-permute-start(bf16[2,4,16,320]{3,1,2,0:T(4,128)(2,1)S(1)} %fusion.87), channel_id=1, source_target_pairs={{4,0},{8,12},{5,1},{9,13},{6,2},{10,14},{7,3},{11,15},{20,16},{24,... | collective-permute-start | bytes 245768 | tf_op jit(solution)/shard_map/ppermute | solution.py:156

commit v16 on v15

--- a/solution.py
+++ b/solution.py
@@ -41,6 +41,15 @@
 
 def bf16(v):
     return v.astype(jnp.bfloat16)
+
+
+def on_stage(active, fn, *args):
+    shapes = jax.eval_shape(fn, *args)
+
+    def idle(*unused):
+        return jax.tree.map(lambda v: jnp.zeros(v.shape, v.dtype), shapes)
+
+    return lax.cond(active, fn, idle, *args)
 
 
 def local(latent, section_weight, out_grad):
@@ -87,10 +96,14 @@
     x0 = take(samples, mine)
     seed = take(grads, mine)
     a0 = bf16(jax.nn.silu(f32(x0)))
-    h1_own = conv(a0, own[0])
-    d_own = conv_t(lax.dynamic_slice_in_dim(seed, low, chan_half, 3), own[1])
-    h1 = bf16(f32(x0) + join(h1_own, conv(a0, other[0])))
-    d_last = d_own + conv_t(lax.dynamic_slice_in_dim(seed, high, chan_half, 3), other[1])
+
+    def first(x0, a0, seed, own, other):
+        h1_own = conv(a0, own[0])
+        d_own = conv_t(lax.dynamic_slice_in_dim(seed, low, chan_half, 3), own[1])
+        h1 = bf16(f32(x0) + join(h1_own, conv(a0, other[0])))
+        return h1, d_own + conv_t(lax.dynamic_slice_in_dim(seed, high, chan_half, 3), other[1])
+
+    h1, d_last = on_stage(stage == 0, first, x0, a0, seed, own, other)
     h1_r = up(0, h1)
     d_last_r = up(0, d_last)
 

time: 62.3 us -> 65.1 us (1.045)
  waiting for transfers between devices: 5.19 us -> 9.22 us
  starting transfers between devices: 7.97 us -> 4.57 us
  other arithmetic: 5.84 us -> 7.56 us
  local copies, waits for them, and re-layouts: 22 us -> 20.6 us
  blocking collectives: 8.11 us -> 9.23 us
  matrix products: 12.3 us -> 13 us
    ppermute x1, waiting for transfers between devices: 0.01 us -> 3.66 us  [local(): other = lax.ppermute(own, 'mp', swap)]
    ppermute x2, starting transfers between devices: 6.16 us -> 2.76 us  [up(): return lax.ppermute(v, 'pipe', pairs)]
    all_gather x1, blocking collectives: 8.11 us -> 9.23 us  [local(): every = lax.all_gather(both, ('dp', 'mp'), axis=0, tiled=True)]
    conv_general_dilated x4, matrix products: 7.05 us -> 7.74 us  [conv_t(): lax.conv_general_dilated(flipped, weight, (1, 1), ((1, 1), (1, 1)), dimen...]
    add x1, other arithmetic: 0.05 us -> 0.73 us  [first(): d_own + conv_t(lax.dynamic_slice_in_dim(seed, high, chan_half, 3), other[1])]
    conv_general_dilated x16 -> x14, local copies, waits for them, and re-layouts: 1.34 us -> 0.73 us  [conv_t(): lax.conv_general_dilated(flipped, weight, (1, 1), ((1, 1), (1, 1)), dimen...]
    unnamed x15 -> x11, local copies, waits for them, and re-layouts: 3.18 us -> 2.84 us
  transfers between devices with their start and end apart: 4 -> 4, of which waited for: 1 -> 2; matrix products, arithmetic and copies ran while one was open for 21% -> 11% of each run, Pallas kernels for 0% -> 0%
where the time goes in v16:
time: 65.1 us; the launch traced here: 64.7 us
  local copies, waits for them, and re-layouts  20.6 us (32%)
  matrix products  13 us (20%)
  blocking collectives  9.23 us (14%)
  waiting for transfers between devices  9.22 us (14%)
  other arithmetic  7.56 us (12%)
  starting transfers between devices  4.57 us (7%)
    all_gather x1, blocking collectives, local(): every = lax.all_gather(both, ('dp', 'mp'), axis=0, tiled=True)  9.23 us
    conv_general_dilated x4, matrix products, conv_t(): lax.conv_general_dilated(flipped, weight, (1, 1), ((1, 1), (1, 1)), dimen...  7.74 us
    ppermute x1, waiting for transfers between devices, local(): lax.ppermute(jnp.where(lower, c0, a_last), 'pipe', [(1, 0), (pipe_size -...  5.55 us
    reshape x1, local copies, waits for them, and re-layouts, local(): return grad.reshape(1, -1)  4.57 us
    another operation x1, local copies, waits for them, and re-layouts, local(): section_weight[0].reshape(2, chan_half, 9, channels).transpose(0, 2, 1, 3)  4.5 us
    conv_general_dilated x4, matrix products, conv(): lax.conv_general_dilated(act, weight, (1, 1), ((1, 1), (1, 1)), dimension...  4.35 us
    ppermute x1, waiting for transfers between devices, local(): other = lax.ppermute(own, 'mp', swap)  3.66 us
    select_n x1, other arithmetic, local(): jnp.where(lane == 0, jnp.concatenate([own, other], 1), jnp.concatenate([o...  3.6 us
  transfers between devices with their start and end apart: 4, of which 2 were waited for; matrix products, arithmetic and copies ran while one was open for 11% of the time, Pallas kernels for 0%

profile of v16, /device:TPU:0, one launch (start us, length us, event | category | flops | bytes accessed | tf_op | source)
XLA Modules:
  0.0 64.7 jit_solution(12388281038283806587)
XLA Ops:
  0.0 2.7 %reshape.97 = bf16[921600]{0:T(1024)(128)(2,1)S(1)} reshape(bf16[1,2,460800]{2,1,0:T(2,128)(2,1)} %param.6) | data formatting | bytes 3686400
  2.7 4.5 %reshape_squeeze.3 = bf16[2,160,9,320]{3,2,1,0:T(8,128)(2,1)} reshape(bf16[921600]{0:T(1024)(128)(2,1)S(1)} %reshape.97) | data formatting | bytes 3686400 | tf_op jit(solution)/shard_map/reshape;squeeze | solution.py:74
  7.2 2.7 %copy.62 = bf16[2,9,160,320]{3,2,1,0:T(8,128)(2,1)S(1)} copy(bf16[2,9,160,320]{3,1,2,0:T(8,128)(2,1)} %bitcast.123) | data formatting | bytes 3686400 | tf_op jit(solution)/shard_map/transpose | solution.py:74
  9.9 0.5 collective-permute-start
  10.7 0.1 fusion.67
  10.8 3.7 %collective-permute-done = bf16[2,160,3,3,320]{4,1,3,2,0:T(8,128)(2,1)} collective-permute-done((bf16[2,160,3,3,320]{4,1,3,2,0:T(8,128)(2,1)S(1)}, bf16[2,160,3,3,320]{4,1,3,2,0:T(8,128)(2,1)}, u32[]{:S(2)}, u32[]{:S(2)}) %collective-permute-start) | collective-permute-done | bytes 1843232 | tf_op jit(solution)/shard_map/ppermute | solution.py:77
  14.5 9.6 %conditional.1 = (bf16[2,4,16,320]{3,1,2,0:T(4,128)(2,1)}, f32[2,4,16,320]{3,1,2,0:T(4,128)}) conditional(s32[]{:T(128)} %convert_element_type.83, () %tuple.17, (bf16[2,4,16,320]{3,1,2,0:T(4,128)(2,1)S(1)}, s32[]{:T(128)}, bf16[2,160,3,3,320]{4,1,3,2,0:T(8,128)(2,1)S(1)}, bf16[2,4,16,320]{3,1,2,0:T(4,128)(2,1)S(1)}, ...), branch_computations={%region_0.1_spmd, %region_1.2_spmd} | conditional | flops 591585280 | bytes 12125168 | solution.py:52
  14.6 0.2 constant_dynamic-slice_fusion
  15.0 0.2 fusion.17
  15.2 1.2 %convolution_select_fusion.1 = f32[4,16,3,320]{3,1,2,0:T(8,128)S(1)} fusion(bf16[2,160,3,3,320]{4,1,3,2,0:T(8,128)(2,1)S(1)} %get-tuple-element.44, bf16[4,2,8,5,160]{4,1,3,2,0:T(2,128)(2,1)S(1)} %fusion.17, pred[16,3]{0,1:T(4,128)(4,1)} %constant.85), kind=kOutput, calls=%fused_computation.1 | convolution fusion | flops 147517440 | bytes 1515568 | tf_op jit(solution)/shard_map/cond/branch_1_fun/conv_general_dilated | solution.py:22
  16.4 0.1 copy.58
  16.6 0.3 rev.24
  17.1 0.2 fusion.18
  17.2 1.8 %convolution_select_fusion = f32[4,16,3,320]{3,1,2,0:T(8,128)S(1)} fusion(bf16[2,160,3,3,320]{4,1,3,2,0:T(8,128)(2,1)} %get-tuple-element.45, bf16[4,2,8,5,160]{4,1,3,2,0:T(2,128)(2,1)S(1)} %fusion.18, pred[16,3]{0,1:T(4,128)(4,1)S(1)} %copy-done.4), kind=kOutput, calls=%fused_computation | convolution fusion | flops 147517440 | bytes 1454128 | tf_op jit(solution)/shard_map/cond/branch_1_fun/conv_general_dilated | solution.py:22
  19.0 0.1 copy.60
  19.2 0.3 rev.26
  19.5 0.7 %add.65 = f32[2,4,16,320]{3,1,2,0:T(4,128)} add(f32[2,4,16,320]{3,1,2,0:T(4,128)S(1)} %rev.24, f32[2,4,16,320]{3,1,2,0:T(4,128)S(1)} %rev.26) | non-fusion elementwise | flops 40960 | bytes 491520 | tf_op jit(solution)/shard_map/cond/branch_1_fun/add | solution.py:104
  20.5 0.2 fusion.10
  20.8 1.8 %convolution_select_fusion.2 = f32[4,16,3,160]{3,1,2,0:T(8,128)S(1)} fusion(bf16[2,160,3,3,320]{4,1,3,2,0:T(8,128)(2,1)} %get-tuple-element.45, bf16[4,2,8,5,320]{4,1,3,2,0:T(2,128)(2,1)S(1)} %fusion.10, pred[16,3]{0,1:T(4,128)(4,1)S(1)} %copy-done.4), kind=kOutput, calls=%fused_computation.2 | convolution fusion | flops 147486720 | bytes 1433648 | tf_op jit(solution)/shard_map/cond/branch_1_fun/conv_general_dilated | solution.py:13
  22.6 0.5 convolution_select_fusion.3
  23.1 0.2 maximum_select_fusion
  23.3 0.1 copy.56
  23.4 0.7 %fusion.16 = bf16[2,4,16,320]{3,1,2,0:T(4,128)(2,1)} fusion(f32[4,2,24,320]{3,0,2,1:T(4,128)S(1)} %bitcast.141, bf16[2,4,16,320]{3,1,2,0:T(4,128)(2,1)S(1)} %get-tuple-element.41), kind=kLoop, calls=%fused_computation.26 | loop fusion | flops 122880 | bytes 327680 | tf_op jit(solution)/shard_map/cond/branch_1_fun/convert_element_type | solution.py:43
  24.1 1.3 %collective-permute-start.1 = (bf16[2,4,16,320]{3,1,2,0:T(4,128)(2,1)}, bf16[2,4,16,320]{3,1,2,0:T(4,128)(2,1)S(1)}, u32[]{:S(2)}, u32[]{:S(2)}) collective-permute-start(bf16[2,4,16,320]{3,1,2,0:T(4,128)(2,1)} %get-tuple-element.51), channel_id=1, source_target_pairs={{0,4},{12,8},{1,5},{13,9},{2,6},{14,10},{3,7},{15,11},{16,20},{28,... | collective-permute-start | bytes 245768 | tf_op jit(solution)/shard_map/ppermute | solution.py:81
  25.4 1.5 %collective-permute-start.2 = (f32[2,4,16,320]{3,1,2,0:T(4,128)}, f32[2,4,16,320]{3,1,2,0:T(4,128)S(1)}, u32[]{:S(2)}, u32[]{:S(2)}) collective-permute-start(f32[2,4,16,320]{3,1,2,0:T(4,128)} %get-tuple-element.52), channel_id=1, source_target_pairs={{0,4},{12,8},{1,5},{13,9},{2,6},{14,10},{3,7},{15,11},{16,20},{28,... | collective-permute-start | bytes 491528 | tf_op jit(solution)/shard_map/ppermute | solution.py:81
  26.9 3.6 %maximum_select_fusion.1 = bf16[2,320,3,3,320]{4,1,3,2,0:T(8,128)(2,1)S(1)} fusion(bf16[2,160,3,3,320]{4,1,3,2,0:T(8,128)(2,1)} %collective-permute-done, bf16[2,160,3,3,320]{4,1,3,2,0:T(8,128)(2,1)S(1)} %bitcast.126, pred[]{:T(512)S(6)} %eq.11), kind=kLoop, calls=%fused_computation.38 | loop fusion | flops 16588800 | bytes 7372801 | tf_op jit(solution)/shard_map/jit(_where)/select_n | solution.py:111
  30.8 1.0 %fusion.29 = f32[4,16,3,320]{3,1,2,0:T(8,128)S(1)} fusion(bf16[2,320,3,3,320]{4,1,3,2,0:T(8,128)(2,1)S(1)} %maximum_select_fusion.1, bf16[4,2,7,2,320]{4,2,1,3,0:T(8,128)(2,1)S(1)} %slice.49, bf16[4,2,8,3,320]{4,2,1,3,0:T(8,128)(2,1)S(1)} %copy.67, pred[16,3]{0,1:T(4,128)(4,1)S(1)} %copy-done.3), kind=kOutput, calls=%fused_computation.47 | convolution fusion | flops 295587840 | bytes 2703872 | tf_op jit(solution)/shard_map/conv_general_dilated | solution.py:13
  31.8 0.1 copy.68
  31.9 0.1 fusion.71
  32.2 1.0 %fusion.27 = f32[4,16,3,320]{3,1,2,0:T(8,128)S(1)} fusion(bf16[2,320,3,3,320]{4,1,3,2,0:T(8,128)(2,1)S(1)} %maximum_select_fusion.1, bf16[4,2,7,2,320]{4,2,1,3,0:T(8,128)(2,1)S(1)} %slice.52, bf16[4,2,8,3,320]{4,2,1,3,0:T(8,128)(2,1)S(1)} %copy.70, pred[16,3]{0,1:T(4,128)(4,1)S(1)} %copy-done.3), kind=kOutput, calls=%fused_computation.45 | convolution fusion | flops 295587840 | bytes 2703872 | tf_op jit(solution)/shard_map/conv_general_dilated | solution.py:13
  33.4 0.2 add_convert_fusion.3
  33.6 0.3 rev.31
  34.0 2.4 %fusion.28 = f32[4,16,3,320]{3,1,2,0:T(8,128)S(1)} fusion(bf16[2,320,3,3,320]{4,1,3,2,0:T(8,128)(2,1)} %copy-done, bf16[4,2,7,2,320]{4,2,1,3,0:T(8,128)(2,1)S(1)} %slice.55, bf16[4,2,8,3,320]{4,2,1,3,0:T(8,128)(2,1)S(1)} %copy.73, pred[16,3]{0,1:T(4,128)(4,1)S(1)} %copy-done.3), kind=kOutput, calls=%fused_computation.46 | convolution fusion | flops 295587840 | bytes 2652208 | tf_op jit(solution)/shard_map/conv_general_dilated | solution.py:22
  36.6 0.3 rev.32
  36.9 0.2 add_convert_fusion.1
  37.1 0.3 rev.33
  37.5 2.4 %fusion.30 = f32[4,16,3,320]{3,1,2,0:T(8,128)S(1)} fusion(bf16[2,320,3,3,320]{4,1,3,2,0:T(8,128)(2,1)} %copy-done, bf16[4,2,7,2,320]{4,2,1,3,0:T(8,128)(2,1)S(1)} %slice.57, bf16[4,2,8,3,320]{4,2,1,3,0:T(8,128)(2,1)S(1)} %copy.76, pred[16,3]{0,1:T(4,128)(4,1)S(1)} %copy-done.3), kind=kOutput, calls=%fused_computation.48 | convolution fusion | flops 295587840 | bytes 2652208 | tf_op jit(solution)/shard_map/conv_general_dilated | solution.py:22
  40.1 0.3 rev.34
  40.4 0.3 fusion.90
  40.7 1.3 %collective-permute-start.3 = (bf16[2,4,16,320]{3,1,2,0:T(4,128)(2,1)S(1)}, bf16[2,4,16,320]{3,1,2,0:T(4,128)(2,1)S(1)}, u32[]{:S(2)}, u32[]{:S(2)}) collective-permute-start(bf16[2,4,16,320]{3,1,2,0:T(4,128)(2,1)S(1)} %fusion.90), channel_id=1, source_target_pairs={{4,0},{8,12},{5,1},{9,13},{6,2},{10,14},{7,3},{11,15},{20,16},{24,... | collective-permute-start | bytes 245768 | tf_op jit(solution)/shard_map/ppermute | solution.py:169
  42.2 5.5 %collective-permute-done.3 = bf16[2,4,16,320]{3,1,2,0:T(4,128)(2,1)S(1)} collective-permute-done((bf16[2,4,16,320]{3,1,2,0:T(4,128)(2,1)S(1)}, bf16[2,4,16,320]{3,1,2,0:T(4,128)(2,1)S(1)}, u32[]{:S(2)}, u32[]{:S(2)}) %collective-permute-start.3) | collective-permute-done | bytes 81952 | tf_op jit(solution)/shard_map/ppermute | solution.py:169
  47.7 0.4 fusion.97
  48.2 0.1 pad_maximum_fusion
  48.3 9.2 %all_gather.3 = bf16[8,4,16,640]{3,2,1,0:T(8,128)(2,1)S(1)} all-gather(bf16[2,4,16,640]{3,2,1,0:T(8,128)(2,1)S(1)} %copy.78), channel_id=1, replica_groups=mesh['groups'=2,'pipe'=4,'dp'=2,'mp'=2] {'dp','mp'}, dimensions={0}, use_global_device_ids=true | all-gather | bytes 819200 | tf_op jit(solution)/shard_map/all_gather | solution.py:177
  57.6 0.2 constant_dynamic-slice_fusion.2
  57.8 0.9 %fusion.35 = f32[160,3,3,320]{3,0,2,1:T(8,128)S(1)} fusion(bf16[8,4,16,320]{3,2,1,0:T(8,128)(2,1)S(1)} %slice.59, bf16[8,4,16,160]{3,2,1,0:T(8,128)(2,1)S(1)} %constant_dynamic-slice_fusion.2), kind=kOutput, calls=%fused_computation.54 | convolution fusion | flops 376832000 | bytes 2334720 | tf_op jit(solution)/shard_map/conv_general_dilated | solution.py:31
  58.6 1.5 %copy.81 = f32[160,3,3,320]{3,2,1,0:T(4,128)S(1)} copy(f32[160,3,3,320]{3,0,2,1:T(8,128)S(1)} %fusion.35) | data formatting | bytes 3686400 | tf_op jit(solution)/shard_map/conv_general_dilated | solution.py:31
  60.1 4.6 %reshape.19 = f32[1,460800]{1,0:T(1,128)} reshape(f32[160,3,3,320]{3,2,1,0:T(4,128)S(1)} %copy.81) | data formatting | bytes 3686400 | tf_op jit(solution)/shard_map/reshape | solution.py:181
  (48 shorter events, 2.1 us)
Async XLA Ops:
  7.2 3.2 %copy-start.1 = (bf16[1,2,2,4,16,320]{5,4,3,2,1,0:T(8,128)(2,1)S(1)}, bf16[1,2,2,4,16,320]{5,4,3,2,1,0:T(8,128)(2,1)}, u32[]{:S(2)}) copy-start(bf16[1,2,2,4,16,320]{5,4,3,2,1,0:T(8,128)(2,1)} %param.5) | copy-start | bytes 491524
  7.2 3.3 %copy-start.2 = (bf16[1,2,2,4,16,320]{5,4,3,2,1,0:T(8,128)(2,1)S(1)}, bf16[1,2,2,4,16,320]{5,4,3,2,1,0:T(8,128)(2,1)}, u32[]{:S(2)}) copy-start(bf16[1,2,2,4,16,320]{5,4,3,2,1,0:T(8,128)(2,1)} %param.7) | copy-start | bytes 491524
  9.9 4.6 %collective-permute-start = (bf16[2,160,3,3,320]{4,1,3,2,0:T(8,128)(2,1)S(1)}, bf16[2,160,3,3,320]{4,1,3,2,0:T(8,128)(2,1)}, u32[]{:S(2)}, u32[]{:S(2)}) collective-permute-start(bf16[2,160,3,3,320]{4,1,3,2,0:T(8,128)(2,1)S(1)} %bitcast.124), channel_id=1, source_target_pairs={{0,1},{1,0},{2,3},{3,2},{4,5},{5,4},{6,7},{7,6},{8,9},{9,8},{10,11... | collective-permute-start | bytes 5529608 | tf_op jit(solution)/shard_map/ppermute | solution.py:77
  15.2 2.0 %copy-start.4 = (pred[16,3]{0,1:T(4,128)(4,1)S(1)}, pred[16,3]{0,1:T(4,128)(4,1)}, u32[]{:S(2)}) copy-start(pred[16,3]{0,1:T(4,128)(4,1)} %constant.85) | copy-start | bytes 148 | tf_op jit(solution)/shard_map/cond
  24.1 6.4 %collective-permute-start.1 = (bf16[2,4,16,320]{3,1,2,0:T(4,128)(2,1)}, bf16[2,4,16,320]{3,1,2,0:T(4,128)(2,1)S(1)}, u32[]{:S(2)}, u32[]{:S(2)}) collective-permute-start(bf16[2,4,16,320]{3,1,2,0:T(4,128)(2,1)} %get-tuple-element.51), channel_id=1, source_target_pairs={{0,4},{12,8},{1,5},{13,9},{2,6},{14,10},{3,7},{15,11},{16,20},{28,... | collective-permute-start | bytes 245768 | tf_op jit(solution)/shard_map/ppermute | solution.py:81
  25.4 5.4 %copy-start.3 = (pred[16,3]{0,1:T(4,128)(4,1)S(1)}, pred[16,3]{0,1:T(4,128)(4,1)}, u32[]{:S(2)}) copy-start(pred[16,3]{0,1:T(4,128)(4,1)} %constant.81) | copy-start | bytes 148
  25.4 8.0 %collective-permute-start.2 = (f32[2,4,16,320]{3,1,2,0:T(4,128)}, f32[2,4,16,320]{3,1,2,0:T(4,128)S(1)}, u32[]{:S(2)}, u32[]{:S(2)}) collective-permute-start(f32[2,4,16,320]{3,1,2,0:T(4,128)} %get-tuple-element.52), channel_id=1, source_target_pairs={{0,4},{12,8},{1,5},{13,9},{2,6},{14,10},{3,7},{15,11},{16,20},{28,... | collective-permute-start | bytes 491528 | tf_op jit(solution)/shard_map/ppermute | solution.py:81
  30.5 2.7 %copy-start = (bf16[2,320,3,3,320]{4,1,3,2,0:T(8,128)(2,1)}, bf16[2,320,3,3,320]{4,1,3,2,0:T(8,128)(2,1)S(1)}, u32[]{:S(2)}) copy-start(bf16[2,320,3,3,320]{4,1,3,2,0:T(8,128)(2,1)S(1)} %maximum_select_fusion.1) | copy-start | bytes 11059204
  40.7 7.0 %collective-permute-start.3 = (bf16[2,4,16,320]{3,1,2,0:T(4,128)(2,1)S(1)}, bf16[2,4,16,320]{3,1,2,0:T(4,128)(2,1)S(1)}, u32[]{:S(2)}, u32[]{:S(2)}) collective-permute-start(bf16[2,4,16,320]{3,1,2,0:T(4,128)(2,1)S(1)} %fusion.90), channel_id=1, source_target_pairs={{4,0},{8,12},{5,1},{9,13},{6,2},{10,14},{7,3},{11,15},{20,16},{24,... | collective-permute-start | bytes 245768 | tf_op jit(solution)/shard_map/ppermute | solution.py:169

commit v17 on v16

--- a/solution.py
+++ b/solution.py
@@ -97,13 +97,15 @@
     seed = take(grads, mine)
     a0 = bf16(jax.nn.silu(f32(x0)))
 
-    def first(x0, a0, seed, own, other):
-        h1_own = conv(a0, own[0])
-        d_own = conv_t(lax.dynamic_slice_in_dim(seed, low, chan_half, 3), own[1])
+    def first_own(a0, seed, own):
+        return conv(a0, own[0]), conv_t(lax.dynamic_slice_in_dim(seed, low, chan_half, 3), own[1])
+
+    def first_other(x0, a0, seed, other, h1_own, d_own):
         h1 = bf16(f32(x0) + join(h1_own, conv(a0, other[0])))
         return h1, d_own + conv_t(lax.dynamic_slice_in_dim(seed, high, chan_half, 3), other[1])
 
-    h1, d_last = on_stage(stage == 0, first, x0, a0, seed, own, other)
+    h1_own, d_own = on_stage(stage == 0, first_own, a0, seed, own)
+    h1, d_last = on_stage(stage == 0, first_other, x0, a0, seed, other, h1_own, d_own)
     h1_r = up(0, h1)
     d_last_r = up(0, d_last)
 

time: 65.1 us -> 62.1 us (0.954)
  waiting for transfers between devices: 9.22 us -> 5.58 us
  local copies, waits for them, and re-layouts: 20.6 us -> 21.5 us
    ppermute x1, waiting for transfers between devices: 3.66 us -> 0.03 us  [local(): other = lax.ppermute(own, 'mp', swap)]
  transfers between devices with their start and end apart: 4 -> 4, of which waited for: 2 -> 1; matrix products, arithmetic and copies ran while one was open for 11% -> 17% of each run, Pallas kernels for 0% -> 0%
where the time goes in v17:
time: 62.1 us; the launch traced here: 61.8 us
  local copies, waits for them, and re-layouts  21.5 us (35%)
  matrix products  13 us (21%)
  blocking collectives  9.25 us (15%)
  other arithmetic  7.13 us (11%)
  waiting for transfers between devices  5.58 us (9%)
  starting transfers between devices  4.59 us (7%)
    all_gather x1, blocking collectives, local(): every = lax.all_gather(both, ('dp', 'mp'), axis=0, tiled=True)  9.25 us
    conv_general_dilated x4, matrix products, conv_t(): lax.conv_general_dilated(flipped, weight, (1, 1), ((1, 1), (1, 1)), dimen...  7.77 us
    ppermute x1, waiting for transfers between devices, local(): lax.ppermute(jnp.where(lower, c0, a_last), 'pipe', [(1, 0), (pipe_size -...  5.54 us
    reshape x1, local copies, waits for them, and re-layouts, local(): return grad.reshape(1, -1)  4.57 us
    another operation x1, local copies, waits for them, and re-layouts, local(): section_weight[0].reshape(2, chan_half, 9, channels).transpose(0, 2, 1, 3)  4.49 us
    conv_general_dilated x4, matrix products, conv(): lax.conv_general_dilated(act, weight, (1, 1), ((1, 1), (1, 1)), dimension...  4.35 us
    select_n x1, other arithmetic, local(): jnp.where(lane == 0, jnp.concatenate([own, other], 1), jnp.concatenate([o...  3.6 us
    unnamed x11, local copies, waits for them, and re-layouts  3.18 us
  transfers between devices with their start and end apart: 4, of which 1 were waited for; matrix products, arithmetic and copies ran while one was open for 17% of the time, Pallas kernels for 0%

profile of v17, /device:TPU:0, one launch (start us, length us, event | category | flops | bytes accessed | tf_op | source)
XLA Modules:
  0.0 61.8 jit_solution(5426736669081132871)
XLA Ops:
  0.0 2.7 %reshape.100 = bf16[921600]{0:T(1024)(128)(2,1)S(1)} reshape(bf16[1,2,460800]{2,1,0:T(2,128)(2,1)} %param.8) | data formatting | bytes 3686400
  2.7 4.5 %reshape_squeeze.3 = bf16[2,160,9,320]{3,2,1,0:T(8,128)(2,1)} reshape(bf16[921600]{0:T(1024)(128)(2,1)S(1)} %reshape.100) | data formatting | bytes 3686400 | tf_op jit(solution)/shard_map/reshape;squeeze | solution.py:74
  7.2 2.7 %copy.72 = bf16[2,9,160,320]{3,2,1,0:T(8,128)(2,1)S(1)} copy(bf16[2,9,160,320]{3,1,2,0:T(8,128)(2,1)} %bitcast.127) | data formatting | bytes 3686400 | tf_op jit(solution)/shard_map/transpose | solution.py:74
  9.8 0.5 collective-permute-start
  10.6 0.1 fusion.66
  10.7 3.6 %conditional.2 = (f32[2,4,16,160]{3,1,2,0:T(4,128)S(1)}, f32[2,4,16,320]{3,1,2,0:T(4,128)S(1)}) conditional(s32[]{:T(128)} %convert_element_type.84, () %tuple.26, (bf16[2,160,3,3,320]{4,1,3,2,0:T(8,128)(2,1)S(1)}, bf16[2,4,16,320]{3,1,2,0:T(4,128)(2,1)S(1)}, s32[]{:T(128)}, bf16[2,4,16,320]{3,1,2,0:T(4,128)(2,1)S(1)}) %tuple.44), branch_computations={%region_0.1_spmd, %region_1.2_spmd} | conditional | flops 295925760 | bytes 6160198 | solution.py:52
  10.9 0.2 constant_dynamic-slice_fusion
  11.2 0.2 fusion.7
  11.4 1.2 %convolution_select_fusion = f32[4,16,3,320]{3,1,2,0:T(8,128)S(1)} fusion(bf16[2,160,3,3,320]{4,1,3,2,0:T(8,128)(2,1)S(1)} %get-tuple-element.50, bf16[4,2,8,5,160]{4,1,3,2,0:T(2,128)(2,1)S(1)} %fusion.7, pred[16,3]{0,1:T(4,128)(4,1)} %constant.94), kind=kOutput, calls=%fused_computation | convolution fusion | flops 147517440 | bytes 1515568 | tf_op jit(solution)/shard_map/cond/branch_1_fun/conv_general_dilated | solution.py:22
  12.8 0.3 rev.22
  13.4 0.2 fusion.4
  13.7 0.5 convolution_select_fusion.1
  14.2 0.1 copy.64
  14.4 6.3 %conditional.3 = (bf16[2,4,16,320]{3,1,2,0:T(4,128)(2,1)S(1)}, f32[2,4,16,320]{3,1,2,0:T(4,128)}) conditional(s32[]{:T(128)} %convert_element_type.84, () %tuple.25, (bf16[2,4,16,320]{3,1,2,0:T(4,128)(2,1)S(1)}, s32[]{:T(128)}, bf16[2,160,3,3,320]{4,1,3,2,0:T(8,128)(2,1)}, bf16[2,4,16,320]{3,1,2,0:T(4,128)(2,1)S(1)}, f32[2,4,16,160]{3,1,2,0:T(4,128)S(1)}, ...), branch_computations={%region_2.3_spmd, %region_3.4_spmd} | conditional | flops 296212480 | bytes 6877032 | solution.py:52
  14.6 0.1 constant_dynamic-slice_fusion.1
  14.9 0.2 fusion.19
  15.1 1.8 %convolution_select_fusion.2 = f32[4,16,3,320]{3,1,2,0:T(8,128)S(1)} fusion(bf16[2,160,3,3,320]{4,1,3,2,0:T(8,128)(2,1)} %get-tuple-element.57, bf16[4,2,8,5,160]{4,1,3,2,0:T(2,128)(2,1)S(1)} %fusion.19, pred[16,3]{0,1:T(4,128)(4,1)} %constant.92), kind=kOutput, calls=%fused_computation.19 | convolution fusion | flops 147517440 | bytes 1454592 | tf_op jit(solution)/shard_map/cond/branch_1_fun/conv_general_dilated | solution.py:22
  17.0 0.3 rev.24
  17.4 0.7 %add.64 = f32[2,4,16,320]{3,1,2,0:T(4,128)} add(f32[2,4,16,320]{3,1,2,0:T(4,128)S(1)} %get-tuple-element.58, f32[2,4,16,320]{3,1,2,0:T(4,128)S(1)} %rev.24) | non-fusion elementwise | flops 40960 | bytes 491520 | tf_op jit(solution)/shard_map/cond/branch_1_fun/add | solution.py:105
  18.4 0.2 fusion.14
  18.6 1.8 %convolution_select_fusion.3 = f32[4,16,3,160]{3,1,2,0:T(8,128)S(1)} fusion(bf16[2,160,3,3,320]{4,1,3,2,0:T(8,128)(2,1)} %get-tuple-element.57, bf16[4,2,8,5,320]{4,1,3,2,0:T(2,128)(2,1)S(1)} %fusion.14, pred[16,3]{0,1:T(4,128)(4,1)S(1)} %copy-done.4), kind=kOutput, calls=%fused_computation.20 | convolution fusion | flops 147486720 | bytes 1433648 | tf_op jit(solution)/shard_map/cond/branch_1_fun/conv_general_dilated | solution.py:13
  20.4 0.1 copy.68
  20.6 0.2 fusion.18
  20.8 1.3 %collective-permute-start.1 = (bf16[2,4,16,320]{3,1,2,0:T(4,128)(2,1)S(1)}, bf16[2,4,16,320]{3,1,2,0:T(4,128)(2,1)S(1)}, u32[]{:S(2)}, u32[]{:S(2)}) collective-permute-start(bf16[2,4,16,320]{3,1,2,0:T(4,128)(2,1)S(1)} %get-tuple-element.67), channel_id=1, source_target_pairs={{0,4},{12,8},{1,5},{13,9},{2,6},{14,10},{3,7},{15,11},{16,20},{28,... | collective-permute-start | bytes 245768 | tf_op jit(solution)/shard_map/ppermute | solution.py:81
  22.1 1.5 %collective-permute-start.2 = (f32[2,4,16,320]{3,1,2,0:T(4,128)}, f32[2,4,16,320]{3,1,2,0:T(4,128)S(1)}, u32[]{:S(2)}, u32[]{:S(2)}) collective-permute-start(f32[2,4,16,320]{3,1,2,0:T(4,128)} %get-tuple-element.68), channel_id=1, source_target_pairs={{0,4},{12,8},{1,5},{13,9},{2,6},{14,10},{3,7},{15,11},{16,20},{28,... | collective-permute-start | bytes 491528 | tf_op jit(solution)/shard_map/ppermute | solution.py:81
  23.6 3.6 %maximum_select_fusion.1 = bf16[2,320,3,3,320]{4,1,3,2,0:T(8,128)(2,1)S(1)} fusion(bf16[2,160,3,3,320]{4,1,3,2,0:T(8,128)(2,1)} %collective-permute-done, bf16[2,160,3,3,320]{4,1,3,2,0:T(8,128)(2,1)S(1)} %bitcast.130, pred[]{:T(512)S(6)} %eq.12), kind=kLoop, calls=%fused_computation.41 | loop fusion | flops 16588800 | bytes 7372801 | tf_op jit(solution)/shard_map/jit(_where)/select_n | solution.py:113
  27.5 1.0 %fusion.28 = f32[4,16,3,320]{3,1,2,0:T(8,128)S(1)} fusion(bf16[2,320,3,3,320]{4,1,3,2,0:T(8,128)(2,1)S(1)} %maximum_select_fusion.1, bf16[4,2,7,2,320]{4,2,1,3,0:T(8,128)(2,1)S(1)} %slice.50, bf16[4,2,8,3,320]{4,2,1,3,0:T(8,128)(2,1)S(1)} %copy.79, pred[16,3]{0,1:T(4,128)(4,1)S(1)} %copy-done.3), kind=kOutput, calls=%fused_computation.50 | convolution fusion | flops 295587840 | bytes 2703872 | tf_op jit(solution)/shard_map/conv_general_dilated | solution.py:13
  28.6 0.1 fusion.70
  28.9 0.3 copy-done
  29.2 1.0 %fusion.26 = f32[4,16,3,320]{3,1,2,0:T(8,128)S(1)} fusion(bf16[2,320,3,3,320]{4,1,3,2,0:T(8,128)(2,1)S(1)} %maximum_select_fusion.1, bf16[4,2,7,2,320]{4,2,1,3,0:T(8,128)(2,1)S(1)} %slice.53, bf16[4,2,8,3,320]{4,2,1,3,0:T(8,128)(2,1)S(1)} %copy.82, pred[16,3]{0,1:T(4,128)(4,1)S(1)} %copy-done.3), kind=kOutput, calls=%fused_computation.48 | convolution fusion | flops 295587840 | bytes 2703872 | tf_op jit(solution)/shard_map/conv_general_dilated | solution.py:13
  30.4 0.2 add_convert_fusion.3
  30.6 0.3 rev.29
  31.1 2.4 %fusion.27 = f32[4,16,3,320]{3,1,2,0:T(8,128)S(1)} fusion(bf16[2,320,3,3,320]{4,1,3,2,0:T(8,128)(2,1)} %copy-done, bf16[4,2,7,2,320]{4,2,1,3,0:T(8,128)(2,1)S(1)} %slice.56, bf16[4,2,8,3,320]{4,2,1,3,0:T(8,128)(2,1)S(1)} %copy.85, pred[16,3]{0,1:T(4,128)(4,1)S(1)} %copy-done.3), kind=kOutput, calls=%fused_computation.49 | convolution fusion | flops 295587840 | bytes 2652208 | tf_op jit(solution)/shard_map/conv_general_dilated | solution.py:22
  33.6 0.3 rev.30
  33.9 0.2 add_convert_fusion.1
  34.1 0.3 rev.31
  34.6 2.4 %fusion.29 = f32[4,16,3,320]{3,1,2,0:T(8,128)S(1)} fusion(bf16[2,320,3,3,320]{4,1,3,2,0:T(8,128)(2,1)} %copy-done, bf16[4,2,7,2,320]{4,2,1,3,0:T(8,128)(2,1)S(1)} %slice.58, bf16[4,2,8,3,320]{4,2,1,3,0:T(8,128)(2,1)S(1)} %copy.88, pred[16,3]{0,1:T(4,128)(4,1)S(1)} %copy-done.3), kind=kOutput, calls=%fused_computation.51 | convolution fusion | flops 295587840 | bytes 2652208 | tf_op jit(solution)/shard_map/conv_general_dilated | solution.py:22
  37.1 0.3 rev.32
  37.5 0.3 fusion.89
  37.8 1.3 %collective-permute-start.3 = (bf16[2,4,16,320]{3,1,2,0:T(4,128)(2,1)S(1)}, bf16[2,4,16,320]{3,1,2,0:T(4,128)(2,1)S(1)}, u32[]{:S(2)}, u32[]{:S(2)}) collective-permute-start(bf16[2,4,16,320]{3,1,2,0:T(4,128)(2,1)S(1)} %fusion.89), channel_id=1, source_target_pairs={{4,0},{8,12},{5,1},{9,13},{6,2},{10,14},{7,3},{11,15},{20,16},{24,... | collective-permute-start | bytes 245768 | tf_op jit(solution)/shard_map/ppermute | solution.py:171
  39.2 5.5 %collective-permute-done.3 = bf16[2,4,16,320]{3,1,2,0:T(4,128)(2,1)S(1)} collective-permute-done((bf16[2,4,16,320]{3,1,2,0:T(4,128)(2,1)S(1)}, bf16[2,4,16,320]{3,1,2,0:T(4,128)(2,1)S(1)}, u32[]{:S(2)}, u32[]{:S(2)}) %collective-permute-start.3) | collective-permute-done | bytes 81952 | tf_op jit(solution)/shard_map/ppermute | solution.py:171
  44.7 0.4 fusion.96
  45.2 0.1 pad_maximum_fusion
  45.3 9.2 %all_gather.3 = bf16[8,4,16,640]{3,2,1,0:T(8,128)(2,1)S(1)} all-gather(bf16[2,4,16,640]{3,2,1,0:T(8,128)(2,1)S(1)} %copy.90), channel_id=1, replica_groups=mesh['groups'=2,'pipe'=4,'dp'=2,'mp'=2] {'dp','mp'}, dimensions={0}, use_global_device_ids=true | all-gather | bytes 819200 | tf_op jit(solution)/shard_map/all_gather | solution.py:179
  54.6 0.2 constant_dynamic-slice_fusion.2
  54.8 0.9 %fusion.34 = f32[160,3,3,320]{3,0,2,1:T(8,128)S(1)} fusion(bf16[8,4,16,320]{3,2,1,0:T(8,128)(2,1)S(1)} %slice.60, bf16[8,4,16,160]{3,2,1,0:T(8,128)(2,1)S(1)} %constant_dynamic-slice_fusion.2), kind=kOutput, calls=%fused_computation.57 | convolution fusion | flops 376832000 | bytes 2334720 | tf_op jit(solution)/shard_map/conv_general_dilated | solution.py:31
  55.7 1.5 %copy.93 = f32[160,3,3,320]{3,2,1,0:T(4,128)S(1)} copy(f32[160,3,3,320]{3,0,2,1:T(8,128)S(1)} %fusion.34) | data formatting | bytes 3686400 | tf_op jit(solution)/shard_map/conv_general_dilated | solution.py:31
  57.2 4.6 %reshape.19 = f32[1,460800]{1,0:T(1,128)} reshape(f32[160,3,3,320]{3,2,1,0:T(4,128)S(1)} %copy.93) | data formatting | bytes 3686400 | tf_op jit(solution)/shard_map/reshape | solution.py:183
  (60 shorter events, 2.9 us)
Async XLA Ops:
  7.2 3.2 %copy-start.1 = (bf16[1,2,2,4,16,320]{5,4,3,2,1,0:T(8,128)(2,1)S(1)}, bf16[1,2,2,4,16,320]{5,4,3,2,1,0:T(8,128)(2,1)}, u32[]{:S(2)}) copy-start(bf16[1,2,2,4,16,320]{5,4,3,2,1,0:T(8,128)(2,1)} %param.7) | copy-start | bytes 491524
  7.2 3.3 %copy-start.2 = (bf16[1,2,2,4,16,320]{5,4,3,2,1,0:T(8,128)(2,1)S(1)}, bf16[1,2,2,4,16,320]{5,4,3,2,1,0:T(8,128)(2,1)}, u32[]{:S(2)}) copy-start(bf16[1,2,2,4,16,320]{5,4,3,2,1,0:T(8,128)(2,1)} %param.9) | copy-start | bytes 491524
  9.8 4.6 %collective-permute-start = (bf16[2,160,3,3,320]{4,1,3,2,0:T(8,128)(2,1)S(1)}, bf16[2,160,3,3,320]{4,1,3,2,0:T(8,128)(2,1)}, u32[]{:S(2)}, u32[]{:S(2)}) collective-permute-start(bf16[2,160,3,3,320]{4,1,3,2,0:T(8,128)(2,1)S(1)} %bitcast.128), channel_id=1, source_target_pairs={{0,1},{1,0},{2,3},{3,2},{4,5},{5,4},{6,7},{7,6},{8,9},{9,8},{10,11... | collective-permute-start | bytes 5529608 | tf_op jit(solution)/shard_map/ppermute | solution.py:77
  11.4 2.3 %copy-start.5 = (pred[16,3]{0,1:T(4,128)(4,1)S(1)}, pred[16,3]{0,1:T(4,128)(4,1)}, u32[]{:S(2)}) copy-start(pred[16,3]{0,1:T(4,128)(4,1)} %constant.94) | copy-start | bytes 148 | tf_op jit(solution)/shard_map/cond
  15.1 3.5 %copy-start.4 = (pred[16,3]{0,1:T(4,128)(4,1)S(1)}, pred[16,3]{0,1:T(4,128)(4,1)}, u32[]{:S(2)}) copy-start(pred[16,3]{0,1:T(4,128)(4,1)} %constant.92) | copy-start | bytes 148 | tf_op jit(solution)/shard_map/cond
  20.8 6.4 %collective-permute-start.1 = (bf16[2,4,16,320]{3,1,2,0:T(4,128)(2,1)S(1)}, bf16[2,4,16,320]{3,1,2,0:T(4,128)(2,1)S(1)}, u32[]{:S(2)}, u32[]{:S(2)}) collective-permute-start(bf16[2,4,16,320]{3,1,2,0:T(4,128)(2,1)S(1)} %get-tuple-element.67), channel_id=1, source_target_pairs={{0,4},{12,8},{1,5},{13,9},{2,6},{14,10},{3,7},{15,11},{16,20},{28,... | collective-permute-start | bytes 245768 | tf_op jit(solution)/shard_map/ppermute | solution.py:81
  22.1 5.4 %copy-start.3 = (pred[16,3]{0,1:T(4,128)(4,1)S(1)}, pred[16,3]{0,1:T(4,128)(4,1)}, u32[]{:S(2)}) copy-start(pred[16,3]{0,1:T(4,128)(4,1)} %constant.88) | copy-start | bytes 148
  22.1 8.3 %collective-permute-start.2 = (f32[2,4,16,320]{3,1,2,0:T(4,128)}, f32[2,4,16,320]{3,1,2,0:T(4,128)S(1)}, u32[]{:S(2)}, u32[]{:S(2)}) collective-permute-start(f32[2,4,16,320]{3,1,2,0:T(4,128)} %get-tuple-element.68), channel_id=1, source_target_pairs={{0,4},{12,8},{1,5},{13,9},{2,6},{14,10},{3,7},{15,11},{16,20},{28,... | collective-permute-start | bytes 491528 | tf_op jit(solution)/shard_map/ppermute | solution.py:81
  27.2 2.0 %copy-start = (bf16[2,320,3,3,320]{4,1,3,2,0:T(8,128)(2,1)}, bf16[2,320,3,3,320]{4,1,3,2,0:T(8,128)(2,1)S(1)}, u32[]{:S(2)}) copy-start(bf16[2,320,3,3,320]{4,1,3,2,0:T(8,128)(2,1)S(1)} %maximum_select_fusion.1) | copy-start | bytes 11059204
  37.8 7.0 %collective-permute-start.3 = (bf16[2,4,16,320]{3,1,2,0:T(4,128)(2,1)S(1)}, bf16[2,4,16,320]{3,1,2,0:T(4,128)(2,1)S(1)}, u32[]{:S(2)}, u32[]{:S(2)}) collective-permute-start(bf16[2,4,16,320]{3,1,2,0:T(4,128)(2,1)S(1)} %fusion.89), channel_id=1, source_target_pairs={{4,0},{8,12},{5,1},{9,13},{6,2},{10,14},{7,3},{11,15},{20,16},{24,... | collective-permute-start | bytes 245768 | tf_op jit(solution)/shard_map/ppermute | solution.py:171

commit v18 on v17

--- a/solution.py
+++ b/solution.py
@@ -100,13 +100,16 @@
     def first_own(a0, seed, own):
         return conv(a0, own[0]), conv_t(lax.dynamic_slice_in_dim(seed, low, chan_half, 3), own[1])
 
-    def first_other(x0, a0, seed, other, h1_own, d_own):
-        h1 = bf16(f32(x0) + join(h1_own, conv(a0, other[0])))
-        return h1, d_own + conv_t(lax.dynamic_slice_in_dim(seed, high, chan_half, 3), other[1])
+    def first_h1(x0, a0, other_enc, h1_own):
+        return bf16(f32(x0) + join(h1_own, conv(a0, other_enc)))
+
+    def first_d(seed, other_dec, d_own):
+        return d_own + conv_t(lax.dynamic_slice_in_dim(seed, high, chan_half, 3), other_dec)
 
     h1_own, d_own = on_stage(stage == 0, first_own, a0, seed, own)
-    h1, d_last = on_stage(stage == 0, first_other, x0, a0, seed, other, h1_own, d_own)
+    h1 = on_stage(stage == 0, first_h1, x0, a0, other[0], h1_own)
     h1_r = up(0, h1)
+    d_last = on_stage(stage == 0, first_d, seed, other[1], d_own)
     d_last_r = up(0, d_last)
 
     other, _ = lax.optimization_barrier((other, h1))

time: 62.1 us -> 61.9 us (level)
  starting transfers between devices: 4.59 us -> 5.61 us
    ppermute x2, starting transfers between devices: 2.78 us -> 3.8 us  [up(): return lax.ppermute(v, 'pipe', pairs)]
    conv_general_dilated x4, matrix products: 7.77 us -> 7.04 us  [conv_t(): lax.conv_general_dilated(flipped, weight, (1, 1), ((1, 1), (1, 1)), dimen...]
    conv_general_dilated x4, matrix products: 4.35 us -> 5.03 us  [conv(): lax.conv_general_dilated(act, weight, (1, 1), ((1, 1), (1, 1)), dimension...]
  transfers between devices with their start and end apart: 4 -> 4, of which waited for: 1 -> 2; matrix products, arithmetic and copies ran while one was open for 17% -> 22% of each run, Pallas kernels for 0% -> 0%
where the time goes in v18:
time: 61.9 us; the launch traced here: 61.5 us
  local copies, waits for them, and re-layouts  21.1 us (34%)
  matrix products  12.9 us (21%)
  blocking collectives  8.79 us (14%)
  other arithmetic  7.13 us (12%)
  starting transfers between devices  5.61 us (9%)
  waiting for transfers between devices  5.19 us (8%)
    all_gather x1, blocking collectives, local(): every = lax.all_gather(both, ('dp', 'mp'), axis=0, tiled=True)  8.79 us
    conv_general_dilated x4, matrix products, conv_t(): lax.conv_general_dilated(flipped, weight, (1, 1), ((1, 1), (1, 1)), dimen...  7.04 us
    ppermute x1, waiting for transfers between devices, local(): lax.ppermute(jnp.where(lower, c0, a_last), 'pipe', [(1, 0), (pipe_size -...  5.09 us
    conv_general_dilated x4, matrix products, conv(): lax.conv_general_dilated(act, weight, (1, 1), ((1, 1), (1, 1)), dimension...  5.03 us
    reshape x1, local copies, waits for them, and re-layouts, local(): return grad.reshape(1, -1)  4.57 us
    another operation x1, local copies, waits for them, and re-layouts, local(): section_weight[0].reshape(2, chan_half, 9, channels).transpose(0, 2, 1, 3)  4.47 us
    ppermute x2, starting transfers between devices, up(): return lax.ppermute(v, 'pipe', pairs)  3.8 us
    select_n x1, other arithmetic, local(): jnp.where(lane == 0, jnp.concatenate([own, other], 1), jnp.concatenate([o...  3.6 us
  transfers between devices with their start and end apart: 4, of which 2 were waited for; matrix products, arithmetic and copies ran while one was open for 22% of the time, Pallas kernels for 0%

profile of v18, /device:TPU:0, one launch (start us, length us, event | category | flops | bytes accessed | tf_op | source)
XLA Modules:
  0.0 61.5 jit_solution(10838757541817788369)
XLA Ops:
  0.0 2.7 %reshape.100 = bf16[921600]{0:T(1024)(128)(2,1)S(1)} reshape(bf16[1,2,460800]{2,1,0:T(2,128)(2,1)} %param.10) | data formatting | bytes 3686400
  2.7 4.5 %reshape_squeeze.3 = bf16[2,160,9,320]{3,2,1,0:T(8,128)(2,1)} reshape(bf16[921600]{0:T(1024)(128)(2,1)S(1)} %reshape.100) | data formatting | bytes 3686400 | tf_op jit(solution)/shard_map/reshape;squeeze | solution.py:74
  7.1 2.7 %copy.72 = bf16[2,9,160,320]{3,2,1,0:T(8,128)(2,1)S(1)} copy(bf16[2,9,160,320]{3,1,2,0:T(8,128)(2,1)} %bitcast.127) | data formatting | bytes 3686400 | tf_op jit(solution)/shard_map/transpose | solution.py:74
  9.8 0.5 collective-permute-start
  10.6 0.1 fusion.66
  10.7 3.6 %conditional.3 = (f32[2,4,16,160]{3,1,2,0:T(4,128)S(1)}, f32[2,4,16,320]{3,1,2,0:T(4,128)S(1)}) conditional(s32[]{:T(128)} %convert_element_type.83, () %tuple.30, (bf16[2,160,3,3,320]{4,1,3,2,0:T(8,128)(2,1)S(1)}, bf16[2,4,16,320]{3,1,2,0:T(4,128)(2,1)S(1)}, s32[]{:T(128)}, bf16[2,4,16,320]{3,1,2,0:T(4,128)(2,1)S(1)}) %tuple.54), branch_computations={%region_0.1_spmd, %region_1.2_spmd} | conditional | flops 295925760 | bytes 6160198 | solution.py:52
  10.8 0.2 constant_dynamic-slice_fusion
  11.2 0.2 fusion.7
  11.7 0.2 fusion.4
  11.9 1.2 %convolution_select_fusion.1 = f32[4,16,3,160]{3,1,2,0:T(8,128)S(1)} fusion(bf16[2,160,3,3,320]{4,1,3,2,0:T(8,128)(2,1)S(1)} %get-tuple-element.56, bf16[4,2,8,5,320]{4,1,3,2,0:T(2,128)(2,1)S(1)} %fusion.4, pred[16,3]{0,1:T(4,128)(4,1)} %constant.96), kind=kOutput, calls=%fused_computation.1 | convolution fusion | flops 147486720 | bytes 1474608 | tf_op jit(solution)/shard_map/cond/branch_1_fun/conv_general_dilated | solution.py:13
  13.1 0.5 convolution_select_fusion
  13.8 0.3 rev.22
  14.1 0.1 copy.64
  14.4 2.7 %conditional.4 = (bf16[2,4,16,320]{3,1,2,0:T(4,128)(2,1)S(1)}) conditional(s32[]{:T(128)} %convert_element_type.83, () %tuple.29, (bf16[2,4,16,320]{3,1,2,0:T(4,128)(2,1)S(1)}, s32[]{:T(128)}, bf16[2,160,3,3,320]{4,1,3,2,0:T(8,128)(2,1)}, bf16[2,4,16,320]{3,1,2,0:T(4,128)(2,1)S(1)}, f32[2,4,16,160]{3,1,2,0:T(4,128)S(1)}) %tuple.32), branch_computations={%region_2.3_spmd, %region_3.4_spmd} | conditional | flops 148346880 | bytes 3082772 | solution.py:52
  14.7 0.2 fusion.12
  14.9 1.8 %convolution_select_fusion.2 = f32[4,16,3,160]{3,1,2,0:T(8,128)S(1)} fusion(bf16[2,160,3,3,320]{4,1,3,2,0:T(8,128)(2,1)} %get-tuple-element.63, bf16[4,2,8,5,320]{4,1,3,2,0:T(2,128)(2,1)S(1)} %fusion.12, pred[16,3]{0,1:T(4,128)(4,1)} %constant.95), kind=kOutput, calls=%fused_computation.19 | convolution fusion | flops 147486720 | bytes 1434112 | tf_op jit(solution)/shard_map/cond/branch_1_fun/conv_general_dilated | solution.py:13
  16.7 0.1 copy.68
  16.9 0.2 fusion.16
  17.1 2.2 %collective-permute-start.1 = (bf16[2,4,16,320]{3,1,2,0:T(4,128)(2,1)S(1)}, bf16[2,4,16,320]{3,1,2,0:T(4,128)(2,1)S(1)}, u32[]{:S(2)}, u32[]{:S(2)}) collective-permute-start(bf16[2,4,16,320]{3,1,2,0:T(4,128)(2,1)S(1)} %get-tuple-element.119), channel_id=1, source_target_pairs={{0,4},{12,8},{1,5},{13,9},{2,6},{14,10},{3,7},{15,11},{16,20},{28,... | collective-permute-start | bytes 245768 | tf_op jit(solution)/shard_map/ppermute | solution.py:81
  19.3 3.7 %conditional.5 = (f32[2,4,16,320]{3,1,2,0:T(4,128)}) conditional(s32[]{:T(128)} %convert_element_type.83, () %tuple.33, (s32[]{:T(128)}, bf16[2,4,16,320]{3,1,2,0:T(4,128)(2,1)S(1)}, bf16[2,160,3,3,320]{4,1,3,2,0:T(8,128)(2,1)}, f32[2,4,16,320]{3,1,2,0:T(4,128)S(1)}) %tuple.34), branch_computations={%region_4.5_spmd, %region_5.6_spmd} | conditional | flops 147865600 | bytes 3794504 | solution.py:52
  19.5 0.1 constant_dynamic-slice_fusion.1
  19.8 0.2 fusion.19
  20.0 1.8 %convolution_select_fusion.3 = f32[4,16,3,320]{3,1,2,0:T(8,128)S(1)} fusion(bf16[2,160,3,3,320]{4,1,3,2,0:T(8,128)(2,1)} %get-tuple-element.67, bf16[4,2,8,5,160]{4,1,3,2,0:T(2,128)(2,1)S(1)} %fusion.19, pred[16,3]{0,1:T(4,128)(4,1)} %constant.94), kind=kOutput, calls=%fused_computation.31 | convolution fusion | flops 147517440 | bytes 1454592 | tf_op jit(solution)/shard_map/cond/branch_1_fun/conv_general_dilated | solution.py:22
  21.9 0.3 rev.24
  22.2 0.7 %add.63 = f32[2,4,16,320]{3,1,2,0:T(4,128)} add(f32[2,4,16,320]{3,1,2,0:T(4,128)S(1)} %get-tuple-element.64, f32[2,4,16,320]{3,1,2,0:T(4,128)S(1)} %rev.24) | non-fusion elementwise | flops 40960 | bytes 491520 | tf_op jit(solution)/shard_map/cond/branch_1_fun/add | solution.py:107
  23.0 1.6 %collective-permute-start.2 = (f32[2,4,16,320]{3,1,2,0:T(4,128)}, f32[2,4,16,320]{3,1,2,0:T(4,128)S(1)}, u32[]{:S(2)}, u32[]{:S(2)}) collective-permute-start(f32[2,4,16,320]{3,1,2,0:T(4,128)} %get-tuple-element.120), channel_id=1, source_target_pairs={{0,4},{12,8},{1,5},{13,9},{2,6},{14,10},{3,7},{15,11},{16,20},{28,... | collective-permute-start | bytes 491528 | tf_op jit(solution)/shard_map/ppermute | solution.py:81
  24.6 3.6 %maximum_select_fusion.1 = bf16[2,320,3,3,320]{4,1,3,2,0:T(8,128)(2,1)S(1)} fusion(bf16[2,160,3,3,320]{4,1,3,2,0:T(8,128)(2,1)} %collective-permute-done, bf16[2,160,3,3,320]{4,1,3,2,0:T(8,128)(2,1)S(1)} %bitcast.130, pred[]{:T(512)S(6)} %eq.12), kind=kLoop, calls=%fused_computation.41 | loop fusion | flops 16588800 | bytes 7372801 | tf_op jit(solution)/shard_map/jit(_where)/select_n | solution.py:116
  28.5 1.0 %fusion.28 = f32[4,16,3,320]{3,1,2,0:T(8,128)S(1)} fusion(bf16[2,320,3,3,320]{4,1,3,2,0:T(8,128)(2,1)S(1)} %maximum_select_fusion.1, bf16[4,2,7,2,320]{4,2,1,3,0:T(8,128)(2,1)S(1)} %slice.51, bf16[4,2,8,3,320]{4,2,1,3,0:T(8,128)(2,1)S(1)} %copy.79, pred[16,3]{0,1:T(4,128)(4,1)S(1)} %copy-done.3), kind=kOutput, calls=%fused_computation.50 | convolution fusion | flops 295587840 | bytes 2703872 | tf_op jit(solution)/shard_map/conv_general_dilated | solution.py:13
  29.6 0.1 fusion.70
  29.9 1.0 %fusion.26 = f32[4,16,3,320]{3,1,2,0:T(8,128)S(1)} fusion(bf16[2,320,3,3,320]{4,1,3,2,0:T(8,128)(2,1)S(1)} %maximum_select_fusion.1, bf16[4,2,7,2,320]{4,2,1,3,0:T(8,128)(2,1)S(1)} %slice.54, bf16[4,2,8,3,320]{4,2,1,3,0:T(8,128)(2,1)S(1)} %copy.82, pred[16,3]{0,1:T(4,128)(4,1)S(1)} %copy-done.3), kind=kOutput, calls=%fused_computation.48 | convolution fusion | flops 295587840 | bytes 2703872 | tf_op jit(solution)/shard_map/conv_general_dilated | solution.py:13
  31.1 0.2 add_convert_fusion.3
  31.3 0.3 rev.29
  31.7 2.4 %fusion.27 = f32[4,16,3,320]{3,1,2,0:T(8,128)S(1)} fusion(bf16[2,320,3,3,320]{4,1,3,2,0:T(8,128)(2,1)} %copy-done, bf16[4,2,7,2,320]{4,2,1,3,0:T(8,128)(2,1)S(1)} %slice.57, bf16[4,2,8,3,320]{4,2,1,3,0:T(8,128)(2,1)S(1)} %copy.85, pred[16,3]{0,1:T(4,128)(4,1)S(1)} %copy-done.3), kind=kOutput, calls=%fused_computation.49 | convolution fusion | flops 295587840 | bytes 2652208 | tf_op jit(solution)/shard_map/conv_general_dilated | solution.py:22
  34.3 0.3 rev.30
  34.6 0.2 add_convert_fusion.1
  34.8 0.3 rev.31
  35.2 2.4 %fusion.29 = f32[4,16,3,320]{3,1,2,0:T(8,128)S(1)} fusion(bf16[2,320,3,3,320]{4,1,3,2,0:T(8,128)(2,1)} %copy-done, bf16[4,2,7,2,320]{4,2,1,3,0:T(8,128)(2,1)S(1)} %slice.59, bf16[4,2,8,3,320]{4,2,1,3,0:T(8,128)(2,1)S(1)} %copy.88, pred[16,3]{0,1:T(4,128)(4,1)S(1)} %copy-done.3), kind=kOutput, calls=%fused_computation.51 | convolution fusion | flops 295587840 | bytes 2652208 | tf_op jit(solution)/shard_map/conv_general_dilated | solution.py:22
  37.8 0.3 rev.32
  38.1 0.3 fusion.89
  38.4 1.3 %collective-permute-start.3 = (bf16[2,4,16,320]{3,1,2,0:T(4,128)(2,1)S(1)}, bf16[2,4,16,320]{3,1,2,0:T(4,128)(2,1)S(1)}, u32[]{:S(2)}, u32[]{:S(2)}) collective-permute-start(bf16[2,4,16,320]{3,1,2,0:T(4,128)(2,1)S(1)} %fusion.89), channel_id=1, source_target_pairs={{4,0},{8,12},{5,1},{9,13},{6,2},{10,14},{7,3},{11,15},{20,16},{24,... | collective-permute-start | bytes 245768 | tf_op jit(solution)/shard_map/ppermute | solution.py:174
  39.9 5.1 %collective-permute-done.3 = bf16[2,4,16,320]{3,1,2,0:T(4,128)(2,1)S(1)} collective-permute-done((bf16[2,4,16,320]{3,1,2,0:T(4,128)(2,1)S(1)}, bf16[2,4,16,320]{3,1,2,0:T(4,128)(2,1)S(1)}, u32[]{:S(2)}, u32[]{:S(2)}) %collective-permute-start.3) | collective-permute-done | bytes 81952 | tf_op jit(solution)/shard_map/ppermute | solution.py:174
  45.0 0.4 fusion.96
  45.4 0.1 pad_maximum_fusion
  45.6 8.8 %all_gather.3 = bf16[8,4,16,640]{3,2,1,0:T(8,128)(2,1)S(1)} all-gather(bf16[2,4,16,640]{3,2,1,0:T(8,128)(2,1)S(1)} %copy.90), channel_id=1, replica_groups=mesh['groups'=2,'pipe'=4,'dp'=2,'mp'=2] {'dp','mp'}, dimensions={0}, use_global_device_ids=true | all-gather | bytes 819200 | tf_op jit(solution)/shard_map/all_gather | solution.py:182
  54.4 0.2 constant_dynamic-slice_fusion.2
  54.6 0.9 %fusion.34 = f32[160,3,3,320]{3,0,2,1:T(8,128)S(1)} fusion(bf16[8,4,16,320]{3,2,1,0:T(8,128)(2,1)S(1)} %slice.61, bf16[8,4,16,160]{3,2,1,0:T(8,128)(2,1)S(1)} %constant_dynamic-slice_fusion.2), kind=kOutput, calls=%fused_computation.57 | convolution fusion | flops 376832000 | bytes 2334720 | tf_op jit(solution)/shard_map/conv_general_dilated | solution.py:31
  55.4 1.5 %copy.93 = f32[160,3,3,320]{3,2,1,0:T(4,128)S(1)} copy(f32[160,3,3,320]{3,0,2,1:T(8,128)S(1)} %fusion.34) | data formatting | bytes 3686400 | tf_op jit(solution)/shard_map/conv_general_dilated | solution.py:31
  57.0 4.6 %reshape.19 = f32[1,460800]{1,0:T(1,128)} reshape(f32[160,3,3,320]{3,2,1,0:T(4,128)S(1)} %copy.93) | data formatting | bytes 3686400 | tf_op jit(solution)/shard_map/reshape | solution.py:186
  (59 shorter events, 2.9 us)
Async XLA Ops:
  7.1 3.2 %copy-start.1 = (bf16[1,2,2,4,16,320]{5,4,3,2,1,0:T(8,128)(2,1)S(1)}, bf16[1,2,2,4,16,320]{5,4,3,2,1,0:T(8,128)(2,1)}, u32[]{:S(2)}) copy-start(bf16[1,2,2,4,16,320]{5,4,3,2,1,0:T(8,128)(2,1)} %param.9) | copy-start | bytes 491524
  7.1 3.3 %copy-start.2 = (bf16[1,2,2,4,16,320]{5,4,3,2,1,0:T(8,128)(2,1)S(1)}, bf16[1,2,2,4,16,320]{5,4,3,2,1,0:T(8,128)(2,1)}, u32[]{:S(2)}) copy-start(bf16[1,2,2,4,16,320]{5,4,3,2,1,0:T(8,128)(2,1)} %param.11) | copy-start | bytes 491524
  9.8 4.6 %collective-permute-start = (bf16[2,160,3,3,320]{4,1,3,2,0:T(8,128)(2,1)S(1)}, bf16[2,160,3,3,320]{4,1,3,2,0:T(8,128)(2,1)}, u32[]{:S(2)}, u32[]{:S(2)}) collective-permute-start(bf16[2,160,3,3,320]{4,1,3,2,0:T(8,128)(2,1)S(1)} %bitcast.128), channel_id=1, source_target_pairs={{0,1},{1,0},{2,3},{3,2},{4,5},{5,4},{6,7},{7,6},{8,9},{9,8},{10,11... | collective-permute-start | bytes 5529608 | tf_op jit(solution)/shard_map/ppermute | solution.py:77
  10.7 2.4 %copy-start.4 = (pred[16,3]{0,1:T(4,128)(4,1)S(1)}, pred[16,3]{0,1:T(4,128)(4,1)}, u32[]{:S(2)}) copy-start(pred[16,3]{0,1:T(4,128)(4,1)} %constant.96) | copy-start | bytes 148 | tf_op jit(solution)/shard_map/cond
  17.1 11.1 %collective-permute-start.1 = (bf16[2,4,16,320]{3,1,2,0:T(4,128)(2,1)S(1)}, bf16[2,4,16,320]{3,1,2,0:T(4,128)(2,1)S(1)}, u32[]{:S(2)}, u32[]{:S(2)}) collective-permute-start(bf16[2,4,16,320]{3,1,2,0:T(4,128)(2,1)S(1)} %get-tuple-element.119), channel_id=1, source_target_pairs={{0,4},{12,8},{1,5},{13,9},{2,6},{14,10},{3,7},{15,11},{16,20},{28,... | collective-permute-start | bytes 245768 | tf_op jit(solution)/shard_map/ppermute | solution.py:81
  23.0 5.5 %copy-start.3 = (pred[16,3]{0,1:T(4,128)(4,1)S(1)}, pred[16,3]{0,1:T(4,128)(4,1)}, u32[]{:S(2)}) copy-start(pred[16,3]{0,1:T(4,128)(4,1)} %constant.90) | copy-start | bytes 148
  23.0 8.1 %collective-permute-start.2 = (f32[2,4,16,320]{3,1,2,0:T(4,128)}, f32[2,4,16,320]{3,1,2,0:T(4,128)S(1)}, u32[]{:S(2)}, u32[]{:S(2)}) collective-permute-start(f32[2,4,16,320]{3,1,2,0:T(4,128)} %get-tuple-element.120), channel_id=1, source_target_pairs={{0,4},{12,8},{1,5},{13,9},{2,6},{14,10},{3,7},{15,11},{16,20},{28,... | collective-permute-start | bytes 491528 | tf_op jit(solution)/shard_map/ppermute | solution.py:81
  28.2 2.7 %copy-start = (bf16[2,320,3,3,320]{4,1,3,2,0:T(8,128)(2,1)}, bf16[2,320,3,3,320]{4,1,3,2,0:T(8,128)(2,1)S(1)}, u32[]{:S(2)}) copy-start(bf16[2,320,3,3,320]{4,1,3,2,0:T(8,128)(2,1)S(1)} %maximum_select_fusion.1) | copy-start | bytes 11059204
  38.4 6.5 %collective-permute-start.3 = (bf16[2,4,16,320]{3,1,2,0:T(4,128)(2,1)S(1)}, bf16[2,4,16,320]{3,1,2,0:T(4,128)(2,1)S(1)}, u32[]{:S(2)}, u32[]{:S(2)}) collective-permute-start(bf16[2,4,16,320]{3,1,2,0:T(4,128)(2,1)S(1)} %fusion.89), channel_id=1, source_target_pairs={{4,0},{8,12},{5,1},{9,13},{6,2},{10,14},{7,3},{11,15},{20,16},{24,... | collective-permute-start | bytes 245768 | tf_op jit(solution)/shard_map/ppermute | solution.py:174

commit v19 on v16

--- a/solution.py
+++ b/solution.py
@@ -92,22 +92,27 @@
                          jnp.concatenate([second, first], -1))
 
     low = lane * chan_half
-    high = (1 - lane) * chan_half
     x0 = take(samples, mine)
     seed = take(grads, mine)
     a0 = bf16(jax.nn.silu(f32(x0)))
 
-    def first(x0, a0, seed, own, other):
-        h1_own = conv(a0, own[0])
-        d_own = conv_t(lax.dynamic_slice_in_dim(seed, low, chan_half, 3), own[1])
-        h1 = bf16(f32(x0) + join(h1_own, conv(a0, other[0])))
-        return h1, d_own + conv_t(lax.dynamic_slice_in_dim(seed, high, chan_half, 3), other[1])
-
-    h1, d_last = on_stage(stage == 0, first, x0, a0, seed, own, other)
-    h1_r = up(0, h1)
-    d_last_r = up(0, d_last)
-
-    other, _ = lax.optimization_barrier((other, h1))
+    def first(samples, grads, own):
+        act_all = bf16(jax.nn.silu(f32(samples)))
+        own_in = lax.dynamic_slice_in_dim(samples, low, chan_half, 3)
+        h1_half = bf16(f32(own_in) + conv(act_all, own[0]))
+        d_part = conv_t(lax.dynamic_slice_in_dim(grads, low, chan_half, 3), own[1])
+        return h1_half, d_part
+
+    h1_half, d_part = on_stage(stage == 0, first, samples, grads, own)
+    straight = [(0, 1), (pipe_size - 1, pipe_size - 2)]
+    across = [(src * 2 + m, dst * 2 + 1 - m) for src, dst in straight for m in range(2)]
+    h1_s, d_s = lax.ppermute((take(h1_half, mine), take(d_part, mine)), "pipe", straight)
+    h1_c, d_c = lax.ppermute((take(h1_half, theirs), take(d_part, theirs)), ("pipe", "mp"), across)
+    h1_r = join(h1_s, h1_c)
+    d_last_r = d_s + d_c
+    h1 = h1_r
+
+    other, _ = lax.optimization_barrier((other, h1_half))
     full = jnp.where(lane == 0, jnp.concatenate([own, other], 1),
                      jnp.concatenate([other, own], 1))
     w_enc, w_dec = full[0], full[1]

time: 65.1 us -> 64 us (0.983)
  waiting for transfers between devices: 9.22 us -> 5.23 us
  local copies, waits for them, and re-layouts: 20.6 us -> 24.4 us
  matrix products: 13 us -> 9.35 us
  starting transfers between devices: 4.57 us -> 7.15 us
    ppermute x1, waiting for transfers between devices: 3.66 us -> 0.01 us  [local(): other = lax.ppermute(own, 'mp', swap)]
    ppermute x2 -> x4, starting transfers between devices: 2.76 us -> 5.34 us  [the longest x2 2.77 us: local(): lax.ppermute((take(h1_half, theirs), take(d_part, theirs)), ('pipe', 'mp'...]
    dynamic_slice x1 -> x2, local copies, waits for them, and re-layouts: 0.04 us -> 2.28 us  [take(): return lax.dynamic_slice_in_dim(v, at, per_lane, 0)]
    conv_general_dilated x4 -> x3, matrix products: 7.74 us -> 5.57 us  [conv_t(): lax.conv_general_dilated(flipped, weight, (1, 1), ((1, 1), (1, 1)), dimen...]
    cond x2 -> x5, local copies, waits for them, and re-layouts: 0.01 us -> 1.76 us  [the longest x2 1.6 us: on_stage(): return lax.cond(active, fn, idle, *args)]
    conv_general_dilated x4 -> x3, matrix products: 4.35 us -> 2.92 us  [conv(): lax.conv_general_dilated(act, weight, (1, 1), ((1, 1), (1, 1)), dimension...]
    add x1 -> x0, other arithmetic: 0.73 us -> none  [first(): d_own + conv_t(lax.dynamic_slice_in_dim(seed, high, chan_half, 3), other[1])]
    rev x4 -> x3, local copies, waits for them, and re-layouts: 1.34 us -> 0.78 us  [conv_t(): return jnp.flip(out, (1, 2))]
  transfers between devices with their start and end apart: 4 -> 6, of which waited for: 2 -> 1; matrix products, arithmetic and copies ran while one was open for 11% -> 26% of each run, Pallas kernels for 0% -> 0%
where the time goes in v19:
time: 64 us; the launch traced here: 63.6 us
  local copies, waits for them, and re-layouts  24.4 us (38%)
  blocking collectives  9.53 us (15%)
  matrix products  9.35 us (15%)
  other arithmetic  7.28 us (11%)
  starting transfers between devices  7.15 us (11%)
  waiting for transfers between devices  5.23 us (8%)
    all_gather x1, blocking collectives, local(): every = lax.all_gather(both, ('dp', 'mp'), axis=0, tiled=True)  9.53 us
    conv_general_dilated x3, matrix products, conv_t(): lax.conv_general_dilated(flipped, weight, (1, 1), ((1, 1), (1, 1)), dimen...  5.57 us
    ppermute x1, waiting for transfers between devices, local(): lax.ppermute(jnp.where(lower, c0, a_last), 'pipe', [(1, 0), (pipe_size -...  5.2 us
    reshape x1, local copies, waits for them, and re-layouts, local(): return grad.reshape(1, -1)  4.57 us
    another operation x1, local copies, waits for them, and re-layouts, local(): section_weight[0].reshape(2, chan_half, 9, channels).transpose(0, 2, 1, 3)  4.5 us
    select_n x1, other arithmetic, local(): jnp.where(lane == 0, jnp.concatenate([own, other], 1), jnp.concatenate([o...  3.6 us
    unnamed x15, local copies, waits for them, and re-layouts  3.21 us
    conv_general_dilated x3, matrix products, conv(): lax.conv_general_dilated(act, weight, (1, 1), ((1, 1), (1, 1)), dimension...  2.92 us
  transfers between devices with their start and end apart: 6, of which 1 were waited for; matrix products, arithmetic and copies ran while one was open for 26% of the time, Pallas kernels for 0%

profile of v19, /device:TPU:0, one launch (start us, length us, event | category | flops | bytes accessed | tf_op | source)
XLA Modules:
  0.0 63.6 jit_solution(11025742631350558728)
XLA Ops:
  0.0 2.7 %reshape.156 = bf16[921600]{0:T(1024)(128)(2,1)S(1)} reshape(bf16[1,2,460800]{2,1,0:T(2,128)(2,1)} %param.6) | data formatting | bytes 3686400
  2.7 4.5 %reshape_squeeze.3 = bf16[2,160,9,320]{3,2,1,0:T(8,128)(2,1)} reshape(bf16[921600]{0:T(1024)(128)(2,1)S(1)} %reshape.156) | data formatting | bytes 3686400 | tf_op jit(solution)/shard_map/reshape;squeeze | solution.py:74
  7.2 2.7 %copy.112 = bf16[2,9,160,320]{3,2,1,0:T(8,128)(2,1)S(1)} copy(bf16[2,9,160,320]{3,1,2,0:T(8,128)(2,1)} %bitcast.113) | data formatting | bytes 3686400 | tf_op jit(solution)/shard_map/transpose | solution.py:74
  9.9 0.5 collective-permute-start.4
  10.4 7.0 %conditional.1 = (bf16[4,4,16,160]{3,1,2,0:T(4,128)(2,1)}, bf16[4,4,16,160]{3,2,1,0:T(8,128)(2,1)}, f32[4,4,16,320]{3,2,1,0:T(8,128)S(1)}) conditional(s32[]{:T(128)} %convert_element_type.105, () %tuple.14, (s32[]{:T(128)}, bf16[4,4,16,320]{3,2,1,0:T(8,128)(2,1)S(1)}, bf16[2,160,3,3,320]{4,1,3,2,0:T(8,128)(2,1)S(1)}, ...), branch_computations={%region_0.1_spmd, %region_1.2_spmd} | conditional | flops 592465920 | bytes 11582946 | solution.py:52
  10.4 0.2 fusion.17
  10.6 0.2 copy.142
  10.9 0.2 fusion.6
  11.2 0.9 %convolution_select_fusion.1 = f32[4,32,3,160]{3,1,2,0:T(8,128)S(1)} fusion(bf16[2,160,3,3,320]{4,1,3,2,0:T(8,128)(2,1)S(1)} %get-tuple-element.15, bf16[4,4,8,5,320]{4,1,3,2,0:T(4,128)(2,1)S(1)} %fusion.6, pred[32,3]{0,1:T(4,128)(4,1)S(1)} %copy-done.4), kind=kOutput, calls=%fused_computation.1 | convolution fusion | flops 294973440 | bytes 1843712 | tf_op jit(solution)/shard_map/cond/branch_1_fun/conv_general_dilated | solution.py:13
  12.1 0.3 copy.109
  12.4 0.8 %fusion.16 = bf16[4,4,16,160]{3,1,2,0:T(4,128)(2,1)} fusion(f32[4,4,24,160]{3,0,2,1:T(4,128)S(1)} %bitcast.128, bf16[4,4,16,320]{3,1,2,0:T(4,128)(2,1)S(1)} %copy.113, s32[]{:T(128)S(6)} %select_n.54), kind=kLoop, calls=%fused_computation.24 | loop fusion | flops 122880 | bytes 327684 | tf_op jit(solution)/shard_map/cond/branch_1_fun/convert_element_type | solution.py:43
  13.2 1.6 %copy.139 = bf16[4,4,16,160]{3,2,1,0:T(8,128)(2,1)} copy(bf16[4,4,16,160]{3,1,2,0:T(4,128)(2,1)} %fusion.16) | data formatting | bytes 163840 | tf_op jit(solution)/shard_map/cond | solution.py:52
  14.8 0.2 copy.114
  15.0 0.2 constant_dynamic-slice_fusion
  15.3 0.2 fusion.12
  15.5 0.8 %convolution_select_fusion = f32[4,32,3,320]{3,1,2,0:T(8,128)S(1)} fusion(bf16[2,160,3,3,320]{4,1,3,2,0:T(8,128)(2,1)S(1)} %get-tuple-element.15, bf16[4,4,8,5,160]{4,1,3,2,0:T(4,128)(2,1)S(1)} %fusion.12, pred[32,3]{0,1:T(4,128)(4,1)S(1)} %copy-done.4), kind=kOutput, calls=%fused_computation | convolution fusion | flops 295034880 | bytes 1925632 | tf_op jit(solution)/shard_map/cond/branch_1_fun/conv_general_dilated | solution.py:22
  16.3 0.4 copy.111
  16.7 0.6 rev.17
  17.4 1.5 %constant_dynamic-slice_fusion.4 = (bf16[2,4,16,160]{3,2,1,0:T(8,128)(2,1)S(1)}, bf16[2,4,16,160]{3,2,1,0:T(8,128)(2,1)}) fusion(bf16[4,4,16,160]{3,2,1,0:T(8,128)(2,1)} %get-tuple-element.43, s32[]{:T(128)S(6)} %select_n.75, s32[]{:T(128)S(6)} %select_n.73), kind=kLoop, calls=%fused_computation.135 | loop fusion | bytes 163848 | tf_op jit(solution)/shard_map/dynamic_slice | solution.py:88
  18.9 1.3 %collective-permute-start = (bf16[2,4,16,160]{3,2,1,0:T(8,128)(2,1)}, bf16[2,4,16,160]{3,2,1,0:T(8,128)(2,1)S(1)}, u32[]{:S(2)}, u32[]{:S(2)}) collective-permute-start(bf16[2,4,16,160]{3,2,1,0:T(8,128)(2,1)} %get-tuple-element.50), channel_id=1, source_target_pairs={{0,4},{12,8},{1,5},{13,9},{2,6},{14,10},{3,7},{15,11},{16,20},{28,... | collective-permute-start | bytes 122888 | tf_op jit(solution)/shard_map/ppermute | solution.py:109
  20.2 1.3 %collective-permute-start.1 = (bf16[2,4,16,160]{3,2,1,0:T(8,128)(2,1)S(1)}, bf16[2,4,16,160]{3,2,1,0:T(8,128)(2,1)S(1)}, u32[]{:S(2)}, u32[]{:S(2)}) collective-permute-start(bf16[2,4,16,160]{3,2,1,0:T(8,128)(2,1)S(1)} %get-tuple-element.49), channel_id=1, source_target_pairs={{0,5},{1,4},{12,9},{13,8},{2,7},{3,6},{14,11},{15,10},{16,21},{17,... | collective-permute-start | bytes 122888 | tf_op jit(solution)/shard_map/ppermute | solution.py:110
  21.5 0.8 %constant_dynamic-slice_fusion.1 = (f32[2,4,16,320]{3,2,1,0:T(8,128)}, f32[2,4,16,320]{3,2,1,0:T(8,128)}) fusion(f32[4,4,16,320]{3,2,1,0:T(8,128)S(1)} %get-tuple-element.44, s32[]{:T(128)S(6)} %select_n.75, s32[]{:T(128)S(6)} %select_n.73), kind=kLoop, calls=%fused_computation.132 | loop fusion | bytes 655368 | tf_op jit(solution)/shard_map/dynamic_slice | solution.py:88
  22.2 1.3 %collective-permute-start.2 = (f32[2,4,16,320]{3,2,1,0:T(8,128)}, f32[2,4,16,320]{3,2,1,0:T(8,128)S(1)}, u32[]{:S(2)}, u32[]{:S(2)}) collective-permute-start(f32[2,4,16,320]{3,2,1,0:T(8,128)} %get-tuple-element.48), channel_id=1, source_target_pairs={{0,4},{12,8},{1,5},{13,9},{2,6},{14,10},{3,7},{15,11},{16,20},{28,... | collective-permute-start | bytes 491528 | tf_op jit(solution)/shard_map/ppermute | solution.py:109
  23.5 1.5 %collective-permute-start.3 = (f32[2,4,16,320]{3,2,1,0:T(8,128)}, f32[2,4,16,320]{3,2,1,0:T(8,128)S(1)}, u32[]{:S(2)}, u32[]{:S(2)}) collective-permute-start(f32[2,4,16,320]{3,2,1,0:T(8,128)} %get-tuple-element.47), channel_id=1, source_target_pairs={{0,5},{1,4},{12,9},{13,8},{2,7},{3,6},{14,11},{15,10},{16,21},{17,... | collective-permute-start | bytes 491528 | tf_op jit(solution)/shard_map/ppermute | solution.py:110
  25.2 0.1 fusion.83
  25.6 0.2 fusion.33
  25.9 3.6 %maximum_select_fusion = bf16[2,320,3,3,320]{4,1,3,2,0:T(8,128)(2,1)S(1)} fusion(bf16[2,160,3,3,320]{4,1,3,2,0:T(8,128)(2,1)} %collective-permute-done.4, bf16[2,160,3,3,320]{4,1,3,2,0:T(8,128)(2,1)S(1)} %bitcast.116, pred[]{:T(512)S(6)} %eq.7), kind=kLoop, calls=%fused_computation.28 | loop fusion | flops 16588800 | bytes 7372801 | tf_op jit(solution)/shard_map/jit(_where)/select_n | solution.py:116
  29.5 1.0 %fusion.24 = f32[4,16,3,320]{3,1,2,0:T(8,128)S(1)} fusion(bf16[2,320,3,3,320]{4,1,3,2,0:T(8,128)(2,1)S(1)} %maximum_select_fusion, bf16[4,2,8,5,320]{4,1,3,2,0:T(2,128)(2,1)S(1)} %fusion.33, pred[16,3]{0,1:T(4,128)(4,1)S(1)} %copy-done.3), kind=kOutput, calls=%fused_computation.37 | convolution fusion | flops 294973440 | bytes 2703872 | tf_op jit(solution)/shard_map/conv_general_dilated | solution.py:13
  30.7 0.1 fusion.85
  31.2 0.2 fusion.34
  31.5 1.0 %fusion.22 = f32[4,16,3,320]{3,1,2,0:T(8,128)S(1)} fusion(bf16[2,320,3,3,320]{4,1,3,2,0:T(8,128)(2,1)S(1)} %maximum_select_fusion, bf16[4,2,8,5,320]{4,1,3,2,0:T(2,128)(2,1)S(1)} %fusion.34, pred[16,3]{0,1:T(4,128)(4,1)S(1)} %copy-done.3), kind=kOutput, calls=%fused_computation.35 | convolution fusion | flops 294973440 | bytes 2703872 | tf_op jit(solution)/shard_map/conv_general_dilated | solution.py:13
  32.7 0.2 add_convert_fusion.3
  32.9 0.1 rev.22
  33.3 0.2 fusion.35
  33.6 2.4 %fusion.23 = f32[4,16,3,320]{3,1,2,0:T(8,128)S(1)} fusion(bf16[2,320,3,3,320]{4,1,3,2,0:T(8,128)(2,1)} %copy-done, bf16[4,2,8,5,320]{4,1,3,2,0:T(2,128)(2,1)S(1)} %fusion.35, pred[16,3]{0,1:T(4,128)(4,1)S(1)} %copy-done.3), kind=kOutput, calls=%fused_computation.36 | convolution fusion | flops 294973440 | bytes 2662448 | tf_op jit(solution)/shard_map/conv_general_dilated | solution.py:22
  36.4 0.1 rev.24
  36.8 0.2 fusion.36
  37.0 2.4 %fusion.25 = f32[4,16,3,320]{3,1,2,0:T(8,128)S(1)} fusion(bf16[2,320,3,3,320]{4,1,3,2,0:T(8,128)(2,1)} %copy-done, bf16[4,2,8,5,320]{4,1,3,2,0:T(2,128)(2,1)S(1)} %fusion.36, pred[16,3]{0,1:T(4,128)(4,1)S(1)} %copy-done.3), kind=kOutput, calls=%fused_computation.38 | convolution fusion | flops 294973440 | bytes 2662448 | tf_op jit(solution)/shard_map/conv_general_dilated | solution.py:22
  39.7 0.3 fusion.74
  40.0 1.3 %collective-permute-start.5 = (bf16[2,4,16,320]{3,2,1,0:T(8,128)(2,1)S(1)}, bf16[2,4,16,320]{3,2,1,0:T(8,128)(2,1)S(1)}, u32[]{:S(2)}, u32[]{:S(2)}) collective-permute-start(bf16[2,4,16,320]{3,2,1,0:T(8,128)(2,1)S(1)} %fusion.74), channel_id=1, source_target_pairs={{4,0},{8,12},{5,1},{9,13},{6,2},{10,14},{7,3},{11,15},{20,16},{24,... | collective-permute-start | bytes 245768 | tf_op jit(solution)/shard_map/ppermute | solution.py:174
  41.3 0.1 fusion.55
  41.4 5.2 %collective-permute-done.5 = bf16[2,4,16,320]{3,2,1,0:T(8,128)(2,1)S(1)} collective-permute-done((bf16[2,4,16,320]{3,2,1,0:T(8,128)(2,1)S(1)}, bf16[2,4,16,320]{3,2,1,0:T(8,128)(2,1)S(1)}, u32[]{:S(2)}, u32[]{:S(2)}) %collective-permute-start.5) | collective-permute-done | bytes 81952 | tf_op jit(solution)/shard_map/ppermute | solution.py:174
  46.6 0.2 fusion.81
  46.9 9.5 %all_gather.3 = bf16[8,4,16,640]{3,2,1,0:T(8,128)(2,1)S(1)} all-gather(bf16[2,4,16,640]{3,2,1,0:T(8,128)(2,1)S(1)} %pad_maximum_fusion), channel_id=1, replica_groups=mesh['groups'=2,'pipe'=4,'dp'=2,'mp'=2] {'dp','mp'}, dimensions={0}, use_global_device_ids=true | all-gather | bytes 819200 | tf_op jit(solution)/shard_map/all_gather | solution.py:182
  56.5 0.2 constant_dynamic-slice_fusion.3
  56.6 0.9 %fusion.30 = f32[160,3,3,320]{3,0,2,1:T(8,128)S(1)} fusion(bf16[8,4,16,320]{3,2,1,0:T(8,128)(2,1)S(1)} %slice.44, bf16[8,4,16,160]{3,2,1,0:T(8,128)(2,1)S(1)} %constant_dynamic-slice_fusion.3), kind=kOutput, calls=%fused_computation.44 | convolution fusion | flops 376832000 | bytes 2334720 | tf_op jit(solution)/shard_map/conv_general_dilated | solution.py:31
  57.5 1.5 %copy.137 = f32[160,3,3,320]{3,2,1,0:T(4,128)S(1)} copy(f32[160,3,3,320]{3,0,2,1:T(8,128)S(1)} %fusion.30) | data formatting | bytes 3686400 | tf_op jit(solution)/shard_map/conv_general_dilated | solution.py:31
  59.0 4.6 %reshape.95 = f32[1,460800]{1,0:T(1,128)} reshape(f32[160,3,3,320]{3,2,1,0:T(4,128)S(1)} %copy.137) | data formatting | bytes 3686400 | tf_op jit(solution)/shard_map/reshape | solution.py:186
  (53 shorter events, 2.9 us)
Async XLA Ops:
  7.2 3.2 %copy-start.1 = (bf16[1,2,2,4,16,320]{5,4,3,2,1,0:T(8,128)(2,1)S(1)}, bf16[1,2,2,4,16,320]{5,4,3,2,1,0:T(8,128)(2,1)}, u32[]{:S(2)}) copy-start(bf16[1,2,2,4,16,320]{5,4,3,2,1,0:T(8,128)(2,1)} %param.5) | copy-start | bytes 491524
  7.2 3.2 %copy-start.2 = (bf16[1,2,2,4,16,320]{5,4,3,2,1,0:T(8,128)(2,1)S(1)}, bf16[1,2,2,4,16,320]{5,4,3,2,1,0:T(8,128)(2,1)}, u32[]{:S(2)}) copy-start(bf16[1,2,2,4,16,320]{5,4,3,2,1,0:T(8,128)(2,1)} %param.7) | copy-start | bytes 491524
  9.9 16.0 %collective-permute-start.4 = (bf16[2,160,3,3,320]{4,1,3,2,0:T(8,128)(2,1)S(1)}, bf16[2,160,3,3,320]{4,1,3,2,0:T(8,128)(2,1)}, u32[]{:S(2)}, u32[]{:S(2)}) collective-permute-start(bf16[2,160,3,3,320]{4,1,3,2,0:T(8,128)(2,1)S(1)} %bitcast.114), channel_id=1, source_target_pairs={{0,1},{1,0},{2,3},{3,2},{4,5},{5,4},{6,7},{7,6},{8,9},{9,8},{10,11... | collective-permute-start | bytes 5529608 | tf_op jit(solution)/shard_map/ppermute | solution.py:77
  10.4 0.8 %copy-start.4 = (pred[32,3]{0,1:T(4,128)(4,1)S(1)}, pred[32,3]{0,1:T(4,128)(4,1)}, u32[]{:S(2)}) copy-start(pred[32,3]{0,1:T(4,128)(4,1)} %constant.75) | copy-start | bytes 292 | tf_op jit(solution)/shard_map/cond
  18.9 6.3 %collective-permute-start = (bf16[2,4,16,160]{3,2,1,0:T(8,128)(2,1)}, bf16[2,4,16,160]{3,2,1,0:T(8,128)(2,1)S(1)}, u32[]{:S(2)}, u32[]{:S(2)}) collective-permute-start(bf16[2,4,16,160]{3,2,1,0:T(8,128)(2,1)} %get-tuple-element.50), channel_id=1, source_target_pairs={{0,4},{12,8},{1,5},{13,9},{2,6},{14,10},{3,7},{15,11},{16,20},{28,... | collective-permute-start | bytes 122888 | tf_op jit(solution)/shard_map/ppermute | solution.py:109
  20.2 5.0 %collective-permute-start.1 = (bf16[2,4,16,160]{3,2,1,0:T(8,128)(2,1)S(1)}, bf16[2,4,16,160]{3,2,1,0:T(8,128)(2,1)S(1)}, u32[]{:S(2)}, u32[]{:S(2)}) collective-permute-start(bf16[2,4,16,160]{3,2,1,0:T(8,128)(2,1)S(1)} %get-tuple-element.49), channel_id=1, source_target_pairs={{0,5},{1,4},{12,9},{13,8},{2,7},{3,6},{14,11},{15,10},{16,21},{17,... | collective-permute-start | bytes 122888 | tf_op jit(solution)/shard_map/ppermute | solution.py:110
  22.2 10.4 %collective-permute-start.2 = (f32[2,4,16,320]{3,2,1,0:T(8,128)}, f32[2,4,16,320]{3,2,1,0:T(8,128)S(1)}, u32[]{:S(2)}, u32[]{:S(2)}) collective-permute-start(f32[2,4,16,320]{3,2,1,0:T(8,128)} %get-tuple-element.48), channel_id=1, source_target_pairs={{0,4},{12,8},{1,5},{13,9},{2,6},{14,10},{3,7},{15,11},{16,20},{28,... | collective-permute-start | bytes 491528 | tf_op jit(solution)/shard_map/ppermute | solution.py:109
  23.5 9.2 %collective-permute-start.3 = (f32[2,4,16,320]{3,2,1,0:T(8,128)}, f32[2,4,16,320]{3,2,1,0:T(8,128)S(1)}, u32[]{:S(2)}, u32[]{:S(2)}) collective-permute-start(f32[2,4,16,320]{3,2,1,0:T(8,128)} %get-tuple-element.47), channel_id=1, source_target_pairs={{0,5},{1,4},{12,9},{13,8},{2,7},{3,6},{14,11},{15,10},{16,21},{17,... | collective-permute-start | bytes 491528 | tf_op jit(solution)/shard_map/ppermute | solution.py:110
  25.8 3.6 %copy-start.3 = (pred[16,3]{0,1:T(4,128)(4,1)S(1)}, pred[16,3]{0,1:T(4,128)(4,1)}, u32[]{:S(2)}) copy-start(pred[16,3]{0,1:T(4,128)(4,1)} %constant.71) | copy-start | bytes 148
  29.5 2.0 %copy-start = (bf16[2,320,3,3,320]{4,1,3,2,0:T(8,128)(2,1)}, bf16[2,320,3,3,320]{4,1,3,2,0:T(8,128)(2,1)S(1)}, u32[]{:S(2)}) copy-start(bf16[2,320,3,3,320]{4,1,3,2,0:T(8,128)(2,1)S(1)} %maximum_select_fusion) | copy-start | bytes 11059204
  40.0 6.7 %collective-permute-start.5 = (bf16[2,4,16,320]{3,2,1,0:T(8,128)(2,1)S(1)}, bf16[2,4,16,320]{3,2,1,0:T(8,128)(2,1)S(1)}, u32[]{:S(2)}, u32[]{:S(2)}) collective-permute-start(bf16[2,4,16,320]{3,2,1,0:T(8,128)(2,1)S(1)} %fusion.74), channel_id=1, source_target_pairs={{4,0},{8,12},{5,1},{9,13},{6,2},{10,14},{7,3},{11,15},{20,16},{24,... | collective-permute-start | bytes 245768 | tf_op jit(solution)/shard_map/ppermute | solution.py:174

commit v20 on v18

--- a/solution.py
+++ b/solution.py
@@ -25,6 +25,14 @@
         preferred_element_type=jnp.float32,
     )
     return jnp.flip(out, (1, 2))
+
+
+def conv_flipped(flipped, weight):
+    return lax.conv_general_dilated(
+        flipped, weight, (1, 1), ((1, 1), (1, 1)),
+        dimension_numbers=("NHWC", "IHWO", "NHWC"),
+        preferred_element_type=jnp.float32,
+    )
 
 
 def weight_grad(act, cot):
@@ -98,13 +106,17 @@
     a0 = bf16(jax.nn.silu(f32(x0)))
 
     def first_own(a0, seed, own):
-        return conv(a0, own[0]), conv_t(lax.dynamic_slice_in_dim(seed, low, chan_half, 3), own[1])
+        flipped = jnp.flip(seed, (1, 2))
+        d_own = conv_flipped(lax.dynamic_slice_in_dim(flipped, low, chan_half, 3), own[1])
+        return conv(a0, own[0]), d_own
 
     def first_h1(x0, a0, other_enc, h1_own):
         return bf16(f32(x0) + join(h1_own, conv(a0, other_enc)))
 
     def first_d(seed, other_dec, d_own):
-        return d_own + conv_t(lax.dynamic_slice_in_dim(seed, high, chan_half, 3), other_dec)
+        flipped = jnp.flip(seed, (1, 2))
+        d_other = conv_flipped(lax.dynamic_slice_in_dim(flipped, high, chan_half, 3), other_dec)
+        return jnp.flip(d_own + d_other, (1, 2))
 
     h1_own, d_own = on_stage(stage == 0, first_own, a0, seed, own)
     h1 = on_stage(stage == 0, first_h1, x0, a0, other[0], h1_own)

time: 61.9 us -> 61.1 us (0.987)
  waiting for transfers between devices: 5.19 us -> 6.18 us
  other arithmetic: 7.13 us -> 6.47 us
    conv_general_dilated x4 -> x2, matrix products: 7.04 us -> 4.76 us  [conv_t(): lax.conv_general_dilated(flipped, weight, (1, 1), ((1, 1), (1, 1)), dimen...]
    conv_general_dilated x0 -> x2, matrix products: none -> 2.28 us  [conv_flipped(): lax.conv_general_dilated(flipped, weight, (1, 1), ((1, 1), (1, 1)), dimen...]
    ppermute x1, waiting for transfers between devices: 0.1 us -> 1.08 us  [local(): other = lax.ppermute(own, 'mp', swap)]
    rev x4 -> x2, local copies, waits for them, and re-layouts: 1.34 us -> 0.67 us  [conv_t(): return jnp.flip(out, (1, 2))]
    add x1, other arithmetic: 0.73 us -> 0.06 us  [first_d(): return jnp.flip(d_own + d_other, (1, 2))]
    conv_general_dilated x4, matrix products: 5.03 us -> 4.36 us  [conv(): lax.conv_general_dilated(act, weight, (1, 1), ((1, 1), (1, 1)), dimension...]
  transfers between devices with their start and end apart: 4 -> 4, of which waited for: 2 -> 2; matrix products, arithmetic and copies ran while one was open for 22% -> 20% of each run, Pallas kernels for 0% -> 0%
where the time goes in v20:
time: 61.1 us; the launch traced here: 60.7 us
  local copies, waits for them, and re-layouts  20.8 us (34%)
  matrix products  12.3 us (20%)
  blocking collectives  8.79 us (14%)
  other arithmetic  6.47 us (11%)
  waiting for transfers between devices  6.18 us (10%)
  starting transfers between devices  5.49 us (9%)
    all_gather x1, blocking collectives, local(): every = lax.all_gather(both, ('dp', 'mp'), axis=0, tiled=True)  8.79 us
    ppermute x1, waiting for transfers between devices, local(): lax.ppermute(jnp.where(lower, c0, a_last), 'pipe', [(1, 0), (pipe_size -...  5.09 us
    conv_general_dilated x2, matrix products, conv_t(): lax.conv_general_dilated(flipped, weight, (1, 1), ((1, 1), (1, 1)), dimen...  4.76 us
    reshape x1, local copies, waits for them, and re-layouts, local(): return grad.reshape(1, -1)  4.57 us
    another operation x1, local copies, waits for them, and re-layouts, local(): section_weight[0].reshape(2, chan_half, 9, channels).transpose(0, 2, 1, 3)  4.47 us
    conv_general_dilated x4, matrix products, conv(): lax.conv_general_dilated(act, weight, (1, 1), ((1, 1), (1, 1)), dimension...  4.36 us
    ppermute x2, starting transfers between devices, up(): return lax.ppermute(v, 'pipe', pairs)  3.68 us
    select_n x1, other arithmetic, local(): jnp.where(lane == 0, jnp.concatenate([own, other], 1), jnp.concatenate([o...  3.6 us
  transfers between devices with their start and end apart: 4, of which 2 were waited for; matrix products, arithmetic and copies ran while one was open for 20% of the time, Pallas kernels for 0%

profile of v20, /device:TPU:0, one launch (start us, length us, event | category | flops | bytes accessed | tf_op | source)
XLA Modules:
  0.0 60.7 jit_solution(1006946981016055921)
XLA Ops:
  0.0 2.7 %reshape.100 = bf16[921600]{0:T(1024)(128)(2,1)S(1)} reshape(bf16[1,2,460800]{2,1,0:T(2,128)(2,1)} %param.10) | data formatting | bytes 3686400
  2.7 4.5 %reshape_squeeze.3 = bf16[2,160,9,320]{3,2,1,0:T(8,128)(2,1)} reshape(bf16[921600]{0:T(1024)(128)(2,1)S(1)} %reshape.100) | data formatting | bytes 3686400 | tf_op jit(solution)/shard_map/reshape;squeeze | solution.py:82
  7.1 2.7 %copy.72 = bf16[2,9,160,320]{3,2,1,0:T(8,128)(2,1)S(1)} copy(bf16[2,9,160,320]{3,1,2,0:T(8,128)(2,1)} %bitcast.129) | data formatting | bytes 3686400 | tf_op jit(solution)/shard_map/transpose | solution.py:82
  9.8 0.5 collective-permute-start
  10.6 0.1 fusion.67
  10.7 2.6 %conditional.3 = (f32[2,4,16,160]{3,1,2,0:T(4,128)S(1)}, f32[2,4,16,320]{3,1,2,0:T(4,128)S(1)}) conditional(s32[]{:T(128)} %convert_element_type.83, () %tuple.30, (bf16[2,160,3,3,320]{4,1,3,2,0:T(8,128)(2,1)S(1)}, bf16[2,4,16,320]{3,1,2,0:T(4,128)(2,1)S(1)}, bf16[2,4,16,320]{3,1,2,0:T(4,128)(2,1)S(1)}, s32[]{:T(128)}) %tuple.54), branch_computations={%region_0.1_spmd, %region_1.2_spmd} | conditional | flops 295925760 | bytes 5914902 | solution.py:60
  10.9 0.2 dynamic-slice_bitcast_fusion
  11.2 0.2 fusion.7
  11.7 0.2 fusion.4
  11.9 0.5 convolution_select_fusion.1
  12.5 0.5 convolution_select_fusion
  13.1 0.1 copy.64
  13.3 1.1 %collective-permute-done = bf16[2,160,3,3,320]{4,1,3,2,0:T(8,128)(2,1)} collective-permute-done((bf16[2,160,3,3,320]{4,1,3,2,0:T(8,128)(2,1)S(1)}, bf16[2,160,3,3,320]{4,1,3,2,0:T(8,128)(2,1)}, u32[]{:S(2)}, u32[]{:S(2)}) %collective-permute-start) | collective-permute-done | bytes 1843232 | tf_op jit(solution)/shard_map/ppermute | solution.py:85
  14.4 2.7 %conditional.4 = (bf16[2,4,16,320]{3,1,2,0:T(4,128)(2,1)S(1)}) conditional(s32[]{:T(128)} %convert_element_type.83, () %tuple.29, (bf16[2,4,16,320]{3,1,2,0:T(4,128)(2,1)S(1)}, s32[]{:T(128)}, bf16[2,160,3,3,320]{4,1,3,2,0:T(8,128)(2,1)}, bf16[2,4,16,320]{3,1,2,0:T(4,128)(2,1)S(1)}, f32[2,4,16,160]{3,1,2,0:T(4,128)S(1)}) %tuple.32), branch_computations={%region_2.3_spmd, %region_3.4_spmd} | conditional | flops 148346880 | bytes 3082772 | solution.py:60
  14.7 0.2 fusion.12
  14.9 1.8 %convolution_select_fusion.2 = f32[4,16,3,160]{3,1,2,0:T(8,128)S(1)} fusion(bf16[2,160,3,3,320]{4,1,3,2,0:T(8,128)(2,1)} %get-tuple-element.63, bf16[4,2,8,5,320]{4,1,3,2,0:T(2,128)(2,1)S(1)} %fusion.12, pred[16,3]{0,1:T(4,128)(4,1)} %constant.95), kind=kOutput, calls=%fused_computation.18 | convolution fusion | flops 147486720 | bytes 1434112 | tf_op jit(solution)/shard_map/cond/branch_1_fun/conv_general_dilated | solution.py:13
  16.7 0.1 copy.68
  16.9 0.2 fusion.16
  17.1 2.2 %collective-permute-start.1 = (bf16[2,4,16,320]{3,1,2,0:T(4,128)(2,1)S(1)}, bf16[2,4,16,320]{3,1,2,0:T(4,128)(2,1)S(1)}, u32[]{:S(2)}, u32[]{:S(2)}) collective-permute-start(bf16[2,4,16,320]{3,1,2,0:T(4,128)(2,1)S(1)} %get-tuple-element.119), channel_id=1, source_target_pairs={{0,4},{12,8},{1,5},{13,9},{2,6},{14,10},{3,7},{15,11},{16,20},{28,... | collective-permute-start | bytes 245768 | tf_op jit(solution)/shard_map/ppermute | solution.py:89
  19.3 3.0 %conditional.5 = (f32[2,4,16,320]{3,1,2,0:T(4,128)S(1)}) conditional(s32[]{:T(128)} %convert_element_type.83, () %tuple.33, (bf16[2,4,16,320]{3,1,2,0:T(4,128)(2,1)S(1)}, s32[]{:T(128)}, bf16[2,160,3,3,320]{4,1,3,2,0:T(8,128)(2,1)}, f32[2,4,16,320]{3,1,2,0:T(4,128)S(1)}) %tuple.34), branch_computations={%region_4.5_spmd, %region_5.6_spmd} | conditional | flops 147865600 | bytes 3548744 | solution.py:60
  19.5 0.1 dynamic-slice_bitcast_fusion.1
  19.8 0.2 fusion.20
  20.0 1.8 %convolution_select_fusion.3 = f32[4,16,3,320]{3,1,2,0:T(8,128)S(1)} fusion(bf16[2,160,3,3,320]{4,1,3,2,0:T(8,128)(2,1)} %get-tuple-element.67, bf16[4,2,8,5,160]{4,1,3,2,0:T(2,128)(2,1)S(1)} %fusion.20, pred[16,3]{0,1:T(4,128)(4,1)} %constant.94), kind=kOutput, calls=%fused_computation.30 | convolution fusion | flops 147517440 | bytes 1454592 | tf_op jit(solution)/shard_map/cond/branch_1_fun/conv_general_dilated | solution.py:31
  21.8 0.1 copy.70
  22.0 0.3 rev.20
  22.3 1.5 %collective-permute-start.2 = (f32[2,4,16,320]{3,1,2,0:T(4,128)S(1)}, f32[2,4,16,320]{3,1,2,0:T(4,128)S(1)}, u32[]{:S(2)}, u32[]{:S(2)}) collective-permute-start(f32[2,4,16,320]{3,1,2,0:T(4,128)S(1)} %get-tuple-element.120), channel_id=1, source_target_pairs={{0,4},{12,8},{1,5},{13,9},{2,6},{14,10},{3,7},{15,11},{16,20},{28,... | collective-permute-start | bytes 491528 | tf_op jit(solution)/shard_map/ppermute | solution.py:89
  23.8 3.6 %maximum_select_fusion.1 = bf16[2,320,3,3,320]{4,1,3,2,0:T(8,128)(2,1)S(1)} fusion(bf16[2,160,3,3,320]{4,1,3,2,0:T(8,128)(2,1)} %collective-permute-done, bf16[2,160,3,3,320]{4,1,3,2,0:T(8,128)(2,1)S(1)} %bitcast.132, pred[]{:T(512)S(6)} %eq.12), kind=kLoop, calls=%fused_computation.40 | loop fusion | flops 16588800 | bytes 7372801 | tf_op jit(solution)/shard_map/jit(_where)/select_n | solution.py:128
  27.7 1.0 %fusion.29 = f32[4,16,3,320]{3,1,2,0:T(8,128)S(1)} fusion(bf16[2,320,3,3,320]{4,1,3,2,0:T(8,128)(2,1)S(1)} %maximum_select_fusion.1, bf16[4,2,7,2,320]{4,2,1,3,0:T(8,128)(2,1)S(1)} %slice.51, bf16[4,2,8,3,320]{4,2,1,3,0:T(8,128)(2,1)S(1)} %copy.79, pred[16,3]{0,1:T(4,128)(4,1)S(1)} %copy-done.3), kind=kOutput, calls=%fused_computation.49 | convolution fusion | flops 295587840 | bytes 2703872 | tf_op jit(solution)/shard_map/conv_general_dilated | solution.py:13
  28.8 0.1 fusion.71
  29.1 1.0 %fusion.27 = f32[4,16,3,320]{3,1,2,0:T(8,128)S(1)} fusion(bf16[2,320,3,3,320]{4,1,3,2,0:T(8,128)(2,1)S(1)} %maximum_select_fusion.1, bf16[4,2,7,2,320]{4,2,1,3,0:T(8,128)(2,1)S(1)} %slice.54, bf16[4,2,8,3,320]{4,2,1,3,0:T(8,128)(2,1)S(1)} %copy.82, pred[16,3]{0,1:T(4,128)(4,1)S(1)} %copy-done.3), kind=kOutput, calls=%fused_computation.47 | convolution fusion | flops 295587840 | bytes 2703872 | tf_op jit(solution)/shard_map/conv_general_dilated | solution.py:13
  30.3 0.2 add_convert_fusion.3
  30.5 0.3 rev.25
  30.9 2.4 %fusion.28 = f32[4,16,3,320]{3,1,2,0:T(8,128)S(1)} fusion(bf16[2,320,3,3,320]{4,1,3,2,0:T(8,128)(2,1)} %copy-done, bf16[4,2,7,2,320]{4,2,1,3,0:T(8,128)(2,1)S(1)} %slice.57, bf16[4,2,8,3,320]{4,2,1,3,0:T(8,128)(2,1)S(1)} %copy.85, pred[16,3]{0,1:T(4,128)(4,1)S(1)} %copy-done.3), kind=kOutput, calls=%fused_computation.48 | convolution fusion | flops 295587840 | bytes 2652208 | tf_op jit(solution)/shard_map/conv_general_dilated | solution.py:22
  33.5 0.3 rev.26
  33.8 0.2 add_convert_fusion.1
  34.0 0.3 rev.27
  34.5 2.4 %fusion.30 = f32[4,16,3,320]{3,1,2,0:T(8,128)S(1)} fusion(bf16[2,320,3,3,320]{4,1,3,2,0:T(8,128)(2,1)} %copy-done, bf16[4,2,7,2,320]{4,2,1,3,0:T(8,128)(2,1)S(1)} %slice.59, bf16[4,2,8,3,320]{4,2,1,3,0:T(8,128)(2,1)S(1)} %copy.88, pred[16,3]{0,1:T(4,128)(4,1)S(1)} %copy-done.3), kind=kOutput, calls=%fused_computation.50 | convolution fusion | flops 295587840 | bytes 2652208 | tf_op jit(solution)/shard_map/conv_general_dilated | solution.py:22
  37.0 0.3 rev.28
  37.3 0.3 fusion.90
  37.7 1.3 %collective-permute-start.3 = (bf16[2,4,16,320]{3,1,2,0:T(4,128)(2,1)S(1)}, bf16[2,4,16,320]{3,1,2,0:T(4,128)(2,1)S(1)}, u32[]{:S(2)}, u32[]{:S(2)}) collective-permute-start(bf16[2,4,16,320]{3,1,2,0:T(4,128)(2,1)S(1)} %fusion.90), channel_id=1, source_target_pairs={{4,0},{8,12},{5,1},{9,13},{6,2},{10,14},{7,3},{11,15},{20,16},{24,... | collective-permute-start | bytes 245768 | tf_op jit(solution)/shard_map/ppermute | solution.py:186
  39.1 5.1 %collective-permute-done.3 = bf16[2,4,16,320]{3,1,2,0:T(4,128)(2,1)S(1)} collective-permute-done((bf16[2,4,16,320]{3,1,2,0:T(4,128)(2,1)S(1)}, bf16[2,4,16,320]{3,1,2,0:T(4,128)(2,1)S(1)}, u32[]{:S(2)}, u32[]{:S(2)}) %collective-permute-start.3) | collective-permute-done | bytes 81952 | tf_op jit(solution)/shard_map/ppermute | solution.py:186
  44.2 0.4 fusion.97
  44.6 0.1 pad_maximum_fusion
  44.8 8.8 %all_gather.3 = bf16[8,4,16,640]{3,2,1,0:T(8,128)(2,1)S(1)} all-gather(bf16[2,4,16,640]{3,2,1,0:T(8,128)(2,1)S(1)} %copy.90), channel_id=1, replica_groups=mesh['groups'=2,'pipe'=4,'dp'=2,'mp'=2] {'dp','mp'}, dimensions={0}, use_global_device_ids=true | all-gather | bytes 819200 | tf_op jit(solution)/shard_map/all_gather | solution.py:194
  53.6 0.2 constant_dynamic-slice_fusion
  53.8 0.9 %fusion.35 = f32[160,3,3,320]{3,0,2,1:T(8,128)S(1)} fusion(bf16[8,4,16,320]{3,2,1,0:T(8,128)(2,1)S(1)} %slice.61, bf16[8,4,16,160]{3,2,1,0:T(8,128)(2,1)S(1)} %constant_dynamic-slice_fusion), kind=kOutput, calls=%fused_computation.56 | convolution fusion | flops 376832000 | bytes 2334720 | tf_op jit(solution)/shard_map/conv_general_dilated | solution.py:39
  54.6 1.5 %copy.93 = f32[160,3,3,320]{3,2,1,0:T(4,128)S(1)} copy(f32[160,3,3,320]{3,0,2,1:T(8,128)S(1)} %fusion.35) | data formatting | bytes 3686400 | tf_op jit(solution)/shard_map/conv_general_dilated | solution.py:39
  56.2 4.6 %reshape.19 = f32[1,460800]{1,0:T(1,128)} reshape(f32[160,3,3,320]{3,2,1,0:T(4,128)S(1)} %copy.93) | data formatting | bytes 3686400 | tf_op jit(solution)/shard_map/reshape | solution.py:198
  (57 shorter events, 2.8 us)
Async XLA Ops:
  7.1 3.2 %copy-start.1 = (bf16[1,2,2,4,16,320]{5,4,3,2,1,0:T(8,128)(2,1)S(1)}, bf16[1,2,2,4,16,320]{5,4,3,2,1,0:T(8,128)(2,1)}, u32[]{:S(2)}) copy-start(bf16[1,2,2,4,16,320]{5,4,3,2,1,0:T(8,128)(2,1)} %param.9) | copy-start | bytes 491524
  7.1 3.3 %copy-start.2 = (bf16[1,2,2,4,16,320]{5,4,3,2,1,0:T(8,128)(2,1)S(1)}, bf16[1,2,2,4,16,320]{5,4,3,2,1,0:T(8,128)(2,1)}, u32[]{:S(2)}) copy-start(bf16[1,2,2,4,16,320]{5,4,3,2,1,0:T(8,128)(2,1)} %param.11) | copy-start | bytes 491524
  9.8 4.6 %collective-permute-start = (bf16[2,160,3,3,320]{4,1,3,2,0:T(8,128)(2,1)S(1)}, bf16[2,160,3,3,320]{4,1,3,2,0:T(8,128)(2,1)}, u32[]{:S(2)}, u32[]{:S(2)}) collective-permute-start(bf16[2,160,3,3,320]{4,1,3,2,0:T(8,128)(2,1)S(1)} %bitcast.130), channel_id=1, source_target_pairs={{0,1},{1,0},{2,3},{3,2},{4,5},{5,4},{6,7},{7,6},{8,9},{9,8},{10,11... | collective-permute-start | bytes 5529608 | tf_op jit(solution)/shard_map/ppermute | solution.py:85
  10.7 1.2 %copy-start.4 = (pred[16,3]{0,1:T(4,128)(4,1)S(1)}, pred[16,3]{0,1:T(4,128)(4,1)}, u32[]{:S(2)}) copy-start(pred[16,3]{0,1:T(4,128)(4,1)} %constant.96) | copy-start | bytes 148 | tf_op jit(solution)/shard_map/cond
  17.1 10.3 %collective-permute-start.1 = (bf16[2,4,16,320]{3,1,2,0:T(4,128)(2,1)S(1)}, bf16[2,4,16,320]{3,1,2,0:T(4,128)(2,1)S(1)}, u32[]{:S(2)}, u32[]{:S(2)}) collective-permute-start(bf16[2,4,16,320]{3,1,2,0:T(4,128)(2,1)S(1)} %get-tuple-element.119), channel_id=1, source_target_pairs={{0,4},{12,8},{1,5},{13,9},{2,6},{14,10},{3,7},{15,11},{16,20},{28,... | collective-permute-start | bytes 245768 | tf_op jit(solution)/shard_map/ppermute | solution.py:89
  22.3 5.4 %copy-start.3 = (pred[16,3]{0,1:T(4,128)(4,1)S(1)}, pred[16,3]{0,1:T(4,128)(4,1)}, u32[]{:S(2)}) copy-start(pred[16,3]{0,1:T(4,128)(4,1)} %constant.90) | copy-start | bytes 148
  22.3 8.0 %collective-permute-start.2 = (f32[2,4,16,320]{3,1,2,0:T(4,128)S(1)}, f32[2,4,16,320]{3,1,2,0:T(4,128)S(1)}, u32[]{:S(2)}, u32[]{:S(2)}) collective-permute-start(f32[2,4,16,320]{3,1,2,0:T(4,128)S(1)} %get-tuple-element.120), channel_id=1, source_target_pairs={{0,4},{12,8},{1,5},{13,9},{2,6},{14,10},{3,7},{15,11},{16,20},{28,... | collective-permute-start | bytes 491528 | tf_op jit(solution)/shard_map/ppermute | solution.py:89
  27.4 2.7 %copy-start = (bf16[2,320,3,3,320]{4,1,3,2,0:T(8,128)(2,1)}, bf16[2,320,3,3,320]{4,1,3,2,0:T(8,128)(2,1)S(1)}, u32[]{:S(2)}) copy-start(bf16[2,320,3,3,320]{4,1,3,2,0:T(8,128)(2,1)S(1)} %maximum_select_fusion.1) | copy-start | bytes 11059204
  37.7 6.5 %collective-permute-start.3 = (bf16[2,4,16,320]{3,1,2,0:T(4,128)(2,1)S(1)}, bf16[2,4,16,320]{3,1,2,0:T(4,128)(2,1)S(1)}, u32[]{:S(2)}, u32[]{:S(2)}) collective-permute-start(bf16[2,4,16,320]{3,1,2,0:T(4,128)(2,1)S(1)} %fusion.90), channel_id=1, source_target_pairs={{4,0},{8,12},{5,1},{9,13},{6,2},{10,14},{7,3},{11,15},{20,16},{24,... | collective-permute-start | bytes 245768 | tf_op jit(solution)/shard_map/ppermute | solution.py:186

commit v21 on v20

--- a/solution.py
+++ b/solution.py
@@ -157,31 +157,34 @@
     u_last = f32(current) + f32(h1_r)
     a_last = bf16(jax.nn.silu(u_last))
     b_last = d_last_r * silu_slope(u_last)
-    skip = {1: bf16(b_last)}
+    def flip(v):
+        return jnp.flip(v, (1, 2))
+
+    skip_f = {1: flip(bf16(b_last))}
     cot = bf16(f32(seed) + b_last)
+    cot_f = flip(cot)
 
     for t in range(1, half):
         if t > 1:
             cot = up(t - 1, cot)
+            cot_f = flip(cot)
         dec_c[t] = cot
-        d = conv_t(cot, w_dec)
-        b = d * silu_slope(dec_u[t])
-        g = bf16(f32(cot) + b)
+        b_f = conv_flipped(cot_f, w_dec) * flip(silu_slope(dec_u[t]))
+        g_f = bf16(f32(cot_f) + b_f)
         if t < half - 1:
-            skip[t + 1] = bf16(b)
-            cot = g
+            skip_f[t + 1] = bf16(b_f)
+            cot = flip(g_f)
         else:
-            cot = bf16(f32(g) + b)
+            cot_f = bf16(f32(g_f) + b_f)
 
     enc_c = {}
     for t in range(half - 1, 0, -1):
         if t < half - 1:
-            cot = bf16(f32(down(t + 1, cot)) + f32(skip[t + 1]))
-        enc_c[t] = cot
-        d = conv_t(cot, w_enc)
-        b = d * silu_slope(f32(enc_in[t]))
-        cot = bf16(f32(cot) + b)
-    c0 = bf16(f32(cot) + f32(skip[1]))
+            cot_f = bf16(f32(flip(down(t + 1, flip(cot_f)))) + f32(skip_f[t + 1]))
+        enc_c[t] = flip(cot_f)
+        b_f = conv_flipped(cot_f, w_enc) * flip(silu_slope(f32(enc_in[t])))
+        cot_f = bf16(f32(cot_f) + b_f)
+    c0 = flip(bf16(f32(cot_f) + f32(skip_f[1])))
 
     sent = lax.ppermute(jnp.where(lower, c0, a_last), "pipe", [(1, 0), (pipe_size - 2, pipe_size - 1)])
     acts_lo = jnp.stack([a0] + [enc_act[t] for t in range(1, half)])

time: 61.1 us -> 64.5 us (1.056)
  matrix products: 12.3 us -> 14.1 us
  other arithmetic: 6.47 us -> 7.84 us
    conv_general_dilated x2 -> x0, matrix products: 4.76 us -> none  [conv_t(): lax.conv_general_dilated(flipped, weight, (1, 1), ((1, 1), (1, 1)), dimen...]
    conv_general_dilated x4, matrix products: 4.36 us -> 7.66 us  [conv(): lax.conv_general_dilated(act, weight, (1, 1), ((1, 1), (1, 1)), dimension...]
    conv_general_dilated x2 -> x4, matrix products: 2.28 us -> 5.57 us  [conv_flipped(): lax.conv_general_dilated(flipped, weight, (1, 1), ((1, 1), (1, 1)), dimen...]
    select_n x1, other arithmetic: 3.6 us -> 4.95 us  [local(): jnp.where(lane == 0, jnp.concatenate([own, other], 1), jnp.concatenate([o...]
    rev x6 -> x7, local copies, waits for them, and re-layouts: 1.35 us -> 1.86 us  [flip(): return jnp.flip(v, (1, 2))]
    unnamed x11 -> x13, local copies, waits for them, and re-layouts: 2.84 us -> 2.84 us
  transfers between devices with their start and end apart: 4 -> 4, of which waited for: 2 -> 2; matrix products, arithmetic and copies ran while one was open for 20% -> 28% of each run, Pallas kernels for 0% -> 0%
where the time goes in v21:
time: 64.5 us; the launch traced here: 64.2 us
  local copies, waits for them, and re-layouts  21.4 us (33%)
  matrix products  14.1 us (22%)
  blocking collectives  8.79 us (14%)
  other arithmetic  7.84 us (12%)
  waiting for transfers between devices  5.89 us (9%)
  starting transfers between devices  5.49 us (9%)
    all_gather x1, blocking collectives, local(): every = lax.all_gather(both, ('dp', 'mp'), axis=0, tiled=True)  8.79 us
    conv_general_dilated x4, matrix products, conv(): lax.conv_general_dilated(act, weight, (1, 1), ((1, 1), (1, 1)), dimension...  7.66 us
    conv_general_dilated x4, matrix products, conv_flipped(): lax.conv_general_dilated(flipped, weight, (1, 1), ((1, 1), (1, 1)), dimen...  5.57 us
    select_n x1, other arithmetic, local(): jnp.where(lane == 0, jnp.concatenate([own, other], 1), jnp.concatenate([o...  4.95 us
    ppermute x1, waiting for transfers between devices, local(): lax.ppermute(jnp.where(lower, c0, a_last), 'pipe', [(1, 0), (pipe_size -...  4.79 us
    reshape x1, local copies, waits for them, and re-layouts, local(): return grad.reshape(1, -1)  4.57 us
    another operation x1, local copies, waits for them, and re-layouts, local(): section_weight[0].reshape(2, chan_half, 9, channels).transpose(0, 2, 1, 3)  4.48 us
    ppermute x2, starting transfers between devices, up(): return lax.ppermute(v, 'pipe', pairs)  3.68 us
  transfers between devices with their start and end apart: 4, of which 2 were waited for; matrix products, arithmetic and copies ran while one was open for 28% of the time, Pallas kernels for 0%

profile of v21, /device:TPU:0, one launch (start us, length us, event | category | flops | bytes accessed | tf_op | source)
XLA Modules:
  0.0 64.2 jit_solution(7434430004186134854)
XLA Ops:
  0.0 2.7 %reshape.100 = bf16[921600]{0:T(1024)(128)(2,1)S(1)} reshape(bf16[1,2,460800]{2,1,0:T(2,128)(2,1)} %param.10) | data formatting | bytes 3686400
  2.7 4.5 %reshape_squeeze.3 = bf16[2,160,9,320]{3,2,1,0:T(8,128)(2,1)} reshape(bf16[921600]{0:T(1024)(128)(2,1)S(1)} %reshape.100) | data formatting | bytes 3686400 | tf_op jit(solution)/shard_map/reshape;squeeze | solution.py:82
  7.2 2.7 %copy.72 = bf16[2,9,160,320]{3,2,1,0:T(8,128)(2,1)S(1)} copy(bf16[2,9,160,320]{3,1,2,0:T(8,128)(2,1)} %bitcast.141) | data formatting | bytes 3686400 | tf_op jit(solution)/shard_map/transpose | solution.py:82
  9.8 0.5 collective-permute-start
  10.7 2.6 %conditional.3 = (f32[2,4,16,160]{3,1,2,0:T(4,128)S(1)}, f32[2,4,16,320]{3,1,2,0:T(4,128)S(1)}) conditional(s32[]{:T(128)} %convert_element_type.83, () %tuple.30, (bf16[2,160,3,3,320]{4,1,3,2,0:T(8,128)(2,1)S(1)}, bf16[2,4,16,320]{3,1,2,0:T(4,128)(2,1)S(1)}, bf16[2,4,16,320]{3,1,2,0:T(4,128)(2,1)S(1)}, s32[]{:T(128)}) %tuple.54), branch_computations={%region_0.1_spmd, %region_1.2_spmd} | conditional | flops 295925760 | bytes 5914902 | solution.py:60
  10.9 0.2 dynamic-slice_bitcast_fusion
  11.2 0.2 fusion.7
  11.7 0.2 fusion.4
  11.9 0.5 convolution_select_fusion.1
  12.5 0.5 convolution_select_fusion
  13.1 0.1 copy.64
  13.3 1.1 %collective-permute-done = bf16[2,160,3,3,320]{4,1,3,2,0:T(8,128)(2,1)} collective-permute-done((bf16[2,160,3,3,320]{4,1,3,2,0:T(8,128)(2,1)S(1)}, bf16[2,160,3,3,320]{4,1,3,2,0:T(8,128)(2,1)}, u32[]{:S(2)}, u32[]{:S(2)}) %collective-permute-start) | collective-permute-done | bytes 1843232 | tf_op jit(solution)/shard_map/ppermute | solution.py:85
  14.4 2.7 %conditional.4 = (bf16[2,4,16,320]{3,1,2,0:T(4,128)(2,1)S(1)}) conditional(s32[]{:T(128)} %convert_element_type.83, () %tuple.29, (bf16[2,4,16,320]{3,1,2,0:T(4,128)(2,1)S(1)}, s32[]{:T(128)}, bf16[2,160,3,3,320]{4,1,3,2,0:T(8,128)(2,1)}, bf16[2,4,16,320]{3,1,2,0:T(4,128)(2,1)S(1)}, f32[2,4,16,160]{3,1,2,0:T(4,128)S(1)}) %tuple.32), branch_computations={%region_2.3_spmd, %region_3.4_spmd} | conditional | flops 148346880 | bytes 3082772 | solution.py:60
  14.7 0.2 fusion.12
  15.0 1.8 %convolution_select_fusion.2 = f32[4,16,3,160]{3,1,2,0:T(8,128)S(1)} fusion(bf16[2,160,3,3,320]{4,1,3,2,0:T(8,128)(2,1)} %get-tuple-element.63, bf16[4,2,8,5,320]{4,1,3,2,0:T(2,128)(2,1)S(1)} %fusion.12, pred[16,3]{0,1:T(4,128)(4,1)} %constant.95), kind=kOutput, calls=%fused_computation.18 | convolution fusion | flops 147486720 | bytes 1434112 | tf_op jit(solution)/shard_map/cond/branch_1_fun/conv_general_dilated | solution.py:13
  16.8 0.1 copy.68
  16.9 0.2 fusion.16
  17.1 2.2 %collective-permute-start.1 = (bf16[2,4,16,320]{3,1,2,0:T(4,128)(2,1)S(1)}, bf16[2,4,16,320]{3,1,2,0:T(4,128)(2,1)S(1)}, u32[]{:S(2)}, u32[]{:S(2)}) collective-permute-start(bf16[2,4,16,320]{3,1,2,0:T(4,128)(2,1)S(1)} %get-tuple-element.119), channel_id=1, source_target_pairs={{0,4},{12,8},{1,5},{13,9},{2,6},{14,10},{3,7},{15,11},{16,20},{28,... | collective-permute-start | bytes 245768 | tf_op jit(solution)/shard_map/ppermute | solution.py:89
  19.3 3.0 %conditional.5 = (f32[2,4,16,320]{3,1,2,0:T(4,128)S(1)}) conditional(s32[]{:T(128)} %convert_element_type.83, () %tuple.33, (bf16[2,4,16,320]{3,1,2,0:T(4,128)(2,1)S(1)}, s32[]{:T(128)}, bf16[2,160,3,3,320]{4,1,3,2,0:T(8,128)(2,1)}, f32[2,4,16,320]{3,1,2,0:T(4,128)S(1)}) %tuple.34), branch_computations={%region_4.5_spmd, %region_5.6_spmd} | conditional | flops 147865600 | bytes 3548744 | solution.py:60
  19.5 0.1 dynamic-slice_bitcast_fusion.1
  19.8 0.2 fusion.20
  20.0 1.8 %convolution_select_fusion.3 = f32[4,16,3,320]{3,1,2,0:T(8,128)S(1)} fusion(bf16[2,160,3,3,320]{4,1,3,2,0:T(8,128)(2,1)} %get-tuple-element.67, bf16[4,2,8,5,160]{4,1,3,2,0:T(2,128)(2,1)S(1)} %fusion.20, pred[16,3]{0,1:T(4,128)(4,1)} %constant.94), kind=kOutput, calls=%fused_computation.30 | convolution fusion | flops 147517440 | bytes 1454592 | tf_op jit(solution)/shard_map/cond/branch_1_fun/conv_general_dilated | solution.py:31
  22.0 0.3 rev.24
  22.3 1.5 %collective-permute-start.2 = (f32[2,4,16,320]{3,1,2,0:T(4,128)S(1)}, f32[2,4,16,320]{3,1,2,0:T(4,128)S(1)}, u32[]{:S(2)}, u32[]{:S(2)}) collective-permute-start(f32[2,4,16,320]{3,1,2,0:T(4,128)S(1)} %get-tuple-element.120), channel_id=1, source_target_pairs={{0,4},{12,8},{1,5},{13,9},{2,6},{14,10},{3,7},{15,11},{16,20},{28,... | collective-permute-start | bytes 491528 | tf_op jit(solution)/shard_map/ppermute | solution.py:89
  23.8 5.0 %maximum_select_fusion.1 = bf16[2,320,3,3,320]{4,1,3,2,0:T(8,128)(2,1)} fusion(bf16[2,160,3,3,320]{4,1,3,2,0:T(8,128)(2,1)} %collective-permute-done, bf16[2,160,3,3,320]{4,1,3,2,0:T(8,128)(2,1)S(1)} %bitcast.144, pred[]{:T(512)S(6)} %eq.12), kind=kLoop, calls=%fused_computation.40 | loop fusion | flops 16588800 | bytes 7372801 | tf_op jit(solution)/shard_map/jit(_where)/select_n | solution.py:128
  28.8 0.2 fusion.81
  29.0 0.3 rev.33
  29.4 2.6 %fusion.29 = f32[4,16,3,320]{3,1,2,0:T(8,128)S(1)} fusion(bf16[2,320,3,3,320]{4,1,3,2,0:T(8,128)(2,1)} %maximum_select_fusion.1, bf16[4,2,7,2,320]{4,2,1,3,0:T(8,128)(2,1)S(1)} %slice.51, bf16[4,2,8,3,320]{4,2,1,3,0:T(8,128)(2,1)S(1)} %copy.79, pred[16,3]{0,1:T(4,128)(4,1)S(1)} %copy-done.2), kind=kOutput, calls=%fused_computation.49 | convolution fusion | flops 295587840 | bytes 2652208 | tf_op jit(solution)/shard_map/conv_general_dilated | solution.py:13
  32.2 0.2 fusion.73
  32.4 0.3 rev.32
  33.0 2.7 %fusion.27 = f32[4,16,3,320]{3,1,2,0:T(8,128)S(1)} fusion(bf16[2,320,3,3,320]{4,1,3,2,0:T(8,128)(2,1)} %maximum_select_fusion.1, bf16[4,2,7,2,320]{4,2,1,3,0:T(8,128)(2,1)S(1)} %slice.54, bf16[4,2,8,3,320]{4,2,1,3,0:T(8,128)(2,1)S(1)} %copy.82, pred[16,3]{0,1:T(4,128)(4,1)S(1)} %copy-done.2), kind=kOutput, calls=%fused_computation.47 | convolution fusion | flops 295587840 | bytes 2652208 | tf_op jit(solution)/shard_map/conv_general_dilated | solution.py:13
  35.8 0.2 fusion.111
  36.1 0.3 rev.34
  36.4 0.3 rev.31
  36.8 2.5 %fusion.28 = f32[4,16,3,320]{3,1,2,0:T(8,128)S(1)} fusion(bf16[2,320,3,3,320]{4,1,3,2,0:T(8,128)(2,1)} %maximum_select_fusion.1, bf16[4,2,7,2,320]{4,2,1,3,0:T(8,128)(2,1)S(1)} %slice.57, bf16[4,2,8,3,320]{4,2,1,3,0:T(8,128)(2,1)S(1)} %copy.85, pred[16,3]{0,1:T(4,128)(4,1)S(1)} %copy-done.2), kind=kOutput, calls=%fused_computation.48 | convolution fusion | flops 295587840 | bytes 2652208 | tf_op jit(solution)/shard_map/conv_general_dilated | solution.py:31
  39.7 0.7 %fusion.30 = f32[4,16,3,320]{3,1,2,0:T(8,128)S(1)} fusion(bf16[2,320,3,3,320]{4,1,3,2,0:T(8,128)(2,1)S(1)} %bitcast.146, bf16[4,2,7,2,320]{4,2,1,3,0:T(8,128)(2,1)S(1)} %slice.59, bf16[4,2,8,3,320]{4,2,1,3,0:T(8,128)(2,1)S(1)} %copy.88, pred[16,3]{0,1:T(4,128)(4,1)S(1)} %copy-done.2), kind=kOutput, calls=%fused_computation.50 | convolution fusion | flops 295587840 | bytes 2703872 | tf_op jit(solution)/shard_map/conv_general_dilated | solution.py:31
  40.7 0.3 rev.35
  41.0 0.2 fusion.90
  41.1 1.3 %collective-permute-start.3 = (bf16[2,4,16,320]{3,1,2,0:T(4,128)(2,1)S(1)}, bf16[2,4,16,320]{3,1,2,0:T(4,128)(2,1)S(1)}, u32[]{:S(2)}, u32[]{:S(2)}) collective-permute-start(bf16[2,4,16,320]{3,1,2,0:T(4,128)(2,1)S(1)} %fusion.90), channel_id=1, source_target_pairs={{4,0},{8,12},{5,1},{9,13},{6,2},{10,14},{7,3},{11,15},{20,16},{24,... | collective-permute-start | bytes 245768 | tf_op jit(solution)/shard_map/ppermute | solution.py:189
  42.6 0.3 rev.36
  42.9 4.8 %collective-permute-done.3 = bf16[2,4,16,320]{3,1,2,0:T(4,128)(2,1)S(1)} collective-permute-done((bf16[2,4,16,320]{3,1,2,0:T(4,128)(2,1)S(1)}, bf16[2,4,16,320]{3,1,2,0:T(4,128)(2,1)S(1)}, u32[]{:S(2)}, u32[]{:S(2)}) %collective-permute-start.3) | collective-permute-done | bytes 81952 | tf_op jit(solution)/shard_map/ppermute | solution.py:189
  47.7 0.4 fusion.97
  48.1 0.1 pad_maximum_fusion
  48.3 8.8 %all_gather.3 = bf16[8,4,16,640]{3,2,1,0:T(8,128)(2,1)S(1)} all-gather(bf16[2,4,16,640]{3,2,1,0:T(8,128)(2,1)S(1)} %copy.90), channel_id=1, replica_groups=mesh['groups'=2,'pipe'=4,'dp'=2,'mp'=2] {'dp','mp'}, dimensions={0}, use_global_device_ids=true | all-gather | bytes 819200 | tf_op jit(solution)/shard_map/all_gather | solution.py:197
  57.1 0.2 constant_dynamic-slice_fusion
  57.3 0.9 %fusion.35 = f32[160,3,3,320]{3,0,2,1:T(8,128)S(1)} fusion(bf16[8,4,16,320]{3,2,1,0:T(8,128)(2,1)S(1)} %slice.61, bf16[8,4,16,160]{3,2,1,0:T(8,128)(2,1)S(1)} %constant_dynamic-slice_fusion), kind=kOutput, calls=%fused_computation.56 | convolution fusion | flops 376832000 | bytes 2334720 | tf_op jit(solution)/shard_map/conv_general_dilated | solution.py:39
  58.1 1.5 %copy.93 = f32[160,3,3,320]{3,2,1,0:T(4,128)S(1)} copy(f32[160,3,3,320]{3,0,2,1:T(8,128)S(1)} %fusion.35) | data formatting | bytes 3686400 | tf_op jit(solution)/shard_map/conv_general_dilated | solution.py:39
  59.7 4.6 %reshape.19 = f32[1,460800]{1,0:T(1,128)} reshape(f32[160,3,3,320]{3,2,1,0:T(4,128)S(1)} %copy.93) | data formatting | bytes 3686400 | tf_op jit(solution)/shard_map/reshape | solution.py:201
  (63 shorter events, 3.2 us)
Async XLA Ops:
  7.2 3.2 %copy-start = (bf16[1,2,2,4,16,320]{5,4,3,2,1,0:T(8,128)(2,1)S(1)}, bf16[1,2,2,4,16,320]{5,4,3,2,1,0:T(8,128)(2,1)}, u32[]{:S(2)}) copy-start(bf16[1,2,2,4,16,320]{5,4,3,2,1,0:T(8,128)(2,1)} %param.9) | copy-start | bytes 491524
  7.2 3.3 %copy-start.1 = (bf16[1,2,2,4,16,320]{5,4,3,2,1,0:T(8,128)(2,1)S(1)}, bf16[1,2,2,4,16,320]{5,4,3,2,1,0:T(8,128)(2,1)}, u32[]{:S(2)}) copy-start(bf16[1,2,2,4,16,320]{5,4,3,2,1,0:T(8,128)(2,1)} %param.11) | copy-start | bytes 491524
  9.8 4.6 %collective-permute-start = (bf16[2,160,3,3,320]{4,1,3,2,0:T(8,128)(2,1)S(1)}, bf16[2,160,3,3,320]{4,1,3,2,0:T(8,128)(2,1)}, u32[]{:S(2)}, u32[]{:S(2)}) collective-permute-start(bf16[2,160,3,3,320]{4,1,3,2,0:T(8,128)(2,1)S(1)} %bitcast.142), channel_id=1, source_target_pairs={{0,1},{1,0},{2,3},{3,2},{4,5},{5,4},{6,7},{7,6},{8,9},{9,8},{10,11... | collective-permute-start | bytes 5529608 | tf_op jit(solution)/shard_map/ppermute | solution.py:85
  10.7 1.2 %copy-start.3 = (pred[16,3]{0,1:T(4,128)(4,1)S(1)}, pred[16,3]{0,1:T(4,128)(4,1)}, u32[]{:S(2)}) copy-start(pred[16,3]{0,1:T(4,128)(4,1)} %constant.96) | copy-start | bytes 148 | tf_op jit(solution)/shard_map/cond
  17.1 11.6 %collective-permute-start.1 = (bf16[2,4,16,320]{3,1,2,0:T(4,128)(2,1)S(1)}, bf16[2,4,16,320]{3,1,2,0:T(4,128)(2,1)S(1)}, u32[]{:S(2)}, u32[]{:S(2)}) collective-permute-start(bf16[2,4,16,320]{3,1,2,0:T(4,128)(2,1)S(1)} %get-tuple-element.119), channel_id=1, source_target_pairs={{0,4},{12,8},{1,5},{13,9},{2,6},{14,10},{3,7},{15,11},{16,20},{28,... | collective-permute-start | bytes 245768 | tf_op jit(solution)/shard_map/ppermute | solution.py:89
  22.3 7.1 %copy-start.2 = (pred[16,3]{0,1:T(4,128)(4,1)S(1)}, pred[16,3]{0,1:T(4,128)(4,1)}, u32[]{:S(2)}) copy-start(pred[16,3]{0,1:T(4,128)(4,1)} %constant.90) | copy-start | bytes 148
  22.3 13.5 %collective-permute-start.2 = (f32[2,4,16,320]{3,1,2,0:T(4,128)S(1)}, f32[2,4,16,320]{3,1,2,0:T(4,128)S(1)}, u32[]{:S(2)}, u32[]{:S(2)}) collective-permute-start(f32[2,4,16,320]{3,1,2,0:T(4,128)S(1)} %get-tuple-element.120), channel_id=1, source_target_pairs={{0,4},{12,8},{1,5},{13,9},{2,6},{14,10},{3,7},{15,11},{16,20},{28,... | collective-permute-start | bytes 491528 | tf_op jit(solution)/shard_map/ppermute | solution.py:89
  33.0 6.7 %slice-start = ((s8[4423680]{0:T(1024)(128)(4,1)}), s8[229376]{0:T(1024)(128)(4,1)S(1)}, s32[]{:S(2)}) async-start(s8[4423680]{0:T(1024)(128)(4,1)} %bitcast.145), calls=%async_computation | async-start | bytes 458752
  36.7 3.0 %slice-start.1 = ((s8[4423680]{0:T(1024)(128)(4,1)}), s8[4194304]{0:T(1024)(128)(4,1)S(1)}, s32[]{:S(2)}) async-start(s8[4423680]{0:T(1024)(128)(4,1)} %bitcast.145), calls=%async_computation.1 | async-start | bytes 8388608
  41.1 6.5 %collective-permute-start.3 = (bf16[2,4,16,320]{3,1,2,0:T(4,128)(2,1)S(1)}, bf16[2,4,16,320]{3,1,2,0:T(4,128)(2,1)S(1)}, u32[]{:S(2)}, u32[]{:S(2)}) collective-permute-start(bf16[2,4,16,320]{3,1,2,0:T(4,128)(2,1)S(1)} %fusion.90), channel_id=1, source_target_pairs={{4,0},{8,12},{5,1},{9,13},{6,2},{10,14},{7,3},{11,15},{20,16},{24,... | collective-permute-start | bytes 245768 | tf_op jit(solution)/shard_map/ppermute | solution.py:189

commit v22 on v20

--- a/solution.py
+++ b/solution.py
@@ -118,7 +118,7 @@
         d_other = conv_flipped(lax.dynamic_slice_in_dim(flipped, high, chan_half, 3), other_dec)
         return jnp.flip(d_own + d_other, (1, 2))
 
-    h1_own, d_own = on_stage(stage == 0, first_own, a0, seed, own)
+    h1_own, d_own = first_own(a0, seed, own)
     h1 = on_stage(stage == 0, first_h1, x0, a0, other[0], h1_own)
     h1_r = up(0, h1)
     d_last = on_stage(stage == 0, first_d, seed, other[1], d_own)

time: 61.1 us -> 62.8 us (1.028)
  local copies, waits for them, and re-layouts: 20.8 us -> 21.8 us
    rev x1, local copies, waits for them, and re-layouts: 0.33 us -> 1.44 us  [first_d(): return jnp.flip(d_own + d_other, (1, 2))]
    convert_element_type x6, other arithmetic: 1.03 us -> 1.68 us  [bf16(): return v.astype(jnp.bfloat16)]
where the time goes in v22:
time: 62.8 us; the launch traced here: 62.5 us
  local copies, waits for them, and re-layouts  21.8 us (35%)
  matrix products  12.3 us (20%)
  blocking collectives  8.81 us (14%)
  waiting for transfers between devices  6.75 us (11%)
  other arithmetic  6.73 us (11%)
  starting transfers between devices  5.45 us (9%)
    all_gather x1, blocking collectives, local(): every = lax.all_gather(both, ('dp', 'mp'), axis=0, tiled=True)  8.81 us
    ppermute x1, waiting for transfers between devices, local(): lax.ppermute(jnp.where(lower, c0, a_last), 'pipe', [(1, 0), (pipe_size -...  5.09 us
    conv_general_dilated x2, matrix products, conv_t(): lax.conv_general_dilated(flipped, weight, (1, 1), ((1, 1), (1, 1)), dimen...  4.75 us
    reshape x1, local copies, waits for them, and re-layouts, local(): return grad.reshape(1, -1)  4.57 us
    another operation x1, local copies, waits for them, and re-layouts, local(): section_weight[0].reshape(2, chan_half, 9, channels).transpose(0, 2, 1, 3)  4.5 us
    conv_general_dilated x4, matrix products, conv(): lax.conv_general_dilated(act, weight, (1, 1), ((1, 1), (1, 1)), dimension...  4.36 us
    ppermute x2, starting transfers between devices, up(): return lax.ppermute(v, 'pipe', pairs)  3.64 us
    select_n x1, other arithmetic, local(): jnp.where(lane == 0, jnp.concatenate([own, other], 1), jnp.concatenate([o...  3.6 us
  transfers between devices with their start and end apart: 4, of which 2 were waited for; matrix products, arithmetic and copies ran while one was open for 20% of the time, Pallas kernels for 0%

profile of v22, /device:TPU:0, one launch (start us, length us, event | category | flops | bytes accessed | tf_op | source)
XLA Modules:
  0.0 62.5 jit_solution(13975734162400904185)
XLA Ops:
  0.0 2.7 %reshape.100 = bf16[921600]{0:T(1024)(128)(2,1)S(1)} reshape(bf16[1,2,460800]{2,1,0:T(2,128)(2,1)} %param.8) | data formatting | bytes 3686400
  2.7 4.5 %reshape_squeeze.3 = bf16[2,160,9,320]{3,2,1,0:T(8,128)(2,1)} reshape(bf16[921600]{0:T(1024)(128)(2,1)S(1)} %reshape.100) | data formatting | bytes 3686400 | tf_op jit(solution)/shard_map/reshape;squeeze | solution.py:82
  7.2 2.7 %copy.66 = bf16[2,9,160,320]{3,2,1,0:T(8,128)(2,1)S(1)} copy(bf16[2,9,160,320]{3,1,2,0:T(8,128)(2,1)} %bitcast.127) | data formatting | bytes 3686400 | tf_op jit(solution)/shard_map/transpose | solution.py:82
  9.9 0.5 collective-permute-start
  10.5 0.1 fusion.65
  10.9 0.3 rev.25
  11.4 0.5 convolution_select_fusion.3
  11.9 0.1 copy.69
  12.1 0.5 convolution_select_fusion.2
  12.6 0.1 copy.74
  12.8 1.7 %collective-permute-done = bf16[2,160,3,3,320]{4,1,3,2,0:T(8,128)(2,1)} collective-permute-done((bf16[2,160,3,3,320]{4,1,3,2,0:T(8,128)(2,1)S(1)}, bf16[2,160,3,3,320]{4,1,3,2,0:T(8,128)(2,1)}, u32[]{:S(2)}, u32[]{:S(2)}) %collective-permute-start) | collective-permute-done | bytes 1843232 | tf_op jit(solution)/shard_map/ppermute | solution.py:85
  14.5 3.3 %conditional.2 = (bf16[2,4,16,320]{3,1,2,0:T(4,128)(2,1)}) conditional(s32[]{:T(128)} %convert_element_type.82, () %tuple.21, (bf16[2,4,16,320]{3,1,2,0:T(4,128)(2,1)S(1)}, s32[]{:T(128)}, bf16[2,160,3,3,320]{4,1,3,2,0:T(8,128)(2,1)}, bf16[2,4,16,320]{3,1,2,0:T(4,128)(2,1)S(1)}, f32[2,4,16,160]{3,1,2,0:T(4,128)S(1)}) %tuple.22), branch_computations={%region_0.1_spmd, %region_1.2_spmd} | conditional | flops 148346880 | bytes 3082772 | solution.py:60
  14.7 0.2 fusion.2
  15.0 1.8 %convolution_select_fusion = f32[4,16,3,160]{3,1,2,0:T(8,128)S(1)} fusion(bf16[2,160,3,3,320]{4,1,3,2,0:T(8,128)(2,1)} %get-tuple-element.51, bf16[4,2,8,5,320]{4,1,3,2,0:T(2,128)(2,1)S(1)} %fusion.2, pred[16,3]{0,1:T(4,128)(4,1)} %constant.90), kind=kOutput, calls=%fused_computation | convolution fusion | flops 147486720 | bytes 1434112 | tf_op jit(solution)/shard_map/cond/branch_1_fun/conv_general_dilated | solution.py:13
  16.8 0.1 copy.62
  16.9 0.9 %fusion.6 = bf16[2,4,16,320]{3,1,2,0:T(4,128)(2,1)} fusion(f32[2,4,16,160]{3,1,2,0:T(4,128)S(1)} %slice_bitcast_fusion, f32[2,4,16,160]{3,1,2,0:T(4,128)S(1)} %get-tuple-element.49, bf16[2,4,16,320]{3,1,2,0:T(4,128)(2,1)S(1)} %get-tuple-element.47, pred[]{:T(512)S(6)} %eq.3), kind=kLoop, calls=%fused_computation.9 | loop fusion | flops 245760 | bytes 327681 | tf_op jit(solution)/shard_map/cond/branch_1_fun/convert_element_type | solution.py:51
  17.8 2.2 %collective-permute-start.1 = (bf16[2,4,16,320]{3,1,2,0:T(4,128)(2,1)}, bf16[2,4,16,320]{3,1,2,0:T(4,128)(2,1)S(1)}, u32[]{:S(2)}, u32[]{:S(2)}) collective-permute-start(bf16[2,4,16,320]{3,1,2,0:T(4,128)(2,1)} %get-tuple-element.91), channel_id=1, source_target_pairs={{0,4},{12,8},{1,5},{13,9},{2,6},{14,10},{3,7},{15,11},{16,20},{28,... | collective-permute-start | bytes 245768 | tf_op jit(solution)/shard_map/ppermute | solution.py:89
  20.0 4.1 %conditional.3 = (f32[2,4,16,320]{3,1,2,0:T(4,128)}) conditional(s32[]{:T(128)} %convert_element_type.82, () %tuple.23, (bf16[2,4,16,320]{3,1,2,0:T(4,128)(2,1)S(1)}, s32[]{:T(128)}, bf16[2,160,3,3,320]{4,1,3,2,0:T(8,128)(2,1)}, f32[2,4,16,320]{3,1,2,0:T(4,128)S(1)}) %tuple.24), branch_computations={%region_2.3_spmd, %region_3.4_spmd} | conditional | flops 147865600 | bytes 3548744 | solution.py:60
  20.2 0.1 dynamic-slice_bitcast_fusion
  20.5 0.2 fusion.10
  20.6 1.8 %convolution_select_fusion.1 = f32[4,16,3,320]{3,1,2,0:T(8,128)S(1)} fusion(bf16[2,160,3,3,320]{4,1,3,2,0:T(8,128)(2,1)} %get-tuple-element.55, bf16[4,2,8,5,160]{4,1,3,2,0:T(2,128)(2,1)S(1)} %fusion.10, pred[16,3]{0,1:T(4,128)(4,1)} %constant.89), kind=kOutput, calls=%fused_computation.12 | convolution fusion | flops 147517440 | bytes 1454592 | tf_op jit(solution)/shard_map/cond/branch_1_fun/conv_general_dilated | solution.py:31
  22.6 1.4 %rev.19 = f32[2,4,16,320]{3,1,2,0:T(4,128)} reverse(f32[2,4,16,320]{3,1,2,0:T(4,128)S(1)} %fusion.9), dimensions={1,2} | reverse | bytes 327680 | tf_op jit(solution)/shard_map/cond/branch_1_fun/jit(_flip)/rev | solution.py:119
  24.1 1.5 %collective-permute-start.2 = (f32[2,4,16,320]{3,1,2,0:T(4,128)}, f32[2,4,16,320]{3,1,2,0:T(4,128)S(1)}, u32[]{:S(2)}, u32[]{:S(2)}) collective-permute-start(f32[2,4,16,320]{3,1,2,0:T(4,128)} %get-tuple-element.92), channel_id=1, source_target_pairs={{0,4},{12,8},{1,5},{13,9},{2,6},{14,10},{3,7},{15,11},{16,20},{28,... | collective-permute-start | bytes 491528 | tf_op jit(solution)/shard_map/ppermute | solution.py:89
  25.5 3.6 %maximum_select_fusion.1 = bf16[2,320,3,3,320]{4,1,3,2,0:T(8,128)(2,1)S(1)} fusion(bf16[2,160,3,3,320]{4,1,3,2,0:T(8,128)(2,1)} %collective-permute-done, bf16[2,160,3,3,320]{4,1,3,2,0:T(8,128)(2,1)S(1)} %bitcast.131, pred[]{:T(512)S(6)} %eq.11), kind=kLoop, calls=%fused_computation.22 | loop fusion | flops 16588800 | bytes 7372801 | tf_op jit(solution)/shard_map/jit(_where)/select_n | solution.py:128
  29.4 1.0 %fusion.19 = f32[4,16,3,320]{3,1,2,0:T(8,128)S(1)} fusion(bf16[2,320,3,3,320]{4,1,3,2,0:T(8,128)(2,1)S(1)} %maximum_select_fusion.1, bf16[4,2,7,2,320]{4,2,1,3,0:T(8,128)(2,1)S(1)} %slice.55, bf16[4,2,8,3,320]{4,2,1,3,0:T(8,128)(2,1)S(1)} %copy.77, pred[16,3]{0,1:T(4,128)(4,1)S(1)} %copy-done.3), kind=kOutput, calls=%fused_computation.31 | convolution fusion | flops 295587840 | bytes 2703872 | tf_op jit(solution)/shard_map/conv_general_dilated | solution.py:13
  30.4 0.1 copy.78
  30.6 0.1 fusion.69
  30.8 1.0 %fusion.17 = f32[4,16,3,320]{3,1,2,0:T(8,128)S(1)} fusion(bf16[2,320,3,3,320]{4,1,3,2,0:T(8,128)(2,1)S(1)} %maximum_select_fusion.1, bf16[4,2,7,2,320]{4,2,1,3,0:T(8,128)(2,1)S(1)} %slice.58, bf16[4,2,8,3,320]{4,2,1,3,0:T(8,128)(2,1)S(1)} %copy.80, pred[16,3]{0,1:T(4,128)(4,1)S(1)} %copy-done.3), kind=kOutput, calls=%fused_computation.29 | convolution fusion | flops 295587840 | bytes 2703872 | tf_op jit(solution)/shard_map/conv_general_dilated | solution.py:13
  31.9 0.1 copy.81
  32.0 0.2 add_convert_fusion.3
  32.2 0.3 rev.26
  32.7 2.4 %fusion.18 = f32[4,16,3,320]{3,1,2,0:T(8,128)S(1)} fusion(bf16[2,320,3,3,320]{4,1,3,2,0:T(8,128)(2,1)} %copy-done, bf16[4,2,7,2,320]{4,2,1,3,0:T(8,128)(2,1)S(1)} %slice.61, bf16[4,2,8,3,320]{4,2,1,3,0:T(8,128)(2,1)S(1)} %copy.83, pred[16,3]{0,1:T(4,128)(4,1)S(1)} %copy-done.3), kind=kOutput, calls=%fused_computation.30 | convolution fusion | flops 295587840 | bytes 2652208 | tf_op jit(solution)/shard_map/conv_general_dilated | solution.py:22
  35.2 0.3 rev.27
  35.5 0.2 add_convert_fusion.1
  35.8 0.3 rev.28
  36.2 2.4 %fusion.20 = f32[4,16,3,320]{3,1,2,0:T(8,128)S(1)} fusion(bf16[2,320,3,3,320]{4,1,3,2,0:T(8,128)(2,1)} %copy-done, bf16[4,2,7,2,320]{4,2,1,3,0:T(8,128)(2,1)S(1)} %slice.63, bf16[4,2,8,3,320]{4,2,1,3,0:T(8,128)(2,1)S(1)} %copy.86, pred[16,3]{0,1:T(4,128)(4,1)S(1)} %copy-done.3), kind=kOutput, calls=%fused_computation.32 | convolution fusion | flops 295587840 | bytes 2652208 | tf_op jit(solution)/shard_map/conv_general_dilated | solution.py:22
  38.6 0.1 copy.87
  38.7 0.3 rev.29
  39.0 0.3 fusion.95
  39.4 1.3 %collective-permute-start.3 = (bf16[2,4,16,320]{3,1,2,0:T(4,128)(2,1)S(1)}, bf16[2,4,16,320]{3,1,2,0:T(4,128)(2,1)S(1)}, u32[]{:S(2)}, u32[]{:S(2)}) collective-permute-start(bf16[2,4,16,320]{3,1,2,0:T(4,128)(2,1)S(1)} %fusion.95), channel_id=1, source_target_pairs={{4,0},{8,12},{5,1},{9,13},{6,2},{10,14},{7,3},{11,15},{20,16},{24,... | collective-permute-start | bytes 245768 | tf_op jit(solution)/shard_map/ppermute | solution.py:186
  40.8 5.1 %collective-permute-done.3 = bf16[2,4,16,320]{3,1,2,0:T(4,128)(2,1)S(1)} collective-permute-done((bf16[2,4,16,320]{3,1,2,0:T(4,128)(2,1)S(1)}, bf16[2,4,16,320]{3,1,2,0:T(4,128)(2,1)S(1)}, u32[]{:S(2)}, u32[]{:S(2)}) %collective-permute-start.3) | collective-permute-done | bytes 81952 | tf_op jit(solution)/shard_map/ppermute | solution.py:186
  45.9 0.4 fusion.102
  46.3 0.1 pad_maximum_fusion
  46.5 8.8 %all_gather.3 = bf16[8,4,16,640]{3,2,1,0:T(8,128)(2,1)S(1)} all-gather(bf16[2,4,16,640]{3,2,1,0:T(8,128)(2,1)S(1)} %copy.88), channel_id=1, replica_groups=mesh['groups'=2,'pipe'=4,'dp'=2,'mp'=2] {'dp','mp'}, dimensions={0}, use_global_device_ids=true | all-gather | bytes 819200 | tf_op jit(solution)/shard_map/all_gather | solution.py:194
  55.3 0.2 constant_dynamic-slice_fusion.1
  55.5 0.9 %fusion.26 = f32[160,3,3,320]{3,0,2,1:T(8,128)S(1)} fusion(bf16[8,4,16,320]{3,2,1,0:T(8,128)(2,1)S(1)} %slice.65, bf16[8,4,16,160]{3,2,1,0:T(8,128)(2,1)S(1)} %constant_dynamic-slice_fusion.1), kind=kOutput, calls=%fused_computation.43 | convolution fusion | flops 376832000 | bytes 2334720 | tf_op jit(solution)/shard_map/conv_general_dilated | solution.py:39
  56.4 1.5 %copy.91 = f32[160,3,3,320]{3,2,1,0:T(4,128)S(1)} copy(f32[160,3,3,320]{3,0,2,1:T(8,128)S(1)} %fusion.26) | data formatting | bytes 3686400 | tf_op jit(solution)/shard_map/conv_general_dilated | solution.py:39
  57.9 4.6 %reshape.19 = f32[1,460800]{1,0:T(1,128)} reshape(f32[160,3,3,320]{3,2,1,0:T(4,128)S(1)} %copy.91) | data formatting | bytes 3686400 | tf_op jit(solution)/shard_map/reshape | solution.py:198
  (52 shorter events, 2.2 us)
Async XLA Ops:
  7.2 3.2 %copy-start.1 = (bf16[1,2,2,4,16,320]{5,4,3,2,1,0:T(8,128)(2,1)S(1)}, bf16[1,2,2,4,16,320]{5,4,3,2,1,0:T(8,128)(2,1)}, u32[]{:S(2)}) copy-start(bf16[1,2,2,4,16,320]{5,4,3,2,1,0:T(8,128)(2,1)} %param.7) | copy-start | bytes 491524
  7.2 3.5 %copy-start.2 = (bf16[1,2,2,4,16,320]{5,4,3,2,1,0:T(8,128)(2,1)S(1)}, bf16[1,2,2,4,16,320]{5,4,3,2,1,0:T(8,128)(2,1)}, u32[]{:S(2)}) copy-start(bf16[1,2,2,4,16,320]{5,4,3,2,1,0:T(8,128)(2,1)} %param.9) | copy-start | bytes 491524
  9.8 1.5 %copy-start.3 = (pred[16,3]{0,1:T(4,128)(4,1)S(1)}, pred[16,3]{0,1:T(4,128)(4,1)}, u32[]{:S(2)}) copy-start(pred[16,3]{0,1:T(4,128)(4,1)} %constant.83) | copy-start | bytes 148
  9.9 4.6 %collective-permute-start = (bf16[2,160,3,3,320]{4,1,3,2,0:T(8,128)(2,1)S(1)}, bf16[2,160,3,3,320]{4,1,3,2,0:T(8,128)(2,1)}, u32[]{:S(2)}, u32[]{:S(2)}) collective-permute-start(bf16[2,160,3,3,320]{4,1,3,2,0:T(8,128)(2,1)S(1)} %bitcast.128), channel_id=1, source_target_pairs={{0,1},{1,0},{2,3},{3,2},{4,5},{5,4},{6,7},{7,6},{8,9},{9,8},{10,11... | collective-permute-start | bytes 5529608 | tf_op jit(solution)/shard_map/ppermute | solution.py:85
  17.8 11.4 %collective-permute-start.1 = (bf16[2,4,16,320]{3,1,2,0:T(4,128)(2,1)}, bf16[2,4,16,320]{3,1,2,0:T(4,128)(2,1)S(1)}, u32[]{:S(2)}, u32[]{:S(2)}) collective-permute-start(bf16[2,4,16,320]{3,1,2,0:T(4,128)(2,1)} %get-tuple-element.91), channel_id=1, source_target_pairs={{0,4},{12,8},{1,5},{13,9},{2,6},{14,10},{3,7},{15,11},{16,20},{28,... | collective-permute-start | bytes 245768 | tf_op jit(solution)/shard_map/ppermute | solution.py:89
  24.1 7.9 %collective-permute-start.2 = (f32[2,4,16,320]{3,1,2,0:T(4,128)}, f32[2,4,16,320]{3,1,2,0:T(4,128)S(1)}, u32[]{:S(2)}, u32[]{:S(2)}) collective-permute-start(f32[2,4,16,320]{3,1,2,0:T(4,128)} %get-tuple-element.92), channel_id=1, source_target_pairs={{0,4},{12,8},{1,5},{13,9},{2,6},{14,10},{3,7},{15,11},{16,20},{28,... | collective-permute-start | bytes 491528 | tf_op jit(solution)/shard_map/ppermute | solution.py:89
  29.1 2.7 %copy-start = (bf16[2,320,3,3,320]{4,1,3,2,0:T(8,128)(2,1)}, bf16[2,320,3,3,320]{4,1,3,2,0:T(8,128)(2,1)S(1)}, u32[]{:S(2)}) copy-start(bf16[2,320,3,3,320]{4,1,3,2,0:T(8,128)(2,1)S(1)} %maximum_select_fusion.1) | copy-start | bytes 11059204
  39.4 6.5 %collective-permute-start.3 = (bf16[2,4,16,320]{3,1,2,0:T(4,128)(2,1)S(1)}, bf16[2,4,16,320]{3,1,2,0:T(4,128)(2,1)S(1)}, u32[]{:S(2)}, u32[]{:S(2)}) collective-permute-start(bf16[2,4,16,320]{3,1,2,0:T(4,128)(2,1)S(1)} %fusion.95), channel_id=1, source_target_pairs={{4,0},{8,12},{5,1},{9,13},{6,2},{10,14},{7,3},{11,15},{20,16},{24,... | collective-permute-start | bytes 245768 | tf_op jit(solution)/shard_map/ppermute | solution.py:186
